TPU v7x, 32 devices: a whole 2x2x4 slice. The times are simulated.
32 devices in a mesh: groups: 2 (over y), wide: 16 (over z, x, core).
Axes of the slice: x: 2, y: 2, z: 4, core: 2. Of those that a mesh axis runs over, the one named last changes fastest.
Arguments:
- epoch_rows: bfloat16 [65536, 256], P(('groups', 'wide')), parts along dimension 0
- row_object: int32 [65536], P(('groups', 'wide')), parts along dimension 0, may hold values from -1 to 127, as said below
- object_slot: int32 [256], P('groups'), parts along dimension 0, may hold values from 0 to 127, as said below
- master: float32 [4, 196608], P('groups'), parts along dimension 0, may hold values from -0.21875 to 0.21875
- momentum: float32 [4, 196608], P('groups'), parts along dimension 0, may hold values from -1.8 to 1.8
- teacher: float32 [4, 196608], P('groups'), parts along dimension 0, may hold values from -0.21875 to 0.21875
Outputs:
- new_master: float32 [4, 196608], P('groups'), parts along dimension 0
- new_momentum: float32 [4, 196608], P('groups'), parts along dimension 0
- new_teacher: float32 [4, 196608], P('groups'), parts along dimension 0
- embeddings: float32 [256, 256], P(('groups', 'wide')), parts along dimension 0
There are 2 independent parts, one for each index of `groups`. A program takes and returns all parts, laid end to end along the dimension named above; each array names one. Nothing has to cross between parts.
Inputs may be any that keep to these rules, and one draw needn't show every extreme that they name: `row_object`: each object has 64 to 256 rows. The rows that one device stores for the objects of one owning device are at most 128, and some owning device gets 128 rows from some device in every draw. `object_slot`: A permutation: the object with slot p is owned by device p // 8 of the wide axis, at place p % 8.
All inputs are finite; a program needn't handle non-finite values.
Results may differ from a plain program's by a relative error of at most 0.01.
Values may be sent and summed in bfloat16 or wider, within the bound.
No kernel may reach another device: no remote copies, remote signals or barrier semaphores. Data moves between devices by JAX's collectives and lax.ppermute only.
A program may use at most 256 MiB of HBM per device.

v0:
```python
import jax
import jax.numpy as jnp
from jax import lax
from jax.sharding import PartitionSpec as P

KER = 3
SEQ = 256


tau_student = 1.0
tau_teacher = 0.5
momentum_rate = 0.9
learn_rate = 0.05
ema_rate = 0.996


def delayed(states, offset):
    length = states.shape[1]
    return jnp.concatenate(
        [jnp.zeros_like(states[:, :offset]), states[:, : length - offset]], axis=1
    )


def advanced(states, offset):
    length = states.shape[1]
    return jnp.concatenate([states[:, offset:], jnp.zeros_like(states[:, :offset])], axis=1)


def silu_slope(values):
    gate_value = jax.nn.sigmoid(values)
    return gate_value * (1.0 + values * (1.0 - gate_value))


def run_network(states, weights):
    stacked_list = []
    preacts = []
    for layer_at in range(weights.shape[0]):
        offset = 4**layer_at
        stacked = jnp.concatenate(
            [delayed(states, tap_index * offset) for tap_index in range(KER)], axis=2
        )
        preact = jnp.dot(
            stacked.reshape(-1, stacked.shape[2]),
            weights[layer_at],
            preferred_element_type=jnp.float32,
        ).reshape(states.shape)
        states = (states.astype(jnp.float32) + jax.nn.silu(preact)).astype(jnp.bfloat16)
        stacked_list.append(stacked)
        preacts.append(preact)
    return (states, stacked_list, preacts)


def route_rows(epoch_rows, row_object, object_slot):
    wide_count = lax.axis_size("wide")
    objects_all = object_slot.shape[0]
    per_dev = objects_all // wide_count
    rows_total = epoch_rows.shape[0]
    feat_width = epoch_rows.shape[1]
    capacity = rows_total // wide_count
    live_rows = row_object >= 0
    safe_object = jnp.maximum(row_object, 0)
    match_table = safe_object[:, None] == jnp.arange(objects_all, dtype=jnp.int32)[None, :]
    slot_of = jnp.sum(jnp.where(match_table, object_slot[None, :], 0), axis=1)
    owner_dev = slot_of // per_dev
    local_place = slot_of % per_dev
    owner_hot = (
        owner_dev[:, None] == jnp.arange(wide_count, dtype=jnp.int32)[None, :]
    ) & live_rows[:, None]
    running = jnp.cumsum(owner_hot.astype(jnp.int32), axis=0)
    send_rank = jnp.sum(jnp.where(owner_hot, running, 0), axis=1) - 1
    send_index = jnp.where(live_rows, owner_dev * capacity + send_rank, rows_total)
    send_rows = jnp.zeros_like(epoch_rows).at[send_index].set(epoch_rows, mode="drop")
    send_code = (
        jnp.full((rows_total,), -1.0, jnp.bfloat16)
        .at[send_index]
        .set(local_place.astype(jnp.bfloat16), mode="drop")
    )
    got_rows, got_code = (
        lax.all_to_all(
            send_rows.reshape(wide_count, capacity, feat_width),
            "wide",
            split_axis=0,
            concat_axis=0,
            tiled=True,
        ),
        lax.all_to_all(
            send_code.reshape(wide_count, capacity), "wide", split_axis=0, concat_axis=0, tiled=True
        ),
    )
    place_code = got_code.reshape(-1).astype(jnp.int32)
    place_hot = place_code[:, None] == jnp.arange(per_dev, dtype=jnp.int32)[None, :]
    arrival = jnp.cumsum(place_hot.astype(jnp.int32), axis=0)
    position = jnp.sum(jnp.where(place_hot, arrival, 0), axis=1) - 1
    counts = jnp.sum(place_hot.astype(jnp.int32), axis=0)
    target = jnp.where(place_code >= 0, place_code * SEQ + position, per_dev * SEQ)
    sequences = (
        jnp.zeros((per_dev * SEQ, feat_width), jnp.bfloat16)
        .at[target]
        .set(got_rows.reshape(-1, feat_width), mode="drop")
    )
    return (sequences.reshape(per_dev, SEQ, feat_width), counts)


def all_reduce_wide(grads):
    wide_count = lax.axis_size("wide")
    layer_total, rows, cols = grads.shape
    piece = rows // wide_count
    blocks = grads.reshape(layer_total, wide_count, piece, cols)
    parts = lax.all_to_all(blocks, "wide", split_axis=1, concat_axis=1, tiled=True)
    mine = jnp.sum(parts, axis=1, keepdims=True)
    whole = lax.all_to_all(
        jnp.broadcast_to(mine, blocks.shape), "wide", split_axis=1, concat_axis=1, tiled=True
    )
    return whole.reshape(layer_total, rows * cols)


def local(epoch_rows, row_object, object_slot, master, momentum, teacher):
    objects_all = object_slot.shape[0]
    feat_width = epoch_rows.shape[1]
    layer_total = master.shape[0]
    student_w = master.astype(jnp.bfloat16).reshape(layer_total, KER * feat_width, feat_width)
    teacher_w = teacher.astype(jnp.bfloat16).reshape(layer_total, KER * feat_width, feat_width)
    sequences, counts = route_rows(epoch_rows, row_object, object_slot)
    valid_mask = (jnp.arange(SEQ, dtype=jnp.int32)[None, :] < counts[:, None]).astype(jnp.float32)[
        :, :, None
    ]
    teacher_out = run_network(sequences, teacher_w)[0]
    student_out, stacked_list, preacts = run_network(sequences, student_w)
    partial_sum = jnp.sum(valid_mask * teacher_out.astype(jnp.float32), axis=(0, 1))
    number = jnp.sum(counts).astype(jnp.float32)
    wide_count = lax.axis_size("wide")
    stats = jnp.concatenate([partial_sum, jnp.full((128,), number, jnp.float32)])
    gathered = lax.all_to_all(
        jnp.broadcast_to(stats[None, :], (wide_count, stats.shape[0])),
        "wide", split_axis=0, concat_axis=0, tiled=True,
    )
    stats_all = jnp.sum(gathered, axis=0)
    total_sum = stats_all[:feat_width]
    count_all = stats_all[feat_width]
    center = total_sum / count_all
    teacher_prob = jax.nn.softmax((teacher_out.astype(jnp.float32) - center) / tau_teacher, axis=-1)
    student_f = student_out.astype(jnp.float32)
    student_prob = jax.nn.softmax(student_f / tau_student, axis=-1)
    embeddings = jnp.sum(valid_mask * student_f, axis=1) / counts.astype(jnp.float32)[:, None]
    upstream = valid_mask * (student_prob - teacher_prob) / (tau_student * objects_all)
    gradients = [None] * layer_total
    for layer_at in reversed(range(layer_total)):
        delta_bf = (upstream * silu_slope(preacts[layer_at])).astype(jnp.bfloat16)
        flat_delta = delta_bf.reshape(-1, feat_width)
        weight_grad = lax.dot_general(
            stacked_list[layer_at].reshape(-1, KER * feat_width),
            flat_delta,
            (((0,), (0,)), ((), ())),
            preferred_element_type=jnp.float32,
        )
        gradients[layer_at] = weight_grad
        if layer_at > 0:
            back_rows = lax.dot_general(
                flat_delta,
                student_w[layer_at],
                (((1,), (1,)), ((), ())),
                preferred_element_type=jnp.float32,
            ).reshape(sequences.shape[0], SEQ, KER, feat_width)
            offset = 4**layer_at
            for tap_index in range(KER):
                upstream = upstream + advanced(back_rows[:, :, tap_index], tap_index * offset)
    stacked_grads = jnp.stack(gradients)
    full_grad = all_reduce_wide(stacked_grads)
    new_momentum = momentum_rate * momentum + full_grad
    new_master = master - learn_rate * new_momentum
    new_teacher = ema_rate * teacher + (1.0 - ema_rate) * new_master
    return (new_master, new_momentum, new_teacher, embeddings)


def solution(mesh):
    in_specs = (
        P(("groups", "wide"), None),
        P(("groups", "wide")),
        P("groups"),
        P("groups", None),
        P("groups", None),
        P("groups", None),
    )
    out_specs = (
        P("groups", None),
        P("groups", None),
        P("groups", None),
        P(("groups", "wide"), None),
    )
    return jax.shard_map(local, mesh=mesh, in_specs=in_specs, out_specs=out_specs, check_vma=False)
```

profile of v0, /device:TPU:0, one launch (start us, length us, event | category | flops | bytes accessed | tf_op | source)
XLA Modules:
  0.0 215.0 jit_solution(12654413529897513360)
XLA Ops:
  2.0 1.3 select_reduce_fusion
  4.1 4.5 %reduce-window.14 = s32[16,16,128]{2,1,0:T(8,128)S(1)} reduce-window(s32[16,16,128]{2,1,0:T(8,128)S(1)} %fusion.69, s32[]{:T(128)} %constant.38.clone.1), window={size=1x1x128 pad=0_0x0_0x127_0}, to_apply=%region_1.2 | reduce-window | flops 4161536 | bytes 262148 | tf_op jit(solution)/shard_map/reduce-window
  10.1 14.6 %scatter_custom_fusion = bf16[2048]{0:T(1024)(128)(2,1)S(1)} fusion(s32[2048]{0:T(1024)S(1)} %get-tuple-element.21, bf16[2048]{0:T(1024)(128)(2,1)S(1)} %get-tuple-element.20, bf16[]{:T(256)} %constant.36.clone.1), kind=kCustom, calls=%fused_computation.130 | custom fusion | bytes 4098 | tf_op jit(solution)/shard_map/scatter | solution.py:76
  25.3 7.4 %all-to-all-start = ((bf16[16,1,128]{2,1,0:T(2,128)(2,1)}), bf16[16,1,128]{2,1,0:T(2,128)(2,1)S(1)}, u32[]{:S(2)}, u32[]{:S(2)}) async-start(bf16[16,1,128]{2,1,0:T(2,128)(2,1)} %copy.78), calls=%async_computation | async-start | bytes 16384 | tf_op jit(solution)/shard_map/all_to_all | solution.py:86
  32.7 1.7 convert_element_type.110
  34.4 10.7 %scatter_custom_fusion.1 = bf16[2048,256]{1,0:T(8,128)(2,1)} fusion(s32[2048]{0:T(1024)S(1)} %get-tuple-element.21, bf16[2048,256]{1,0:T(8,128)(2,1)} %param.6, bf16[]{:T(256)} %constant.32.clone.1), kind=kCustom, calls=%fused_computation.76 | custom fusion | bytes 1049088 | tf_op jit(solution)/shard_map/scatter | solution.py:72
  45.1 6.1 %all-to-all-start.1 = ((bf16[16,128,256]{2,1,0:T(8,128)(2,1)}), bf16[16,128,256]{2,1,0:T(8,128)(2,1)}, u32[]{:S(2)}, u32[]{:S(2)}) async-start(bf16[16,128,256]{2,1,0:T(8,128)(2,1)} %bitcast.11), calls=%async_computation.1 | async-start | bytes 2097152 | tf_op jit(solution)/shard_map/all_to_all | solution.py:79
  51.2 8.3 %slice_reduce_fusion.3 = (bf16[196608]{0:T(1024)(128)(2,1)S(1)}, bf16[196608]{0:T(1024)(128)(2,1)S(1)}) fusion(bf16[2,196608]{1,0:T(2,128)(2,1)S(1)} %convert_element_type.110), kind=kLoop, calls=%fused_computation.73 | loop fusion | bytes 1572864 | tf_op jit(solution)/shard_map/slice | solution.py:44
  61.1 8.3 %slice_reduce_fusion = (bf16[196608]{0:T(1024)(128)(2,1)S(1)}, bf16[196608]{0:T(1024)(128)(2,1)S(1)}) fusion(bf16[2,196608]{1,0:T(2,128)(2,1)S(1)} %convert_element_type.115), kind=kLoop, calls=%fused_computation.70 | loop fusion | bytes 1572864 | tf_op jit(solution)/shard_map/slice | solution.py:44
  69.4 0.9 squeeze.28
  70.2 0.9 reshape.265
  71.2 2.3 %reduce-window.16 = s32[8,16,128]{2,1,0:T(8,128)S(1)} reduce-window(s32[8,16,128]{2,1,0:T(8,128)S(1)} %fusion.72, s32[]{:T(128)} %constant.38.clone.1), window={size=1x1x128 pad=0_0x0_0x127_0}, to_apply=%region_5.6 | reduce-window | flops 2080768 | bytes 131076 | tf_op jit(solution)/shard_map/reduce-window.2
  75.5 10.2 %scatter_custom_fusion.2 = bf16[2048,256]{1,0:T(8,128)(2,1)S(1)} fusion(s32[2048]{0:T(1024)S(1)} %bitcast.140, bf16[2048,256]{1,0:T(8,128)(2,1)} %bitcast.12, bf16[]{:T(256)} %constant.32.clone.1), kind=kCustom, calls=%fused_computation.74 | custom fusion | bytes 1049088 | tf_op jit(solution)/shard_map/scatter | solution.py:99
  85.6 2.5 %fusion.18 = (bf16[8,256,256]{2,1,0:T(8,128)(2,1)S(1)}, f32[8,256,256]{2,1,0:T(8,128)}) fusion(bf16[8,256,256]{2,1,0:T(8,128)(2,1)S(1)} %bitcast.119, bf16[768,256,1]{1,0,2:T(8,128)(2,1)S(1)} %reshape.263, bf16[8,254,256]{2,1,0:T(8,128)(2,1)S(1)} %bitcast.120, bf16[8,255,256]{2,1,0:T(8,128)(2,1)S(1)} %bitcast.121), kind=kOutput, calls=%fused_computation.29 | convolution fusion | flops 827850752 | bytes 6672384 | tf_op jit(solution)/shard_map/dot_general | solution.py:42
  88.2 1.5 fusion.19
  89.9 2.5 %fusion.99 = (bf16[8,256]{1,0:T(8,128)(2,1)S(1)}, bf16[8,256,256]{2,1,0:T(8,128)(2,1)S(1)}, f32[8,256,256]{2,1,0:T(8,128)}) fusion(bf16[8,256,256]{2,1,0:T(8,128)(2,1)S(1)} %get-tuple-element.22, bf16[768,256]{1,0:T(8,128)(2,1)S(1)} %copy-done.7, bf16[8,248,256]{2,1,0:T(8,128)(2,1)S(1)} %slice.98, bf16[8,252,256]{2,1,0:T(8,128)(2,1)S(1)} %bitcast.128), kind=kOutput, calls=%fused_computation.144 | convolution fusion | flops 828372992 | bytes 6639616 | tf_op jit(solution)/shard_map/dot_general | solution.py:42
  92.3 2.9 %fusion.27 = (f32[8,256]{1,0:T(8,128)S(1)}, f32[256]{0:T(256)S(1)}, bf16[8,256,256]{2,1,0:T(8,128)(2,1)}) fusion(bf16[8,256,256]{2,1,0:T(8,128)(2,1)S(1)} %get-tuple-element.17, f32[8,256]{1,0:T(8,128)S(1)} %fusion.77, bf16[768,256]{1,0:T(8,128)(2,1)S(1)} %copy-done.8, bf16[8,248,256]{2,1,0:T(8,128)(2,1)S(1)} %slice.102, ...), kind=kOutput, calls=%fused_computation.37 | convolution fusion | flops 830994176 | bytes 5604352 | tf_op jit(solution)/shard_map/dot_general | solution.py:42
  95.8 5.9 %all-to-all-start.2 = ((f32[16,1,384]{2,1,0:T(1,128)}), f32[16,1,384]{2,1,0:T(1,128)S(1)}, u32[]{:S(2)}, u32[]{:S(2)}) async-start(f32[16,1,384]{2,1,0:T(1,128)} %broadcast_in_dim.43), calls=%async_computation.2 | async-start | bytes 49152 | tf_op jit(solution)/shard_map/all_to_all | solution.py:133
  101.9 6.4 %all-to-all-done.2 = f32[16,1,384]{2,1,0:T(1,128)S(1)} async-done(((f32[16,1,384]{2,1,0:T(1,128)}), f32[16,1,384]{2,1,0:T(1,128)S(1)}, u32[]{:S(2)}, u32[]{:S(2)}) %all-to-all-start.2) | async-done | bytes 24608 | tf_op jit(solution)/shard_map/all_to_all | solution.py:133
  109.6 3.8 %fusion = f32[8,256,256]{2,1,0:T(8,128)} fusion(bf16[8,256,256]{2,1,0:T(8,128)(2,1)} %get-tuple-element.25, f32[256]{0:T(256)S(1)} %slice_divide_fusion), kind=kOutput, calls=%fused_computation.3 | output fusion | flops 3674622 | bytes 3146752 | tf_op jit(solution)/shard_map/div | solution.py:141
  113.3 2.2 %fusion.31 = f32[8,256,256]{2,1,0:T(8,128)S(1)} fusion(bf16[8,256,256]{2,1,0:T(8,128)(2,1)} %get-tuple-element.25, f32[256]{0:T(256)S(1)} %slice_divide_fusion), kind=kOutput, calls=%fused_computation.40 | output fusion | flops 3672319 | bytes 3146752 | tf_op jit(solution)/shard_map/sub | solution.py:141
  115.8 9.4 %multiply_convert_fusion = (bf16[8,256,256]{2,1,0:T(8,128)(2,1)S(1)}, f32[8,256,256]{2,1,0:T(8,128)S(1)}) fusion(f32[8,256,256]{2,1,0:T(8,128)} %get-tuple-element.24, f32[8,256,256]{2,1,0:T(8,128)S(1)} %copy-done.12, f32[8,256,256]{2,1,0:T(8,128)S(1)} %fusion.31, bf16[8,256,256]{2,1,0:T(8,128)(2,1)S(1)} %copy-done.15, f32[8,256]{1,0:T(8,128)S(1)} %reduce_max.24, ...), kind=kOutput, calls=%fused_computation.50 | output fusion | flops 9439487 | bytes 10502144 | tf_op jit(solution)/shard_map/div | solution.py:143
  125.3 1.0 fusion.92
  126.3 1.0 fusion.44
  127.9 1.4 copy-done.13
  129.4 1.6 fusion.49
  131.1 38.7 %all_to_all.30 = f32[2,16,48,256]{3,2,0,1:T(8,128)S(1)} all-to-all(f32[2,16,48,256]{3,2,0,1:T(8,128)S(1)} %pad_maximum_fusion), channel_id=1, replica_groups=mesh['groups'=2,'wide'=16] {'wide'}, dimensions={1} | all-to-all | bytes 3145728 | tf_op jit(solution)/shard_map/all_to_all | solution.py:109
  169.9 1.3 broadcast_in_dim.44
  171.2 4.9 %all-to-all-start.4 = ((f32[2,16,48,256]{3,2,0,1:T(8,128)}), f32[2,16,48,256]{3,2,0,1:T(8,128)S(1)}, u32[]{:S(2)}, u32[]{:S(2)}) async-start(f32[2,16,48,256]{3,2,0,1:T(8,128)} %broadcast_in_dim.44), calls=%async_computation.4 | async-start | bytes 3145728 | tf_op jit(solution)/shard_map/all_to_all | solution.py:111
  176.9 31.3 %all-to-all-done.4 = f32[2,16,48,256]{3,2,0,1:T(8,128)S(1)} async-done(((f32[2,16,48,256]{3,2,0,1:T(8,128)}), f32[2,16,48,256]{3,2,0,1:T(8,128)S(1)}, u32[]{:S(2)}, u32[]{:S(2)}) %all-to-all-start.4) | async-done | bytes 1572896 | tf_op jit(solution)/shard_map/all_to_all | solution.py:111
  208.3 1.2 copy.110
  210.2 4.8 %multiply_add_fusion = (f32[2,196608]{1,0:T(2,128)}, f32[2,196608]{1,0:T(2,128)}, f32[2,196608]{1,0:T(2,128)}) fusion(f32[2,196608]{1,0:T(2,128)S(1)} %copy-done, f32[2,196608]{1,0:T(2,128)S(1)} %copy-done.1, f32[2,196608]{1,0:T(2,128)S(1)} %bitcast.118, f32[2,196608]{1,0:T(2,128)S(1)} %copy-done.2), kind=kLoop, calls=%fused_computation.59 | loop fusion | flops 2752512 | bytes 11010048 | tf_op jit(solution)/shard_map/add | solution.py:171
  (74 shorter events, 11.8 us)
Async XLA Ops:
  25.3 19.8 %all-to-all-start = ((bf16[16,1,128]{2,1,0:T(2,128)(2,1)}), bf16[16,1,128]{2,1,0:T(2,128)(2,1)S(1)}, u32[]{:S(2)}, u32[]{:S(2)}) async-start(bf16[16,1,128]{2,1,0:T(2,128)(2,1)} %copy.78), calls=%async_computation | async-start | bytes 16384 | tf_op jit(solution)/shard_map/all_to_all | solution.py:86
  45.1 30.4 %all-to-all-start.1 = ((bf16[16,128,256]{2,1,0:T(8,128)(2,1)}), bf16[16,128,256]{2,1,0:T(8,128)(2,1)}, u32[]{:S(2)}, u32[]{:S(2)}) async-start(bf16[16,128,256]{2,1,0:T(8,128)(2,1)} %bitcast.11), calls=%async_computation.1 | async-start | bytes 2097152 | tf_op jit(solution)/shard_map/all_to_all | solution.py:79
  51.2 9.3 %copy-start = (f32[2,196608]{1,0:T(2,128)S(1)}, f32[2,196608]{1,0:T(2,128)}, u32[]{:S(2)}) copy-start(f32[2,196608]{1,0:T(2,128)} %param.11) | copy-start | bytes 4718596
  74.7 0.7 copy-start.10
  85.6 2.6 %copy-start.9 = (bf16[768,256,1]{1,0,2:T(8,128)(2,1)S(1)}, bf16[768,256,1]{1,0,2:T(8,128)(2,1)}, u32[]{:S(2)}) copy-start(bf16[768,256,1]{1,0,2:T(8,128)(2,1)} %reshape.265) | copy-start | bytes 1179652
  88.1 1.7 copy-start.5
  88.2 1.6 copy-start.3
  88.2 1.6 copy-start.7
  89.8 2.5 %copy-start.8 = (bf16[768,256]{1,0:T(8,128)(2,1)S(1)}, bf16[768,256]{1,0:T(8,128)(2,1)}, u32[]{:S(2)}) copy-start(bf16[768,256]{1,0:T(8,128)(2,1)} %squeeze.28) | copy-start | bytes 1179652
  92.3 2.9 %copy-start.14 = (bf16[8,256,256]{2,1,0:T(8,128)(2,1)}, bf16[8,256,256]{2,1,0:T(8,128)(2,1)S(1)}, u32[]{:S(2)}) copy-start(bf16[8,256,256]{2,1,0:T(8,128)(2,1)S(1)} %get-tuple-element.17) | copy-start | bytes 3145732
  95.8 12.5 %all-to-all-start.2 = ((f32[16,1,384]{2,1,0:T(1,128)}), f32[16,1,384]{2,1,0:T(1,128)S(1)}, u32[]{:S(2)}, u32[]{:S(2)}) async-start(f32[16,1,384]{2,1,0:T(1,128)} %broadcast_in_dim.43), calls=%async_computation.2 | async-start | bytes 49152 | tf_op jit(solution)/shard_map/all_to_all | solution.py:133
  113.3 2.2 %copy-start.12 = (f32[8,256,256]{2,1,0:T(8,128)S(1)}, f32[8,256,256]{2,1,0:T(8,128)}, u32[]{:S(2)}) copy-start(f32[8,256,256]{2,1,0:T(8,128)} %fusion) | copy-start | bytes 6291460
  113.3 2.5 %copy-start.15 = (bf16[8,256,256]{2,1,0:T(8,128)(2,1)S(1)}, bf16[8,256,256]{2,1,0:T(8,128)(2,1)}, u32[]{:S(2)}) copy-start(bf16[8,256,256]{2,1,0:T(8,128)(2,1)} %copy-done.14) | copy-start | bytes 3145732
  115.8 9.4 %copy-start.4 = (bf16[8,248,256]{2,1,0:T(8,128)(2,1)S(1)}, bf16[8,248,256]{2,1,0:T(8,128)(2,1)}, u32[]{:S(2)}) copy-start(bf16[8,248,256]{2,1,0:T(8,128)(2,1)} %copy-done.3) | copy-start | bytes 3047428
  115.8 9.4 %copy-start.6 = (bf16[8,256,256]{2,1,0:T(8,128)(2,1)S(1)}, bf16[8,256,256]{2,1,0:T(8,128)(2,1)}, u32[]{:S(2)}) copy-start(bf16[8,256,256]{2,1,0:T(8,128)(2,1)} %copy-done.5) | copy-start | bytes 3145732
  127.8 1.6 copy-start.13
  169.9 6.3 %copy-start.11 = (s32[8]{0:T(128)S(1)}, s32[8]{0:T(128)}, u32[]{:S(2)}) copy-start(s32[8]{0:T(128)} %copy-done.10) | copy-start | bytes 100
  171.2 36.9 %all-to-all-start.4 = ((f32[2,16,48,256]{3,2,0,1:T(8,128)}), f32[2,16,48,256]{3,2,0,1:T(8,128)S(1)}, u32[]{:S(2)}, u32[]{:S(2)}) async-start(f32[2,16,48,256]{3,2,0,1:T(8,128)} %broadcast_in_dim.44), calls=%async_computation.4 | async-start | bytes 3145728 | tf_op jit(solution)/shard_map/all_to_all | solution.py:111
  208.3 1.4 copy-start.1
  208.3 1.9 copy-start.2
where the time goes:
time: 219 us; the launch traced here: 215 us
  local copies, waits for them, and re-layouts  63.1 us (29%)
  blocking collectives  38.7 us (18%)
  waiting for transfers between devices  37.7 us (17%)
  other arithmetic  36.4 us (17%)
  starting transfers between devices  24.3 us (11%)
  matrix products  13 us (6%)
    all_to_all x1, blocking collectives, all_reduce_wide(): lax.all_to_all(blocks, 'wide', split_axis=1, concat_axis=1, tiled=True)  38.7 us
    all_to_all x1, waiting for transfers between devices, all_reduce_wide(): lax.all_to_all(jnp.broadcast_to(mine, blocks.shape), 'wide', split_axis=1...  31.3 us
    slice x2, local copies, waits for them, and re-layouts, run_network(): weights[layer_at]  16.6 us
    scatter x1, local copies, waits for them, and re-layouts, route_rows(): send_code = jnp.full((rows_total,), -1.0, jnp.bfloat16).at[send_index].se...  14.6 us
    scatter x1, local copies, waits for them, and re-layouts, route_rows(): jnp.zeros_like(epoch_rows).at[send_index].set(epoch_rows, mode='drop')  10.7 us
    scatter x1, local copies, waits for them, and re-layouts, route_rows(): sequences = jnp.zeros((per_dev * SEQ, feat_width), jnp.bfloat16).at[targe...  10.2 us
    div x1, other arithmetic, local(): student_prob = jax.nn.softmax(student_f / tau_student, axis=-1)  9.42 us
    dot_general x4, matrix products, run_network(): jnp.dot(stacked.reshape(-1, stacked.shape[2]), weights[layer_at], preferr...  9.34 us
  transfers between devices with their start and end apart: 4, of which 2 were waited for; matrix products, arithmetic and copies ran while one was open for 17% of the time, Pallas kernels for 0%

commit v1 on v0

--- a/solution.py
+++ b/solution.py
@@ -103,15 +103,25 @@
 
 def all_reduce_wide(grads):
     wide_count = lax.axis_size("wide")
-    layer_total, rows, cols = grads.shape
-    piece = rows // wide_count
-    blocks = grads.reshape(layer_total, wide_count, piece, cols)
-    parts = lax.all_to_all(blocks, "wide", split_axis=1, concat_axis=1, tiled=True)
-    mine = jnp.sum(parts, axis=1, keepdims=True)
-    whole = lax.all_to_all(
-        jnp.broadcast_to(mine, blocks.shape), "wide", split_axis=1, concat_axis=1, tiled=True
-    )
-    return whole.reshape(layer_total, rows * cols)
+    steps = wide_count.bit_length() - 1
+    assert 1 << steps == wide_count
+    me = lax.axis_index("wide")
+    buf = grads
+    for step in range(steps):
+        bit = (me >> step) & 1
+        half = buf.shape[1] // 2
+        keep = lax.dynamic_slice_in_dim(buf, bit * half, half, axis=1)
+        send = lax.dynamic_slice_in_dim(buf, (1 - bit) * half, half, axis=1)
+        pairs = [(i, i ^ (1 << step)) for i in range(wide_count)]
+        buf = keep + lax.ppermute(send, "wide", pairs)
+    for step in reversed(range(steps)):
+        bit = (me >> step) & 1
+        pairs = [(i, i ^ (1 << step)) for i in range(wide_count)]
+        got = lax.ppermute(buf, "wide", pairs)
+        low = jnp.where(bit == 0, buf, got)
+        high = jnp.where(bit == 0, got, buf)
+        buf = jnp.concatenate([low, high], axis=1)
+    return buf.reshape(buf.shape[0], -1)
 
 
 def local(epoch_rows, row_object, object_slot, master, momentum, teacher):

time: 219 us -> 207 us (0.945); the launches traced: 215 us -> 207 us
  blocking collectives: 38.7 us -> 0 us
  waiting for transfers between devices: 37.7 us -> 53.3 us
  local copies, waits for them, and re-layouts: 63.1 us -> 75 us
  other arithmetic: 36.4 us -> 41.4 us
  starting transfers between devices: 24.3 us -> 21.5 us
    ppermute x0 -> x8, waiting for transfers between devices: none -> 46.8 us  [the longest x4 26.1 us: all_reduce_wide(): buf = keep + lax.ppermute(send, 'wide', pairs)]
    all_to_all x1 -> x0, blocking collectives: 38.7 us -> none  [all_reduce_wide(): lax.all_to_all(blocks, 'wide', split_axis=1, concat_axis=1, tiled=True)]
    all_to_all x1 -> x0, waiting for transfers between devices: 31.3 us -> none  [all_reduce_wide(): lax.all_to_all(jnp.broadcast_to(mine, blocks.shape), 'wide', split_axis=1...]
    scatter x1, local copies, waits for them, and re-layouts: 10.2 us -> 22.5 us  [route_rows(): sequences = jnp.zeros((per_dev * SEQ, feat_width), jnp.bfloat16).at[targe...]
    all_to_all x1 -> x0, starting transfers between devices: 4.93 us -> none  [all_reduce_wide(): lax.all_to_all(jnp.broadcast_to(mine, blocks.shape), 'wide', split_axis=1...]
    add x0 -> x4, other arithmetic: none -> 2.38 us  [all_reduce_wide(): buf = keep + lax.ppermute(send, 'wide', pairs)]
    unnamed x33 -> x29, local copies, waits for them, and re-layouts: 3.62 us -> 4.54 us
  transfers between devices with their start and end apart: 4 -> 11, of which waited for: 2 -> 9; matrix products, arithmetic and copies ran while one was open for 17% -> 18% of each run, Pallas kernels for 0% -> 0%
where the time goes in v1:
time: 207 us
  local copies, waits for them, and re-layouts  75 us (36%)
  waiting for transfers between devices  53.3 us (26%)
  other arithmetic  41.4 us (20%)
  starting transfers between devices  21.5 us (10%)
  matrix products  13.4 us (6%)
    ppermute x4, waiting for transfers between devices, all_reduce_wide(): buf = keep + lax.ppermute(send, 'wide', pairs)  26.1 us
    scatter x1, local copies, waits for them, and re-layouts, route_rows(): sequences = jnp.zeros((per_dev * SEQ, feat_width), jnp.bfloat16).at[targe...  22.5 us
    ppermute x4, waiting for transfers between devices, all_reduce_wide(): got = lax.ppermute(buf, 'wide', pairs)  20.7 us
    slice x2, local copies, waits for them, and re-layouts, run_network(): weights[layer_at]  16.6 us
    scatter x1, local copies, waits for them, and re-layouts, route_rows(): send_code = jnp.full((rows_total,), -1.0, jnp.bfloat16).at[send_index].se...  14.6 us
    div x1, other arithmetic, local(): student_prob = jax.nn.softmax(student_f / tau_student, axis=-1)  11.6 us
    scatter x1, local copies, waits for them, and re-layouts, route_rows(): jnp.zeros_like(epoch_rows).at[send_index].set(epoch_rows, mode='drop')  10.7 us
    dot_general x4, matrix products, run_network(): jnp.dot(stacked.reshape(-1, stacked.shape[2]), weights[layer_at], preferr...  9.83 us
  transfers between devices with their start and end apart: 11, of which 9 were waited for; matrix products, arithmetic and copies ran while one was open for 18% of the time, Pallas kernels for 0%

profile of v1, /device:TPU:0, one launch (start us, length us, event | category | flops | bytes accessed | tf_op | source)
XLA Modules:
  0.0 206.7 jit_solution(14075046255907292595)
XLA Ops:
  2.0 1.3 select_reduce_fusion
  4.1 4.5 %reduce-window.14 = s32[16,16,128]{2,1,0:T(8,128)S(1)} reduce-window(s32[16,16,128]{2,1,0:T(8,128)S(1)} %fusion.71, s32[]{:T(128)} %constant.32.clone.1), window={size=1x1x128 pad=0_0x0_0x127_0}, to_apply=%region_1.2 | reduce-window | flops 4161536 | bytes 262148 | tf_op jit(solution)/shard_map/reduce-window
  10.1 14.6 %scatter_custom_fusion = bf16[2048]{0:T(1024)(128)(2,1)S(1)} fusion(s32[2048]{0:T(1024)S(1)} %get-tuple-element.29, bf16[2048]{0:T(1024)(128)(2,1)S(1)} %get-tuple-element.28, bf16[]{:T(256)} %constant.37.clone.1), kind=kCustom, calls=%fused_computation.155 | custom fusion | bytes 4098 | tf_op jit(solution)/shard_map/scatter | solution.py:76
  25.3 7.4 %all-to-all-start = ((bf16[16,1,128]{2,1,0:T(2,128)(2,1)}), bf16[16,1,128]{2,1,0:T(2,128)(2,1)S(1)}, u32[]{:S(2)}, u32[]{:S(2)}) async-start(bf16[16,1,128]{2,1,0:T(2,128)(2,1)} %copy.70), calls=%async_computation | async-start | bytes 16384 | tf_op jit(solution)/shard_map/all_to_all | solution.py:86
  32.7 1.7 convert_element_type.115
  34.4 10.7 %scatter_custom_fusion.1 = bf16[2048,256]{1,0:T(8,128)(2,1)} fusion(s32[2048]{0:T(1024)S(1)} %get-tuple-element.29, bf16[2048,256]{1,0:T(8,128)(2,1)} %param.6, bf16[]{:T(256)} %constant.36.clone.1), kind=kCustom, calls=%fused_computation.85 | custom fusion | bytes 1049088 | tf_op jit(solution)/shard_map/scatter | solution.py:72
  45.1 6.3 %all-to-all-start.1 = ((bf16[16,128,256]{2,1,0:T(8,128)(2,1)}), bf16[16,128,256]{2,1,0:T(8,128)(2,1)}, u32[]{:S(2)}, u32[]{:S(2)}) async-start(bf16[16,128,256]{2,1,0:T(8,128)(2,1)} %bitcast.11), calls=%async_computation.1 | async-start | bytes 2097152 | tf_op jit(solution)/shard_map/all_to_all | solution.py:79
  51.4 8.3 %slice_reduce_fusion = (bf16[196608]{0:T(1024)(128)(2,1)S(1)}, bf16[196608]{0:T(1024)(128)(2,1)S(1)}) fusion(bf16[2,196608]{1,0:T(2,128)(2,1)S(1)} %convert_element_type.115), kind=kLoop, calls=%fused_computation.78 | loop fusion | bytes 1572864 | tf_op jit(solution)/shard_map/slice | solution.py:44
  61.2 8.3 %slice_reduce_fusion.3 = (bf16[196608]{0:T(1024)(128)(2,1)S(1)}, bf16[196608]{0:T(1024)(128)(2,1)S(1)}) fusion(bf16[2,196608]{1,0:T(2,128)(2,1)S(1)} %convert_element_type.110), kind=kLoop, calls=%fused_computation.81 | loop fusion | bytes 1572864 | tf_op jit(solution)/shard_map/slice | solution.py:44
  71.4 2.3 %reduce-window.16 = s32[8,16,128]{2,1,0:T(8,128)S(1)} reduce-window(s32[8,16,128]{2,1,0:T(8,128)S(1)} %fusion.74, s32[]{:T(128)} %constant.32.clone.1), window={size=1x1x128 pad=0_0x0_0x127_0}, to_apply=%region_5.6 | reduce-window | flops 2080768 | bytes 131076 | tf_op jit(solution)/shard_map/reduce-window.2
  75.7 22.5 %scatter_custom_fusion.2 = bf16[2048,256]{1,0:T(8,128)(2,1)S(1)} fusion(s32[2048]{0:T(1024)S(1)} %bitcast.133, bf16[2048,256]{1,0:T(8,128)(2,1)} %bitcast.12, bf16[]{:T(256)} %constant.36.clone.1), kind=kCustom, calls=%fused_computation.83 | custom fusion | bytes 1049088 | tf_op jit(solution)/shard_map/scatter | solution.py:99
  98.3 2.9 %fusion.19 = bf16[8,256,256]{2,1,0:T(8,128)(2,1)S(1)} fusion(bf16[8,256,256]{2,1,0:T(8,128)(2,1)S(1)} %bitcast.114, bf16[768,256,1]{1,0,2:T(8,128)(2,1)} %reshape.259, bf16[8,254,256]{2,1,0:T(8,128)(2,1)S(1)} %bitcast.115, bf16[8,255,256]{2,1,0:T(8,128)(2,1)S(1)} %bitcast.116), kind=kOutput, calls=%fused_computation.30 | convolution fusion | flops 827850752 | bytes 4575232 | tf_op jit(solution)/shard_map/dot_general | solution.py:42
  101.3 2.5 %fusion.18 = (bf16[8,256,256]{2,1,0:T(8,128)(2,1)S(1)}, f32[8,256,256]{2,1,0:T(8,128)}) fusion(bf16[8,256,256]{2,1,0:T(8,128)(2,1)S(1)} %bitcast.117, bf16[768,256,1]{1,0,2:T(8,128)(2,1)S(1)} %copy-done.11, bf16[8,254,256]{2,1,0:T(8,128)(2,1)S(1)} %bitcast.118, bf16[8,255,256]{2,1,0:T(8,128)(2,1)S(1)} %bitcast.119), kind=kOutput, calls=%fused_computation.29 | convolution fusion | flops 827850752 | bytes 6672384 | tf_op jit(solution)/shard_map/dot_general | solution.py:42
  103.9 2.5 %fusion.100 = (bf16[8,256]{1,0:T(8,128)(2,1)S(1)}, bf16[8,256,256]{2,1,0:T(8,128)(2,1)S(1)}, f32[8,256,256]{2,1,0:T(8,128)}) fusion(bf16[8,256,256]{2,1,0:T(8,128)(2,1)S(1)} %get-tuple-element.30, bf16[768,256]{1,0:T(8,128)(2,1)S(1)} %copy-done.10, bf16[8,248,256]{2,1,0:T(8,128)(2,1)S(1)} %slice.98, bf16[8,252,256]{2,1,0:T(8,128)(2,1)S(1)} %bitcast.123), kind=kOutput, calls=%fused_computation.168 | convolution fusion | flops 828372992 | bytes 6639616 | tf_op jit(solution)/shard_map/dot_general | solution.py:42
  106.4 2.0 fusion.27
  109.0 6.1 %all-to-all-start.2 = ((f32[16,1,384]{2,1,0:T(1,128)}), f32[16,1,384]{2,1,0:T(1,128)S(1)}, u32[]{:S(2)}, u32[]{:S(2)}) async-start(f32[16,1,384]{2,1,0:T(1,128)} %broadcast_in_dim.41), calls=%async_computation.2 | async-start | bytes 49152 | tf_op jit(solution)/shard_map/all_to_all | solution.py:143
  115.2 6.4 %all-to-all-done.2 = f32[16,1,384]{2,1,0:T(1,128)S(1)} async-done(((f32[16,1,384]{2,1,0:T(1,128)}), f32[16,1,384]{2,1,0:T(1,128)S(1)}, u32[]{:S(2)}, u32[]{:S(2)}) %all-to-all-start.2) | async-done | bytes 24608 | tf_op jit(solution)/shard_map/all_to_all | solution.py:143
  122.8 1.9 fusion.31
  124.7 2.2 %fusion = f32[8,256,256]{2,1,0:T(8,128)} fusion(bf16[8,256,256]{2,1,0:T(8,128)(2,1)S(1)} %get-tuple-element.33, f32[256]{0:T(256)S(1)} %slice_divide_fusion), kind=kOutput, calls=%fused_computation.3 | output fusion | flops 3674622 | bytes 3146752 | tf_op jit(solution)/shard_map/div | solution.py:151
  126.9 11.6 %multiply_convert_fusion = (bf16[8,256,256]{2,1,0:T(8,128)(2,1)S(1)}, f32[8,256,256]{2,1,0:T(8,128)S(1)}) fusion(f32[8,256,256]{2,1,0:T(8,128)} %get-tuple-element.32, f32[8,256,256]{2,1,0:T(8,128)} %fusion, f32[8,256,256]{2,1,0:T(8,128)} %fusion.31, bf16[8,256,256]{2,1,0:T(8,128)(2,1)} %copy-done.13, f32[8,256]{1,0:T(8,128)S(1)} %reduce_max.24, ...), kind=kOutput, calls=%fused_computation.50 | output fusion | flops 9439487 | bytes 10502144 | tf_op jit(solution)/shard_map/div | solution.py:153
  143.0 1.6 convolution_bitcast_fusion.1
  145.5 2.6 %collective-permute-done = f32[2,384,256]{2,1,0:T(8,128)} collective-permute-done((f32[2,384,256]{2,1,0:T(8,128)}, f32[2,384,256]{2,1,0:T(8,128)}, u32[]{:S(2)}, u32[]{:S(2)}) %collective-permute-start) | collective-permute-done | bytes 786464 | tf_op jit(solution)/shard_map/ppermute | solution.py:116
  148.1 1.3 fusion.54
  150.8 10.8 %collective-permute-done.1 = f32[2,192,256]{2,1,0:T(8,128)S(1)} collective-permute-done((f32[2,192,256]{2,1,0:T(8,128)S(1)}, f32[2,192,256]{2,1,0:T(8,128)S(1)}, u32[]{:S(2)}, u32[]{:S(2)}) %collective-permute-start.1) | collective-permute-done | bytes 393248 | tf_op jit(solution)/shard_map/ppermute | solution.py:116
  163.1 5.7 %collective-permute-done.2 = f32[2,96,256]{2,1,0:T(8,128)S(1)} collective-permute-done((f32[2,96,256]{2,1,0:T(8,128)S(1)}, f32[2,96,256]{2,1,0:T(8,128)S(1)}, u32[]{:S(2)}, u32[]{:S(2)}) %collective-permute-start.2) | collective-permute-done | bytes 196640 | tf_op jit(solution)/shard_map/ppermute | solution.py:116
  169.4 7.0 %collective-permute-done.3 = f32[2,48,256]{2,1,0:T(8,128)S(1)} collective-permute-done((f32[2,48,256]{2,1,0:T(8,128)S(1)}, f32[2,48,256]{2,1,0:T(8,128)S(1)}, u32[]{:S(2)}, u32[]{:S(2)}) %collective-permute-start.3) | collective-permute-done | bytes 98336 | tf_op jit(solution)/shard_map/ppermute | solution.py:116
  176.5 5.6 %collective-permute-done.4 = f32[2,48,256]{2,1,0:T(8,128)S(1)} collective-permute-done((f32[2,48,256]{2,1,0:T(8,128)S(1)}, f32[2,48,256]{2,1,0:T(8,128)S(1)}, u32[]{:S(2)}, u32[]{:S(2)}) %collective-permute-start.4) | collective-permute-done | bytes 98336 | tf_op jit(solution)/shard_map/ppermute | solution.py:120
  182.2 5.7 %collective-permute-done.5 = f32[2,96,256]{2,1,0:T(8,128)S(1)} collective-permute-done((f32[2,96,256]{2,1,0:T(8,128)S(1)}, f32[2,96,256]{2,1,0:T(8,128)S(1)}, u32[]{:S(2)}, u32[]{:S(2)}) %collective-permute-start.5) | collective-permute-done | bytes 196640 | tf_op jit(solution)/shard_map/ppermute | solution.py:120
  188.0 7.8 %collective-permute-done.6 = f32[2,192,256]{2,1,0:T(8,128)S(1)} collective-permute-done((f32[2,192,256]{2,1,0:T(8,128)S(1)}, f32[2,192,256]{2,1,0:T(8,128)S(1)}, u32[]{:S(2)}, u32[]{:S(2)}) %collective-permute-start.6) | collective-permute-done | bytes 393248 | tf_op jit(solution)/shard_map/ppermute | solution.py:120
  196.7 1.7 collective-permute-done.7
  198.4 1.3 broadcast_select_fusion.1
  201.7 4.8 %multiply_add_fusion = (f32[2,196608]{1,0:T(2,128)}, f32[2,196608]{1,0:T(2,128)}, f32[2,196608]{1,0:T(2,128)}) fusion(f32[2,196608]{1,0:T(2,128)S(1)} %copy-done, f32[2,196608]{1,0:T(2,128)S(1)} %copy-done.1, f32[2,196608]{1,0:T(2,128)S(1)} %bitcast.113, f32[2,196608]{1,0:T(2,128)S(1)} %copy-done.3), kind=kLoop, calls=%fused_computation.63 | loop fusion | flops 2752512 | bytes 11010048 | tf_op jit(solution)/shard_map/add | solution.py:181
  (95 shorter events, 23.0 us)
Async XLA Ops:
  25.3 19.8 %all-to-all-start = ((bf16[16,1,128]{2,1,0:T(2,128)(2,1)}), bf16[16,1,128]{2,1,0:T(2,128)(2,1)S(1)}, u32[]{:S(2)}, u32[]{:S(2)}) async-start(bf16[16,1,128]{2,1,0:T(2,128)(2,1)} %copy.70), calls=%async_computation | async-start | bytes 16384 | tf_op jit(solution)/shard_map/all_to_all | solution.py:86
  45.1 30.6 %all-to-all-start.1 = ((bf16[16,128,256]{2,1,0:T(8,128)(2,1)}), bf16[16,128,256]{2,1,0:T(8,128)(2,1)}, u32[]{:S(2)}, u32[]{:S(2)}) async-start(bf16[16,128,256]{2,1,0:T(8,128)(2,1)} %bitcast.11), calls=%async_computation.1 | async-start | bytes 2097152 | tf_op jit(solution)/shard_map/all_to_all | solution.py:79
  51.4 9.2 %copy-start.1 = (f32[2,196608]{1,0:T(2,128)S(1)}, f32[2,196608]{1,0:T(2,128)}, u32[]{:S(2)}) copy-start(f32[2,196608]{1,0:T(2,128)} %param.9) | copy-start | bytes 4718596
  98.3 3.0 %copy-start.4 = (bf16[2048,256]{1,0:T(8,128)(2,1)}, bf16[2048,256]{1,0:T(8,128)(2,1)S(1)}, u32[]{:S(2)}) copy-start(bf16[2048,256]{1,0:T(8,128)(2,1)S(1)} %scatter_custom_fusion.2) | copy-start | bytes 3145732
  98.3 3.0 %copy-start.11 = (bf16[768,256,1]{1,0,2:T(8,128)(2,1)S(1)}, bf16[768,256,1]{1,0,2:T(8,128)(2,1)}, u32[]{:S(2)}) copy-start(bf16[768,256,1]{1,0,2:T(8,128)(2,1)} %reshape.257) | copy-start | bytes 1179652
  101.3 2.6 %copy-start.10 = (bf16[768,256]{1,0:T(8,128)(2,1)S(1)}, bf16[768,256]{1,0:T(8,128)(2,1)}, u32[]{:S(2)}) copy-start(bf16[768,256]{1,0:T(8,128)(2,1)} %squeeze.26) | copy-start | bytes 1179652
  103.8 2.6 %copy-start.8 = (bf16[8,256,256]{2,1,0:T(8,128)(2,1)}, bf16[8,256,256]{2,1,0:T(8,128)(2,1)S(1)}, u32[]{:S(2)}) copy-start(bf16[8,256,256]{2,1,0:T(8,128)(2,1)S(1)} %get-tuple-element.30) | copy-start | bytes 3145732
  103.8 2.5 %copy-start.6 = (bf16[8,248,256]{2,1,0:T(8,128)(2,1)}, bf16[8,248,256]{2,1,0:T(8,128)(2,1)S(1)}, u32[]{:S(2)}) copy-start(bf16[8,248,256]{2,1,0:T(8,128)(2,1)S(1)} %slice.98) | copy-start | bytes 3047428
  106.3 2.0 copy-start.13
  109.0 12.7 %all-to-all-start.2 = ((f32[16,1,384]{2,1,0:T(1,128)}), f32[16,1,384]{2,1,0:T(1,128)S(1)}, u32[]{:S(2)}, u32[]{:S(2)}) async-start(f32[16,1,384]{2,1,0:T(1,128)} %broadcast_in_dim.41), calls=%async_computation.2 | async-start | bytes 49152 | tf_op jit(solution)/shard_map/all_to_all | solution.py:143
  126.9 11.6 %copy-start.7 = (bf16[8,248,256]{2,1,0:T(8,128)(2,1)S(1)}, bf16[8,248,256]{2,1,0:T(8,128)(2,1)}, u32[]{:S(2)}) copy-start(bf16[8,248,256]{2,1,0:T(8,128)(2,1)} %copy-done.6) | copy-start | bytes 3047428
  126.9 11.6 %copy-start.9 = (bf16[8,256,256]{2,1,0:T(8,128)(2,1)S(1)}, bf16[8,256,256]{2,1,0:T(8,128)(2,1)}, u32[]{:S(2)}) copy-start(bf16[8,256,256]{2,1,0:T(8,128)(2,1)} %copy-done.8) | copy-start | bytes 3145732
  141.1 1.2 copy-start.5
  141.1 1.9 copy-start.12
  145.5 2.6 %collective-permute-start = (f32[2,384,256]{2,1,0:T(8,128)}, f32[2,384,256]{2,1,0:T(8,128)}, u32[]{:S(2)}, u32[]{:S(2)}) collective-permute-start(f32[2,384,256]{2,1,0:T(8,128)} %fusion.52), channel_id=1, source_target_pairs={{0,1},{1,0},{2,3},{3,2},{4,5},{5,4},{6,7},{7,6},{8,9},{9,8},{10,11... | collective-permute-start | bytes 2359304 | tf_op jit(solution)/shard_map/ppermute | solution.py:116
  149.4 0.9 copy-start.2
  150.3 11.2 %collective-permute-start.1 = (f32[2,192,256]{2,1,0:T(8,128)S(1)}, f32[2,192,256]{2,1,0:T(8,128)S(1)}, u32[]{:S(2)}, u32[]{:S(2)}) collective-permute-start(f32[2,192,256]{2,1,0:T(8,128)S(1)} %constant_dynamic-slice_fusion.1), channel_id=1, source_target_pairs={{0,2},{1,3},{2,0},{3,1},{4,6},{5,7},{6,4},{7,5},{8,10},{9,11},{10,... | collective-permute-start | bytes 1179656 | tf_op jit(solution)/shard_map/ppermute | solution.py:116
  162.6 6.2 %collective-permute-start.2 = (f32[2,96,256]{2,1,0:T(8,128)S(1)}, f32[2,96,256]{2,1,0:T(8,128)S(1)}, u32[]{:S(2)}, u32[]{:S(2)}) collective-permute-start(f32[2,96,256]{2,1,0:T(8,128)S(1)} %constant_dynamic-slice_fusion), channel_id=1, source_target_pairs={{0,4},{1,5},{2,6},{3,7},{4,0},{5,1},{6,2},{7,3},{8,12},{9,13},{10,... | collective-permute-start | bytes 589832 | tf_op jit(solution)/shard_map/ppermute | solution.py:116
  168.9 7.5 %collective-permute-start.3 = (f32[2,48,256]{2,1,0:T(8,128)S(1)}, f32[2,48,256]{2,1,0:T(8,128)S(1)}, u32[]{:S(2)}, u32[]{:S(2)}) collective-permute-start(f32[2,48,256]{2,1,0:T(8,128)S(1)} %constant_dynamic-slice_fusion.2), channel_id=1, source_target_pairs={{0,8},{1,9},{2,10},{3,11},{4,12},{5,13},{6,14},{7,15},{8,0},{9,1},... | collective-permute-start | bytes 294920 | tf_op jit(solution)/shard_map/ppermute | solution.py:116
  176.4 5.7 %collective-permute-start.4 = (f32[2,48,256]{2,1,0:T(8,128)S(1)}, f32[2,48,256]{2,1,0:T(8,128)S(1)}, u32[]{:S(2)}, u32[]{:S(2)}) collective-permute-start(f32[2,48,256]{2,1,0:T(8,128)S(1)} %dynamic-slice_add_fusion.2), channel_id=1, source_target_pairs={{0,8},{1,9},{2,10},{3,11},{4,12},{5,13},{6,14},{7,15},{8,0},{9,1},... | collective-permute-start | bytes 294920 | tf_op jit(solution)/shard_map/ppermute | solution.py:120
  182.1 5.7 %collective-permute-start.5 = (f32[2,96,256]{2,1,0:T(8,128)S(1)}, f32[2,96,256]{2,1,0:T(8,128)S(1)}, u32[]{:S(2)}, u32[]{:S(2)}) collective-permute-start(f32[2,96,256]{2,1,0:T(8,128)S(1)} %pad_maximum_fusion.2), channel_id=1, source_target_pairs={{0,4},{1,5},{2,6},{3,7},{4,0},{5,1},{6,2},{7,3},{8,12},{9,13},{10,... | collective-permute-start | bytes 589832 | tf_op jit(solution)/shard_map/ppermute | solution.py:120
  188.0 7.8 %collective-permute-start.6 = (f32[2,192,256]{2,1,0:T(8,128)S(1)}, f32[2,192,256]{2,1,0:T(8,128)S(1)}, u32[]{:S(2)}, u32[]{:S(2)}) collective-permute-start(f32[2,192,256]{2,1,0:T(8,128)S(1)} %pad_maximum_fusion.1), channel_id=1, source_target_pairs={{0,2},{1,3},{2,0},{3,1},{4,6},{5,7},{6,4},{7,5},{8,10},{9,11},{10,... | collective-permute-start | bytes 1179656 | tf_op jit(solution)/shard_map/ppermute | solution.py:120
  195.9 2.5 %collective-permute-start.7 = (f32[2,384,256]{2,1,0:T(8,128)S(1)}, f32[2,384,256]{2,1,0:T(8,128)}, u32[]{:S(2)}, u32[]{:S(2)}) collective-permute-start(f32[2,384,256]{2,1,0:T(8,128)S(1)} %pad_maximum_fusion), channel_id=1, source_target_pairs={{0,1},{1,0},{2,3},{3,2},{4,5},{5,4},{6,7},{7,6},{8,9},{9,8},{10,11... | collective-permute-start | bytes 2359304 | tf_op jit(solution)/shard_map/ppermute | solution.py:120
  199.8 1.4 copy-start
  199.8 1.9 copy-start.3

commit v2 on v1

--- a/solution.py
+++ b/solution.py
@@ -128,8 +128,8 @@
     objects_all = object_slot.shape[0]
     feat_width = epoch_rows.shape[1]
     layer_total = master.shape[0]
-    student_w = master.astype(jnp.bfloat16).reshape(layer_total, KER * feat_width, feat_width)
-    teacher_w = teacher.astype(jnp.bfloat16).reshape(layer_total, KER * feat_width, feat_width)
+    student_w = lax.optimization_barrier(master.reshape(layer_total, KER * feat_width, feat_width)).astype(jnp.bfloat16)
+    teacher_w = lax.optimization_barrier(teacher.reshape(layer_total, KER * feat_width, feat_width)).astype(jnp.bfloat16)
     sequences, counts = route_rows(epoch_rows, row_object, object_slot)
     valid_mask = (jnp.arange(SEQ, dtype=jnp.int32)[None, :] < counts[:, None]).astype(jnp.float32)[
         :, :, None

time: 207 us -> 210 us (1.014)
  local copies, waits for them, and re-layouts: 75 us -> 50.4 us
  waiting for transfers between devices: 53.3 us -> 68 us
  other arithmetic: 41.4 us -> 50 us
  matrix products: 13.4 us -> 16.2 us
    all_to_all x1, waiting for transfers between devices: 0.01 us -> 16.7 us  [route_rows(): lax.all_to_all(send_rows.reshape(wide_count, capacity, feat_width), 'wide...]
    slice x2 -> x1, local copies, waits for them, and re-layouts: 16.6 us -> 1.02 us  [run_network(): weights[layer_at]]
    scatter x1, local copies, waits for them, and re-layouts: 22.5 us -> 10.7 us  [route_rows(): sequences = jnp.zeros((per_dev * SEQ, feat_width), jnp.bfloat16).at[targe...]
    unnamed x29 -> x51, local copies, waits for them, and re-layouts: 4.54 us -> 8.85 us
    dot_general x4, matrix products: 9.83 us -> 12.6 us  [run_network(): jnp.dot(stacked.reshape(-1, stacked.shape[2]), weights[layer_at], preferr...]
    squeeze x4 -> x0, local copies, waits for them, and re-layouts: 2.78 us -> none  [run_network(): weights[layer_at]]
    convert_element_type x2 -> x0, other arithmetic: 2.28 us -> none  [the longest x1 1.71 us: local(): teacher.astype(jnp.bfloat16)]
    select_n x4, other arithmetic: 1.39 us -> 3.52 us  [all_reduce_wide(): low = jnp.where(bit == 0, buf, got)]
  transfers between devices with their start and end apart: 11 -> 11, of which waited for: 9 -> 10; matrix products, arithmetic and copies ran while one was open for 18% -> 9% of each run, Pallas kernels for 0% -> 0%
where the time goes in v2:
time: 210 us; the launch traced here: 209 us
  waiting for transfers between devices  68 us (32%)
  local copies, waits for them, and re-layouts  50.4 us (24%)
  other arithmetic  50 us (24%)
  starting transfers between devices  22.6 us (11%)
  matrix products  16.2 us (8%)
    ppermute x4, waiting for transfers between devices, all_reduce_wide(): buf = keep + lax.ppermute(send, 'wide', pairs)  25.5 us
    ppermute x4, waiting for transfers between devices, all_reduce_wide(): got = lax.ppermute(buf, 'wide', pairs)  20.8 us
    all_to_all x1, waiting for transfers between devices, route_rows(): lax.all_to_all(send_rows.reshape(wide_count, capacity, feat_width), 'wide...  16.7 us
    scatter x1, local copies, waits for them, and re-layouts, route_rows(): send_code = jnp.full((rows_total,), -1.0, jnp.bfloat16).at[send_index].se...  14.6 us
    dot_general x4, matrix products, run_network(): jnp.dot(stacked.reshape(-1, stacked.shape[2]), weights[layer_at], preferr...  12.6 us
    div x1, other arithmetic, local(): student_prob = jax.nn.softmax(student_f / tau_student, axis=-1)  11.6 us
    scatter x1, local copies, waits for them, and re-layouts, route_rows(): jnp.zeros_like(epoch_rows).at[send_index].set(epoch_rows, mode='drop')  10.7 us
    scatter x1, local copies, waits for them, and re-layouts, route_rows(): sequences = jnp.zeros((per_dev * SEQ, feat_width), jnp.bfloat16).at[targe...  10.7 us
  transfers between devices with their start and end apart: 11, of which 10 were waited for; matrix products, arithmetic and copies ran while one was open for 9% of the time, Pallas kernels for 0%

profile of v2, /device:TPU:0, one launch (start us, length us, event | category | flops | bytes accessed | tf_op | source)
XLA Modules:
  0.0 209.0 jit_solution(8783772235882020910)
XLA Ops:
  2.0 1.3 select_reduce_fusion
  4.1 4.5 %reduce-window.14 = s32[16,16,128]{2,1,0:T(8,128)S(1)} reduce-window(s32[16,16,128]{2,1,0:T(8,128)S(1)} %fusion.70, s32[]{:T(128)} %constant.32.clone.1), window={size=1x1x128 pad=0_0x0_0x127_0}, to_apply=%region_1.2 | reduce-window | flops 4161536 | bytes 262148 | tf_op jit(solution)/shard_map/reduce-window
  10.1 14.6 %scatter_custom_fusion = bf16[2048]{0:T(1024)(128)(2,1)S(1)} fusion(s32[2048]{0:T(1024)S(1)} %get-tuple-element.25, bf16[2048]{0:T(1024)(128)(2,1)S(1)} %get-tuple-element.24, bf16[]{:T(256)} %constant.37.clone.1), kind=kCustom, calls=%fused_computation.155 | custom fusion | bytes 4098 | tf_op jit(solution)/shard_map/scatter | solution.py:76
  25.3 7.4 %all-to-all-start = ((bf16[16,1,128]{2,1,0:T(2,128)(2,1)}), bf16[16,1,128]{2,1,0:T(2,128)(2,1)S(1)}, u32[]{:S(2)}, u32[]{:S(2)}) async-start(bf16[16,1,128]{2,1,0:T(2,128)(2,1)} %copy.72), calls=%async_computation | async-start | bytes 16384 | tf_op jit(solution)/shard_map/all_to_all | solution.py:86
  32.7 10.7 %scatter_custom_fusion.1 = bf16[2048,256]{1,0:T(8,128)(2,1)} fusion(s32[2048]{0:T(1024)S(1)} %get-tuple-element.25, bf16[2048,256]{1,0:T(8,128)(2,1)} %param.6, bf16[]{:T(256)} %constant.36.clone.1), kind=kCustom, calls=%fused_computation.83 | custom fusion | bytes 1049088 | tf_op jit(solution)/shard_map/scatter | solution.py:72
  43.4 6.2 %all-to-all-start.1 = ((bf16[16,128,256]{2,1,0:T(8,128)(2,1)}), bf16[16,128,256]{2,1,0:T(8,128)(2,1)}, u32[]{:S(2)}, u32[]{:S(2)}) async-start(bf16[16,128,256]{2,1,0:T(8,128)(2,1)} %bitcast.139), calls=%async_computation.1 | async-start | bytes 2097152 | tf_op jit(solution)/shard_map/all_to_all | solution.py:79
  51.5 2.3 %reduce-window.16 = s32[8,16,128]{2,1,0:T(8,128)S(1)} reduce-window(s32[8,16,128]{2,1,0:T(8,128)S(1)} %fusion.73, s32[]{:T(128)} %constant.32.clone.1), window={size=1x1x128 pad=0_0x0_0x127_0}, to_apply=%region_5.6 | reduce-window | flops 2080768 | bytes 131076 | tf_op jit(solution)/shard_map/reduce-window.2
  55.8 16.7 %all-to-all-done.1 = bf16[16,128,256]{2,1,0:T(8,128)(2,1)} async-done(((bf16[16,128,256]{2,1,0:T(8,128)(2,1)}), bf16[16,128,256]{2,1,0:T(8,128)(2,1)}, u32[]{:S(2)}, u32[]{:S(2)}) %all-to-all-start.1) | async-done | bytes 1048608 | tf_op jit(solution)/shard_map/all_to_all | solution.py:79
  72.6 10.7 %scatter_custom_fusion.2 = bf16[2048,256]{1,0:T(8,128)(2,1)} fusion(s32[2048]{0:T(1024)S(1)} %bitcast.165, bf16[2048,256]{1,0:T(8,128)(2,1)} %bitcast.12, bf16[]{:T(256)} %constant.36.clone.1), kind=kCustom, calls=%fused_computation.81 | custom fusion | bytes 1049088 | tf_op jit(solution)/shard_map/scatter | solution.py:99
  83.2 4.2 %fusion.19 = bf16[8,256,256]{2,1,0:T(8,128)(2,1)S(1)} fusion(bf16[8,256,256]{2,1,0:T(8,128)(2,1)} %bitcast.144, bf16[2,768,256]{2,1,0:T(8,128)(2,1)} %bitcast.156, bf16[8,254,256]{2,1,0:T(8,128)(2,1)} %bitcast.145, bf16[8,255,256]{2,1,0:T(8,128)(2,1)} %bitcast.146), kind=kOutput, calls=%fused_computation.30 | convolution fusion | flops 827850752 | bytes 5636096 | tf_op jit(solution)/shard_map/dot_general | solution.py:42
  87.5 2.5 %fusion.18 = (bf16[8,256,256]{2,1,0:T(8,128)(2,1)S(1)}, f32[8,256,256]{2,1,0:T(8,128)}) fusion(bf16[8,256,256]{2,1,0:T(8,128)(2,1)S(1)} %bitcast.147, bf16[2,768,256]{2,1,0:T(8,128)(2,1)S(1)} %bitcast.141, bf16[8,254,256]{2,1,0:T(8,128)(2,1)S(1)} %bitcast.148, bf16[8,255,256]{2,1,0:T(8,128)(2,1)S(1)} %bitcast.149), kind=kOutput, calls=%fused_computation.29 | convolution fusion | flops 827850752 | bytes 7733248 | tf_op jit(solution)/shard_map/dot_general | solution.py:42
  90.1 3.1 %fusion.99 = (bf16[8,256]{1,0:T(8,128)(2,1)}, bf16[8,256,256]{2,1,0:T(8,128)(2,1)S(1)}, f32[8,256,256]{2,1,0:T(8,128)}) fusion(bf16[8,256,256]{2,1,0:T(8,128)(2,1)S(1)} %get-tuple-element.26, bf16[2,768,256]{2,1,0:T(8,128)(2,1)S(1)} %bitcast.142, bf16[8,248,256]{2,1,0:T(8,128)(2,1)S(1)} %slice.94, bf16[8,252,256]{2,1,0:T(8,128)(2,1)S(1)} %bitcast.153), kind=kOutput, calls=%fused_computation.168 | convolution fusion | flops 828372992 | bytes 7704576 | tf_op jit(solution)/shard_map/dot_general | solution.py:42
  93.2 2.9 %fusion.27 = (f32[8,256]{1,0:T(8,128)S(1)}, f32[256]{0:T(256)S(1)}, bf16[8,256,256]{2,1,0:T(8,128)(2,1)}) fusion(bf16[8,256,256]{2,1,0:T(8,128)(2,1)S(1)} %get-tuple-element.13, f32[8,256]{1,0:T(8,128)S(1)} %fusion.78, bf16[2,768,256]{2,1,0:T(8,128)(2,1)S(1)} %bitcast.157, bf16[8,248,256]{2,1,0:T(8,128)(2,1)S(1)} %slice.98, ...), kind=kOutput, calls=%fused_computation.37 | convolution fusion | flops 830994176 | bytes 6669312 | tf_op jit(solution)/shard_map/dot_general | solution.py:42
  96.7 6.9 %all-to-all-start.2 = ((f32[16,1,384]{2,1,0:T(1,128)}), f32[16,1,384]{2,1,0:T(1,128)}, u32[]{:S(2)}, u32[]{:S(2)}) async-start(f32[16,1,384]{2,1,0:T(1,128)} %broadcast_in_dim.41), calls=%async_computation.2 | async-start | bytes 49152 | tf_op jit(solution)/shard_map/all_to_all | solution.py:143
  105.4 4.9 %all-to-all-done.2 = f32[16,1,384]{2,1,0:T(1,128)} async-done(((f32[16,1,384]{2,1,0:T(1,128)}), f32[16,1,384]{2,1,0:T(1,128)}, u32[]{:S(2)}, u32[]{:S(2)}) %all-to-all-start.2) | async-done | bytes 24608 | tf_op jit(solution)/shard_map/all_to_all | solution.py:143
  110.3 1.4 reduce_sum.100
  112.9 1.3 slice_divide_fusion
  114.7 3.4 %fusion.31 = f32[8,256,256]{2,1,0:T(8,128)} fusion(bf16[8,256,256]{2,1,0:T(8,128)(2,1)} %get-tuple-element.29, f32[256]{0:T(256)S(1)} %slice_divide_fusion), kind=kOutput, calls=%fused_computation.40 | output fusion | flops 3672319 | bytes 3146752 | tf_op jit(solution)/shard_map/sub | solution.py:151
  118.2 3.8 %fusion = f32[8,256,256]{2,1,0:T(8,128)} fusion(bf16[8,256,256]{2,1,0:T(8,128)(2,1)} %get-tuple-element.29, f32[256]{0:T(256)} %copy-done.21), kind=kOutput, calls=%fused_computation.3 | output fusion | flops 3674622 | bytes 3146752 | tf_op jit(solution)/shard_map/div | solution.py:151
  121.9 11.6 %multiply_convert_fusion = (bf16[8,256,256]{2,1,0:T(8,128)(2,1)S(1)}, f32[8,256,256]{2,1,0:T(8,128)S(1)}) fusion(f32[8,256,256]{2,1,0:T(8,128)} %get-tuple-element.28, f32[8,256,256]{2,1,0:T(8,128)} %fusion, f32[8,256,256]{2,1,0:T(8,128)} %fusion.31, bf16[8,256,256]{2,1,0:T(8,128)(2,1)} %copy-done.23, f32[8,256]{1,0:T(8,128)S(1)} %reduce_max.24, ...), kind=kOutput, calls=%fused_computation.50 | output fusion | flops 9439487 | bytes 10502144 | tf_op jit(solution)/shard_map/div | solution.py:153
  138.0 1.6 convolution_bitcast_fusion.1
  140.7 2.6 %collective-permute-done = f32[2,384,256]{2,1,0:T(8,128)} collective-permute-done((f32[2,384,256]{2,1,0:T(8,128)}, f32[2,384,256]{2,1,0:T(8,128)}, u32[]{:S(2)}, u32[]{:S(2)}) %collective-permute-start) | collective-permute-done | bytes 786464 | tf_op jit(solution)/shard_map/ppermute | solution.py:116
  143.4 1.5 fusion.54
  146.2 10.9 %collective-permute-done.1 = f32[2,192,256]{2,1,0:T(8,128)} collective-permute-done((f32[2,192,256]{2,1,0:T(8,128)S(1)}, f32[2,192,256]{2,1,0:T(8,128)}, u32[]{:S(2)}, u32[]{:S(2)}) %collective-permute-start.1) | collective-permute-done | bytes 393248 | tf_op jit(solution)/shard_map/ppermute | solution.py:116
  159.3 6.0 %collective-permute-done.2 = f32[2,96,256]{2,1,0:T(8,128)} collective-permute-done((f32[2,96,256]{2,1,0:T(8,128)}, f32[2,96,256]{2,1,0:T(8,128)}, u32[]{:S(2)}, u32[]{:S(2)}) %collective-permute-start.2) | collective-permute-done | bytes 196640 | tf_op jit(solution)/shard_map/ppermute | solution.py:116
  167.5 6.0 %collective-permute-done.3 = f32[2,48,256]{2,1,0:T(8,128)S(1)} collective-permute-done((f32[2,48,256]{2,1,0:T(8,128)S(1)}, f32[2,48,256]{2,1,0:T(8,128)S(1)}, u32[]{:S(2)}, u32[]{:S(2)}) %collective-permute-start.3) | collective-permute-done | bytes 98336 | tf_op jit(solution)/shard_map/ppermute | solution.py:116
  174.5 5.8 %collective-permute-done.4 = f32[2,48,256]{2,1,0:T(8,128)S(1)} collective-permute-done((f32[2,48,256]{2,1,0:T(8,128)S(1)}, f32[2,48,256]{2,1,0:T(8,128)S(1)}, u32[]{:S(2)}, u32[]{:S(2)}) %collective-permute-start.4) | collective-permute-done | bytes 98336 | tf_op jit(solution)/shard_map/ppermute | solution.py:120
  180.4 5.8 %collective-permute-done.5 = f32[2,96,256]{2,1,0:T(8,128)} collective-permute-done((f32[2,96,256]{2,1,0:T(8,128)S(1)}, f32[2,96,256]{2,1,0:T(8,128)}, u32[]{:S(2)}, u32[]{:S(2)}) %collective-permute-start.5) | collective-permute-done | bytes 196640 | tf_op jit(solution)/shard_map/ppermute | solution.py:120
  188.5 7.3 %collective-permute-done.6 = f32[2,192,256]{2,1,0:T(8,128)} collective-permute-done((f32[2,192,256]{2,1,0:T(8,128)S(1)}, f32[2,192,256]{2,1,0:T(8,128)}, u32[]{:S(2)}, u32[]{:S(2)}) %collective-permute-start.6) | collective-permute-done | bytes 393248 | tf_op jit(solution)/shard_map/ppermute | solution.py:120
  199.4 1.9 collective-permute-done.7
  201.3 1.3 broadcast_select_fusion.1
  204.2 4.8 %multiply_add_fusion = (f32[2,196608]{1,0:T(2,128)}, f32[2,196608]{1,0:T(2,128)}, f32[2,196608]{1,0:T(2,128)}) fusion(f32[2,196608]{1,0:T(2,128)S(1)} %copy-done, f32[2,196608]{1,0:T(2,128)S(1)} %copy-done.1, f32[2,196608]{1,0:T(2,128)S(1)} %bitcast.138, f32[2,196608]{1,0:T(2,128)S(1)} %copy-done.9), kind=kLoop, calls=%fused_computation.65 | loop fusion | flops 2752512 | bytes 11010048 | tf_op jit(solution)/shard_map/add | solution.py:181
  (109 shorter events, 31.6 us)
Async XLA Ops:
  4.1 45.5 %copy-start = (f32[2,196608]{1,0:T(2,128)S(1)}, f32[2,196608]{1,0:T(2,128)}, u32[]{:S(2)}) copy-start(f32[2,196608]{1,0:T(2,128)} %param.11) | copy-start | bytes 4718596
  25.3 18.0 %all-to-all-start = ((bf16[16,1,128]{2,1,0:T(2,128)(2,1)}), bf16[16,1,128]{2,1,0:T(2,128)(2,1)S(1)}, u32[]{:S(2)}, u32[]{:S(2)}) async-start(bf16[16,1,128]{2,1,0:T(2,128)(2,1)} %copy.72), calls=%async_computation | async-start | bytes 16384 | tf_op jit(solution)/shard_map/all_to_all | solution.py:86
  43.4 7.2 %copy-start.1 = (f32[2,196608]{1,0:T(2,128)S(1)}, f32[2,196608]{1,0:T(2,128)}, u32[]{:S(2)}) copy-start(f32[2,196608]{1,0:T(2,128)} %param.9) | copy-start | bytes 4718596
  43.4 29.2 %all-to-all-start.1 = ((bf16[16,128,256]{2,1,0:T(8,128)(2,1)}), bf16[16,128,256]{2,1,0:T(8,128)(2,1)}, u32[]{:S(2)}, u32[]{:S(2)}) async-start(bf16[16,128,256]{2,1,0:T(8,128)(2,1)} %bitcast.139), calls=%async_computation.1 | async-start | bytes 2097152 | tf_op jit(solution)/shard_map/all_to_all | solution.py:79
  55.1 32.4 %copy-start.19 = (s32[8]{0:T(128)}, s32[8]{0:T(128)S(1)}, u32[]{:S(2)}) copy-start(s32[8]{0:T(128)S(1)} %get-tuple-element.7) | copy-start | bytes 100
  55.8 37.4 %copy-start.18 = (f32[8,256]{1,0:T(8,128)}, f32[8,256]{1,0:T(8,128)S(1)}, u32[]{:S(2)}) copy-start(f32[8,256]{1,0:T(8,128)S(1)} %fusion.78) | copy-start | bytes 24580
  83.2 4.3 %copy-start.6 = (bf16[1,2,768,256]{3,2,1,0:T(8,128)(2,1)S(1)}, bf16[1,2,768,256]{3,2,1,0:T(8,128)(2,1)}, u32[]{:S(2)}) copy-start(bf16[1,2,768,256]{3,2,1,0:T(8,128)(2,1)} %copy.109) | copy-start | bytes 2359300
  83.2 4.3 %copy-start.10 = (bf16[2048,256]{1,0:T(8,128)(2,1)S(1)}, bf16[2048,256]{1,0:T(8,128)(2,1)}, u32[]{:S(2)}) copy-start(bf16[2048,256]{1,0:T(8,128)(2,1)} %scatter_custom_fusion.2) | copy-start | bytes 3145732
  90.0 3.2 %copy-start.14 = (bf16[8,256,256]{2,1,0:T(8,128)(2,1)}, bf16[8,256,256]{2,1,0:T(8,128)(2,1)S(1)}, u32[]{:S(2)}) copy-start(bf16[8,256,256]{2,1,0:T(8,128)(2,1)S(1)} %get-tuple-element.26) | copy-start | bytes 3145732
  90.1 3.1 %copy-start.12 = (bf16[8,248,256]{2,1,0:T(8,128)(2,1)}, bf16[8,248,256]{2,1,0:T(8,128)(2,1)S(1)}, u32[]{:S(2)}) copy-start(bf16[8,248,256]{2,1,0:T(8,128)(2,1)S(1)} %slice.94) | copy-start | bytes 3047428
  90.1 3.1 %copy-start.16 = (bf16[1,2,768,256]{3,2,1,0:T(8,128)(2,1)S(1)}, bf16[1,2,768,256]{3,2,1,0:T(8,128)(2,1)}, u32[]{:S(2)}) copy-start(bf16[1,2,768,256]{3,2,1,0:T(8,128)(2,1)} %copy.108) | copy-start | bytes 2359300
  93.2 2.9 %copy-start.23 = (bf16[8,256,256]{2,1,0:T(8,128)(2,1)}, bf16[8,256,256]{2,1,0:T(8,128)(2,1)S(1)}, u32[]{:S(2)}) copy-start(bf16[8,256,256]{2,1,0:T(8,128)(2,1)S(1)} %get-tuple-element.13) | copy-start | bytes 3145732
  96.7 13.5 %all-to-all-start.2 = ((f32[16,1,384]{2,1,0:T(1,128)}), f32[16,1,384]{2,1,0:T(1,128)}, u32[]{:S(2)}, u32[]{:S(2)}) async-start(f32[16,1,384]{2,1,0:T(1,128)} %broadcast_in_dim.41), calls=%async_computation.2 | async-start | bytes 49152 | tf_op jit(solution)/shard_map/all_to_all | solution.py:143
  121.9 11.6 %copy-start.13 = (bf16[8,248,256]{2,1,0:T(8,128)(2,1)S(1)}, bf16[8,248,256]{2,1,0:T(8,128)(2,1)}, u32[]{:S(2)}) copy-start(bf16[8,248,256]{2,1,0:T(8,128)(2,1)} %copy-done.12) | copy-start | bytes 3047428
  121.9 11.6 %copy-start.15 = (bf16[8,256,256]{2,1,0:T(8,128)(2,1)S(1)}, bf16[8,256,256]{2,1,0:T(8,128)(2,1)}, u32[]{:S(2)}) copy-start(bf16[8,256,256]{2,1,0:T(8,128)(2,1)} %copy-done.14) | copy-start | bytes 3145732
  134.6 5.0 %copy-start.3 = (f32[1,768,256]{2,1,0:T(8,128)}, f32[1,768,256]{2,1,0:T(8,128)S(1)}, u32[]{:S(2)}) copy-start(f32[1,768,256]{2,1,0:T(8,128)S(1)} %convolution_bitcast_fusion) | copy-start | bytes 2359300
  136.1 1.2 copy-start.11
  136.1 1.9 copy-start.22
  139.6 1.1 copy-start.4
  140.7 2.6 %collective-permute-start = (f32[2,384,256]{2,1,0:T(8,128)}, f32[2,384,256]{2,1,0:T(8,128)}, u32[]{:S(2)}, u32[]{:S(2)}) collective-permute-start(f32[2,384,256]{2,1,0:T(8,128)} %fusion.52), channel_id=1, source_target_pairs={{0,1},{1,0},{2,3},{3,2},{4,5},{5,4},{6,7},{7,6},{8,9},{9,8},{10,11... | collective-permute-start | bytes 2359304 | tf_op jit(solution)/shard_map/ppermute | solution.py:116
  144.8 0.9 copy-start.5
  145.7 11.3 %collective-permute-start.1 = (f32[2,192,256]{2,1,0:T(8,128)S(1)}, f32[2,192,256]{2,1,0:T(8,128)}, u32[]{:S(2)}, u32[]{:S(2)}) collective-permute-start(f32[2,192,256]{2,1,0:T(8,128)S(1)} %constant_dynamic-slice_fusion.1), channel_id=1, source_target_pairs={{0,2},{1,3},{2,0},{3,1},{4,6},{5,7},{6,4},{7,5},{8,10},{9,11},{10,... | collective-permute-start | bytes 1179656 | tf_op jit(solution)/shard_map/ppermute | solution.py:116
  158.9 6.4 %collective-permute-start.2 = (f32[2,96,256]{2,1,0:T(8,128)}, f32[2,96,256]{2,1,0:T(8,128)}, u32[]{:S(2)}, u32[]{:S(2)}) collective-permute-start(f32[2,96,256]{2,1,0:T(8,128)} %constant_dynamic-slice_fusion), channel_id=1, source_target_pairs={{0,4},{1,5},{2,6},{3,7},{4,0},{5,1},{6,2},{7,3},{8,12},{9,13},{10,... | collective-permute-start | bytes 589832 | tf_op jit(solution)/shard_map/ppermute | solution.py:116
  167.0 6.5 %collective-permute-start.3 = (f32[2,48,256]{2,1,0:T(8,128)S(1)}, f32[2,48,256]{2,1,0:T(8,128)S(1)}, u32[]{:S(2)}, u32[]{:S(2)}) collective-permute-start(f32[2,48,256]{2,1,0:T(8,128)S(1)} %constant_dynamic-slice_fusion.2), channel_id=1, source_target_pairs={{0,8},{1,9},{2,10},{3,11},{4,12},{5,13},{6,14},{7,15},{8,0},{9,1},... | collective-permute-start | bytes 294920 | tf_op jit(solution)/shard_map/ppermute | solution.py:116
  174.4 5.9 %collective-permute-start.4 = (f32[2,48,256]{2,1,0:T(8,128)S(1)}, f32[2,48,256]{2,1,0:T(8,128)S(1)}, u32[]{:S(2)}, u32[]{:S(2)}) collective-permute-start(f32[2,48,256]{2,1,0:T(8,128)S(1)} %dynamic-slice_add_fusion.2), channel_id=1, source_target_pairs={{0,8},{1,9},{2,10},{3,11},{4,12},{5,13},{6,14},{7,15},{8,0},{9,1},... | collective-permute-start | bytes 294920 | tf_op jit(solution)/shard_map/ppermute | solution.py:120
  180.3 5.8 %collective-permute-start.5 = (f32[2,96,256]{2,1,0:T(8,128)S(1)}, f32[2,96,256]{2,1,0:T(8,128)}, u32[]{:S(2)}, u32[]{:S(2)}) collective-permute-start(f32[2,96,256]{2,1,0:T(8,128)S(1)} %pad_maximum_fusion.2), channel_id=1, source_target_pairs={{0,4},{1,5},{2,6},{3,7},{4,0},{5,1},{6,2},{7,3},{8,12},{9,13},{10,... | collective-permute-start | bytes 589832 | tf_op jit(solution)/shard_map/ppermute | solution.py:120
  187.1 0.7 copy-start.8
  187.1 11.5 %copy-start.20 = (s32[8]{0:T(128)S(1)}, s32[8]{0:T(128)}, u32[]{:S(2)}) copy-start(s32[8]{0:T(128)} %copy-done.19) | copy-start | bytes 100
  187.9 7.9 %collective-permute-start.6 = (f32[2,192,256]{2,1,0:T(8,128)S(1)}, f32[2,192,256]{2,1,0:T(8,128)}, u32[]{:S(2)}, u32[]{:S(2)}) collective-permute-start(f32[2,192,256]{2,1,0:T(8,128)S(1)} %pad_maximum_fusion.1), channel_id=1, source_target_pairs={{0,2},{1,3},{2,0},{3,1},{4,6},{5,7},{6,4},{7,5},{8,10},{9,11},{10,... | collective-permute-start | bytes 1179656 | tf_op jit(solution)/shard_map/ppermute | solution.py:120
  197.0 0.7 copy-start.2
  198.7 2.6 %collective-permute-start.7 = (f32[2,384,256]{2,1,0:T(8,128)}, f32[2,384,256]{2,1,0:T(8,128)}, u32[]{:S(2)}, u32[]{:S(2)}) collective-permute-start(f32[2,384,256]{2,1,0:T(8,128)} %pad_maximum_fusion), channel_id=1, source_target_pairs={{0,1},{1,0},{2,3},{3,2},{4,5},{5,4},{6,7},{7,6},{8,9},{9,8},{10,11... | collective-permute-start | bytes 2359304 | tf_op jit(solution)/shard_map/ppermute | solution.py:120
  202.8 1.4 copy-start.9
  (3 other events, 2.0 us)

commit v3 on v2

--- a/solution.py
+++ b/solution.py
@@ -68,14 +68,16 @@
     ) & live_rows[:, None]
     running = jnp.cumsum(owner_hot.astype(jnp.int32), axis=0)
     send_rank = jnp.sum(jnp.where(owner_hot, running, 0), axis=1) - 1
-    send_index = jnp.where(live_rows, owner_dev * capacity + send_rank, rows_total)
-    send_rows = jnp.zeros_like(epoch_rows).at[send_index].set(epoch_rows, mode="drop")
-    send_code = (
-        jnp.full((rows_total,), -1.0, jnp.bfloat16)
-        .at[send_index]
-        .set(local_place.astype(jnp.bfloat16), mode="drop")
-    )
-    got_rows, got_code = (
+    send_index = jnp.where(live_rows, owner_dev * capacity + send_rank, -1)
+    pick = (
+        jnp.arange(rows_total, dtype=jnp.int32)[:, None] == send_index[None, :]
+    ).astype(jnp.bfloat16)
+    send_rows = jnp.dot(pick, epoch_rows, preferred_element_type=jnp.float32).astype(jnp.bfloat16)
+    place_hot = (
+        (local_place[:, None] == jnp.arange(per_dev, dtype=jnp.int32)[None, :]) & live_rows[:, None]
+    ).astype(jnp.bfloat16)
+    send_place = jnp.dot(pick, place_hot, preferred_element_type=jnp.float32).astype(jnp.bfloat16)
+    got_rows, got_place = (
         lax.all_to_all(
             send_rows.reshape(wide_count, capacity, feat_width),
             "wide",
@@ -84,20 +86,27 @@
             tiled=True,
         ),
         lax.all_to_all(
-            send_code.reshape(wide_count, capacity), "wide", split_axis=0, concat_axis=0, tiled=True
+            send_place.reshape(wide_count, capacity, per_dev),
+            "wide",
+            split_axis=0,
+            concat_axis=0,
+            tiled=True,
         ),
     )
-    place_code = got_code.reshape(-1).astype(jnp.int32)
-    place_hot = place_code[:, None] == jnp.arange(per_dev, dtype=jnp.int32)[None, :]
+    place_hot = got_place.reshape(-1, per_dev) > 0
     arrival = jnp.cumsum(place_hot.astype(jnp.int32), axis=0)
     position = jnp.sum(jnp.where(place_hot, arrival, 0), axis=1) - 1
+    place_code = jnp.sum(
+        jnp.where(place_hot, jnp.arange(per_dev, dtype=jnp.int32)[None, :], 0), axis=1
+    )
     counts = jnp.sum(place_hot.astype(jnp.int32), axis=0)
-    target = jnp.where(place_code >= 0, place_code * SEQ + position, per_dev * SEQ)
-    sequences = (
-        jnp.zeros((per_dev * SEQ, feat_width), jnp.bfloat16)
-        .at[target]
-        .set(got_rows.reshape(-1, feat_width), mode="drop")
-    )
+    target = jnp.where(jnp.any(place_hot, axis=1), place_code * SEQ + position, -1)
+    put = (
+        jnp.arange(per_dev * SEQ, dtype=jnp.int32)[:, None] == target[None, :]
+    ).astype(jnp.bfloat16)
+    sequences = jnp.dot(
+        put, got_rows.reshape(-1, feat_width), preferred_element_type=jnp.float32
+    ).astype(jnp.bfloat16)
     return (sequences.reshape(per_dev, SEQ, feat_width), counts)
 
 

time: 210 us -> 176 us (0.84)
  local copies, waits for them, and re-layouts: 50.4 us -> 11.3 us
  matrix products: 16.2 us -> 25.4 us
  other arithmetic: 50 us -> 45.7 us
  waiting for transfers between devices: 68 us -> 70.8 us
  starting transfers between devices: 22.6 us -> 20.3 us
    scatter x3 -> x0, local copies, waits for them, and re-layouts: 35.9 us -> none  [the longest x1 14.6 us: route_rows(): send_code = jnp.full((rows_total,), -1.0, jnp.bfloat16).at[send_index].se...]
    dot_general x0 -> x3, matrix products: none -> 12.4 us  [the longest x1 4.48 us: route_rows(): jnp.dot(put, got_rows.reshape(-1, feat_width), preferred_element_type=jnp...]
    dot_general x4, matrix products: 12.6 us -> 9.38 us  [run_network(): jnp.dot(stacked.reshape(-1, stacked.shape[2]), weights[layer_at], preferr...]
    all_to_all x1, waiting for transfers between devices: 0.01 us -> 2.47 us  [route_rows(): lax.all_to_all(send_place.reshape(wide_count, capacity, per_dev), 'wide',...]
    unnamed x51 -> x42, local copies, waits for them, and re-layouts: 8.85 us -> 7.9 us
  transfers between devices with their start and end apart: 11 -> 11, of which waited for: 10 -> 11; matrix products, arithmetic and copies ran while one was open for 9% -> 7% of each run, Pallas kernels for 0% -> 0%
where the time goes in v3:
time: 176 us; the launch traced here: 175 us
  waiting for transfers between devices  70.8 us (40%)
  other arithmetic  45.7 us (26%)
  matrix products  25.4 us (14%)
  starting transfers between devices  20.3 us (12%)
  local copies, waits for them, and re-layouts  11.3 us (6%)
  between operations  1.77 us (1%)
    ppermute x4, waiting for transfers between devices, all_reduce_wide(): buf = keep + lax.ppermute(send, 'wide', pairs)  26.1 us
    ppermute x4, waiting for transfers between devices, all_reduce_wide(): got = lax.ppermute(buf, 'wide', pairs)  21.1 us
    all_to_all x1, waiting for transfers between devices, route_rows(): lax.all_to_all(send_rows.reshape(wide_count, capacity, feat_width), 'wide...  15.4 us
    div x1, other arithmetic, local(): student_prob = jax.nn.softmax(student_f / tau_student, axis=-1)  11.6 us
    dot_general x4, matrix products, run_network(): jnp.dot(stacked.reshape(-1, stacked.shape[2]), weights[layer_at], preferr...  9.38 us
    unnamed x42, local copies, waits for them, and re-layouts  7.9 us
    all_to_all x1, starting transfers between devices, route_rows(): lax.all_to_all(send_place.reshape(wide_count, capacity, per_dev), 'wide',...  7.36 us
    another operation x5, other arithmetic  7.27 us
  transfers between devices with their start and end apart: 11, of which 11 were waited for; matrix products, arithmetic and copies ran while one was open for 7% of the time, Pallas kernels for 0%

profile of v3, /device:TPU:0, one launch (start us, length us, event | category | flops | bytes accessed | tf_op | source)
XLA Modules:
  0.0 175.3 jit_solution(1066699312555565415)
XLA Ops:
  2.1 1.3 select_reduce_fusion
  4.2 4.5 %reduce-window.14 = s32[16,16,128]{2,1,0:T(8,128)S(1)} reduce-window(s32[16,16,128]{2,1,0:T(8,128)S(1)} %fusion.80, s32[]{:T(128)} %constant.32.clone.1), window={size=1x1x128 pad=0_0x0_0x127_0}, to_apply=%region_1.2 | reduce-window | flops 4161536 | bytes 262148 | tf_op jit(solution)/shard_map/reduce-window
  10.2 3.8 %fusion.53 = bf16[16,128,8]{1,2,0:T(8,128)(2,1)} fusion(s32[2048]{0:T(1024)S(1)} %get-tuple-element.27, s32[2048]{0:T(1024)S(1)} %get-tuple-element.26, pred[2048]{0:T(1024)(128)(4,1)S(1)} %broadcast_compare_fusion.1), kind=kOutput, calls=%fused_computation.78 | convolution fusion | flops 71352320 | bytes 51200 | tf_op jit(solution)/shard_map/dot_general | solution.py:79
  14.0 7.4 %all-to-all-start = ((bf16[16,128,8]{1,2,0:T(8,128)(2,1)}), bf16[16,128,8]{1,2,0:T(8,128)(2,1)S(1)}, u32[]{:S(2)}, u32[]{:S(2)}) async-start(bf16[16,128,8]{1,2,0:T(8,128)(2,1)} %fusion.53), calls=%async_computation | async-start | bytes 65536 | tf_op jit(solution)/shard_map/all_to_all | solution.py:88
  21.4 4.2 %fusion.25 = bf16[2048,256]{1,0:T(8,128)(2,1)} fusion(bf16[2048,256]{1,0:T(8,128)(2,1)S(1)} %copy-done, s32[2048]{0:T(1024)S(1)} %get-tuple-element.27), kind=kOutput, calls=%fused_computation.35 | convolution fusion | flops 2152202240 | bytes 2105344 | tf_op jit(solution)/shard_map/dot_general | solution.py:75
  25.5 2.5 %all-to-all-done = bf16[16,128,8]{1,2,0:T(8,128)(2,1)S(1)} async-done(((bf16[16,128,8]{1,2,0:T(8,128)(2,1)}), bf16[16,128,8]{1,2,0:T(8,128)(2,1)S(1)}, u32[]{:S(2)}, u32[]{:S(2)}) %all-to-all-start) | async-done | bytes 32800 | tf_op jit(solution)/shard_map/all_to_all | solution.py:88
  28.0 4.5 %all-to-all-start.1 = ((bf16[16,128,256]{2,1,0:T(8,128)(2,1)}), bf16[16,128,256]{2,1,0:T(8,128)(2,1)}, u32[]{:S(2)}, u32[]{:S(2)}) async-start(bf16[16,128,256]{2,1,0:T(8,128)(2,1)} %bitcast.149), calls=%async_computation.1 | async-start | bytes 2097152 | tf_op jit(solution)/shard_map/all_to_all | solution.py:81
  34.9 2.3 %reduce-window.16 = s32[8,16,128]{2,1,0:T(8,128)S(1)} reduce-window(s32[8,16,128]{2,1,0:T(8,128)S(1)} %bitcast.156, s32[]{:T(128)} %constant.32.clone.1), window={size=1x1x128 pad=0_0x0_0x127_0}, to_apply=%region_6.7 | reduce-window | flops 2080768 | bytes 131076 | tf_op jit(solution)/shard_map/reduce-window.2
  39.9 15.4 %all-to-all-done.1 = bf16[16,128,256]{2,1,0:T(8,128)(2,1)} async-done(((bf16[16,128,256]{2,1,0:T(8,128)(2,1)}), bf16[16,128,256]{2,1,0:T(8,128)(2,1)}, u32[]{:S(2)}, u32[]{:S(2)}) %all-to-all-start.1) | async-done | bytes 1048608 | tf_op jit(solution)/shard_map/all_to_all | solution.py:81
  55.3 4.5 %fusion.24 = bf16[2048,256]{1,0:T(8,128)(2,1)S(1)} fusion(bf16[2048,256]{1,0:T(8,128)(2,1)} %bitcast.10, s32[2048]{0:T(1024)S(1)} %fusion.84), kind=kOutput, calls=%fused_computation.34 | convolution fusion | flops 2152202240 | bytes 2105344 | tf_op jit(solution)/shard_map/dot_general | solution.py:107
  59.8 1.5 fusion.28
  61.4 2.5 %fusion.27 = (bf16[8,256,256]{2,1,0:T(8,128)(2,1)S(1)}, f32[8,256,256]{2,1,0:T(8,128)}) fusion(bf16[8,256,256]{2,1,0:T(8,128)(2,1)S(1)} %bitcast.162, bf16[2,768,256]{2,1,0:T(8,128)(2,1)S(1)} %bitcast.145, bf16[8,254,256]{2,1,0:T(8,128)(2,1)S(1)} %bitcast.163, bf16[8,255,256]{2,1,0:T(8,128)(2,1)S(1)} %bitcast.164), kind=kOutput, calls=%fused_computation.37 | convolution fusion | flops 827850752 | bytes 7733248 | tf_op jit(solution)/shard_map/dot_general | solution.py:42
  64.0 2.5 %fusion.106 = (bf16[8,256]{1,0:T(8,128)(2,1)S(1)}, bf16[8,256,256]{2,1,0:T(8,128)(2,1)S(1)}, f32[8,256,256]{2,1,0:T(8,128)}) fusion(bf16[8,256,256]{2,1,0:T(8,128)(2,1)S(1)} %get-tuple-element.28, bf16[2,768,256]{2,1,0:T(8,128)(2,1)S(1)} %bitcast.146, bf16[8,248,256]{2,1,0:T(8,128)(2,1)S(1)} %slice.94, bf16[8,252,256]{2,1,0:T(8,128)(2,1)S(1)} %bitcast.150), kind=kOutput, calls=%fused_computation.173 | convolution fusion | flops 828372992 | bytes 7704576 | tf_op jit(solution)/shard_map/dot_general | solution.py:42
  66.5 2.9 %fusion.36 = (f32[8,256]{1,0:T(8,128)S(1)}, f32[256]{0:T(256)S(1)}, bf16[8,256,256]{2,1,0:T(8,128)(2,1)}) fusion(bf16[8,256,256]{2,1,0:T(8,128)(2,1)S(1)} %get-tuple-element.13, f32[8,256]{1,0:T(8,128)S(1)} %fusion.87, bf16[2,768,256]{2,1,0:T(8,128)(2,1)S(1)} %bitcast.154, bf16[8,248,256]{2,1,0:T(8,128)(2,1)S(1)} %slice.98, ...), kind=kOutput, calls=%fused_computation.45 | convolution fusion | flops 830994176 | bytes 6669312 | tf_op jit(solution)/shard_map/dot_general | solution.py:42
  70.0 6.8 %all-to-all-start.2 = ((f32[16,1,384]{2,1,0:T(1,128)}), f32[16,1,384]{2,1,0:T(1,128)S(1)}, u32[]{:S(2)}, u32[]{:S(2)}) async-start(f32[16,1,384]{2,1,0:T(1,128)} %broadcast_in_dim.40), calls=%async_computation.2 | async-start | bytes 49152 | tf_op jit(solution)/shard_map/all_to_all | solution.py:152
  77.6 5.8 %all-to-all-done.2 = f32[16,1,384]{2,1,0:T(1,128)S(1)} async-done(((f32[16,1,384]{2,1,0:T(1,128)}), f32[16,1,384]{2,1,0:T(1,128)S(1)}, u32[]{:S(2)}, u32[]{:S(2)}) %all-to-all-start.2) | async-done | bytes 24608 | tf_op jit(solution)/shard_map/all_to_all | solution.py:152
  84.6 3.5 %fusion.40 = f32[8,256,256]{2,1,0:T(8,128)} fusion(bf16[8,256,256]{2,1,0:T(8,128)(2,1)} %get-tuple-element.31, f32[256]{0:T(256)S(1)} %slice_divide_fusion), kind=kOutput, calls=%fused_computation.48 | output fusion | flops 3672319 | bytes 3146752 | tf_op jit(solution)/shard_map/sub | solution.py:160
  88.0 3.8 %fusion = f32[8,256,256]{2,1,0:T(8,128)} fusion(bf16[8,256,256]{2,1,0:T(8,128)(2,1)} %get-tuple-element.31, f32[256]{0:T(256)S(1)} %slice_divide_fusion), kind=kOutput, calls=%fused_computation | output fusion | flops 3674622 | bytes 3146752 | tf_op jit(solution)/shard_map/div | solution.py:160
  91.9 11.6 %multiply_convert_fusion = (bf16[8,256,256]{2,1,0:T(8,128)(2,1)S(1)}, f32[8,256,256]{2,1,0:T(8,128)S(1)}) fusion(f32[8,256,256]{2,1,0:T(8,128)} %get-tuple-element.30, f32[8,256,256]{2,1,0:T(8,128)} %fusion, f32[8,256,256]{2,1,0:T(8,128)} %fusion.40, bf16[8,256,256]{2,1,0:T(8,128)(2,1)} %copy-done.18, f32[8,256]{1,0:T(8,128)S(1)} %reduce_max.24, ...), kind=kOutput, calls=%fused_computation.58 | output fusion | flops 9439487 | bytes 10502144 | tf_op jit(solution)/shard_map/div | solution.py:162
  107.9 1.6 convolution_bitcast_fusion.1
  111.3 2.6 %collective-permute-done = f32[2,384,256]{2,1,0:T(8,128)} collective-permute-done((f32[2,384,256]{2,1,0:T(8,128)}, f32[2,384,256]{2,1,0:T(8,128)}, u32[]{:S(2)}, u32[]{:S(2)}) %collective-permute-start) | collective-permute-done | bytes 786464 | tf_op jit(solution)/shard_map/ppermute | solution.py:125
  114.0 1.3 fusion.66
  116.7 10.8 %collective-permute-done.1 = f32[2,192,256]{2,1,0:T(8,128)S(1)} collective-permute-done((f32[2,192,256]{2,1,0:T(8,128)S(1)}, f32[2,192,256]{2,1,0:T(8,128)S(1)}, u32[]{:S(2)}, u32[]{:S(2)}) %collective-permute-start.1) | collective-permute-done | bytes 393248 | tf_op jit(solution)/shard_map/ppermute | solution.py:125
  129.0 5.7 %collective-permute-done.2 = f32[2,96,256]{2,1,0:T(8,128)S(1)} collective-permute-done((f32[2,96,256]{2,1,0:T(8,128)S(1)}, f32[2,96,256]{2,1,0:T(8,128)S(1)}, u32[]{:S(2)}, u32[]{:S(2)}) %collective-permute-start.2) | collective-permute-done | bytes 196640 | tf_op jit(solution)/shard_map/ppermute | solution.py:125
  135.2 7.0 %collective-permute-done.3 = f32[2,48,256]{2,1,0:T(8,128)S(1)} collective-permute-done((f32[2,48,256]{2,1,0:T(8,128)S(1)}, f32[2,48,256]{2,1,0:T(8,128)S(1)}, u32[]{:S(2)}, u32[]{:S(2)}) %collective-permute-start.3) | collective-permute-done | bytes 98336 | tf_op jit(solution)/shard_map/ppermute | solution.py:125
  142.4 5.6 %collective-permute-done.4 = f32[2,48,256]{2,1,0:T(8,128)S(1)} collective-permute-done((f32[2,48,256]{2,1,0:T(8,128)S(1)}, f32[2,48,256]{2,1,0:T(8,128)S(1)}, u32[]{:S(2)}, u32[]{:S(2)}) %collective-permute-start.4) | collective-permute-done | bytes 98336 | tf_op jit(solution)/shard_map/ppermute | solution.py:129
  148.1 5.7 %collective-permute-done.5 = f32[2,96,256]{2,1,0:T(8,128)S(1)} collective-permute-done((f32[2,96,256]{2,1,0:T(8,128)S(1)}, f32[2,96,256]{2,1,0:T(8,128)S(1)}, u32[]{:S(2)}, u32[]{:S(2)}) %collective-permute-start.5) | collective-permute-done | bytes 196640 | tf_op jit(solution)/shard_map/ppermute | solution.py:129
  154.6 7.9 %collective-permute-done.6 = f32[2,192,256]{2,1,0:T(8,128)} collective-permute-done((f32[2,192,256]{2,1,0:T(8,128)S(1)}, f32[2,192,256]{2,1,0:T(8,128)}, u32[]{:S(2)}, u32[]{:S(2)}) %collective-permute-start.6) | collective-permute-done | bytes 393248 | tf_op jit(solution)/shard_map/ppermute | solution.py:129
  165.3 1.9 %collective-permute-done.7 = f32[2,384,256]{2,1,0:T(8,128)} collective-permute-done((f32[2,384,256]{2,1,0:T(8,128)}, f32[2,384,256]{2,1,0:T(8,128)}, u32[]{:S(2)}, u32[]{:S(2)}) %collective-permute-start.7) | collective-permute-done | bytes 786464 | tf_op jit(solution)/shard_map/ppermute | solution.py:129
  167.2 1.2 broadcast_select_fusion.1
  168.6 1.2 copy.77
  170.5 4.8 %multiply_add_fusion = (f32[2,196608]{1,0:T(2,128)}, f32[2,196608]{1,0:T(2,128)}, f32[2,196608]{1,0:T(2,128)}) fusion(f32[2,196608]{1,0:T(2,128)S(1)} %copy-done.1, f32[2,196608]{1,0:T(2,128)S(1)} %copy-done.3, f32[2,196608]{1,0:T(2,128)S(1)} %bitcast.144, f32[2,196608]{1,0:T(2,128)S(1)} %copy-done.8), kind=kLoop, calls=%fused_computation.73 | loop fusion | flops 2752512 | bytes 11010048 | tf_op jit(solution)/shard_map/add | solution.py:190
  (99 shorter events, 25.1 us)
Async XLA Ops:
  0.6 20.7 %copy-start = (bf16[2048,256]{1,0:T(8,128)(2,1)S(1)}, bf16[2048,256]{1,0:T(8,128)(2,1)}, u32[]{:S(2)}) copy-start(bf16[2048,256]{1,0:T(8,128)(2,1)} %param.6) | copy-start | bytes 3145732
  14.0 14.0 %all-to-all-start = ((bf16[16,128,8]{1,2,0:T(8,128)(2,1)}), bf16[16,128,8]{1,2,0:T(8,128)(2,1)S(1)}, u32[]{:S(2)}, u32[]{:S(2)}) async-start(bf16[16,128,8]{1,2,0:T(8,128)(2,1)} %fusion.53), calls=%async_computation | async-start | bytes 65536 | tf_op jit(solution)/shard_map/all_to_all | solution.py:88
  25.5 7.0 %copy-start.1 = (f32[2,196608]{1,0:T(2,128)S(1)}, f32[2,196608]{1,0:T(2,128)}, u32[]{:S(2)}) copy-start(f32[2,196608]{1,0:T(2,128)} %param.11) | copy-start | bytes 4718596
  28.0 27.3 %all-to-all-start.1 = ((bf16[16,128,256]{2,1,0:T(8,128)(2,1)}), bf16[16,128,256]{2,1,0:T(8,128)(2,1)}, u32[]{:S(2)}, u32[]{:S(2)}) async-start(bf16[16,128,256]{2,1,0:T(8,128)(2,1)} %bitcast.149), calls=%async_computation.1 | async-start | bytes 2097152 | tf_op jit(solution)/shard_map/all_to_all | solution.py:81
  32.5 1.7 copy-start.2
  55.3 4.5 %copy-start.14 = (bf16[1,2,768,256]{3,2,1,0:T(8,128)(2,1)S(1)}, bf16[1,2,768,256]{3,2,1,0:T(8,128)(2,1)}, u32[]{:S(2)}) copy-start(bf16[1,2,768,256]{3,2,1,0:T(8,128)(2,1)} %copy.83) | copy-start | bytes 2359300
  59.8 1.6 copy-start.15
  63.9 2.6 %copy-start.12 = (bf16[8,256,256]{2,1,0:T(8,128)(2,1)}, bf16[8,256,256]{2,1,0:T(8,128)(2,1)S(1)}, u32[]{:S(2)}) copy-start(bf16[8,256,256]{2,1,0:T(8,128)(2,1)S(1)} %get-tuple-element.28) | copy-start | bytes 3145732
  64.0 2.5 %copy-start.10 = (bf16[8,248,256]{2,1,0:T(8,128)(2,1)}, bf16[8,248,256]{2,1,0:T(8,128)(2,1)S(1)}, u32[]{:S(2)}) copy-start(bf16[8,248,256]{2,1,0:T(8,128)(2,1)S(1)} %slice.94) | copy-start | bytes 3047428
  66.5 2.9 %copy-start.18 = (bf16[8,256,256]{2,1,0:T(8,128)(2,1)}, bf16[8,256,256]{2,1,0:T(8,128)(2,1)S(1)}, u32[]{:S(2)}) copy-start(bf16[8,256,256]{2,1,0:T(8,128)(2,1)S(1)} %get-tuple-element.13) | copy-start | bytes 3145732
  70.0 13.4 %all-to-all-start.2 = ((f32[16,1,384]{2,1,0:T(1,128)}), f32[16,1,384]{2,1,0:T(1,128)S(1)}, u32[]{:S(2)}, u32[]{:S(2)}) async-start(f32[16,1,384]{2,1,0:T(1,128)} %broadcast_in_dim.40), calls=%async_computation.2 | async-start | bytes 49152 | tf_op jit(solution)/shard_map/all_to_all | solution.py:152
  91.9 11.6 %copy-start.11 = (bf16[8,248,256]{2,1,0:T(8,128)(2,1)S(1)}, bf16[8,248,256]{2,1,0:T(8,128)(2,1)}, u32[]{:S(2)}) copy-start(bf16[8,248,256]{2,1,0:T(8,128)(2,1)} %copy-done.10) | copy-start | bytes 3047428
  91.9 11.6 %copy-start.13 = (bf16[8,256,256]{2,1,0:T(8,128)(2,1)S(1)}, bf16[8,256,256]{2,1,0:T(8,128)(2,1)}, u32[]{:S(2)}) copy-start(bf16[8,256,256]{2,1,0:T(8,128)(2,1)} %copy-done.12) | copy-start | bytes 3145732
  103.5 1.0 copy-start.9
  106.0 1.2 copy-start.16
  106.0 1.9 %copy-start.17 = (f32[8,256,256]{2,1,0:T(8,128)S(1)}, f32[8,256,256]{2,1,0:T(8,128)}, u32[]{:S(2)}) copy-start(f32[8,256,256]{2,1,0:T(8,128)} %get-tuple-element.29) | copy-start | bytes 6291460
  109.5 0.9 copy-start.4
  111.3 2.6 %collective-permute-start = (f32[2,384,256]{2,1,0:T(8,128)}, f32[2,384,256]{2,1,0:T(8,128)}, u32[]{:S(2)}, u32[]{:S(2)}) collective-permute-start(f32[2,384,256]{2,1,0:T(8,128)} %fusion.64), channel_id=1, source_target_pairs={{0,1},{1,0},{2,3},{3,2},{4,5},{5,4},{6,7},{7,6},{8,9},{9,8},{10,11... | collective-permute-start | bytes 2359304 | tf_op jit(solution)/shard_map/ppermute | solution.py:125
  115.3 0.9 copy-start.5
  116.2 11.2 %collective-permute-start.1 = (f32[2,192,256]{2,1,0:T(8,128)S(1)}, f32[2,192,256]{2,1,0:T(8,128)S(1)}, u32[]{:S(2)}, u32[]{:S(2)}) collective-permute-start(f32[2,192,256]{2,1,0:T(8,128)S(1)} %constant_dynamic-slice_fusion.1), channel_id=1, source_target_pairs={{0,2},{1,3},{2,0},{3,1},{4,6},{5,7},{6,4},{7,5},{8,10},{9,11},{10,... | collective-permute-start | bytes 1179656 | tf_op jit(solution)/shard_map/ppermute | solution.py:125
  128.5 6.2 %collective-permute-start.2 = (f32[2,96,256]{2,1,0:T(8,128)S(1)}, f32[2,96,256]{2,1,0:T(8,128)S(1)}, u32[]{:S(2)}, u32[]{:S(2)}) collective-permute-start(f32[2,96,256]{2,1,0:T(8,128)S(1)} %constant_dynamic-slice_fusion), channel_id=1, source_target_pairs={{0,4},{1,5},{2,6},{3,7},{4,0},{5,1},{6,2},{7,3},{8,12},{9,13},{10,... | collective-permute-start | bytes 589832 | tf_op jit(solution)/shard_map/ppermute | solution.py:125
  134.7 7.5 %collective-permute-start.3 = (f32[2,48,256]{2,1,0:T(8,128)S(1)}, f32[2,48,256]{2,1,0:T(8,128)S(1)}, u32[]{:S(2)}, u32[]{:S(2)}) collective-permute-start(f32[2,48,256]{2,1,0:T(8,128)S(1)} %constant_dynamic-slice_fusion.2), channel_id=1, source_target_pairs={{0,8},{1,9},{2,10},{3,11},{4,12},{5,13},{6,14},{7,15},{8,0},{9,1},... | collective-permute-start | bytes 294920 | tf_op jit(solution)/shard_map/ppermute | solution.py:125
  142.3 5.7 %collective-permute-start.4 = (f32[2,48,256]{2,1,0:T(8,128)S(1)}, f32[2,48,256]{2,1,0:T(8,128)S(1)}, u32[]{:S(2)}, u32[]{:S(2)}) collective-permute-start(f32[2,48,256]{2,1,0:T(8,128)S(1)} %dynamic-slice_add_fusion.2), channel_id=1, source_target_pairs={{0,8},{1,9},{2,10},{3,11},{4,12},{5,13},{6,14},{7,15},{8,0},{9,1},... | collective-permute-start | bytes 294920 | tf_op jit(solution)/shard_map/ppermute | solution.py:129
  148.0 5.7 %collective-permute-start.5 = (f32[2,96,256]{2,1,0:T(8,128)S(1)}, f32[2,96,256]{2,1,0:T(8,128)S(1)}, u32[]{:S(2)}, u32[]{:S(2)}) collective-permute-start(f32[2,96,256]{2,1,0:T(8,128)S(1)} %pad_maximum_fusion.2), channel_id=1, source_target_pairs={{0,4},{1,5},{2,6},{3,7},{4,0},{5,1},{6,2},{7,3},{8,12},{9,13},{10,... | collective-permute-start | bytes 589832 | tf_op jit(solution)/shard_map/ppermute | solution.py:129
  153.8 0.7 copy-start.6
  153.8 0.7 copy-start.7
  154.5 7.9 %collective-permute-start.6 = (f32[2,192,256]{2,1,0:T(8,128)S(1)}, f32[2,192,256]{2,1,0:T(8,128)}, u32[]{:S(2)}, u32[]{:S(2)}) collective-permute-start(f32[2,192,256]{2,1,0:T(8,128)S(1)} %pad_maximum_fusion.1), channel_id=1, source_target_pairs={{0,2},{1,3},{2,0},{3,1},{4,6},{5,7},{6,4},{7,5},{8,10},{9,11},{10,... | collective-permute-start | bytes 1179656 | tf_op jit(solution)/shard_map/ppermute | solution.py:129
  164.6 2.6 %collective-permute-start.7 = (f32[2,384,256]{2,1,0:T(8,128)}, f32[2,384,256]{2,1,0:T(8,128)}, u32[]{:S(2)}, u32[]{:S(2)}) collective-permute-start(f32[2,384,256]{2,1,0:T(8,128)} %pad_maximum_fusion), channel_id=1, source_target_pairs={{0,1},{1,0},{2,3},{3,2},{4,5},{5,4},{6,7},{7,6},{8,9},{9,8},{10,11... | collective-permute-start | bytes 2359304 | tf_op jit(solution)/shard_map/ppermute | solution.py:129
  168.6 1.4 copy-start.3
  168.6 1.9 %copy-start.8 = (f32[2,196608]{1,0:T(2,128)S(1)}, f32[2,196608]{1,0:T(2,128)}, u32[]{:S(2)}) copy-start(f32[2,196608]{1,0:T(2,128)} %param.10) | copy-start | bytes 4718596

commit v4 on v3

--- a/solution.py
+++ b/solution.py
@@ -29,6 +29,13 @@
 def silu_slope(values):
     gate_value = jax.nn.sigmoid(values)
     return gate_value * (1.0 + values * (1.0 - gate_value))
+
+
+def softmax_rows(values):
+    shifted = values - lax.optimization_barrier(jnp.max(values, axis=-1, keepdims=True))
+    raised = jnp.exp(shifted)
+    total = lax.optimization_barrier(jnp.sum(raised, axis=-1, keepdims=True))
+    return raised / total
 
 
 def run_network(states, weights):
@@ -157,9 +164,9 @@
     total_sum = stats_all[:feat_width]
     count_all = stats_all[feat_width]
     center = total_sum / count_all
-    teacher_prob = jax.nn.softmax((teacher_out.astype(jnp.float32) - center) / tau_teacher, axis=-1)
+    teacher_prob = softmax_rows((teacher_out.astype(jnp.float32) - center) / tau_teacher)
     student_f = student_out.astype(jnp.float32)
-    student_prob = jax.nn.softmax(student_f / tau_student, axis=-1)
+    student_prob = softmax_rows(student_f / tau_student)
     embeddings = jnp.sum(valid_mask * student_f, axis=1) / counts.astype(jnp.float32)[:, None]
     upstream = valid_mask * (student_prob - teacher_prob) / (tau_student * objects_all)
     gradients = [None] * layer_total

time: 176 us -> 156 us (0.89)
  other arithmetic: 45.7 us -> 25.5 us
    div x2 -> x0, other arithmetic: 15.4 us -> none  [the longest x1 11.6 us: local(): student_prob = jax.nn.softmax(student_f / tau_student, axis=-1)]
    convert_element_type x0 -> x1, other arithmetic: none -> 3.69 us  [local(): delta_bf = (upstream * silu_slope(preacts[layer_at])).astype(jnp.bfloat16)]
    sub x1 -> x0, other arithmetic: 3.46 us -> none  [local(): jax.nn.softmax((teacher_out.astype(jnp.float32) - center) / tau_teacher,...]
    select_n x4, other arithmetic: 2.5 us -> 0.22 us  [all_reduce_wide(): low = jnp.where(bit == 0, buf, got)]
  transfers between devices with their start and end apart: 11 -> 11, of which waited for: 11 -> 11; matrix products, arithmetic and copies ran while one was open for 7% -> 6% of each run, Pallas kernels for 0% -> 0%
where the time goes in v4:
time: 156 us; the launch traced here: 155 us
  waiting for transfers between devices  72 us (46%)
  matrix products  25.8 us (17%)
  other arithmetic  25.5 us (16%)
  starting transfers between devices  20.5 us (13%)
  local copies, waits for them, and re-layouts  9.59 us (6%)
  between operations  1.91 us (1%)
    ppermute x4, waiting for transfers between devices, all_reduce_wide(): buf = keep + lax.ppermute(send, 'wide', pairs)  25.8 us
    ppermute x4, waiting for transfers between devices, all_reduce_wide(): got = lax.ppermute(buf, 'wide', pairs)  20.6 us
    all_to_all x1, waiting for transfers between devices, route_rows(): lax.all_to_all(send_rows.reshape(wide_count, capacity, feat_width), 'wide...  16.6 us
    dot_general x4, matrix products, run_network(): jnp.dot(stacked.reshape(-1, stacked.shape[2]), weights[layer_at], preferr...  8.33 us
    all_to_all x1, starting transfers between devices, route_rows(): lax.all_to_all(send_place.reshape(wide_count, capacity, per_dev), 'wide',...  7.36 us
    another operation x5, other arithmetic  7.27 us
    all_to_all x1, starting transfers between devices, local(): lax.all_to_all(jnp.broadcast_to(stats[None, :], (wide_count, stats.shape[...  6.83 us
    unnamed x42, local copies, waits for them, and re-layouts  6.72 us
  transfers between devices with their start and end apart: 11, of which 11 were waited for; matrix products, arithmetic and copies ran while one was open for 6% of the time, Pallas kernels for 0%

profile of v4, /device:TPU:0, one launch (start us, length us, event | category | flops | bytes accessed | tf_op | source)
XLA Modules:
  0.0 155.2 jit_solution(4331117007706528296)
XLA Ops:
  2.1 1.3 select_reduce_fusion
  4.2 4.5 %reduce-window.14 = s32[16,16,128]{2,1,0:T(8,128)S(1)} reduce-window(s32[16,16,128]{2,1,0:T(8,128)S(1)} %fusion.66, s32[]{:T(128)} %constant.32.clone.1), window={size=1x1x128 pad=0_0x0_0x127_0}, to_apply=%region_1.2 | reduce-window | flops 4161536 | bytes 262148 | tf_op jit(solution)/shard_map/reduce-window
  10.2 3.8 %fusion.46 = bf16[16,128,8]{1,2,0:T(8,128)(2,1)} fusion(s32[2048]{0:T(1024)S(1)} %get-tuple-element.28, s32[2048]{0:T(1024)S(1)} %get-tuple-element.27, pred[2048]{0:T(1024)(128)(4,1)S(1)} %broadcast_compare_fusion.1), kind=kOutput, calls=%fused_computation.76 | convolution fusion | flops 71352320 | bytes 51200 | tf_op jit(solution)/shard_map/dot_general | solution.py:86
  14.0 7.4 %all-to-all-start = ((bf16[16,128,8]{1,2,0:T(8,128)(2,1)}), bf16[16,128,8]{1,2,0:T(8,128)(2,1)S(1)}, u32[]{:S(2)}, u32[]{:S(2)}) async-start(bf16[16,128,8]{1,2,0:T(8,128)(2,1)} %fusion.46), calls=%async_computation | async-start | bytes 65536 | tf_op jit(solution)/shard_map/all_to_all | solution.py:95
  21.4 4.2 %fusion.22 = bf16[2048,256]{1,0:T(8,128)(2,1)} fusion(bf16[2048,256]{1,0:T(8,128)(2,1)S(1)} %copy-done, s32[2048]{0:T(1024)S(1)} %get-tuple-element.28), kind=kOutput, calls=%fused_computation.32 | convolution fusion | flops 2152202240 | bytes 2105344 | tf_op jit(solution)/shard_map/dot_general | solution.py:82
  25.5 2.5 %all-to-all-done = bf16[16,128,8]{1,2,0:T(8,128)(2,1)S(1)} async-done(((bf16[16,128,8]{1,2,0:T(8,128)(2,1)}), bf16[16,128,8]{1,2,0:T(8,128)(2,1)S(1)}, u32[]{:S(2)}, u32[]{:S(2)}) %all-to-all-start) | async-done | bytes 32800 | tf_op jit(solution)/shard_map/all_to_all | solution.py:95
  28.0 4.5 %all-to-all-start.1 = ((bf16[16,128,256]{2,1,0:T(8,128)(2,1)}), bf16[16,128,256]{2,1,0:T(8,128)(2,1)}, u32[]{:S(2)}, u32[]{:S(2)}) async-start(bf16[16,128,256]{2,1,0:T(8,128)(2,1)} %bitcast.159), calls=%async_computation.1 | async-start | bytes 2097152 | tf_op jit(solution)/shard_map/all_to_all | solution.py:88
  32.6 1.6 %copy-done.3 = f32[2,196608]{1,0:T(2,128)S(1)} copy-done((f32[2,196608]{1,0:T(2,128)S(1)}, f32[2,196608]{1,0:T(2,128)}, u32[]{:S(2)}) %copy-start.3) | copy-done | bytes 1572888
  34.4 2.3 %reduce-window.16 = s32[8,16,128]{2,1,0:T(8,128)S(1)} reduce-window(s32[8,16,128]{2,1,0:T(8,128)S(1)} %bitcast.166, s32[]{:T(128)} %constant.32.clone.1), window={size=1x1x128 pad=0_0x0_0x127_0}, to_apply=%region_6.7 | reduce-window | flops 2080768 | bytes 131076 | tf_op jit(solution)/shard_map/reduce-window.2
  38.7 16.6 %all-to-all-done.1 = bf16[16,128,256]{2,1,0:T(8,128)(2,1)} async-done(((bf16[16,128,256]{2,1,0:T(8,128)(2,1)}), bf16[16,128,256]{2,1,0:T(8,128)(2,1)}, u32[]{:S(2)}, u32[]{:S(2)}) %all-to-all-start.1) | async-done | bytes 1048608 | tf_op jit(solution)/shard_map/all_to_all | solution.py:88
  55.3 4.4 %fusion.21 = bf16[2048,256]{1,0:T(8,128)(2,1)S(1)} fusion(bf16[2048,256]{1,0:T(8,128)(2,1)} %bitcast.10, s32[2048]{0:T(1024)S(1)} %fusion.70), kind=kOutput, calls=%fused_computation.31 | convolution fusion | flops 2152202240 | bytes 2105344 | tf_op jit(solution)/shard_map/dot_general | solution.py:114
  59.7 1.5 fusion.25
  61.3 2.5 %fusion.24 = (bf16[8,256,256]{2,1,0:T(8,128)(2,1)S(1)}, f32[8,256,256]{2,1,0:T(8,128)}) fusion(bf16[8,256,256]{2,1,0:T(8,128)(2,1)S(1)} %bitcast.175, bf16[2,768,256]{2,1,0:T(8,128)(2,1)S(1)} %bitcast.155, bf16[8,254,256]{2,1,0:T(8,128)(2,1)S(1)} %bitcast.176, bf16[8,255,256]{2,1,0:T(8,128)(2,1)S(1)} %bitcast.177), kind=kOutput, calls=%fused_computation.34 | convolution fusion | flops 827850752 | bytes 7733248 | tf_op jit(solution)/shard_map/dot_general | solution.py:49
  63.9 2.5 %fusion.89 = (bf16[8,256]{1,0:T(8,128)(2,1)S(1)}, bf16[8,256,256]{2,1,0:T(8,128)(2,1)S(1)}, f32[8,256,256]{2,1,0:T(8,128)}) fusion(bf16[8,256,256]{2,1,0:T(8,128)(2,1)S(1)} %get-tuple-element.29, bf16[2,768,256]{2,1,0:T(8,128)(2,1)S(1)} %bitcast.156, bf16[8,248,256]{2,1,0:T(8,128)(2,1)S(1)} %slice.94, bf16[8,252,256]{2,1,0:T(8,128)(2,1)S(1)} %bitcast.160), kind=kOutput, calls=%fused_computation.166 | convolution fusion | flops 828372992 | bytes 7704576 | tf_op jit(solution)/shard_map/dot_general | solution.py:49
  66.4 1.8 %fusion.32 = (f32[8,256]{1,0:T(8,128)S(1)}, f32[8,256]{1,0:T(8,128)S(1)}, f32[256]{0:T(256)S(1)}, bf16[8,256,256]{2,1,0:T(8,128)(2,1)S(1)}) fusion(bf16[8,256,256]{2,1,0:T(8,128)(2,1)S(1)} %get-tuple-element.14, f32[8,256]{1,0:T(8,128)S(1)} %fusion.73, f32[8,256]{1,0:T(8,128)S(1)} %bitcast.167, bf16[2,768,256]{2,1,0:T(8,128)(2,1)S(1)} %bitcast.164, ...), kind=kOutput, calls=%fused_computation.42 | convolution fusion | flops 832040704 | bytes 6685696 | tf_op jit(solution)/shard_map/dot_general | solution.py:49
  68.9 6.8 %all-to-all-start.2 = ((f32[16,1,384]{2,1,0:T(1,128)}), f32[16,1,384]{2,1,0:T(1,128)S(1)}, u32[]{:S(2)}, u32[]{:S(2)}) async-start(f32[16,1,384]{2,1,0:T(1,128)} %broadcast_in_dim.47), calls=%async_computation.2 | async-start | bytes 49152 | tf_op jit(solution)/shard_map/all_to_all | solution.py:159
  75.8 6.5 %all-to-all-done.2 = f32[16,1,384]{2,1,0:T(1,128)S(1)} async-done(((f32[16,1,384]{2,1,0:T(1,128)}), f32[16,1,384]{2,1,0:T(1,128)S(1)}, u32[]{:S(2)}, u32[]{:S(2)}) %all-to-all-start.2) | async-done | bytes 24608 | tf_op jit(solution)/shard_map/all_to_all | solution.py:159
  84.8 3.7 %multiply_convert_fusion = bf16[8,256,256]{2,1,0:T(8,128)(2,1)S(1)} fusion(f32[8,256,256]{2,1,0:T(8,128)S(1)} %copy-done.6, f32[8,256]{1,0:T(8,128)S(1)} %fusion.39, f32[8,256]{1,0:T(8,128)S(1)} %fusion.36, f32[256]{0:T(256)S(1)} %slice_divide_fusion, bf16[8,256,256]{2,1,0:T(8,128)(2,1)S(1)} %get-tuple-element.32, f32[8,256]{1,0:T(8,128)S(1)} %get-tuple-element.5, ...), kind=kLoop, calls=%fused_computation.58 | loop fusion | flops 10485760 | bytes 5284864 | tf_op jit(solution)/shard_map/convert_element_type | solution.py:174
  88.5 1.0 convolution_bitcast_fusion
  91.4 1.1 copy-done.18
  93.2 3.1 %convolution_bitcast_fusion.1 = f32[1,768,256]{2,1,0:T(8,128)S(1)} fusion(f32[8,256,3,256]{3,1,0,2:T(8,128)S(1)} %fusion.47, f32[8,256,256]{2,1,0:T(8,128)S(1)} %copy-done.18, f32[8,248,256]{2,1,0:T(8,128)S(1)} %slice.104, f32[8,252,256]{2,1,0:T(8,128)S(1)} %slice.102, bf16[8,256,256]{2,1,0:T(8,128)(2,1)S(1)} %copy-done.9, ...), kind=kOutput, calls=%fused_computation.75 | convolution fusion | flops 836239360 | bytes 14394368 | tf_op jit(solution)/shard_map/dot_general | solution.py:176
  97.3 2.3 %collective-permute-done = f32[2,384,256]{2,1,0:T(8,128)S(1)} collective-permute-done((f32[2,384,256]{2,1,0:T(8,128)S(1)}, f32[2,384,256]{2,1,0:T(8,128)S(1)}, u32[]{:S(2)}, u32[]{:S(2)}) %collective-permute-start) | collective-permute-done | bytes 786464 | tf_op jit(solution)/shard_map/ppermute | solution.py:132
  99.6 1.1 fusion.56
  101.2 10.8 %collective-permute-done.1 = f32[2,192,256]{2,1,0:T(8,128)S(1)} collective-permute-done((f32[2,192,256]{2,1,0:T(8,128)S(1)}, f32[2,192,256]{2,1,0:T(8,128)S(1)}, u32[]{:S(2)}, u32[]{:S(2)}) %collective-permute-start.1) | collective-permute-done | bytes 393248 | tf_op jit(solution)/shard_map/ppermute | solution.py:132
  112.5 5.7 %collective-permute-done.2 = f32[2,96,256]{2,1,0:T(8,128)S(1)} collective-permute-done((f32[2,96,256]{2,1,0:T(8,128)S(1)}, f32[2,96,256]{2,1,0:T(8,128)S(1)}, u32[]{:S(2)}, u32[]{:S(2)}) %collective-permute-start.2) | collective-permute-done | bytes 196640 | tf_op jit(solution)/shard_map/ppermute | solution.py:132
  118.8 7.0 %collective-permute-done.3 = f32[2,48,256]{2,1,0:T(8,128)S(1)} collective-permute-done((f32[2,48,256]{2,1,0:T(8,128)S(1)}, f32[2,48,256]{2,1,0:T(8,128)S(1)}, u32[]{:S(2)}, u32[]{:S(2)}) %collective-permute-start.3) | collective-permute-done | bytes 98336 | tf_op jit(solution)/shard_map/ppermute | solution.py:132
  125.9 5.6 %collective-permute-done.4 = f32[2,48,256]{2,1,0:T(8,128)S(1)} collective-permute-done((f32[2,48,256]{2,1,0:T(8,128)S(1)}, f32[2,48,256]{2,1,0:T(8,128)S(1)}, u32[]{:S(2)}, u32[]{:S(2)}) %collective-permute-start.4) | collective-permute-done | bytes 98336 | tf_op jit(solution)/shard_map/ppermute | solution.py:136
  131.6 5.7 %collective-permute-done.5 = f32[2,96,256]{2,1,0:T(8,128)S(1)} collective-permute-done((f32[2,96,256]{2,1,0:T(8,128)S(1)}, f32[2,96,256]{2,1,0:T(8,128)S(1)}, u32[]{:S(2)}, u32[]{:S(2)}) %collective-permute-start.5) | collective-permute-done | bytes 196640 | tf_op jit(solution)/shard_map/ppermute | solution.py:136
  137.4 7.8 %collective-permute-done.6 = f32[2,192,256]{2,1,0:T(8,128)S(1)} collective-permute-done((f32[2,192,256]{2,1,0:T(8,128)S(1)}, f32[2,192,256]{2,1,0:T(8,128)S(1)}, u32[]{:S(2)}, u32[]{:S(2)}) %collective-permute-start.6) | collective-permute-done | bytes 393248 | tf_op jit(solution)/shard_map/ppermute | solution.py:136
  146.1 1.6 %collective-permute-done.7 = f32[2,384,256]{2,1,0:T(8,128)S(1)} collective-permute-done((f32[2,384,256]{2,1,0:T(8,128)S(1)}, f32[2,384,256]{2,1,0:T(8,128)S(1)}, u32[]{:S(2)}, u32[]{:S(2)}) %collective-permute-start.7) | collective-permute-done | bytes 786464 | tf_op jit(solution)/shard_map/ppermute | solution.py:136
  148.0 1.2 copy.77
  150.2 5.0 %multiply_add_fusion = (f32[2,196608]{1,0:T(2,128)}, f32[2,196608]{1,0:T(2,128)}, f32[2,196608]{1,0:T(2,128)}) fusion(f32[2,196608]{1,0:T(2,128)S(1)} %copy-done.2, f32[2,196608]{1,0:T(2,128)S(1)} %copy-done.4, f32[2,196608]{1,0:T(2,128)S(1)} %bitcast.154, f32[2,196608]{1,0:T(2,128)S(1)} %copy-done.7), kind=kLoop, calls=%fused_computation.71 | loop fusion | flops 2752512 | bytes 11010048 | tf_op jit(solution)/shard_map/add | solution.py:197
  (99 shorter events, 16.0 us)
Async XLA Ops:
  0.6 20.7 %copy-start = (bf16[2048,256]{1,0:T(8,128)(2,1)S(1)}, bf16[2048,256]{1,0:T(8,128)(2,1)}, u32[]{:S(2)}) copy-start(bf16[2048,256]{1,0:T(8,128)(2,1)} %param.6) | copy-start | bytes 3145732
  14.0 14.0 %all-to-all-start = ((bf16[16,128,8]{1,2,0:T(8,128)(2,1)}), bf16[16,128,8]{1,2,0:T(8,128)(2,1)S(1)}, u32[]{:S(2)}, u32[]{:S(2)}) async-start(bf16[16,128,8]{1,2,0:T(8,128)(2,1)} %fusion.46), calls=%async_computation | async-start | bytes 65536 | tf_op jit(solution)/shard_map/all_to_all | solution.py:95
  25.5 7.0 %copy-start.1 = (f32[2,196608]{1,0:T(2,128)S(1)}, f32[2,196608]{1,0:T(2,128)}, u32[]{:S(2)}) copy-start(f32[2,196608]{1,0:T(2,128)} %param.11) | copy-start | bytes 4718596
  28.0 27.3 %all-to-all-start.1 = ((bf16[16,128,256]{2,1,0:T(8,128)(2,1)}), bf16[16,128,256]{2,1,0:T(8,128)(2,1)}, u32[]{:S(2)}, u32[]{:S(2)}) async-start(bf16[16,128,256]{2,1,0:T(8,128)(2,1)} %bitcast.159), calls=%async_computation.1 | async-start | bytes 2097152 | tf_op jit(solution)/shard_map/all_to_all | solution.py:88
  32.5 1.7 %copy-start.3 = (f32[2,196608]{1,0:T(2,128)S(1)}, f32[2,196608]{1,0:T(2,128)}, u32[]{:S(2)}) copy-start(f32[2,196608]{1,0:T(2,128)} %param.9) | copy-start | bytes 4718596
  32.6 27.1 %copy-start.14 = (bf16[1,2,768,256]{3,2,1,0:T(8,128)(2,1)}, bf16[1,2,768,256]{3,2,1,0:T(8,128)(2,1)S(1)}, u32[]{:S(2)}) copy-start(bf16[1,2,768,256]{3,2,1,0:T(8,128)(2,1)S(1)} %copy.83) | copy-start | bytes 2359300
  59.7 1.6 %copy-start.16 = (bf16[2048,256]{1,0:T(8,128)(2,1)}, bf16[2048,256]{1,0:T(8,128)(2,1)S(1)}, u32[]{:S(2)}) copy-start(bf16[2048,256]{1,0:T(8,128)(2,1)S(1)} %fusion.21) | copy-start | bytes 3145732
  63.8 2.6 %copy-start.12 = (bf16[8,256,256]{2,1,0:T(8,128)(2,1)}, bf16[8,256,256]{2,1,0:T(8,128)(2,1)S(1)}, u32[]{:S(2)}) copy-start(bf16[8,256,256]{2,1,0:T(8,128)(2,1)S(1)} %get-tuple-element.29) | copy-start | bytes 3145732
  63.9 2.5 %copy-start.10 = (bf16[8,248,256]{2,1,0:T(8,128)(2,1)}, bf16[8,248,256]{2,1,0:T(8,128)(2,1)S(1)}, u32[]{:S(2)}) copy-start(bf16[8,248,256]{2,1,0:T(8,128)(2,1)S(1)} %slice.94) | copy-start | bytes 3047428
  63.9 2.5 %copy-start.15 = (bf16[1,2,768,256]{3,2,1,0:T(8,128)(2,1)S(1)}, bf16[1,2,768,256]{3,2,1,0:T(8,128)(2,1)}, u32[]{:S(2)}) copy-start(bf16[1,2,768,256]{3,2,1,0:T(8,128)(2,1)} %copy-done.14) | copy-start | bytes 2359300
  66.4 1.9 %copy-start.8 = (bf16[8,256,256]{2,1,0:T(8,128)(2,1)}, bf16[8,256,256]{2,1,0:T(8,128)(2,1)S(1)}, u32[]{:S(2)}) copy-start(bf16[8,256,256]{2,1,0:T(8,128)(2,1)S(1)} %get-tuple-element.14) | copy-start | bytes 3145732
  68.9 13.4 %all-to-all-start.2 = ((f32[16,1,384]{2,1,0:T(1,128)}), f32[16,1,384]{2,1,0:T(1,128)S(1)}, u32[]{:S(2)}, u32[]{:S(2)}) async-start(f32[16,1,384]{2,1,0:T(1,128)} %broadcast_in_dim.47), calls=%async_computation.2 | async-start | bytes 49152 | tf_op jit(solution)/shard_map/all_to_all | solution.py:159
  82.3 2.4 %copy-start.6 = (f32[8,256,256]{2,1,0:T(8,128)S(1)}, f32[8,256,256]{2,1,0:T(8,128)}, u32[]{:S(2)}) copy-start(f32[8,256,256]{2,1,0:T(8,128)} %get-tuple-element.31) | copy-start | bytes 6291460
  84.8 3.7 %copy-start.11 = (bf16[8,248,256]{2,1,0:T(8,128)(2,1)S(1)}, bf16[8,248,256]{2,1,0:T(8,128)(2,1)}, u32[]{:S(2)}) copy-start(bf16[8,248,256]{2,1,0:T(8,128)(2,1)} %copy-done.10) | copy-start | bytes 3047428
  84.8 3.7 %copy-start.13 = (bf16[8,256,256]{2,1,0:T(8,128)(2,1)S(1)}, bf16[8,256,256]{2,1,0:T(8,128)(2,1)}, u32[]{:S(2)}) copy-start(bf16[8,256,256]{2,1,0:T(8,128)(2,1)} %copy-done.12) | copy-start | bytes 3145732
  91.0 1.6 %copy-start.18 = (f32[8,256,256]{2,1,0:T(8,128)S(1)}, f32[8,256,256]{2,1,0:T(8,128)}, u32[]{:S(2)}) copy-start(f32[8,256,256]{2,1,0:T(8,128)} %get-tuple-element.30) | copy-start | bytes 6291460
  91.2 1.7 %copy-start.9 = (bf16[8,256,256]{2,1,0:T(8,128)(2,1)S(1)}, bf16[8,256,256]{2,1,0:T(8,128)(2,1)}, u32[]{:S(2)}) copy-start(bf16[8,256,256]{2,1,0:T(8,128)(2,1)} %copy-done.8) | copy-start | bytes 3145732
  91.2 2.0 %copy-start.17 = (bf16[2048,256]{1,0:T(8,128)(2,1)S(1)}, bf16[2048,256]{1,0:T(8,128)(2,1)}, u32[]{:S(2)}) copy-start(bf16[2048,256]{1,0:T(8,128)(2,1)} %copy-done.16) | copy-start | bytes 3145732
  96.3 0.9 copy-start.5
  97.3 2.4 %collective-permute-start = (f32[2,384,256]{2,1,0:T(8,128)S(1)}, f32[2,384,256]{2,1,0:T(8,128)S(1)}, u32[]{:S(2)}, u32[]{:S(2)}) collective-permute-start(f32[2,384,256]{2,1,0:T(8,128)S(1)} %fusion.54), channel_id=1, source_target_pairs={{0,1},{1,0},{2,3},{3,2},{4,5},{5,4},{6,7},{7,6},{8,9},{9,8},{10,11... | collective-permute-start | bytes 2359304 | tf_op jit(solution)/shard_map/ppermute | solution.py:132
  100.8 11.2 %collective-permute-start.1 = (f32[2,192,256]{2,1,0:T(8,128)S(1)}, f32[2,192,256]{2,1,0:T(8,128)S(1)}, u32[]{:S(2)}, u32[]{:S(2)}) collective-permute-start(f32[2,192,256]{2,1,0:T(8,128)S(1)} %constant_dynamic-slice_fusion.1), channel_id=1, source_target_pairs={{0,2},{1,3},{2,0},{3,1},{4,6},{5,7},{6,4},{7,5},{8,10},{9,11},{10,... | collective-permute-start | bytes 1179656 | tf_op jit(solution)/shard_map/ppermute | solution.py:132
  112.1 6.2 %collective-permute-start.2 = (f32[2,96,256]{2,1,0:T(8,128)S(1)}, f32[2,96,256]{2,1,0:T(8,128)S(1)}, u32[]{:S(2)}, u32[]{:S(2)}) collective-permute-start(f32[2,96,256]{2,1,0:T(8,128)S(1)} %constant_dynamic-slice_fusion), channel_id=1, source_target_pairs={{0,4},{1,5},{2,6},{3,7},{4,0},{5,1},{6,2},{7,3},{8,12},{9,13},{10,... | collective-permute-start | bytes 589832 | tf_op jit(solution)/shard_map/ppermute | solution.py:132
  118.3 7.5 %collective-permute-start.3 = (f32[2,48,256]{2,1,0:T(8,128)S(1)}, f32[2,48,256]{2,1,0:T(8,128)S(1)}, u32[]{:S(2)}, u32[]{:S(2)}) collective-permute-start(f32[2,48,256]{2,1,0:T(8,128)S(1)} %constant_dynamic-slice_fusion.2), channel_id=1, source_target_pairs={{0,8},{1,9},{2,10},{3,11},{4,12},{5,13},{6,14},{7,15},{8,0},{9,1},... | collective-permute-start | bytes 294920 | tf_op jit(solution)/shard_map/ppermute | solution.py:132
  125.8 5.7 %collective-permute-start.4 = (f32[2,48,256]{2,1,0:T(8,128)S(1)}, f32[2,48,256]{2,1,0:T(8,128)S(1)}, u32[]{:S(2)}, u32[]{:S(2)}) collective-permute-start(f32[2,48,256]{2,1,0:T(8,128)S(1)} %dynamic-slice_add_fusion.2), channel_id=1, source_target_pairs={{0,8},{1,9},{2,10},{3,11},{4,12},{5,13},{6,14},{7,15},{8,0},{9,1},... | collective-permute-start | bytes 294920 | tf_op jit(solution)/shard_map/ppermute | solution.py:136
  131.6 5.7 %collective-permute-start.5 = (f32[2,96,256]{2,1,0:T(8,128)S(1)}, f32[2,96,256]{2,1,0:T(8,128)S(1)}, u32[]{:S(2)}, u32[]{:S(2)}) collective-permute-start(f32[2,96,256]{2,1,0:T(8,128)S(1)} %pad_maximum_fusion.2), channel_id=1, source_target_pairs={{0,4},{1,5},{2,6},{3,7},{4,0},{5,1},{6,2},{7,3},{8,12},{9,13},{10,... | collective-permute-start | bytes 589832 | tf_op jit(solution)/shard_map/ppermute | solution.py:136
  137.4 7.8 %collective-permute-start.6 = (f32[2,192,256]{2,1,0:T(8,128)S(1)}, f32[2,192,256]{2,1,0:T(8,128)S(1)}, u32[]{:S(2)}, u32[]{:S(2)}) collective-permute-start(f32[2,192,256]{2,1,0:T(8,128)S(1)} %pad_maximum_fusion.1), channel_id=1, source_target_pairs={{0,2},{1,3},{2,0},{3,1},{4,6},{5,7},{6,4},{7,5},{8,10},{9,11},{10,... | collective-permute-start | bytes 1179656 | tf_op jit(solution)/shard_map/ppermute | solution.py:136
  145.3 2.4 %collective-permute-start.7 = (f32[2,384,256]{2,1,0:T(8,128)S(1)}, f32[2,384,256]{2,1,0:T(8,128)S(1)}, u32[]{:S(2)}, u32[]{:S(2)}) collective-permute-start(f32[2,384,256]{2,1,0:T(8,128)S(1)} %pad_maximum_fusion), channel_id=1, source_target_pairs={{0,1},{1,0},{2,3},{3,2},{4,5},{5,4},{6,7},{7,6},{8,9},{9,8},{10,11... | collective-permute-start | bytes 2359304 | tf_op jit(solution)/shard_map/ppermute | solution.py:136
  147.8 1.4 copy-start.7
  147.9 1.8 %copy-start.2 = (f32[2,196608]{1,0:T(2,128)S(1)}, f32[2,196608]{1,0:T(2,128)}, u32[]{:S(2)}) copy-start(f32[2,196608]{1,0:T(2,128)} %param.11) | copy-start | bytes 4718596
  147.9 2.3 %copy-start.4 = (f32[2,196608]{1,0:T(2,128)S(1)}, f32[2,196608]{1,0:T(2,128)}, u32[]{:S(2)}) copy-start(f32[2,196608]{1,0:T(2,128)} %param.9) | copy-start | bytes 4718596

commit v5 on v4

--- a/solution.py
+++ b/solution.py
@@ -79,11 +79,14 @@
     pick = (
         jnp.arange(rows_total, dtype=jnp.int32)[:, None] == send_index[None, :]
     ).astype(jnp.bfloat16)
-    send_rows = jnp.dot(pick, epoch_rows, preferred_element_type=jnp.float32).astype(jnp.bfloat16)
     place_hot = (
         (local_place[:, None] == jnp.arange(per_dev, dtype=jnp.int32)[None, :]) & live_rows[:, None]
     ).astype(jnp.bfloat16)
-    send_place = jnp.dot(pick, place_hot, preferred_element_type=jnp.float32).astype(jnp.bfloat16)
+    sent = jnp.dot(
+        pick, jnp.concatenate([epoch_rows, place_hot], axis=1), preferred_element_type=jnp.float32
+    ).astype(jnp.bfloat16)
+    send_rows = sent[:, :feat_width]
+    send_place = sent[:, feat_width:]
     got_rows, got_place = (
         lax.all_to_all(
             send_rows.reshape(wide_count, capacity, feat_width),
@@ -130,6 +133,7 @@
         send = lax.dynamic_slice_in_dim(buf, (1 - bit) * half, half, axis=1)
         pairs = [(i, i ^ (1 << step)) for i in range(wide_count)]
         buf = keep + lax.ppermute(send, "wide", pairs)
+    buf = buf.astype(jnp.bfloat16)
     for step in reversed(range(steps)):
         bit = (me >> step) & 1
         pairs = [(i, i ^ (1 << step)) for i in range(wide_count)]
@@ -137,7 +141,7 @@
         low = jnp.where(bit == 0, buf, got)
         high = jnp.where(bit == 0, got, buf)
         buf = jnp.concatenate([low, high], axis=1)
-    return buf.reshape(buf.shape[0], -1)
+    return buf.reshape(buf.shape[0], -1).astype(jnp.float32)
 
 
 def local(epoch_rows, row_object, object_slot, master, momentum, teacher):

time: 156 us -> 153 us (0.981)
  matrix products: 25.8 us -> 21.5 us
  local copies, waits for them, and re-layouts: 9.59 us -> 13.8 us
  waiting for transfers between devices: 72 us -> 69 us
    ppermute x4, waiting for transfers between devices: 20.6 us -> 16 us  [all_reduce_wide(): got = lax.ppermute(buf, 'wide', pairs)]
    dot_general x2 -> x1, matrix products: 7.9 us -> 4.85 us  [route_rows(): jnp.dot(pick, jnp.concatenate([epoch_rows, place_hot], axis=1), preferred...]
    all_to_all x1, waiting for transfers between devices: 2.47 us -> 5.38 us  [route_rows(): lax.all_to_all(send_place.reshape(wide_count, capacity, per_dev), 'wide',...]
    reshape x0 -> x2, local copies, waits for them, and re-layouts: none -> 1.87 us  [the longest x1 1.24 us: route_rows(): send_rows.reshape(wide_count, capacity, feat_width)]
    unnamed x42 -> x40, local copies, waits for them, and re-layouts: 6.72 us -> 6.57 us
  transfers between devices with their start and end apart: 11 -> 11, of which waited for: 11 -> 11; matrix products, arithmetic and copies ran while one was open for 6% -> 5% of each run, Pallas kernels for 0% -> 0%
where the time goes in v5:
time: 153 us; the launch traced here: 152 us
  waiting for transfers between devices  69 us (45%)
  other arithmetic  25.5 us (17%)
  matrix products  21.5 us (14%)
  starting transfers between devices  20.7 us (14%)
  local copies, waits for them, and re-layouts  13.8 us (9%)
  between operations  1.87 us (1%)
    ppermute x4, waiting for transfers between devices, all_reduce_wide(): buf = keep + lax.ppermute(send, 'wide', pairs)  25.4 us
    all_to_all x1, waiting for transfers between devices, route_rows(): lax.all_to_all(send_rows.reshape(wide_count, capacity, feat_width), 'wide...  16.4 us
    ppermute x4, waiting for transfers between devices, all_reduce_wide(): got = lax.ppermute(buf, 'wide', pairs)  16 us
    dot_general x4, matrix products, run_network(): jnp.dot(stacked.reshape(-1, stacked.shape[2]), weights[layer_at], preferr...  8.34 us
    all_to_all x1, starting transfers between devices, route_rows(): lax.all_to_all(send_place.reshape(wide_count, capacity, per_dev), 'wide',...  7.34 us
    another operation x5, other arithmetic  7.27 us
    all_to_all x1, starting transfers between devices, local(): lax.all_to_all(jnp.broadcast_to(stats[None, :], (wide_count, stats.shape[...  6.81 us
    unnamed x40, local copies, waits for them, and re-layouts  6.57 us
  transfers between devices with their start and end apart: 11, of which 11 were waited for; matrix products, arithmetic and copies ran while one was open for 5% of the time, Pallas kernels for 0%

profile of v5, /device:TPU:0, one launch (start us, length us, event | category | flops | bytes accessed | tf_op | source)
XLA Modules:
  0.0 152.3 jit_solution(15965422367035592475)
XLA Ops:
  2.0 1.3 select_reduce_fusion
  4.1 4.5 %reduce-window.14 = s32[16,16,128]{2,1,0:T(8,128)S(1)} reduce-window(s32[16,16,128]{2,1,0:T(8,128)S(1)} %fusion.61, s32[]{:T(128)} %constant.32.clone.1), window={size=1x1x128 pad=0_0x0_0x127_0}, to_apply=%region_1.2 | reduce-window | flops 4161536 | bytes 262148 | tf_op jit(solution)/shard_map/reduce-window
  10.4 4.8 %fusion.19 = bf16[2048,264]{0,1:T(8,128)(2,1)S(1)} fusion(s32[2048]{0:T(1024)S(1)} %get-tuple-element.28, bf16[2048,8]{1,0:T(8,128)(2,1)S(1)} %copy.90, bf16[2048,256]{1,0:T(8,128)(2,1)} %param.6), kind=kOutput, calls=%fused_computation.29 | convolution fusion | flops 2221490176 | bytes 2170880 | tf_op jit(solution)/shard_map/dot_general | solution.py:85
  15.9 7.3 %all-to-all-start = ((bf16[16,128,8]{1,2,0:T(8,128)(2,1)}), bf16[16,128,8]{1,2,0:T(8,128)(2,1)S(1)}, u32[]{:S(2)}, u32[]{:S(2)}) async-start(bf16[16,128,8]{1,2,0:T(8,128)(2,1)} %slice_bitcast_fusion.10), calls=%async_computation | async-start | bytes 65536 | tf_op jit(solution)/shard_map/all_to_all | solution.py:98
  23.3 1.2 copy_bitcast_fusion.2
  24.5 5.4 %all-to-all-done = bf16[16,128,8]{1,2,0:T(8,128)(2,1)S(1)} async-done(((bf16[16,128,8]{1,2,0:T(8,128)(2,1)}), bf16[16,128,8]{1,2,0:T(8,128)(2,1)S(1)}, u32[]{:S(2)}, u32[]{:S(2)}) %all-to-all-start) | async-done | bytes 32800 | tf_op jit(solution)/shard_map/all_to_all | solution.py:98
  29.9 4.5 %all-to-all-start.1 = ((bf16[16,128,256]{1,2,0:T(8,128)(2,1)}), bf16[16,128,256]{1,2,0:T(8,128)(2,1)}, u32[]{:S(2)}, u32[]{:S(2)}) async-start(bf16[16,128,256]{1,2,0:T(8,128)(2,1)} %copy_bitcast_fusion.2), calls=%async_computation.1 | async-start | bytes 2097152 | tf_op jit(solution)/shard_map/all_to_all | solution.py:91
  36.5 2.3 %reduce-window.16 = s32[8,16,128]{2,1,0:T(8,128)S(1)} reduce-window(s32[8,16,128]{2,1,0:T(8,128)S(1)} %bitcast.169, s32[]{:T(128)} %constant.32.clone.1), window={size=1x1x128 pad=0_0x0_0x127_0}, to_apply=%region_6.7 | reduce-window | flops 2080768 | bytes 131076 | tf_op jit(solution)/shard_map/reduce-window.2
  40.8 16.4 %all-to-all-done.1 = bf16[16,128,256]{1,2,0:T(8,128)(2,1)} async-done(((bf16[16,128,256]{1,2,0:T(8,128)(2,1)}), bf16[16,128,256]{1,2,0:T(8,128)(2,1)}, u32[]{:S(2)}, u32[]{:S(2)}) %all-to-all-start.1) | async-done | bytes 1048608 | tf_op jit(solution)/shard_map/all_to_all | solution.py:91
  57.2 1.5 copy.92
  58.7 3.2 %fusion.20 = bf16[2048,256]{1,0:T(8,128)(2,1)S(1)} fusion(bf16[2048,256]{1,0:T(8,128)(2,1)S(1)} %bitcast.162, s32[2048]{0:T(1024)S(1)} %fusion.67), kind=kOutput, calls=%fused_computation.30 | convolution fusion | flops 2152202240 | bytes 2105344 | tf_op jit(solution)/shard_map/dot_general | solution.py:117
  61.9 1.5 fusion.22
  63.5 2.5 %fusion.21 = (bf16[8,256,256]{2,1,0:T(8,128)(2,1)S(1)}, f32[8,256,256]{2,1,0:T(8,128)}) fusion(bf16[8,256,256]{2,1,0:T(8,128)(2,1)S(1)} %bitcast.178, bf16[2,768,256]{2,1,0:T(8,128)(2,1)S(1)} %bitcast.158, bf16[8,254,256]{2,1,0:T(8,128)(2,1)S(1)} %bitcast.179, bf16[8,255,256]{2,1,0:T(8,128)(2,1)S(1)} %bitcast.180), kind=kOutput, calls=%fused_computation.31 | convolution fusion | flops 827850752 | bytes 7733248 | tf_op jit(solution)/shard_map/dot_general | solution.py:49
  66.1 2.5 %fusion.87 = (bf16[8,256]{1,0:T(8,128)(2,1)S(1)}, bf16[8,256,256]{2,1,0:T(8,128)(2,1)S(1)}, f32[8,256,256]{2,1,0:T(8,128)}) fusion(bf16[8,256,256]{2,1,0:T(8,128)(2,1)S(1)} %get-tuple-element.29, bf16[2,768,256]{2,1,0:T(8,128)(2,1)S(1)} %bitcast.159, bf16[8,248,256]{2,1,0:T(8,128)(2,1)S(1)} %slice.104, bf16[8,252,256]{2,1,0:T(8,128)(2,1)S(1)} %bitcast.163), kind=kOutput, calls=%fused_computation.168 | convolution fusion | flops 828372992 | bytes 7704576 | tf_op jit(solution)/shard_map/dot_general | solution.py:49
  68.6 1.8 %fusion.29 = (f32[8,256]{1,0:T(8,128)S(1)}, f32[8,256]{1,0:T(8,128)S(1)}, f32[256]{0:T(256)S(1)}, bf16[8,256,256]{2,1,0:T(8,128)(2,1)S(1)}) fusion(bf16[8,256,256]{2,1,0:T(8,128)(2,1)S(1)} %get-tuple-element.14, f32[8,256]{1,0:T(8,128)S(1)} %fusion.70, f32[8,256]{1,0:T(8,128)S(1)} %bitcast.170, bf16[2,768,256]{2,1,0:T(8,128)(2,1)S(1)} %bitcast.167, ...), kind=kOutput, calls=%fused_computation.39 | convolution fusion | flops 832040704 | bytes 6685696 | tf_op jit(solution)/shard_map/dot_general | solution.py:49
  71.1 6.8 %all-to-all-start.2 = ((f32[16,1,384]{2,1,0:T(1,128)}), f32[16,1,384]{2,1,0:T(1,128)S(1)}, u32[]{:S(2)}, u32[]{:S(2)}) async-start(f32[16,1,384]{2,1,0:T(1,128)} %broadcast_in_dim.47), calls=%async_computation.2 | async-start | bytes 49152 | tf_op jit(solution)/shard_map/all_to_all | solution.py:163
  78.7 5.8 %all-to-all-done.2 = f32[16,1,384]{2,1,0:T(1,128)S(1)} async-done(((f32[16,1,384]{2,1,0:T(1,128)}), f32[16,1,384]{2,1,0:T(1,128)S(1)}, u32[]{:S(2)}, u32[]{:S(2)}) %all-to-all-start.2) | async-done | bytes 24608 | tf_op jit(solution)/shard_map/all_to_all | solution.py:163
  87.0 3.7 %multiply_convert_fusion = bf16[8,256,256]{2,1,0:T(8,128)(2,1)S(1)} fusion(f32[8,256,256]{2,1,0:T(8,128)S(1)} %copy-done.4, f32[8,256]{1,0:T(8,128)S(1)} %fusion.36, f32[8,256]{1,0:T(8,128)S(1)} %fusion.33, f32[256]{0:T(256)S(1)} %slice_divide_fusion, bf16[8,256,256]{2,1,0:T(8,128)(2,1)S(1)} %get-tuple-element.32, f32[8,256]{1,0:T(8,128)S(1)} %get-tuple-element.5, ...), kind=kLoop, calls=%fused_computation.55 | loop fusion | flops 10485760 | bytes 5284864 | tf_op jit(solution)/shard_map/convert_element_type | solution.py:178
  90.7 1.0 convolution_bitcast_fusion
  93.6 1.1 copy-done.17
  95.4 3.1 %convolution_bitcast_fusion.1 = f32[1,768,256]{2,1,0:T(8,128)S(1)} fusion(f32[8,256,3,256]{3,1,0,2:T(8,128)S(1)} %fusion.46, f32[8,256,256]{2,1,0:T(8,128)S(1)} %copy-done.17, f32[8,248,256]{2,1,0:T(8,128)S(1)} %slice.114, f32[8,252,256]{2,1,0:T(8,128)S(1)} %slice.112, bf16[8,256,256]{2,1,0:T(8,128)(2,1)S(1)} %copy-done.9, ...), kind=kOutput, calls=%fused_computation.75 | convolution fusion | flops 836239360 | bytes 14394368 | tf_op jit(solution)/shard_map/dot_general | solution.py:180
  99.5 2.4 %collective-permute-done = f32[2,384,256]{2,1,0:T(8,128)} collective-permute-done((f32[2,384,256]{2,1,0:T(8,128)S(1)}, f32[2,384,256]{2,1,0:T(8,128)}, u32[]{:S(2)}, u32[]{:S(2)}) %collective-permute-start) | collective-permute-done | bytes 786464 | tf_op jit(solution)/shard_map/ppermute | solution.py:135
  101.9 1.3 fusion.53
  103.8 10.8 %collective-permute-done.1 = f32[2,192,256]{2,1,0:T(8,128)S(1)} collective-permute-done((f32[2,192,256]{2,1,0:T(8,128)S(1)}, f32[2,192,256]{2,1,0:T(8,128)S(1)}, u32[]{:S(2)}, u32[]{:S(2)}) %collective-permute-start.1) | collective-permute-done | bytes 393248 | tf_op jit(solution)/shard_map/ppermute | solution.py:135
  115.1 5.7 %collective-permute-done.2 = f32[2,96,256]{2,1,0:T(8,128)S(1)} collective-permute-done((f32[2,96,256]{2,1,0:T(8,128)S(1)}, f32[2,96,256]{2,1,0:T(8,128)S(1)}, u32[]{:S(2)}, u32[]{:S(2)}) %collective-permute-start.2) | collective-permute-done | bytes 196640 | tf_op jit(solution)/shard_map/ppermute | solution.py:135
  121.4 6.5 %collective-permute-done.3 = f32[2,48,256]{2,1,0:T(8,128)S(1)} collective-permute-done((f32[2,48,256]{2,1,0:T(8,128)S(1)}, f32[2,48,256]{2,1,0:T(8,128)S(1)}, u32[]{:S(2)}, u32[]{:S(2)}) %collective-permute-start.3) | collective-permute-done | bytes 98336 | tf_op jit(solution)/shard_map/ppermute | solution.py:135
  127.9 5.0 %collective-permute-done.4 = bf16[2,48,256]{2,1,0:T(8,128)(2,1)S(1)} collective-permute-done((bf16[2,48,256]{2,1,0:T(8,128)(2,1)S(1)}, bf16[2,48,256]{2,1,0:T(8,128)(2,1)S(1)}, u32[]{:S(2)}, u32[]{:S(2)}) %collective-permute-start.4) | collective-permute-done | bytes 49184 | tf_op jit(solution)/shard_map/ppermute | solution.py:140
  133.0 4.6 %collective-permute-done.5 = bf16[2,96,256]{2,1,0:T(8,128)(2,1)S(1)} collective-permute-done((bf16[2,96,256]{2,1,0:T(8,128)(2,1)S(1)}, bf16[2,96,256]{2,1,0:T(8,128)(2,1)S(1)}, u32[]{:S(2)}, u32[]{:S(2)}) %collective-permute-start.5) | collective-permute-done | bytes 98336 | tf_op jit(solution)/shard_map/ppermute | solution.py:140
  138.0 5.4 %collective-permute-done.6 = bf16[2,192,256]{2,1,0:T(8,128)(2,1)S(1)} collective-permute-done((bf16[2,192,256]{2,1,0:T(8,128)(2,1)S(1)}, bf16[2,192,256]{2,1,0:T(8,128)(2,1)S(1)}, u32[]{:S(2)}, u32[]{:S(2)}) %collective-permute-start.6) | collective-permute-done | bytes 196640 | tf_op jit(solution)/shard_map/ppermute | solution.py:140
  144.3 1.0 collective-permute-done.7
  145.6 1.2 copy.125
  147.5 4.8 %multiply_add_fusion = (f32[2,196608]{1,0:T(2,128)}, f32[2,196608]{1,0:T(2,128)}, f32[2,196608]{1,0:T(2,128)}) fusion(f32[2,196608]{1,0:T(2,128)S(1)} %copy-done, f32[2,196608]{1,0:T(2,128)S(1)} %copy-done.2, f32[2,196608]{1,0:T(2,128)S(1)} %bitcast.157, f32[2,196608]{1,0:T(2,128)S(1)} %copy-done.6), kind=kLoop, calls=%fused_computation.71 | loop fusion | flops 2752512 | bytes 11010048 | tf_op jit(solution)/shard_map/add | solution.py:201
  (101 shorter events, 19.2 us)
Async XLA Ops:
  15.9 14.0 %all-to-all-start = ((bf16[16,128,8]{1,2,0:T(8,128)(2,1)}), bf16[16,128,8]{1,2,0:T(8,128)(2,1)S(1)}, u32[]{:S(2)}, u32[]{:S(2)}) async-start(bf16[16,128,8]{1,2,0:T(8,128)(2,1)} %slice_bitcast_fusion.10), calls=%async_computation | async-start | bytes 65536 | tf_op jit(solution)/shard_map/all_to_all | solution.py:98
  23.3 11.2 %copy-start = (f32[2,196608]{1,0:T(2,128)S(1)}, f32[2,196608]{1,0:T(2,128)}, u32[]{:S(2)}) copy-start(f32[2,196608]{1,0:T(2,128)} %param.11) | copy-start | bytes 4718596
  24.5 10.9 %copy-start.1 = (f32[2,196608]{1,0:T(2,128)S(1)}, f32[2,196608]{1,0:T(2,128)}, u32[]{:S(2)}) copy-start(f32[2,196608]{1,0:T(2,128)} %param.9) | copy-start | bytes 4718596
  29.9 27.3 %all-to-all-start.1 = ((bf16[16,128,256]{1,2,0:T(8,128)(2,1)}), bf16[16,128,256]{1,2,0:T(8,128)(2,1)}, u32[]{:S(2)}, u32[]{:S(2)}) async-start(bf16[16,128,256]{1,2,0:T(8,128)(2,1)} %copy_bitcast_fusion.2), calls=%async_computation.1 | async-start | bytes 2097152 | tf_op jit(solution)/shard_map/all_to_all | solution.py:91
  58.7 3.2 %copy-start.14 = (bf16[1,2,768,256]{3,2,1,0:T(8,128)(2,1)S(1)}, bf16[1,2,768,256]{3,2,1,0:T(8,128)(2,1)}, u32[]{:S(2)}) copy-start(bf16[1,2,768,256]{3,2,1,0:T(8,128)(2,1)} %copy.132) | copy-start | bytes 2359300
  61.9 1.6 %copy-start.15 = (bf16[2048,256]{1,0:T(8,128)(2,1)}, bf16[2048,256]{1,0:T(8,128)(2,1)S(1)}, u32[]{:S(2)}) copy-start(bf16[2048,256]{1,0:T(8,128)(2,1)S(1)} %fusion.20) | copy-start | bytes 3145732
  61.9 1.6 %copy-start.5 = (bf16[1,2,768,256]{3,2,1,0:T(8,128)(2,1)S(1)}, bf16[1,2,768,256]{3,2,1,0:T(8,128)(2,1)}, u32[]{:S(2)}) copy-start(bf16[1,2,768,256]{3,2,1,0:T(8,128)(2,1)} %copy.133) | copy-start | bytes 2359300
  66.0 2.6 %copy-start.12 = (bf16[8,256,256]{2,1,0:T(8,128)(2,1)}, bf16[8,256,256]{2,1,0:T(8,128)(2,1)S(1)}, u32[]{:S(2)}) copy-start(bf16[8,256,256]{2,1,0:T(8,128)(2,1)S(1)} %get-tuple-element.29) | copy-start | bytes 3145732
  66.1 2.5 %copy-start.10 = (bf16[8,248,256]{2,1,0:T(8,128)(2,1)}, bf16[8,248,256]{2,1,0:T(8,128)(2,1)S(1)}, u32[]{:S(2)}) copy-start(bf16[8,248,256]{2,1,0:T(8,128)(2,1)S(1)} %slice.104) | copy-start | bytes 3047428
  68.6 1.9 %copy-start.8 = (bf16[8,256,256]{2,1,0:T(8,128)(2,1)}, bf16[8,256,256]{2,1,0:T(8,128)(2,1)S(1)}, u32[]{:S(2)}) copy-start(bf16[8,256,256]{2,1,0:T(8,128)(2,1)S(1)} %get-tuple-element.14) | copy-start | bytes 3145732
  71.1 13.4 %all-to-all-start.2 = ((f32[16,1,384]{2,1,0:T(1,128)}), f32[16,1,384]{2,1,0:T(1,128)S(1)}, u32[]{:S(2)}, u32[]{:S(2)}) async-start(f32[16,1,384]{2,1,0:T(1,128)} %broadcast_in_dim.47), calls=%async_computation.2 | async-start | bytes 49152 | tf_op jit(solution)/shard_map/all_to_all | solution.py:163
  84.5 2.4 %copy-start.4 = (f32[8,256,256]{2,1,0:T(8,128)S(1)}, f32[8,256,256]{2,1,0:T(8,128)}, u32[]{:S(2)}) copy-start(f32[8,256,256]{2,1,0:T(8,128)} %get-tuple-element.31) | copy-start | bytes 6291460
  87.0 3.7 %copy-start.11 = (bf16[8,248,256]{2,1,0:T(8,128)(2,1)S(1)}, bf16[8,248,256]{2,1,0:T(8,128)(2,1)}, u32[]{:S(2)}) copy-start(bf16[8,248,256]{2,1,0:T(8,128)(2,1)} %copy-done.10) | copy-start | bytes 3047428
  87.0 3.7 %copy-start.13 = (bf16[8,256,256]{2,1,0:T(8,128)(2,1)S(1)}, bf16[8,256,256]{2,1,0:T(8,128)(2,1)}, u32[]{:S(2)}) copy-start(bf16[8,256,256]{2,1,0:T(8,128)(2,1)} %copy-done.12) | copy-start | bytes 3145732
  90.7 1.0 copy-start.7
  93.2 1.6 %copy-start.17 = (f32[8,256,256]{2,1,0:T(8,128)S(1)}, f32[8,256,256]{2,1,0:T(8,128)}, u32[]{:S(2)}) copy-start(f32[8,256,256]{2,1,0:T(8,128)} %get-tuple-element.30) | copy-start | bytes 6291460
  93.4 1.7 %copy-start.9 = (bf16[8,256,256]{2,1,0:T(8,128)(2,1)S(1)}, bf16[8,256,256]{2,1,0:T(8,128)(2,1)}, u32[]{:S(2)}) copy-start(bf16[8,256,256]{2,1,0:T(8,128)(2,1)} %copy-done.8) | copy-start | bytes 3145732
  93.4 2.0 %copy-start.16 = (bf16[2048,256]{1,0:T(8,128)(2,1)S(1)}, bf16[2048,256]{1,0:T(8,128)(2,1)}, u32[]{:S(2)}) copy-start(bf16[2048,256]{1,0:T(8,128)(2,1)} %copy-done.15) | copy-start | bytes 3145732
  98.5 0.9 copy-start.3
  99.5 2.5 %collective-permute-start = (f32[2,384,256]{2,1,0:T(8,128)S(1)}, f32[2,384,256]{2,1,0:T(8,128)}, u32[]{:S(2)}, u32[]{:S(2)}) collective-permute-start(f32[2,384,256]{2,1,0:T(8,128)S(1)} %fusion.51), channel_id=1, source_target_pairs={{0,1},{1,0},{2,3},{3,2},{4,5},{5,4},{6,7},{7,6},{8,9},{9,8},{10,11... | collective-permute-start | bytes 2359304 | tf_op jit(solution)/shard_map/ppermute | solution.py:135
  103.3 11.2 %collective-permute-start.1 = (f32[2,192,256]{2,1,0:T(8,128)S(1)}, f32[2,192,256]{2,1,0:T(8,128)S(1)}, u32[]{:S(2)}, u32[]{:S(2)}) collective-permute-start(f32[2,192,256]{2,1,0:T(8,128)S(1)} %constant_dynamic-slice_fusion.1), channel_id=1, source_target_pairs={{0,2},{1,3},{2,0},{3,1},{4,6},{5,7},{6,4},{7,5},{8,10},{9,11},{10,... | collective-permute-start | bytes 1179656 | tf_op jit(solution)/shard_map/ppermute | solution.py:135
  114.6 6.2 %collective-permute-start.2 = (f32[2,96,256]{2,1,0:T(8,128)S(1)}, f32[2,96,256]{2,1,0:T(8,128)S(1)}, u32[]{:S(2)}, u32[]{:S(2)}) collective-permute-start(f32[2,96,256]{2,1,0:T(8,128)S(1)} %constant_dynamic-slice_fusion), channel_id=1, source_target_pairs={{0,4},{1,5},{2,6},{3,7},{4,0},{5,1},{6,2},{7,3},{8,12},{9,13},{10,... | collective-permute-start | bytes 589832 | tf_op jit(solution)/shard_map/ppermute | solution.py:135
  120.9 7.0 %collective-permute-start.3 = (f32[2,48,256]{2,1,0:T(8,128)S(1)}, f32[2,48,256]{2,1,0:T(8,128)S(1)}, u32[]{:S(2)}, u32[]{:S(2)}) collective-permute-start(f32[2,48,256]{2,1,0:T(8,128)S(1)} %constant_dynamic-slice_fusion.2), channel_id=1, source_target_pairs={{0,8},{1,9},{2,10},{3,11},{4,12},{5,13},{6,14},{7,15},{8,0},{9,1},... | collective-permute-start | bytes 294920 | tf_op jit(solution)/shard_map/ppermute | solution.py:135
  127.9 5.1 %collective-permute-start.4 = (bf16[2,48,256]{2,1,0:T(8,128)(2,1)S(1)}, bf16[2,48,256]{2,1,0:T(8,128)(2,1)S(1)}, u32[]{:S(2)}, u32[]{:S(2)}) collective-permute-start(bf16[2,48,256]{2,1,0:T(8,128)(2,1)S(1)} %add_convert_fusion.2), channel_id=1, source_target_pairs={{0,8},{1,9},{2,10},{3,11},{4,12},{5,13},{6,14},{7,15},{8,0},{9,1},... | collective-permute-start | bytes 147464 | tf_op jit(solution)/shard_map/ppermute | solution.py:140
  132.9 4.7 %collective-permute-start.5 = (bf16[2,96,256]{2,1,0:T(8,128)(2,1)S(1)}, bf16[2,96,256]{2,1,0:T(8,128)(2,1)S(1)}, u32[]{:S(2)}, u32[]{:S(2)}) collective-permute-start(bf16[2,96,256]{2,1,0:T(8,128)(2,1)S(1)} %pad_maximum_fusion.2), channel_id=1, source_target_pairs={{0,4},{1,5},{2,6},{3,7},{4,0},{5,1},{6,2},{7,3},{8,12},{9,13},{10,... | collective-permute-start | bytes 294920 | tf_op jit(solution)/shard_map/ppermute | solution.py:140
  137.7 5.7 %collective-permute-start.6 = (bf16[2,192,256]{2,1,0:T(8,128)(2,1)S(1)}, bf16[2,192,256]{2,1,0:T(8,128)(2,1)S(1)}, u32[]{:S(2)}, u32[]{:S(2)}) collective-permute-start(bf16[2,192,256]{2,1,0:T(8,128)(2,1)S(1)} %pad_maximum_fusion.1), channel_id=1, source_target_pairs={{0,2},{1,3},{2,0},{3,1},{4,6},{5,7},{6,4},{7,5},{8,10},{9,11},{10,... | collective-permute-start | bytes 589832 | tf_op jit(solution)/shard_map/ppermute | solution.py:140
  143.5 1.8 %collective-permute-start.7 = (bf16[2,384,256]{2,1,0:T(8,128)(2,1)S(1)}, bf16[2,384,256]{2,1,0:T(8,128)(2,1)S(1)}, u32[]{:S(2)}, u32[]{:S(2)}) collective-permute-start(bf16[2,384,256]{2,1,0:T(8,128)(2,1)S(1)} %pad_maximum_fusion), channel_id=1, source_target_pairs={{0,1},{1,0},{2,3},{3,2},{4,5},{5,4},{6,7},{7,6},{8,9},{9,8},{10,11... | collective-permute-start | bytes 1179656 | tf_op jit(solution)/shard_map/ppermute | solution.py:140
  145.6 1.4 copy-start.2
  145.6 1.9 %copy-start.6 = (f32[2,196608]{1,0:T(2,128)S(1)}, f32[2,196608]{1,0:T(2,128)}, u32[]{:S(2)}) copy-start(f32[2,196608]{1,0:T(2,128)} %param.10) | copy-start | bytes 4718596

commit v6 on v5

--- a/solution.py
+++ b/solution.py
@@ -85,25 +85,20 @@
     sent = jnp.dot(
         pick, jnp.concatenate([epoch_rows, place_hot], axis=1), preferred_element_type=jnp.float32
     ).astype(jnp.bfloat16)
-    send_rows = sent[:, :feat_width]
-    send_place = sent[:, feat_width:]
-    got_rows, got_place = (
-        lax.all_to_all(
-            send_rows.reshape(wide_count, capacity, feat_width),
-            "wide",
-            split_axis=0,
-            concat_axis=0,
-            tiled=True,
-        ),
-        lax.all_to_all(
-            send_place.reshape(wide_count, capacity, per_dev),
-            "wide",
-            split_axis=0,
-            concat_axis=0,
-            tiled=True,
-        ),
-    )
-    place_hot = got_place.reshape(-1, per_dev) > 0
+    meta_rows = 16
+    meta = sent[:, feat_width:].reshape(wide_count, capacity * per_dev)
+    meta = jnp.pad(meta, ((0, 0), (0, meta_rows * feat_width - capacity * per_dev)))
+    payload = jnp.concatenate(
+        [
+            sent[:, :feat_width].reshape(wide_count, capacity, feat_width),
+            meta.reshape(wide_count, meta_rows, feat_width),
+        ],
+        axis=1,
+    )
+    got = lax.all_to_all(payload, "wide", split_axis=0, concat_axis=0, tiled=True)
+    got_meta = got[:, capacity:, :].reshape(wide_count, meta_rows * feat_width)
+    got_place = got_meta[:, : capacity * per_dev].reshape(wide_count, capacity, per_dev)
+    place_hot = jnp.pad(got_place > 0, ((0, 0), (0, meta_rows), (0, 0))).reshape(-1, per_dev)
     arrival = jnp.cumsum(place_hot.astype(jnp.int32), axis=0)
     position = jnp.sum(jnp.where(place_hot, arrival, 0), axis=1) - 1
     place_code = jnp.sum(
@@ -115,7 +110,7 @@
         jnp.arange(per_dev * SEQ, dtype=jnp.int32)[:, None] == target[None, :]
     ).astype(jnp.bfloat16)
     sequences = jnp.dot(
-        put, got_rows.reshape(-1, feat_width), preferred_element_type=jnp.float32
+        put, got.reshape(-1, feat_width), preferred_element_type=jnp.float32
     ).astype(jnp.bfloat16)
     return (sequences.reshape(per_dev, SEQ, feat_width), counts)
 

time: 153 us -> 159 us (1.039)
  matrix products: 21.5 us -> 25.8 us
  starting transfers between devices: 20.7 us -> 16.9 us
  local copies, waits for them, and re-layouts: 13.8 us -> 15.9 us
  waiting for transfers between devices: 69 us -> 70.6 us
    all_to_all x2 -> x1, starting transfers between devices: 11.9 us -> 7.4 us  [route_rows(): lax.all_to_all(payload, 'wide', split_axis=0, concat_axis=0, tiled=True)]
    dot_general x4, matrix products: 8.34 us -> 11 us  [run_network(): jnp.dot(stacked.reshape(-1, stacked.shape[2]), weights[layer_at], preferr...]
    dot_general x1, matrix products: 3.18 us -> 4.81 us  [route_rows(): jnp.dot(put, got.reshape(-1, feat_width), preferred_element_type=jnp.floa...]
    all_to_all x2 -> x1, waiting for transfers between devices: 21.8 us -> 23.4 us  [route_rows(): lax.all_to_all(payload, 'wide', split_axis=0, concat_axis=0, tiled=True)]
    unnamed x40 -> x42, local copies, waits for them, and re-layouts: 6.57 us -> 7.5 us
    another operation x5 -> x6, other arithmetic: 7.27 us -> 7.3 us
  transfers between devices with their start and end apart: 11 -> 10, of which waited for: 11 -> 10; matrix products, arithmetic and copies ran while one was open for 5% -> 2% of each run, Pallas kernels for 0% -> 0%
where the time goes in v6:
time: 159 us; the launch traced here: 158 us
  waiting for transfers between devices  70.6 us (44%)
  other arithmetic  27 us (17%)
  matrix products  25.8 us (16%)
  starting transfers between devices  16.9 us (11%)
  local copies, waits for them, and re-layouts  15.9 us (10%)
  between operations  1.94 us (1%)
    ppermute x4, waiting for transfers between devices, all_reduce_wide(): buf = keep + lax.ppermute(send, 'wide', pairs)  25.4 us
    all_to_all x1, waiting for transfers between devices, route_rows(): lax.all_to_all(payload, 'wide', split_axis=0, concat_axis=0, tiled=True)  23.4 us
    ppermute x4, waiting for transfers between devices, all_reduce_wide(): got = lax.ppermute(buf, 'wide', pairs)  16 us
    dot_general x4, matrix products, run_network(): jnp.dot(stacked.reshape(-1, stacked.shape[2]), weights[layer_at], preferr...  11 us
    unnamed x42, local copies, waits for them, and re-layouts  7.5 us
    all_to_all x1, starting transfers between devices, local(): lax.all_to_all(jnp.broadcast_to(stats[None, :], (wide_count, stats.shape[...  7.49 us
    all_to_all x1, starting transfers between devices, route_rows(): lax.all_to_all(payload, 'wide', split_axis=0, concat_axis=0, tiled=True)  7.4 us
    another operation x6, other arithmetic  7.3 us
  transfers between devices with their start and end apart: 10, of which 10 were waited for; matrix products, arithmetic and copies ran while one was open for 2% of the time, Pallas kernels for 0%

profile of v6, /device:TPU:0, one launch (start us, length us, event | category | flops | bytes accessed | tf_op | source)
XLA Modules:
  0.0 158.1 jit_solution(8536084632855453400)
XLA Ops:
  2.0 1.3 select_reduce_fusion
  4.1 4.5 %reduce-window.14 = s32[16,16,128]{2,1,0:T(8,128)S(1)} reduce-window(s32[16,16,128]{2,1,0:T(8,128)S(1)} %fusion.61, s32[]{:T(128)} %constant.35.clone.1), window={size=1x1x128 pad=0_0x0_0x127_0}, to_apply=%region_1.2 | reduce-window | flops 4161536 | bytes 262148 | tf_op jit(solution)/shard_map/reduce-window
  10.4 4.8 %fusion.19 = bf16[2048,264]{0,1:T(8,128)(2,1)S(1)} fusion(s32[2048]{0:T(1024)S(1)} %get-tuple-element.26, bf16[2048,8]{1,0:T(8,128)(2,1)S(1)} %copy.130, bf16[2048,256]{1,0:T(8,128)(2,1)} %param.6), kind=kOutput, calls=%fused_computation.29 | convolution fusion | flops 2221490176 | bytes 2170880 | tf_op jit(solution)/shard_map/dot_general | solution.py:85
  18.1 1.1 pad_maximum_fusion
  19.2 7.4 %all-to-all-start = ((bf16[16,144,256]{2,1,0:T(8,128)(2,1)}), bf16[16,144,256]{2,1,0:T(8,128)(2,1)}, u32[]{:S(2)}, u32[]{:S(2)}) async-start(bf16[16,144,256]{2,1,0:T(8,128)(2,1)} %pad_maximum_fusion), calls=%async_computation | async-start | bytes 2359296 | tf_op jit(solution)/shard_map/all_to_all | solution.py:98
  26.6 1.0 copy.177
  28.3 23.4 %all-to-all-done = bf16[16,144,256]{2,1,0:T(8,128)(2,1)} async-done(((bf16[16,144,256]{2,1,0:T(8,128)(2,1)}), bf16[16,144,256]{2,1,0:T(8,128)(2,1)}, u32[]{:S(2)}, u32[]{:S(2)}) %all-to-all-start) | async-done | bytes 1179680 | tf_op jit(solution)/shard_map/all_to_all | solution.py:98
  54.5 2.3 %reduce-window.16 = s32[8,18,128]{2,1,0:T(8,128)S(1)} reduce-window(s32[8,18,128]{2,1,0:T(8,128)S(1)} %copy.137, s32[]{:T(128)} %constant.35.clone.1), window={size=1x1x128 pad=0_0x0_0x127_0}, to_apply=%region_6.7 | reduce-window | flops 2340864 | bytes 147460 | tf_op jit(solution)/shard_map/reduce-window.2
  57.8 4.8 %fusion.20 = bf16[2048,256]{1,0:T(8,128)(2,1)S(1)} fusion(bf16[2304,256]{1,0:T(8,128)(2,1)} %bitcast.8, s32[2304]{0:T(1024)S(1)} %add_select_fusion), kind=kOutput, calls=%fused_computation.30 | convolution fusion | flops 2421161984 | bytes 2237440 | tf_op jit(solution)/shard_map/dot_general | solution.py:112
  62.7 1.5 fusion.22
  64.2 1.1 slice.118
  65.3 2.5 %fusion.21 = (bf16[8,256,256]{2,1,0:T(8,128)(2,1)S(1)}, f32[8,256,256]{2,1,0:T(8,128)}) fusion(bf16[8,256,256]{2,1,0:T(8,128)(2,1)S(1)} %bitcast.174, bf16[2,768,256]{2,1,0:T(8,128)(2,1)S(1)} %bitcast.152, bf16[8,254,256]{2,1,0:T(8,128)(2,1)S(1)} %bitcast.175, bf16[8,255,256]{2,1,0:T(8,128)(2,1)S(1)} %bitcast.176), kind=kOutput, calls=%fused_computation.31 | convolution fusion | flops 827850752 | bytes 7733248 | tf_op jit(solution)/shard_map/dot_general | solution.py:49
  67.9 2.6 %fusion.86 = (bf16[8,256]{1,0:T(8,128)(2,1)S(1)}, bf16[8,256,256]{2,1,0:T(8,128)(2,1)}, f32[8,256,256]{2,1,0:T(8,128)}) fusion(bf16[8,256,256]{2,1,0:T(8,128)(2,1)S(1)} %get-tuple-element.27, bf16[2,768,256]{2,1,0:T(8,128)(2,1)S(1)} %bitcast.153, bf16[8,248,256]{2,1,0:T(8,128)(2,1)S(1)} %slice.114, bf16[8,252,256]{2,1,0:T(8,128)(2,1)S(1)} %bitcast.156), kind=kOutput, calls=%fused_computation.166 | convolution fusion | flops 828372992 | bytes 7704576 | tf_op jit(solution)/shard_map/dot_general | solution.py:49
  71.3 4.3 %fusion.29 = (f32[8,256]{1,0:T(8,128)S(1)}, f32[8,256]{1,0:T(8,128)S(1)}, f32[256]{0:T(256)S(1)}, bf16[8,256,256]{2,1,0:T(8,128)(2,1)S(1)}) fusion(bf16[8,256,256]{2,1,0:T(8,128)(2,1)} %get-tuple-element.14, f32[8,256]{1,0:T(8,128)S(1)} %fusion.69, f32[8,256]{1,0:T(8,128)S(1)} %bitcast.166, bf16[2,768,256]{2,1,0:T(8,128)(2,1)} %bitcast.159, ...), kind=kOutput, calls=%fused_computation.39 | convolution fusion | flops 832040704 | bytes 6685696 | tf_op jit(solution)/shard_map/dot_general | solution.py:49
  76.2 7.5 %all-to-all-start.1 = ((f32[16,1,384]{2,1,0:T(1,128)}), f32[16,1,384]{2,1,0:T(1,128)S(1)}, u32[]{:S(2)}, u32[]{:S(2)}) async-start(f32[16,1,384]{2,1,0:T(1,128)} %broadcast_in_dim.51), calls=%async_computation.1 | async-start | bytes 49152 | tf_op jit(solution)/shard_map/all_to_all | solution.py:158
  84.5 5.8 %all-to-all-done.1 = f32[16,1,384]{2,1,0:T(1,128)S(1)} async-done(((f32[16,1,384]{2,1,0:T(1,128)}), f32[16,1,384]{2,1,0:T(1,128)S(1)}, u32[]{:S(2)}, u32[]{:S(2)}) %all-to-all-start.1) | async-done | bytes 24608 | tf_op jit(solution)/shard_map/all_to_all | solution.py:158
  92.8 3.7 %multiply_convert_fusion = bf16[8,256,256]{2,1,0:T(8,128)(2,1)S(1)} fusion(f32[8,256,256]{2,1,0:T(8,128)S(1)} %copy-done.4, f32[8,256]{1,0:T(8,128)S(1)} %fusion.36, f32[8,256]{1,0:T(8,128)S(1)} %fusion.33, f32[256]{0:T(256)S(1)} %slice_divide_fusion, bf16[8,256,256]{2,1,0:T(8,128)(2,1)S(1)} %get-tuple-element.30, f32[8,256]{1,0:T(8,128)S(1)} %get-tuple-element.5, ...), kind=kLoop, calls=%fused_computation.55 | loop fusion | flops 10485760 | bytes 5284864 | tf_op jit(solution)/shard_map/convert_element_type | solution.py:173
  96.5 1.0 convolution_bitcast_fusion
  97.6 1.0 fusion.46
  99.4 1.1 copy-done.17
  101.2 3.1 %convolution_bitcast_fusion.1 = f32[1,768,256]{2,1,0:T(8,128)S(1)} fusion(f32[8,256,3,256]{3,1,0,2:T(8,128)S(1)} %fusion.46, f32[8,256,256]{2,1,0:T(8,128)S(1)} %copy-done.17, f32[8,248,256]{2,1,0:T(8,128)S(1)} %slice.124, f32[8,252,256]{2,1,0:T(8,128)S(1)} %slice.122, bf16[8,256,256]{2,1,0:T(8,128)(2,1)S(1)} %copy-done.8, ...), kind=kOutput, calls=%fused_computation.75 | convolution fusion | flops 836239360 | bytes 14394368 | tf_op jit(solution)/shard_map/dot_general | solution.py:175
  105.4 2.4 %collective-permute-done = f32[2,384,256]{2,1,0:T(8,128)} collective-permute-done((f32[2,384,256]{2,1,0:T(8,128)S(1)}, f32[2,384,256]{2,1,0:T(8,128)}, u32[]{:S(2)}, u32[]{:S(2)}) %collective-permute-start) | collective-permute-done | bytes 786464 | tf_op jit(solution)/shard_map/ppermute | solution.py:130
  107.8 1.3 fusion.53
  109.6 10.8 %collective-permute-done.1 = f32[2,192,256]{2,1,0:T(8,128)S(1)} collective-permute-done((f32[2,192,256]{2,1,0:T(8,128)S(1)}, f32[2,192,256]{2,1,0:T(8,128)S(1)}, u32[]{:S(2)}, u32[]{:S(2)}) %collective-permute-start.1) | collective-permute-done | bytes 393248 | tf_op jit(solution)/shard_map/ppermute | solution.py:130
  120.9 5.7 %collective-permute-done.2 = f32[2,96,256]{2,1,0:T(8,128)S(1)} collective-permute-done((f32[2,96,256]{2,1,0:T(8,128)S(1)}, f32[2,96,256]{2,1,0:T(8,128)S(1)}, u32[]{:S(2)}, u32[]{:S(2)}) %collective-permute-start.2) | collective-permute-done | bytes 196640 | tf_op jit(solution)/shard_map/ppermute | solution.py:130
  127.2 6.5 %collective-permute-done.3 = f32[2,48,256]{2,1,0:T(8,128)S(1)} collective-permute-done((f32[2,48,256]{2,1,0:T(8,128)S(1)}, f32[2,48,256]{2,1,0:T(8,128)S(1)}, u32[]{:S(2)}, u32[]{:S(2)}) %collective-permute-start.3) | collective-permute-done | bytes 98336 | tf_op jit(solution)/shard_map/ppermute | solution.py:130
  133.8 5.0 %collective-permute-done.4 = bf16[2,48,256]{2,1,0:T(8,128)(2,1)S(1)} collective-permute-done((bf16[2,48,256]{2,1,0:T(8,128)(2,1)S(1)}, bf16[2,48,256]{2,1,0:T(8,128)(2,1)S(1)}, u32[]{:S(2)}, u32[]{:S(2)}) %collective-permute-start.4) | collective-permute-done | bytes 49184 | tf_op jit(solution)/shard_map/ppermute | solution.py:135
  138.9 4.6 %collective-permute-done.5 = bf16[2,96,256]{2,1,0:T(8,128)(2,1)S(1)} collective-permute-done((bf16[2,96,256]{2,1,0:T(8,128)(2,1)S(1)}, bf16[2,96,256]{2,1,0:T(8,128)(2,1)S(1)}, u32[]{:S(2)}, u32[]{:S(2)}) %collective-permute-start.5) | collective-permute-done | bytes 98336 | tf_op jit(solution)/shard_map/ppermute | solution.py:135
  143.8 5.5 %collective-permute-done.6 = bf16[2,192,256]{2,1,0:T(8,128)(2,1)S(1)} collective-permute-done((bf16[2,192,256]{2,1,0:T(8,128)(2,1)S(1)}, bf16[2,192,256]{2,1,0:T(8,128)(2,1)S(1)}, u32[]{:S(2)}, u32[]{:S(2)}) %collective-permute-start.6) | collective-permute-done | bytes 196640 | tf_op jit(solution)/shard_map/ppermute | solution.py:135
  150.1 1.0 collective-permute-done.7
  151.5 1.2 copy.171
  153.3 4.8 %multiply_add_fusion = (f32[2,196608]{1,0:T(2,128)}, f32[2,196608]{1,0:T(2,128)}, f32[2,196608]{1,0:T(2,128)}) fusion(f32[2,196608]{1,0:T(2,128)S(1)} %copy-done, f32[2,196608]{1,0:T(2,128)S(1)} %copy-done.2, f32[2,196608]{1,0:T(2,128)S(1)} %bitcast.147, f32[2,196608]{1,0:T(2,128)S(1)} %copy-done.5), kind=kLoop, calls=%fused_computation.71 | loop fusion | flops 2752512 | bytes 11010048 | tf_op jit(solution)/shard_map/add | solution.py:196
  (117 shorter events, 21.4 us)
Async XLA Ops:
  15.3 1.0 copy-start.7
  16.3 0.8 slice-start
  18.0 8.5 %copy-start = (f32[2,196608]{1,0:T(2,128)S(1)}, f32[2,196608]{1,0:T(2,128)}, u32[]{:S(2)}) copy-start(f32[2,196608]{1,0:T(2,128)} %param.11) | copy-start | bytes 4718596
  19.2 32.6 %all-to-all-start = ((bf16[16,144,256]{2,1,0:T(8,128)(2,1)}), bf16[16,144,256]{2,1,0:T(8,128)(2,1)}, u32[]{:S(2)}, u32[]{:S(2)}) async-start(bf16[16,144,256]{2,1,0:T(8,128)(2,1)} %pad_maximum_fusion), calls=%async_computation | async-start | bytes 2359296 | tf_op jit(solution)/shard_map/all_to_all | solution.py:98
  26.6 1.7 %copy-start.1 = (f32[2,196608]{1,0:T(2,128)S(1)}, f32[2,196608]{1,0:T(2,128)}, u32[]{:S(2)}) copy-start(f32[2,196608]{1,0:T(2,128)} %param.9) | copy-start | bytes 4718596
  57.8 4.8 %copy-start.14 = (bf16[1,2,768,256]{3,2,1,0:T(8,128)(2,1)S(1)}, bf16[1,2,768,256]{3,2,1,0:T(8,128)(2,1)}, u32[]{:S(2)}) copy-start(bf16[1,2,768,256]{3,2,1,0:T(8,128)(2,1)} %copy.177) | copy-start | bytes 2359300
  62.7 2.7 %copy-start.15 = (bf16[2048,256]{1,0:T(8,128)(2,1)}, bf16[2048,256]{1,0:T(8,128)(2,1)S(1)}, u32[]{:S(2)}) copy-start(bf16[2048,256]{1,0:T(8,128)(2,1)S(1)} %fusion.20) | copy-start | bytes 3145732
  64.2 3.6 %copy-start.13 = (bf16[8,256,256]{2,1,0:T(8,128)(2,1)}, bf16[8,256,256]{2,1,0:T(8,128)(2,1)S(1)}, u32[]{:S(2)}) copy-start(bf16[8,256,256]{2,1,0:T(8,128)(2,1)S(1)} %fusion.22) | copy-start | bytes 3145732
  67.8 2.7 %copy-start.11 = (bf16[8,256,256]{2,1,0:T(8,128)(2,1)}, bf16[8,256,256]{2,1,0:T(8,128)(2,1)S(1)}, u32[]{:S(2)}) copy-start(bf16[8,256,256]{2,1,0:T(8,128)(2,1)S(1)} %get-tuple-element.27) | copy-start | bytes 3145732
  67.9 2.7 %copy-start.9 = (bf16[8,248,256]{2,1,0:T(8,128)(2,1)}, bf16[8,248,256]{2,1,0:T(8,128)(2,1)S(1)}, u32[]{:S(2)}) copy-start(bf16[8,248,256]{2,1,0:T(8,128)(2,1)S(1)} %slice.114) | copy-start | bytes 3047428
  76.2 14.1 %all-to-all-start.1 = ((f32[16,1,384]{2,1,0:T(1,128)}), f32[16,1,384]{2,1,0:T(1,128)S(1)}, u32[]{:S(2)}, u32[]{:S(2)}) async-start(f32[16,1,384]{2,1,0:T(1,128)} %broadcast_in_dim.51), calls=%async_computation.1 | async-start | bytes 49152 | tf_op jit(solution)/shard_map/all_to_all | solution.py:158
  90.3 2.4 %copy-start.4 = (f32[8,256,256]{2,1,0:T(8,128)S(1)}, f32[8,256,256]{2,1,0:T(8,128)}, u32[]{:S(2)}) copy-start(f32[8,256,256]{2,1,0:T(8,128)} %get-tuple-element.29) | copy-start | bytes 6291460
  92.8 3.7 %copy-start.10 = (bf16[8,248,256]{2,1,0:T(8,128)(2,1)S(1)}, bf16[8,248,256]{2,1,0:T(8,128)(2,1)}, u32[]{:S(2)}) copy-start(bf16[8,248,256]{2,1,0:T(8,128)(2,1)} %copy-done.9) | copy-start | bytes 3047428
  92.8 3.7 %copy-start.12 = (bf16[8,256,256]{2,1,0:T(8,128)(2,1)S(1)}, bf16[8,256,256]{2,1,0:T(8,128)(2,1)}, u32[]{:S(2)}) copy-start(bf16[8,256,256]{2,1,0:T(8,128)(2,1)} %copy-done.11) | copy-start | bytes 3145732
  96.5 1.0 copy-start.6
  99.0 1.6 %copy-start.17 = (f32[8,256,256]{2,1,0:T(8,128)S(1)}, f32[8,256,256]{2,1,0:T(8,128)}, u32[]{:S(2)}) copy-start(f32[8,256,256]{2,1,0:T(8,128)} %get-tuple-element.28) | copy-start | bytes 6291460
  99.2 1.7 %copy-start.8 = (bf16[8,256,256]{2,1,0:T(8,128)(2,1)S(1)}, bf16[8,256,256]{2,1,0:T(8,128)(2,1)}, u32[]{:S(2)}) copy-start(bf16[8,256,256]{2,1,0:T(8,128)(2,1)} %get-tuple-element.14) | copy-start | bytes 3145732
  99.2 2.0 %copy-start.16 = (bf16[2048,256]{1,0:T(8,128)(2,1)S(1)}, bf16[2048,256]{1,0:T(8,128)(2,1)}, u32[]{:S(2)}) copy-start(bf16[2048,256]{1,0:T(8,128)(2,1)} %copy-done.15) | copy-start | bytes 3145732
  104.3 0.9 copy-start.3
  105.3 2.5 %collective-permute-start = (f32[2,384,256]{2,1,0:T(8,128)S(1)}, f32[2,384,256]{2,1,0:T(8,128)}, u32[]{:S(2)}, u32[]{:S(2)}) collective-permute-start(f32[2,384,256]{2,1,0:T(8,128)S(1)} %fusion.51), channel_id=1, source_target_pairs={{0,1},{1,0},{2,3},{3,2},{4,5},{5,4},{6,7},{7,6},{8,9},{9,8},{10,11... | collective-permute-start | bytes 2359304 | tf_op jit(solution)/shard_map/ppermute | solution.py:130
  109.1 11.2 %collective-permute-start.1 = (f32[2,192,256]{2,1,0:T(8,128)S(1)}, f32[2,192,256]{2,1,0:T(8,128)S(1)}, u32[]{:S(2)}, u32[]{:S(2)}) collective-permute-start(f32[2,192,256]{2,1,0:T(8,128)S(1)} %constant_dynamic-slice_fusion.1), channel_id=1, source_target_pairs={{0,2},{1,3},{2,0},{3,1},{4,6},{5,7},{6,4},{7,5},{8,10},{9,11},{10,... | collective-permute-start | bytes 1179656 | tf_op jit(solution)/shard_map/ppermute | solution.py:130
  120.4 6.2 %collective-permute-start.2 = (f32[2,96,256]{2,1,0:T(8,128)S(1)}, f32[2,96,256]{2,1,0:T(8,128)S(1)}, u32[]{:S(2)}, u32[]{:S(2)}) collective-permute-start(f32[2,96,256]{2,1,0:T(8,128)S(1)} %constant_dynamic-slice_fusion), channel_id=1, source_target_pairs={{0,4},{1,5},{2,6},{3,7},{4,0},{5,1},{6,2},{7,3},{8,12},{9,13},{10,... | collective-permute-start | bytes 589832 | tf_op jit(solution)/shard_map/ppermute | solution.py:130
  126.7 7.0 %collective-permute-start.3 = (f32[2,48,256]{2,1,0:T(8,128)S(1)}, f32[2,48,256]{2,1,0:T(8,128)S(1)}, u32[]{:S(2)}, u32[]{:S(2)}) collective-permute-start(f32[2,48,256]{2,1,0:T(8,128)S(1)} %constant_dynamic-slice_fusion.2), channel_id=1, source_target_pairs={{0,8},{1,9},{2,10},{3,11},{4,12},{5,13},{6,14},{7,15},{8,0},{9,1},... | collective-permute-start | bytes 294920 | tf_op jit(solution)/shard_map/ppermute | solution.py:130
  133.7 5.1 %collective-permute-start.4 = (bf16[2,48,256]{2,1,0:T(8,128)(2,1)S(1)}, bf16[2,48,256]{2,1,0:T(8,128)(2,1)S(1)}, u32[]{:S(2)}, u32[]{:S(2)}) collective-permute-start(bf16[2,48,256]{2,1,0:T(8,128)(2,1)S(1)} %add_convert_fusion.2), channel_id=1, source_target_pairs={{0,8},{1,9},{2,10},{3,11},{4,12},{5,13},{6,14},{7,15},{8,0},{9,1},... | collective-permute-start | bytes 147464 | tf_op jit(solution)/shard_map/ppermute | solution.py:135
  138.8 4.7 %collective-permute-start.5 = (bf16[2,96,256]{2,1,0:T(8,128)(2,1)S(1)}, bf16[2,96,256]{2,1,0:T(8,128)(2,1)S(1)}, u32[]{:S(2)}, u32[]{:S(2)}) collective-permute-start(bf16[2,96,256]{2,1,0:T(8,128)(2,1)S(1)} %pad_maximum_fusion.3), channel_id=1, source_target_pairs={{0,4},{1,5},{2,6},{3,7},{4,0},{5,1},{6,2},{7,3},{8,12},{9,13},{10,... | collective-permute-start | bytes 294920 | tf_op jit(solution)/shard_map/ppermute | solution.py:135
  143.5 5.7 %collective-permute-start.6 = (bf16[2,192,256]{2,1,0:T(8,128)(2,1)S(1)}, bf16[2,192,256]{2,1,0:T(8,128)(2,1)S(1)}, u32[]{:S(2)}, u32[]{:S(2)}) collective-permute-start(bf16[2,192,256]{2,1,0:T(8,128)(2,1)S(1)} %pad_maximum_fusion.2), channel_id=1, source_target_pairs={{0,2},{1,3},{2,0},{3,1},{4,6},{5,7},{6,4},{7,5},{8,10},{9,11},{10,... | collective-permute-start | bytes 589832 | tf_op jit(solution)/shard_map/ppermute | solution.py:135
  149.4 1.8 %collective-permute-start.7 = (bf16[2,384,256]{2,1,0:T(8,128)(2,1)S(1)}, bf16[2,384,256]{2,1,0:T(8,128)(2,1)S(1)}, u32[]{:S(2)}, u32[]{:S(2)}) collective-permute-start(bf16[2,384,256]{2,1,0:T(8,128)(2,1)S(1)} %pad_maximum_fusion.1), channel_id=1, source_target_pairs={{0,1},{1,0},{2,3},{3,2},{4,5},{5,4},{6,7},{7,6},{8,9},{9,8},{10,11... | collective-permute-start | bytes 1179656 | tf_op jit(solution)/shard_map/ppermute | solution.py:135
  151.4 1.4 copy-start.2
  151.5 1.9 %copy-start.5 = (f32[2,196608]{1,0:T(2,128)S(1)}, f32[2,196608]{1,0:T(2,128)}, u32[]{:S(2)}) copy-start(f32[2,196608]{1,0:T(2,128)} %param.10) | copy-start | bytes 4718596

commit v7 on v5

--- a/solution.py
+++ b/solution.py
@@ -124,19 +124,30 @@
     wide_count = lax.axis_size("wide")
     steps = wide_count.bit_length() - 1
     assert 1 << steps == wide_count
+    order_even = list(range(steps))
+    order_odd = [0] + list(range(2, steps)) + [1] if steps > 2 else order_even
     me = lax.axis_index("wide")
+    odd = me & 1
+
+    def exchange_at(step):
+        pairs = []
+        for i in range(wide_count):
+            dim = (order_odd if i & 1 else order_even)[step]
+            pairs.append((i, i ^ (1 << dim)))
+        bit_even = (me >> order_even[step]) & 1
+        bit_odd = (me >> order_odd[step]) & 1
+        return pairs, jnp.where(odd == 1, bit_odd, bit_even)
+
     buf = grads
     for step in range(steps):
-        bit = (me >> step) & 1
+        pairs, bit = exchange_at(step)
         half = buf.shape[1] // 2
         keep = lax.dynamic_slice_in_dim(buf, bit * half, half, axis=1)
         send = lax.dynamic_slice_in_dim(buf, (1 - bit) * half, half, axis=1)
-        pairs = [(i, i ^ (1 << step)) for i in range(wide_count)]
         buf = keep + lax.ppermute(send, "wide", pairs)
     buf = buf.astype(jnp.bfloat16)
     for step in reversed(range(steps)):
-        bit = (me >> step) & 1
-        pairs = [(i, i ^ (1 << step)) for i in range(wide_count)]
+        pairs, bit = exchange_at(step)
         got = lax.ppermute(buf, "wide", pairs)
         low = jnp.where(bit == 0, buf, got)
         high = jnp.where(bit == 0, got, buf)

time: 153 us -> 151 us (0.987)
    ppermute x4, waiting for transfers between devices: 25.4 us -> 22.6 us  [all_reduce_wide(): buf = keep + lax.ppermute(send, 'wide', pairs)]
  transfers between devices with their start and end apart: 11 -> 11, of which waited for: 11 -> 11; matrix products, arithmetic and copies ran while one was open for 5% -> 6% of each run, Pallas kernels for 0% -> 0%
where the time goes in v7:
time: 151 us
  waiting for transfers between devices  67.6 us (45%)
  other arithmetic  25.5 us (17%)
  matrix products  21.5 us (14%)
  starting transfers between devices  20.4 us (14%)
  local copies, waits for them, and re-layouts  13.8 us (9%)
  between operations  1.89 us (1%)
    ppermute x4, waiting for transfers between devices, all_reduce_wide(): buf = keep + lax.ppermute(send, 'wide', pairs)  22.6 us
    ppermute x4, waiting for transfers between devices, all_reduce_wide(): got = lax.ppermute(buf, 'wide', pairs)  17.4 us
    all_to_all x1, waiting for transfers between devices, route_rows(): lax.all_to_all(send_rows.reshape(wide_count, capacity, feat_width), 'wide...  16.4 us
    dot_general x4, matrix products, run_network(): jnp.dot(stacked.reshape(-1, stacked.shape[2]), weights[layer_at], preferr...  8.34 us
    all_to_all x1, starting transfers between devices, route_rows(): lax.all_to_all(send_place.reshape(wide_count, capacity, per_dev), 'wide',...  7.34 us
    another operation x5, other arithmetic  7.27 us
    all_to_all x1, starting transfers between devices, local(): lax.all_to_all(jnp.broadcast_to(stats[None, :], (wide_count, stats.shape[...  6.81 us
    unnamed x40, local copies, waits for them, and re-layouts  6.57 us
  transfers between devices with their start and end apart: 11, of which 11 were waited for; matrix products, arithmetic and copies ran while one was open for 6% of the time, Pallas kernels for 0%

profile of v7, /device:TPU:0, one launch (start us, length us, event | category | flops | bytes accessed | tf_op | source)
XLA Modules:
  0.0 150.7 jit_solution(16430061297971403450)
XLA Ops:
  2.0 1.3 select_reduce_fusion
  4.1 4.5 %reduce-window.14 = s32[16,16,128]{2,1,0:T(8,128)S(1)} reduce-window(s32[16,16,128]{2,1,0:T(8,128)S(1)} %fusion.61, s32[]{:T(128)} %constant.32.clone.1), window={size=1x1x128 pad=0_0x0_0x127_0}, to_apply=%region_1.2 | reduce-window | flops 4161536 | bytes 262148 | tf_op jit(solution)/shard_map/reduce-window
  10.4 4.8 %fusion.19 = bf16[2048,264]{0,1:T(8,128)(2,1)S(1)} fusion(s32[2048]{0:T(1024)S(1)} %get-tuple-element.28, bf16[2048,8]{1,0:T(8,128)(2,1)S(1)} %copy.90, bf16[2048,256]{1,0:T(8,128)(2,1)} %param.6), kind=kOutput, calls=%fused_computation.29 | convolution fusion | flops 2221490176 | bytes 2170880 | tf_op jit(solution)/shard_map/dot_general | solution.py:85
  15.9 7.3 %all-to-all-start = ((bf16[16,128,8]{1,2,0:T(8,128)(2,1)}), bf16[16,128,8]{1,2,0:T(8,128)(2,1)S(1)}, u32[]{:S(2)}, u32[]{:S(2)}) async-start(bf16[16,128,8]{1,2,0:T(8,128)(2,1)} %slice_bitcast_fusion.10), calls=%async_computation | async-start | bytes 65536 | tf_op jit(solution)/shard_map/all_to_all | solution.py:98
  23.3 1.2 copy_bitcast_fusion.2
  24.5 5.4 %all-to-all-done = bf16[16,128,8]{1,2,0:T(8,128)(2,1)S(1)} async-done(((bf16[16,128,8]{1,2,0:T(8,128)(2,1)}), bf16[16,128,8]{1,2,0:T(8,128)(2,1)S(1)}, u32[]{:S(2)}, u32[]{:S(2)}) %all-to-all-start) | async-done | bytes 32800 | tf_op jit(solution)/shard_map/all_to_all | solution.py:98
  29.9 4.5 %all-to-all-start.1 = ((bf16[16,128,256]{1,2,0:T(8,128)(2,1)}), bf16[16,128,256]{1,2,0:T(8,128)(2,1)}, u32[]{:S(2)}, u32[]{:S(2)}) async-start(bf16[16,128,256]{1,2,0:T(8,128)(2,1)} %copy_bitcast_fusion.2), calls=%async_computation.1 | async-start | bytes 2097152 | tf_op jit(solution)/shard_map/all_to_all | solution.py:91
  36.5 2.3 %reduce-window.16 = s32[8,16,128]{2,1,0:T(8,128)S(1)} reduce-window(s32[8,16,128]{2,1,0:T(8,128)S(1)} %bitcast.169, s32[]{:T(128)} %constant.32.clone.1), window={size=1x1x128 pad=0_0x0_0x127_0}, to_apply=%region_6.7 | reduce-window | flops 2080768 | bytes 131076 | tf_op jit(solution)/shard_map/reduce-window.2
  40.8 16.4 %all-to-all-done.1 = bf16[16,128,256]{1,2,0:T(8,128)(2,1)} async-done(((bf16[16,128,256]{1,2,0:T(8,128)(2,1)}), bf16[16,128,256]{1,2,0:T(8,128)(2,1)}, u32[]{:S(2)}, u32[]{:S(2)}) %all-to-all-start.1) | async-done | bytes 1048608 | tf_op jit(solution)/shard_map/all_to_all | solution.py:91
  57.2 1.5 copy.92
  58.7 3.2 %fusion.20 = bf16[2048,256]{1,0:T(8,128)(2,1)S(1)} fusion(bf16[2048,256]{1,0:T(8,128)(2,1)S(1)} %bitcast.162, s32[2048]{0:T(1024)S(1)} %fusion.67), kind=kOutput, calls=%fused_computation.30 | convolution fusion | flops 2152202240 | bytes 2105344 | tf_op jit(solution)/shard_map/dot_general | solution.py:117
  61.9 1.5 %fusion.22 = bf16[8,256,256]{2,1,0:T(8,128)(2,1)S(1)} fusion(bf16[8,256,256]{2,1,0:T(8,128)(2,1)S(1)} %bitcast.175, bf16[2,768,256]{2,1,0:T(8,128)(2,1)S(1)} %bitcast.166, bf16[8,254,256]{2,1,0:T(8,128)(2,1)S(1)} %bitcast.176, bf16[8,255,256]{2,1,0:T(8,128)(2,1)S(1)} %bitcast.177), kind=kOutput, calls=%fused_computation.32 | convolution fusion | flops 827850752 | bytes 5636096 | tf_op jit(solution)/shard_map/dot_general | solution.py:49
  63.5 2.5 %fusion.21 = (bf16[8,256,256]{2,1,0:T(8,128)(2,1)S(1)}, f32[8,256,256]{2,1,0:T(8,128)}) fusion(bf16[8,256,256]{2,1,0:T(8,128)(2,1)S(1)} %bitcast.178, bf16[2,768,256]{2,1,0:T(8,128)(2,1)S(1)} %bitcast.158, bf16[8,254,256]{2,1,0:T(8,128)(2,1)S(1)} %bitcast.179, bf16[8,255,256]{2,1,0:T(8,128)(2,1)S(1)} %bitcast.180), kind=kOutput, calls=%fused_computation.31 | convolution fusion | flops 827850752 | bytes 7733248 | tf_op jit(solution)/shard_map/dot_general | solution.py:49
  66.1 2.5 %fusion.87 = (bf16[8,256]{1,0:T(8,128)(2,1)S(1)}, bf16[8,256,256]{2,1,0:T(8,128)(2,1)S(1)}, f32[8,256,256]{2,1,0:T(8,128)}) fusion(bf16[8,256,256]{2,1,0:T(8,128)(2,1)S(1)} %get-tuple-element.29, bf16[2,768,256]{2,1,0:T(8,128)(2,1)S(1)} %bitcast.159, bf16[8,248,256]{2,1,0:T(8,128)(2,1)S(1)} %slice.104, bf16[8,252,256]{2,1,0:T(8,128)(2,1)S(1)} %bitcast.163), kind=kOutput, calls=%fused_computation.168 | convolution fusion | flops 828372992 | bytes 7704576 | tf_op jit(solution)/shard_map/dot_general | solution.py:49
  68.6 1.8 %fusion.29 = (f32[8,256]{1,0:T(8,128)S(1)}, f32[8,256]{1,0:T(8,128)S(1)}, f32[256]{0:T(256)S(1)}, bf16[8,256,256]{2,1,0:T(8,128)(2,1)S(1)}) fusion(bf16[8,256,256]{2,1,0:T(8,128)(2,1)S(1)} %get-tuple-element.14, f32[8,256]{1,0:T(8,128)S(1)} %fusion.70, f32[8,256]{1,0:T(8,128)S(1)} %bitcast.170, bf16[2,768,256]{2,1,0:T(8,128)(2,1)S(1)} %bitcast.167, ...), kind=kOutput, calls=%fused_computation.39 | convolution fusion | flops 832040704 | bytes 6685696 | tf_op jit(solution)/shard_map/dot_general | solution.py:49
  71.1 6.8 %all-to-all-start.2 = ((f32[16,1,384]{2,1,0:T(1,128)}), f32[16,1,384]{2,1,0:T(1,128)S(1)}, u32[]{:S(2)}, u32[]{:S(2)}) async-start(f32[16,1,384]{2,1,0:T(1,128)} %broadcast_in_dim.47), calls=%async_computation.2 | async-start | bytes 49152 | tf_op jit(solution)/shard_map/all_to_all | solution.py:174
  78.7 5.8 %all-to-all-done.2 = f32[16,1,384]{2,1,0:T(1,128)S(1)} async-done(((f32[16,1,384]{2,1,0:T(1,128)}), f32[16,1,384]{2,1,0:T(1,128)S(1)}, u32[]{:S(2)}, u32[]{:S(2)}) %all-to-all-start.2) | async-done | bytes 24608 | tf_op jit(solution)/shard_map/all_to_all | solution.py:174
  87.0 3.7 %multiply_convert_fusion = bf16[8,256,256]{2,1,0:T(8,128)(2,1)S(1)} fusion(f32[8,256,256]{2,1,0:T(8,128)S(1)} %copy-done.4, f32[8,256]{1,0:T(8,128)S(1)} %fusion.36, f32[8,256]{1,0:T(8,128)S(1)} %fusion.33, f32[256]{0:T(256)S(1)} %slice_divide_fusion, bf16[8,256,256]{2,1,0:T(8,128)(2,1)S(1)} %get-tuple-element.32, f32[8,256]{1,0:T(8,128)S(1)} %get-tuple-element.5, ...), kind=kLoop, calls=%fused_computation.55 | loop fusion | flops 10485760 | bytes 5284864 | tf_op jit(solution)/shard_map/convert_element_type | solution.py:189
  90.7 1.0 convolution_bitcast_fusion
  93.6 1.1 copy-done.17
  95.4 3.1 %convolution_bitcast_fusion.1 = f32[1,768,256]{2,1,0:T(8,128)S(1)} fusion(f32[8,256,3,256]{3,1,0,2:T(8,128)S(1)} %fusion.46, f32[8,256,256]{2,1,0:T(8,128)S(1)} %copy-done.17, f32[8,248,256]{2,1,0:T(8,128)S(1)} %slice.114, f32[8,252,256]{2,1,0:T(8,128)S(1)} %slice.112, bf16[8,256,256]{2,1,0:T(8,128)(2,1)S(1)} %copy-done.9, ...), kind=kOutput, calls=%fused_computation.75 | convolution fusion | flops 836239360 | bytes 14394368 | tf_op jit(solution)/shard_map/dot_general | solution.py:191
  99.5 2.4 %collective-permute-done = f32[2,384,256]{2,1,0:T(8,128)} collective-permute-done((f32[2,384,256]{2,1,0:T(8,128)S(1)}, f32[2,384,256]{2,1,0:T(8,128)}, u32[]{:S(2)}, u32[]{:S(2)}) %collective-permute-start) | collective-permute-done | bytes 786464 | tf_op jit(solution)/shard_map/ppermute | solution.py:147
  101.9 1.3 fusion.53
  103.8 7.4 %collective-permute-done.1 = f32[2,192,256]{2,1,0:T(8,128)S(1)} collective-permute-done((f32[2,192,256]{2,1,0:T(8,128)S(1)}, f32[2,192,256]{2,1,0:T(8,128)S(1)}, u32[]{:S(2)}, u32[]{:S(2)}) %collective-permute-start.1) | collective-permute-done | bytes 393248 | tf_op jit(solution)/shard_map/ppermute | solution.py:147
  111.7 7.3 %collective-permute-done.2 = f32[2,96,256]{2,1,0:T(8,128)S(1)} collective-permute-done((f32[2,96,256]{2,1,0:T(8,128)S(1)}, f32[2,96,256]{2,1,0:T(8,128)S(1)}, u32[]{:S(2)}, u32[]{:S(2)}) %collective-permute-start.2) | collective-permute-done | bytes 196640 | tf_op jit(solution)/shard_map/ppermute | solution.py:147
  119.1 5.5 %collective-permute-done.3 = f32[2,48,256]{2,1,0:T(8,128)S(1)} collective-permute-done((f32[2,48,256]{2,1,0:T(8,128)S(1)}, f32[2,48,256]{2,1,0:T(8,128)S(1)}, u32[]{:S(2)}, u32[]{:S(2)}) %collective-permute-start.3) | collective-permute-done | bytes 98336 | tf_op jit(solution)/shard_map/ppermute | solution.py:147
  124.8 5.5 %collective-permute-done.4 = bf16[2,48,256]{2,1,0:T(8,128)(2,1)S(1)} collective-permute-done((bf16[2,48,256]{2,1,0:T(8,128)(2,1)S(1)}, bf16[2,48,256]{2,1,0:T(8,128)(2,1)S(1)}, u32[]{:S(2)}, u32[]{:S(2)}) %collective-permute-start.4) | collective-permute-done | bytes 49184 | tf_op jit(solution)/shard_map/ppermute | solution.py:151
  130.4 5.6 %collective-permute-done.5 = bf16[2,96,256]{2,1,0:T(8,128)(2,1)S(1)} collective-permute-done((bf16[2,96,256]{2,1,0:T(8,128)(2,1)S(1)}, bf16[2,96,256]{2,1,0:T(8,128)(2,1)S(1)}, u32[]{:S(2)}, u32[]{:S(2)}) %collective-permute-start.5) | collective-permute-done | bytes 98336 | tf_op jit(solution)/shard_map/ppermute | solution.py:151
  136.5 5.3 %collective-permute-done.6 = bf16[2,192,256]{2,1,0:T(8,128)(2,1)S(1)} collective-permute-done((bf16[2,192,256]{2,1,0:T(8,128)(2,1)S(1)}, bf16[2,192,256]{2,1,0:T(8,128)(2,1)S(1)}, u32[]{:S(2)}, u32[]{:S(2)}) %collective-permute-start.6) | collective-permute-done | bytes 196640 | tf_op jit(solution)/shard_map/ppermute | solution.py:151
  142.7 1.0 collective-permute-done.7
  144.0 1.2 copy.125
  145.9 4.8 %multiply_add_fusion = (f32[2,196608]{1,0:T(2,128)}, f32[2,196608]{1,0:T(2,128)}, f32[2,196608]{1,0:T(2,128)}) fusion(f32[2,196608]{1,0:T(2,128)S(1)} %copy-done, f32[2,196608]{1,0:T(2,128)S(1)} %copy-done.2, f32[2,196608]{1,0:T(2,128)S(1)} %bitcast.157, f32[2,196608]{1,0:T(2,128)S(1)} %copy-done.6), kind=kLoop, calls=%fused_computation.71 | loop fusion | flops 2752512 | bytes 11010048 | tf_op jit(solution)/shard_map/add | solution.py:212
  (101 shorter events, 19.0 us)
Async XLA Ops:
  15.9 14.0 %all-to-all-start = ((bf16[16,128,8]{1,2,0:T(8,128)(2,1)}), bf16[16,128,8]{1,2,0:T(8,128)(2,1)S(1)}, u32[]{:S(2)}, u32[]{:S(2)}) async-start(bf16[16,128,8]{1,2,0:T(8,128)(2,1)} %slice_bitcast_fusion.10), calls=%async_computation | async-start | bytes 65536 | tf_op jit(solution)/shard_map/all_to_all | solution.py:98
  23.3 11.2 %copy-start = (f32[2,196608]{1,0:T(2,128)S(1)}, f32[2,196608]{1,0:T(2,128)}, u32[]{:S(2)}) copy-start(f32[2,196608]{1,0:T(2,128)} %param.11) | copy-start | bytes 4718596
  24.5 10.9 %copy-start.1 = (f32[2,196608]{1,0:T(2,128)S(1)}, f32[2,196608]{1,0:T(2,128)}, u32[]{:S(2)}) copy-start(f32[2,196608]{1,0:T(2,128)} %param.9) | copy-start | bytes 4718596
  29.9 27.3 %all-to-all-start.1 = ((bf16[16,128,256]{1,2,0:T(8,128)(2,1)}), bf16[16,128,256]{1,2,0:T(8,128)(2,1)}, u32[]{:S(2)}, u32[]{:S(2)}) async-start(bf16[16,128,256]{1,2,0:T(8,128)(2,1)} %copy_bitcast_fusion.2), calls=%async_computation.1 | async-start | bytes 2097152 | tf_op jit(solution)/shard_map/all_to_all | solution.py:91
  58.7 3.2 %copy-start.14 = (bf16[1,2,768,256]{3,2,1,0:T(8,128)(2,1)S(1)}, bf16[1,2,768,256]{3,2,1,0:T(8,128)(2,1)}, u32[]{:S(2)}) copy-start(bf16[1,2,768,256]{3,2,1,0:T(8,128)(2,1)} %copy.132) | copy-start | bytes 2359300
  61.9 1.6 %copy-start.15 = (bf16[2048,256]{1,0:T(8,128)(2,1)}, bf16[2048,256]{1,0:T(8,128)(2,1)S(1)}, u32[]{:S(2)}) copy-start(bf16[2048,256]{1,0:T(8,128)(2,1)S(1)} %fusion.20) | copy-start | bytes 3145732
  61.9 1.6 %copy-start.5 = (bf16[1,2,768,256]{3,2,1,0:T(8,128)(2,1)S(1)}, bf16[1,2,768,256]{3,2,1,0:T(8,128)(2,1)}, u32[]{:S(2)}) copy-start(bf16[1,2,768,256]{3,2,1,0:T(8,128)(2,1)} %copy.133) | copy-start | bytes 2359300
  66.0 2.6 %copy-start.12 = (bf16[8,256,256]{2,1,0:T(8,128)(2,1)}, bf16[8,256,256]{2,1,0:T(8,128)(2,1)S(1)}, u32[]{:S(2)}) copy-start(bf16[8,256,256]{2,1,0:T(8,128)(2,1)S(1)} %get-tuple-element.29) | copy-start | bytes 3145732
  66.1 2.5 %copy-start.10 = (bf16[8,248,256]{2,1,0:T(8,128)(2,1)}, bf16[8,248,256]{2,1,0:T(8,128)(2,1)S(1)}, u32[]{:S(2)}) copy-start(bf16[8,248,256]{2,1,0:T(8,128)(2,1)S(1)} %slice.104) | copy-start | bytes 3047428
  68.6 1.9 %copy-start.8 = (bf16[8,256,256]{2,1,0:T(8,128)(2,1)}, bf16[8,256,256]{2,1,0:T(8,128)(2,1)S(1)}, u32[]{:S(2)}) copy-start(bf16[8,256,256]{2,1,0:T(8,128)(2,1)S(1)} %get-tuple-element.14) | copy-start | bytes 3145732
  71.1 13.4 %all-to-all-start.2 = ((f32[16,1,384]{2,1,0:T(1,128)}), f32[16,1,384]{2,1,0:T(1,128)S(1)}, u32[]{:S(2)}, u32[]{:S(2)}) async-start(f32[16,1,384]{2,1,0:T(1,128)} %broadcast_in_dim.47), calls=%async_computation.2 | async-start | bytes 49152 | tf_op jit(solution)/shard_map/all_to_all | solution.py:174
  84.5 2.4 %copy-start.4 = (f32[8,256,256]{2,1,0:T(8,128)S(1)}, f32[8,256,256]{2,1,0:T(8,128)}, u32[]{:S(2)}) copy-start(f32[8,256,256]{2,1,0:T(8,128)} %get-tuple-element.31) | copy-start | bytes 6291460
  87.0 3.7 %copy-start.11 = (bf16[8,248,256]{2,1,0:T(8,128)(2,1)S(1)}, bf16[8,248,256]{2,1,0:T(8,128)(2,1)}, u32[]{:S(2)}) copy-start(bf16[8,248,256]{2,1,0:T(8,128)(2,1)} %copy-done.10) | copy-start | bytes 3047428
  87.0 3.7 %copy-start.13 = (bf16[8,256,256]{2,1,0:T(8,128)(2,1)S(1)}, bf16[8,256,256]{2,1,0:T(8,128)(2,1)}, u32[]{:S(2)}) copy-start(bf16[8,256,256]{2,1,0:T(8,128)(2,1)} %copy-done.12) | copy-start | bytes 3145732
  90.7 1.0 copy-start.7
  93.2 1.6 %copy-start.17 = (f32[8,256,256]{2,1,0:T(8,128)S(1)}, f32[8,256,256]{2,1,0:T(8,128)}, u32[]{:S(2)}) copy-start(f32[8,256,256]{2,1,0:T(8,128)} %get-tuple-element.30) | copy-start | bytes 6291460
  93.4 1.7 %copy-start.9 = (bf16[8,256,256]{2,1,0:T(8,128)(2,1)S(1)}, bf16[8,256,256]{2,1,0:T(8,128)(2,1)}, u32[]{:S(2)}) copy-start(bf16[8,256,256]{2,1,0:T(8,128)(2,1)} %copy-done.8) | copy-start | bytes 3145732
  93.4 2.0 %copy-start.16 = (bf16[2048,256]{1,0:T(8,128)(2,1)S(1)}, bf16[2048,256]{1,0:T(8,128)(2,1)}, u32[]{:S(2)}) copy-start(bf16[2048,256]{1,0:T(8,128)(2,1)} %copy-done.15) | copy-start | bytes 3145732
  98.5 0.9 copy-start.3
  99.5 2.5 %collective-permute-start = (f32[2,384,256]{2,1,0:T(8,128)S(1)}, f32[2,384,256]{2,1,0:T(8,128)}, u32[]{:S(2)}, u32[]{:S(2)}) collective-permute-start(f32[2,384,256]{2,1,0:T(8,128)S(1)} %fusion.51), channel_id=1, source_target_pairs={{0,1},{1,0},{2,3},{3,2},{4,5},{5,4},{6,7},{7,6},{8,9},{9,8},{10,11... | collective-permute-start | bytes 2359304 | tf_op jit(solution)/shard_map/ppermute | solution.py:147
  103.3 7.8 %collective-permute-start.1 = (f32[2,192,256]{2,1,0:T(8,128)S(1)}, f32[2,192,256]{2,1,0:T(8,128)S(1)}, u32[]{:S(2)}, u32[]{:S(2)}) collective-permute-start(f32[2,192,256]{2,1,0:T(8,128)S(1)} %constant_dynamic-slice_fusion.1), channel_id=1, source_target_pairs={{0,2},{1,5},{2,0},{3,7},{4,6},{5,1},{6,4},{7,3},{8,10},{9,13},{10,... | collective-permute-start | bytes 1179656 | tf_op jit(solution)/shard_map/ppermute | solution.py:147
  111.2 7.8 %collective-permute-start.2 = (f32[2,96,256]{2,1,0:T(8,128)S(1)}, f32[2,96,256]{2,1,0:T(8,128)S(1)}, u32[]{:S(2)}, u32[]{:S(2)}) collective-permute-start(f32[2,96,256]{2,1,0:T(8,128)S(1)} %constant_dynamic-slice_fusion), channel_id=1, source_target_pairs={{0,4},{1,9},{2,6},{3,11},{4,0},{5,13},{6,2},{7,15},{8,12},{9,1},{1... | collective-permute-start | bytes 589832 | tf_op jit(solution)/shard_map/ppermute | solution.py:147
  119.1 5.6 %collective-permute-start.3 = (f32[2,48,256]{2,1,0:T(8,128)S(1)}, f32[2,48,256]{2,1,0:T(8,128)S(1)}, u32[]{:S(2)}, u32[]{:S(2)}) collective-permute-start(f32[2,48,256]{2,1,0:T(8,128)S(1)} %constant_dynamic-slice_fusion.2), channel_id=1, source_target_pairs={{0,8},{1,3},{2,10},{3,1},{4,12},{5,7},{6,14},{7,5},{8,0},{9,11},{1... | collective-permute-start | bytes 294920 | tf_op jit(solution)/shard_map/ppermute | solution.py:147
  124.7 5.6 %collective-permute-start.4 = (bf16[2,48,256]{2,1,0:T(8,128)(2,1)S(1)}, bf16[2,48,256]{2,1,0:T(8,128)(2,1)S(1)}, u32[]{:S(2)}, u32[]{:S(2)}) collective-permute-start(bf16[2,48,256]{2,1,0:T(8,128)(2,1)S(1)} %add_convert_fusion.2), channel_id=1, source_target_pairs={{0,8},{1,3},{2,10},{3,1},{4,12},{5,7},{6,14},{7,5},{8,0},{9,11},{1... | collective-permute-start | bytes 147464 | tf_op jit(solution)/shard_map/ppermute | solution.py:151
  130.3 5.7 %collective-permute-start.5 = (bf16[2,96,256]{2,1,0:T(8,128)(2,1)S(1)}, bf16[2,96,256]{2,1,0:T(8,128)(2,1)S(1)}, u32[]{:S(2)}, u32[]{:S(2)}) collective-permute-start(bf16[2,96,256]{2,1,0:T(8,128)(2,1)S(1)} %pad_maximum_fusion.2), channel_id=1, source_target_pairs={{0,4},{1,9},{2,6},{3,11},{4,0},{5,13},{6,2},{7,15},{8,12},{9,1},{1... | collective-permute-start | bytes 294920 | tf_op jit(solution)/shard_map/ppermute | solution.py:151
  136.1 5.7 %collective-permute-start.6 = (bf16[2,192,256]{2,1,0:T(8,128)(2,1)S(1)}, bf16[2,192,256]{2,1,0:T(8,128)(2,1)S(1)}, u32[]{:S(2)}, u32[]{:S(2)}) collective-permute-start(bf16[2,192,256]{2,1,0:T(8,128)(2,1)S(1)} %pad_maximum_fusion.1), channel_id=1, source_target_pairs={{0,2},{1,5},{2,0},{3,7},{4,6},{5,1},{6,4},{7,3},{8,10},{9,13},{10,... | collective-permute-start | bytes 589832 | tf_op jit(solution)/shard_map/ppermute | solution.py:151
  141.9 1.8 %collective-permute-start.7 = (bf16[2,384,256]{2,1,0:T(8,128)(2,1)S(1)}, bf16[2,384,256]{2,1,0:T(8,128)(2,1)S(1)}, u32[]{:S(2)}, u32[]{:S(2)}) collective-permute-start(bf16[2,384,256]{2,1,0:T(8,128)(2,1)S(1)} %pad_maximum_fusion), channel_id=1, source_target_pairs={{0,1},{1,0},{2,3},{3,2},{4,5},{5,4},{6,7},{7,6},{8,9},{9,8},{10,11... | collective-permute-start | bytes 1179656 | tf_op jit(solution)/shard_map/ppermute | solution.py:151
  144.0 1.4 copy-start.2
  144.0 1.9 %copy-start.6 = (f32[2,196608]{1,0:T(2,128)S(1)}, f32[2,196608]{1,0:T(2,128)}, u32[]{:S(2)}) copy-start(f32[2,196608]{1,0:T(2,128)} %param.10) | copy-start | bytes 4718596

commit v8 on v7

--- a/solution.py
+++ b/solution.py
@@ -57,6 +57,23 @@
     return (states, stacked_list, preacts)
 
 
+def prefix_count(hot):
+    rows, width = hot.shape
+    block = 128
+    if rows % block:
+        return jnp.cumsum(hot.astype(jnp.int32), axis=0)
+    blocks = rows // block
+    ramp = jnp.arange(block, dtype=jnp.int32)
+    lower = (ramp[:, None] >= ramp[None, :]).astype(jnp.bfloat16)
+    pieces = hot.astype(jnp.bfloat16).reshape(blocks, block, width)
+    within = jnp.einsum("ij,bjk->bik", lower, pieces, preferred_element_type=jnp.float32)
+    totals = within[:, -1, :].astype(jnp.bfloat16)
+    steps = jnp.arange(blocks, dtype=jnp.int32)
+    before = (steps[:, None] > steps[None, :]).astype(jnp.bfloat16)
+    offsets = jnp.dot(before, totals, preferred_element_type=jnp.float32)
+    return (within + offsets[:, None, :]).reshape(rows, width).astype(jnp.int32)
+
+
 def route_rows(epoch_rows, row_object, object_slot):
     wide_count = lax.axis_size("wide")
     objects_all = object_slot.shape[0]
@@ -73,7 +90,7 @@
     owner_hot = (
         owner_dev[:, None] == jnp.arange(wide_count, dtype=jnp.int32)[None, :]
     ) & live_rows[:, None]
-    running = jnp.cumsum(owner_hot.astype(jnp.int32), axis=0)
+    running = prefix_count(owner_hot)
     send_rank = jnp.sum(jnp.where(owner_hot, running, 0), axis=1) - 1
     send_index = jnp.where(live_rows, owner_dev * capacity + send_rank, -1)
     pick = (
@@ -104,7 +121,7 @@
         ),
     )
     place_hot = got_place.reshape(-1, per_dev) > 0
-    arrival = jnp.cumsum(place_hot.astype(jnp.int32), axis=0)
+    arrival = prefix_count(place_hot)
     position = jnp.sum(jnp.where(place_hot, arrival, 0), axis=1) - 1
     place_code = jnp.sum(
         jnp.where(place_hot, jnp.arange(per_dev, dtype=jnp.int32)[None, :], 0), axis=1

time: 151 us -> 147 us (0.974)
  other arithmetic: 25.5 us -> 18.1 us
  waiting for transfers between devices: 67.6 us -> 70 us
    another operation x5 -> x2, other arithmetic: 7.27 us -> 0.03 us
    all_to_all x1, waiting for transfers between devices: 16.4 us -> 18.8 us  [route_rows(): lax.all_to_all(send_rows.reshape(wide_count, capacity, feat_width), 'wide...]
    unnamed x40 -> x39, local copies, waits for them, and re-layouts: 6.57 us -> 6.55 us
  transfers between devices with their start and end apart: 11 -> 11, of which waited for: 11 -> 11; matrix products, arithmetic and copies ran while one was open for 6% -> 4% of each run, Pallas kernels for 0% -> 0%
where the time goes in v8:
time: 147 us; the launch traced here: 146 us
  waiting for transfers between devices  70 us (48%)
  matrix products  22.1 us (15%)
  starting transfers between devices  20.4 us (14%)
  other arithmetic  18.1 us (12%)
  local copies, waits for them, and re-layouts  13.5 us (9%)
  between operations  1.86 us (1%)
    ppermute x4, waiting for transfers between devices, all_reduce_wide(): buf = keep + lax.ppermute(send, 'wide', pairs)  22.6 us
    all_to_all x1, waiting for transfers between devices, route_rows(): lax.all_to_all(send_rows.reshape(wide_count, capacity, feat_width), 'wide...  18.8 us
    ppermute x4, waiting for transfers between devices, all_reduce_wide(): got = lax.ppermute(buf, 'wide', pairs)  17.4 us
    dot_general x4, matrix products, run_network(): jnp.dot(stacked.reshape(-1, stacked.shape[2]), weights[layer_at], preferr...  8.34 us
    all_to_all x1, starting transfers between devices, route_rows(): lax.all_to_all(send_place.reshape(wide_count, capacity, per_dev), 'wide',...  7.36 us
    all_to_all x1, starting transfers between devices, local(): lax.all_to_all(jnp.broadcast_to(stats[None, :], (wide_count, stats.shape[...  6.81 us
    unnamed x39, local copies, waits for them, and re-layouts  6.55 us
    all_to_all x1, waiting for transfers between devices, local(): lax.all_to_all(jnp.broadcast_to(stats[None, :], (wide_count, stats.shape[...  5.79 us
  transfers between devices with their start and end apart: 11, of which 11 were waited for; matrix products, arithmetic and copies ran while one was open for 4% of the time, Pallas kernels for 0%

profile of v8, /device:TPU:0, one launch (start us, length us, event | category | flops | bytes accessed | tf_op | source)
XLA Modules:
  0.0 146.0 jit_solution(470272195312882300)
XLA Ops:
  2.7 1.3 select_reduce_fusion
  5.7 4.8 %fusion.19 = bf16[2048,264]{0,1:T(8,128)(2,1)S(1)} fusion(s32[2048]{0:T(1024)S(1)} %get-tuple-element.29, bf16[2048,8]{1,0:T(8,128)(2,1)S(1)} %copy.102, bf16[2048,256]{1,0:T(8,128)(2,1)} %param.6), kind=kOutput, calls=%fused_computation.29 | convolution fusion | flops 2221490176 | bytes 2170880 | tf_op jit(solution)/shard_map/dot_general | solution.py:102
  11.2 7.4 %all-to-all-start = ((bf16[16,128,8]{1,2,0:T(8,128)(2,1)}), bf16[16,128,8]{1,2,0:T(8,128)(2,1)S(1)}, u32[]{:S(2)}, u32[]{:S(2)}) async-start(bf16[16,128,8]{1,2,0:T(8,128)(2,1)} %slice_bitcast_fusion.10), calls=%async_computation | async-start | bytes 65536 | tf_op jit(solution)/shard_map/all_to_all | solution.py:115
  18.5 1.2 copy_bitcast_fusion.2
  19.8 5.4 %all-to-all-done = bf16[16,128,8]{1,2,0:T(8,128)(2,1)S(1)} async-done(((bf16[16,128,8]{1,2,0:T(8,128)(2,1)}), bf16[16,128,8]{1,2,0:T(8,128)(2,1)S(1)}, u32[]{:S(2)}, u32[]{:S(2)}) %all-to-all-start) | async-done | bytes 32800 | tf_op jit(solution)/shard_map/all_to_all | solution.py:115
  25.2 4.5 %all-to-all-start.1 = ((bf16[16,128,256]{1,2,0:T(8,128)(2,1)}), bf16[16,128,256]{1,2,0:T(8,128)(2,1)}, u32[]{:S(2)}, u32[]{:S(2)}) async-start(bf16[16,128,256]{1,2,0:T(8,128)(2,1)} %copy_bitcast_fusion.2), calls=%async_computation.1 | async-start | bytes 2097152 | tf_op jit(solution)/shard_map/all_to_all | solution.py:108
  29.7 1.0 copy.141
  33.7 18.8 %all-to-all-done.1 = bf16[16,128,256]{1,2,0:T(8,128)(2,1)} async-done(((bf16[16,128,256]{1,2,0:T(8,128)(2,1)}), bf16[16,128,256]{1,2,0:T(8,128)(2,1)}, u32[]{:S(2)}, u32[]{:S(2)}) %all-to-all-start.1) | async-done | bytes 1048608 | tf_op jit(solution)/shard_map/all_to_all | solution.py:108
  52.5 1.5 %copy.106 = bf16[16,128,256]{2,1,0:T(8,128)(2,1)S(1)} copy(bf16[16,128,256]{1,2,0:T(8,128)(2,1)} %all-to-all-done.1) | data formatting | bytes 2097152 | tf_op jit(solution)/shard_map/all_to_all | solution.py:108
  54.0 3.2 %fusion.20 = bf16[2048,256]{1,0:T(8,128)(2,1)S(1)} fusion(bf16[2048,256]{1,0:T(8,128)(2,1)S(1)} %bitcast.143, s32[2048]{0:T(1024)S(1)} %select_bitcast_fusion), kind=kOutput, calls=%fused_computation.30 | convolution fusion | flops 2152202240 | bytes 2105344 | tf_op jit(solution)/shard_map/dot_general | solution.py:134
  57.2 1.5 %fusion.22 = bf16[8,256,256]{2,1,0:T(8,128)(2,1)S(1)} fusion(bf16[8,256,256]{2,1,0:T(8,128)(2,1)S(1)} %bitcast.152, bf16[2,768,256]{2,1,0:T(8,128)(2,1)S(1)} %bitcast.147, bf16[8,254,256]{2,1,0:T(8,128)(2,1)S(1)} %bitcast.153, bf16[8,255,256]{2,1,0:T(8,128)(2,1)S(1)} %bitcast.154), kind=kOutput, calls=%fused_computation.32 | convolution fusion | flops 827850752 | bytes 5636096 | tf_op jit(solution)/shard_map/dot_general | solution.py:49
  58.8 2.5 %fusion.21 = (bf16[8,256,256]{2,1,0:T(8,128)(2,1)S(1)}, f32[8,256,256]{2,1,0:T(8,128)}) fusion(bf16[8,256,256]{2,1,0:T(8,128)(2,1)S(1)} %bitcast.155, bf16[2,768,256]{2,1,0:T(8,128)(2,1)S(1)} %bitcast.139, bf16[8,254,256]{2,1,0:T(8,128)(2,1)S(1)} %bitcast.156, bf16[8,255,256]{2,1,0:T(8,128)(2,1)S(1)} %bitcast.157), kind=kOutput, calls=%fused_computation.31 | convolution fusion | flops 827850752 | bytes 7733248 | tf_op jit(solution)/shard_map/dot_general | solution.py:49
  61.4 2.5 %fusion.96 = (bf16[8,256]{1,0:T(8,128)(2,1)S(1)}, bf16[8,256,256]{2,1,0:T(8,128)(2,1)S(1)}, f32[8,256,256]{2,1,0:T(8,128)}) fusion(bf16[8,256,256]{2,1,0:T(8,128)(2,1)S(1)} %get-tuple-element.30, bf16[2,768,256]{2,1,0:T(8,128)(2,1)S(1)} %bitcast.140, bf16[8,248,256]{2,1,0:T(8,128)(2,1)S(1)} %slice.97, bf16[8,252,256]{2,1,0:T(8,128)(2,1)S(1)} %bitcast.144), kind=kOutput, calls=%fused_computation.171 | convolution fusion | flops 828372992 | bytes 7704576 | tf_op jit(solution)/shard_map/dot_general | solution.py:49
  63.9 1.8 %fusion.29 = (f32[8,256]{1,0:T(8,128)S(1)}, f32[8,256]{1,0:T(8,128)S(1)}, f32[256]{0:T(256)S(1)}, bf16[8,256,256]{2,1,0:T(8,128)(2,1)S(1)}) fusion(bf16[8,256,256]{2,1,0:T(8,128)(2,1)S(1)} %get-tuple-element.15, f32[8,256]{1,0:T(8,128)S(1)} %fusion.78, f32[8,256]{1,0:T(8,128)S(1)} %bitcast.149, bf16[2,768,256]{2,1,0:T(8,128)(2,1)S(1)} %bitcast.148, ...), kind=kOutput, calls=%fused_computation.39 | convolution fusion | flops 832040704 | bytes 6685696 | tf_op jit(solution)/shard_map/dot_general | solution.py:49
  66.4 6.8 %all-to-all-start.2 = ((f32[16,1,384]{2,1,0:T(1,128)}), f32[16,1,384]{2,1,0:T(1,128)S(1)}, u32[]{:S(2)}, u32[]{:S(2)}) async-start(f32[16,1,384]{2,1,0:T(1,128)} %broadcast_in_dim.40), calls=%async_computation.2 | async-start | bytes 49152 | tf_op jit(solution)/shard_map/all_to_all | solution.py:191
  74.0 5.8 %all-to-all-done.2 = f32[16,1,384]{2,1,0:T(1,128)S(1)} async-done(((f32[16,1,384]{2,1,0:T(1,128)}), f32[16,1,384]{2,1,0:T(1,128)S(1)}, u32[]{:S(2)}, u32[]{:S(2)}) %all-to-all-start.2) | async-done | bytes 24608 | tf_op jit(solution)/shard_map/all_to_all | solution.py:191
  82.2 3.7 %multiply_convert_fusion = bf16[8,256,256]{2,1,0:T(8,128)(2,1)S(1)} fusion(f32[8,256,256]{2,1,0:T(8,128)S(1)} %copy-done.4, f32[8,256]{1,0:T(8,128)S(1)} %fusion.36, f32[8,256]{1,0:T(8,128)S(1)} %fusion.33, f32[256]{0:T(256)S(1)} %slice_divide_fusion, bf16[8,256,256]{2,1,0:T(8,128)(2,1)S(1)} %get-tuple-element.33, f32[8,256]{1,0:T(8,128)S(1)} %get-tuple-element.5, ...), kind=kLoop, calls=%fused_computation.55 | loop fusion | flops 10485760 | bytes 5284864 | tf_op jit(solution)/shard_map/convert_element_type | solution.py:206
  86.0 1.0 convolution_bitcast_fusion
  87.0 1.0 fusion.46
  88.9 1.1 copy-done.17
  90.7 3.1 %convolution_bitcast_fusion.1 = f32[1,768,256]{2,1,0:T(8,128)S(1)} fusion(f32[8,256,3,256]{3,1,0,2:T(8,128)S(1)} %fusion.46, f32[8,256,256]{2,1,0:T(8,128)S(1)} %copy-done.17, f32[8,248,256]{2,1,0:T(8,128)S(1)} %slice.107, f32[8,252,256]{2,1,0:T(8,128)S(1)} %slice.105, bf16[8,256,256]{2,1,0:T(8,128)(2,1)S(1)} %copy-done.9, ...), kind=kOutput, calls=%fused_computation.75 | convolution fusion | flops 836239360 | bytes 14394368 | tf_op jit(solution)/shard_map/dot_general | solution.py:208
  94.8 2.4 %collective-permute-done = f32[2,384,256]{2,1,0:T(8,128)} collective-permute-done((f32[2,384,256]{2,1,0:T(8,128)S(1)}, f32[2,384,256]{2,1,0:T(8,128)}, u32[]{:S(2)}, u32[]{:S(2)}) %collective-permute-start) | collective-permute-done | bytes 786464 | tf_op jit(solution)/shard_map/ppermute | solution.py:164
  97.2 1.3 fusion.53
  99.1 7.4 %collective-permute-done.1 = f32[2,192,256]{2,1,0:T(8,128)S(1)} collective-permute-done((f32[2,192,256]{2,1,0:T(8,128)S(1)}, f32[2,192,256]{2,1,0:T(8,128)S(1)}, u32[]{:S(2)}, u32[]{:S(2)}) %collective-permute-start.1) | collective-permute-done | bytes 393248 | tf_op jit(solution)/shard_map/ppermute | solution.py:164
  107.0 7.3 %collective-permute-done.2 = f32[2,96,256]{2,1,0:T(8,128)S(1)} collective-permute-done((f32[2,96,256]{2,1,0:T(8,128)S(1)}, f32[2,96,256]{2,1,0:T(8,128)S(1)}, u32[]{:S(2)}, u32[]{:S(2)}) %collective-permute-start.2) | collective-permute-done | bytes 196640 | tf_op jit(solution)/shard_map/ppermute | solution.py:164
  114.4 5.5 %collective-permute-done.3 = f32[2,48,256]{2,1,0:T(8,128)S(1)} collective-permute-done((f32[2,48,256]{2,1,0:T(8,128)S(1)}, f32[2,48,256]{2,1,0:T(8,128)S(1)}, u32[]{:S(2)}, u32[]{:S(2)}) %collective-permute-start.3) | collective-permute-done | bytes 98336 | tf_op jit(solution)/shard_map/ppermute | solution.py:164
  120.0 5.5 %collective-permute-done.4 = bf16[2,48,256]{2,1,0:T(8,128)(2,1)S(1)} collective-permute-done((bf16[2,48,256]{2,1,0:T(8,128)(2,1)S(1)}, bf16[2,48,256]{2,1,0:T(8,128)(2,1)S(1)}, u32[]{:S(2)}, u32[]{:S(2)}) %collective-permute-start.4) | collective-permute-done | bytes 49184 | tf_op jit(solution)/shard_map/ppermute | solution.py:168
  125.7 5.6 %collective-permute-done.5 = bf16[2,96,256]{2,1,0:T(8,128)(2,1)S(1)} collective-permute-done((bf16[2,96,256]{2,1,0:T(8,128)(2,1)S(1)}, bf16[2,96,256]{2,1,0:T(8,128)(2,1)S(1)}, u32[]{:S(2)}, u32[]{:S(2)}) %collective-permute-start.5) | collective-permute-done | bytes 98336 | tf_op jit(solution)/shard_map/ppermute | solution.py:168
  131.8 5.3 %collective-permute-done.6 = bf16[2,192,256]{2,1,0:T(8,128)(2,1)S(1)} collective-permute-done((bf16[2,192,256]{2,1,0:T(8,128)(2,1)S(1)}, bf16[2,192,256]{2,1,0:T(8,128)(2,1)S(1)}, u32[]{:S(2)}, u32[]{:S(2)}) %collective-permute-start.6) | collective-permute-done | bytes 196640 | tf_op jit(solution)/shard_map/ppermute | solution.py:168
  138.0 1.0 collective-permute-done.7
  139.3 1.2 copy.137
  141.1 4.8 %multiply_add_fusion = (f32[2,196608]{1,0:T(2,128)}, f32[2,196608]{1,0:T(2,128)}, f32[2,196608]{1,0:T(2,128)}) fusion(f32[2,196608]{1,0:T(2,128)S(1)} %copy-done, f32[2,196608]{1,0:T(2,128)S(1)} %copy-done.2, f32[2,196608]{1,0:T(2,128)S(1)} %bitcast.138, f32[2,196608]{1,0:T(2,128)S(1)} %copy-done.6), kind=kLoop, calls=%fused_computation.71 | loop fusion | flops 2752512 | bytes 11010048 | tf_op jit(solution)/shard_map/add | solution.py:229
  (97 shorter events, 16.7 us)
Async XLA Ops:
  11.2 14.0 %all-to-all-start = ((bf16[16,128,8]{1,2,0:T(8,128)(2,1)}), bf16[16,128,8]{1,2,0:T(8,128)(2,1)S(1)}, u32[]{:S(2)}, u32[]{:S(2)}) async-start(bf16[16,128,8]{1,2,0:T(8,128)(2,1)} %slice_bitcast_fusion.10), calls=%async_computation | async-start | bytes 65536 | tf_op jit(solution)/shard_map/all_to_all | solution.py:115
  18.5 11.2 %copy-start = (f32[2,196608]{1,0:T(2,128)S(1)}, f32[2,196608]{1,0:T(2,128)}, u32[]{:S(2)}) copy-start(f32[2,196608]{1,0:T(2,128)} %param.11) | copy-start | bytes 4718596
  19.8 10.9 %copy-start.1 = (f32[2,196608]{1,0:T(2,128)S(1)}, f32[2,196608]{1,0:T(2,128)}, u32[]{:S(2)}) copy-start(f32[2,196608]{1,0:T(2,128)} %param.9) | copy-start | bytes 4718596
  25.2 27.3 %all-to-all-start.1 = ((bf16[16,128,256]{1,2,0:T(8,128)(2,1)}), bf16[16,128,256]{1,2,0:T(8,128)(2,1)}, u32[]{:S(2)}, u32[]{:S(2)}) async-start(bf16[16,128,256]{1,2,0:T(8,128)(2,1)} %copy_bitcast_fusion.2), calls=%async_computation.1 | async-start | bytes 2097152 | tf_op jit(solution)/shard_map/all_to_all | solution.py:108
  53.9 3.2 %copy-start.14 = (bf16[1,2,768,256]{3,2,1,0:T(8,128)(2,1)S(1)}, bf16[1,2,768,256]{3,2,1,0:T(8,128)(2,1)}, u32[]{:S(2)}) copy-start(bf16[1,2,768,256]{3,2,1,0:T(8,128)(2,1)} %copy.141) | copy-start | bytes 2359300
  57.1 1.6 %copy-start.15 = (bf16[2048,256]{1,0:T(8,128)(2,1)}, bf16[2048,256]{1,0:T(8,128)(2,1)S(1)}, u32[]{:S(2)}) copy-start(bf16[2048,256]{1,0:T(8,128)(2,1)S(1)} %fusion.20) | copy-start | bytes 3145732
  57.2 1.6 %copy-start.5 = (bf16[1,2,768,256]{3,2,1,0:T(8,128)(2,1)S(1)}, bf16[1,2,768,256]{3,2,1,0:T(8,128)(2,1)}, u32[]{:S(2)}) copy-start(bf16[1,2,768,256]{3,2,1,0:T(8,128)(2,1)} %copy.142) | copy-start | bytes 2359300
  61.3 2.6 %copy-start.12 = (bf16[8,256,256]{2,1,0:T(8,128)(2,1)}, bf16[8,256,256]{2,1,0:T(8,128)(2,1)S(1)}, u32[]{:S(2)}) copy-start(bf16[8,256,256]{2,1,0:T(8,128)(2,1)S(1)} %get-tuple-element.30) | copy-start | bytes 3145732
  61.4 2.5 %copy-start.10 = (bf16[8,248,256]{2,1,0:T(8,128)(2,1)}, bf16[8,248,256]{2,1,0:T(8,128)(2,1)S(1)}, u32[]{:S(2)}) copy-start(bf16[8,248,256]{2,1,0:T(8,128)(2,1)S(1)} %slice.97) | copy-start | bytes 3047428
  63.9 1.9 %copy-start.8 = (bf16[8,256,256]{2,1,0:T(8,128)(2,1)}, bf16[8,256,256]{2,1,0:T(8,128)(2,1)S(1)}, u32[]{:S(2)}) copy-start(bf16[8,256,256]{2,1,0:T(8,128)(2,1)S(1)} %get-tuple-element.15) | copy-start | bytes 3145732
  66.4 13.4 %all-to-all-start.2 = ((f32[16,1,384]{2,1,0:T(1,128)}), f32[16,1,384]{2,1,0:T(1,128)S(1)}, u32[]{:S(2)}, u32[]{:S(2)}) async-start(f32[16,1,384]{2,1,0:T(1,128)} %broadcast_in_dim.40), calls=%async_computation.2 | async-start | bytes 49152 | tf_op jit(solution)/shard_map/all_to_all | solution.py:191
  79.8 2.4 %copy-start.4 = (f32[8,256,256]{2,1,0:T(8,128)S(1)}, f32[8,256,256]{2,1,0:T(8,128)}, u32[]{:S(2)}) copy-start(f32[8,256,256]{2,1,0:T(8,128)} %get-tuple-element.32) | copy-start | bytes 6291460
  82.2 3.7 %copy-start.11 = (bf16[8,248,256]{2,1,0:T(8,128)(2,1)S(1)}, bf16[8,248,256]{2,1,0:T(8,128)(2,1)}, u32[]{:S(2)}) copy-start(bf16[8,248,256]{2,1,0:T(8,128)(2,1)} %copy-done.10) | copy-start | bytes 3047428
  82.2 3.7 %copy-start.13 = (bf16[8,256,256]{2,1,0:T(8,128)(2,1)S(1)}, bf16[8,256,256]{2,1,0:T(8,128)(2,1)}, u32[]{:S(2)}) copy-start(bf16[8,256,256]{2,1,0:T(8,128)(2,1)} %copy-done.12) | copy-start | bytes 3145732
  86.0 1.0 copy-start.7
  88.4 1.6 %copy-start.17 = (f32[8,256,256]{2,1,0:T(8,128)S(1)}, f32[8,256,256]{2,1,0:T(8,128)}, u32[]{:S(2)}) copy-start(f32[8,256,256]{2,1,0:T(8,128)} %get-tuple-element.31) | copy-start | bytes 6291460
  88.7 1.7 %copy-start.9 = (bf16[8,256,256]{2,1,0:T(8,128)(2,1)S(1)}, bf16[8,256,256]{2,1,0:T(8,128)(2,1)}, u32[]{:S(2)}) copy-start(bf16[8,256,256]{2,1,0:T(8,128)(2,1)} %copy-done.8) | copy-start | bytes 3145732
  88.7 2.0 %copy-start.16 = (bf16[2048,256]{1,0:T(8,128)(2,1)S(1)}, bf16[2048,256]{1,0:T(8,128)(2,1)}, u32[]{:S(2)}) copy-start(bf16[2048,256]{1,0:T(8,128)(2,1)} %copy-done.15) | copy-start | bytes 3145732
  93.8 0.9 copy-start.3
  94.7 2.5 %collective-permute-start = (f32[2,384,256]{2,1,0:T(8,128)S(1)}, f32[2,384,256]{2,1,0:T(8,128)}, u32[]{:S(2)}, u32[]{:S(2)}) collective-permute-start(f32[2,384,256]{2,1,0:T(8,128)S(1)} %fusion.51), channel_id=1, source_target_pairs={{0,1},{1,0},{2,3},{3,2},{4,5},{5,4},{6,7},{7,6},{8,9},{9,8},{10,11... | collective-permute-start | bytes 2359304 | tf_op jit(solution)/shard_map/ppermute | solution.py:164
  98.6 7.8 %collective-permute-start.1 = (f32[2,192,256]{2,1,0:T(8,128)S(1)}, f32[2,192,256]{2,1,0:T(8,128)S(1)}, u32[]{:S(2)}, u32[]{:S(2)}) collective-permute-start(f32[2,192,256]{2,1,0:T(8,128)S(1)} %constant_dynamic-slice_fusion.1), channel_id=1, source_target_pairs={{0,2},{1,5},{2,0},{3,7},{4,6},{5,1},{6,4},{7,3},{8,10},{9,13},{10,... | collective-permute-start | bytes 1179656 | tf_op jit(solution)/shard_map/ppermute | solution.py:164
  106.5 7.8 %collective-permute-start.2 = (f32[2,96,256]{2,1,0:T(8,128)S(1)}, f32[2,96,256]{2,1,0:T(8,128)S(1)}, u32[]{:S(2)}, u32[]{:S(2)}) collective-permute-start(f32[2,96,256]{2,1,0:T(8,128)S(1)} %constant_dynamic-slice_fusion), channel_id=1, source_target_pairs={{0,4},{1,9},{2,6},{3,11},{4,0},{5,13},{6,2},{7,15},{8,12},{9,1},{1... | collective-permute-start | bytes 589832 | tf_op jit(solution)/shard_map/ppermute | solution.py:164
  114.3 5.6 %collective-permute-start.3 = (f32[2,48,256]{2,1,0:T(8,128)S(1)}, f32[2,48,256]{2,1,0:T(8,128)S(1)}, u32[]{:S(2)}, u32[]{:S(2)}) collective-permute-start(f32[2,48,256]{2,1,0:T(8,128)S(1)} %constant_dynamic-slice_fusion.2), channel_id=1, source_target_pairs={{0,8},{1,3},{2,10},{3,1},{4,12},{5,7},{6,14},{7,5},{8,0},{9,11},{1... | collective-permute-start | bytes 294920 | tf_op jit(solution)/shard_map/ppermute | solution.py:164
  120.0 5.6 %collective-permute-start.4 = (bf16[2,48,256]{2,1,0:T(8,128)(2,1)S(1)}, bf16[2,48,256]{2,1,0:T(8,128)(2,1)S(1)}, u32[]{:S(2)}, u32[]{:S(2)}) collective-permute-start(bf16[2,48,256]{2,1,0:T(8,128)(2,1)S(1)} %add_convert_fusion.2), channel_id=1, source_target_pairs={{0,8},{1,3},{2,10},{3,1},{4,12},{5,7},{6,14},{7,5},{8,0},{9,11},{1... | collective-permute-start | bytes 147464 | tf_op jit(solution)/shard_map/ppermute | solution.py:168
  125.6 5.7 %collective-permute-start.5 = (bf16[2,96,256]{2,1,0:T(8,128)(2,1)S(1)}, bf16[2,96,256]{2,1,0:T(8,128)(2,1)S(1)}, u32[]{:S(2)}, u32[]{:S(2)}) collective-permute-start(bf16[2,96,256]{2,1,0:T(8,128)(2,1)S(1)} %pad_maximum_fusion.2), channel_id=1, source_target_pairs={{0,4},{1,9},{2,6},{3,11},{4,0},{5,13},{6,2},{7,15},{8,12},{9,1},{1... | collective-permute-start | bytes 294920 | tf_op jit(solution)/shard_map/ppermute | solution.py:168
  131.3 5.7 %collective-permute-start.6 = (bf16[2,192,256]{2,1,0:T(8,128)(2,1)S(1)}, bf16[2,192,256]{2,1,0:T(8,128)(2,1)S(1)}, u32[]{:S(2)}, u32[]{:S(2)}) collective-permute-start(bf16[2,192,256]{2,1,0:T(8,128)(2,1)S(1)} %pad_maximum_fusion.1), channel_id=1, source_target_pairs={{0,2},{1,5},{2,0},{3,7},{4,6},{5,1},{6,4},{7,3},{8,10},{9,13},{10,... | collective-permute-start | bytes 589832 | tf_op jit(solution)/shard_map/ppermute | solution.py:168
  137.2 1.8 %collective-permute-start.7 = (bf16[2,384,256]{2,1,0:T(8,128)(2,1)S(1)}, bf16[2,384,256]{2,1,0:T(8,128)(2,1)S(1)}, u32[]{:S(2)}, u32[]{:S(2)}) collective-permute-start(bf16[2,384,256]{2,1,0:T(8,128)(2,1)S(1)} %pad_maximum_fusion), channel_id=1, source_target_pairs={{0,1},{1,0},{2,3},{3,2},{4,5},{5,4},{6,7},{7,6},{8,9},{9,8},{10,11... | collective-permute-start | bytes 1179656 | tf_op jit(solution)/shard_map/ppermute | solution.py:168
  139.3 1.4 copy-start.2
  139.3 1.9 %copy-start.6 = (f32[2,196608]{1,0:T(2,128)S(1)}, f32[2,196608]{1,0:T(2,128)}, u32[]{:S(2)}) copy-start(f32[2,196608]{1,0:T(2,128)} %param.10) | copy-start | bytes 4718596

commit v9 on v8

--- a/solution.py
+++ b/solution.py
@@ -86,48 +86,39 @@
     match_table = safe_object[:, None] == jnp.arange(objects_all, dtype=jnp.int32)[None, :]
     slot_of = jnp.sum(jnp.where(match_table, object_slot[None, :], 0), axis=1)
     owner_dev = slot_of // per_dev
-    local_place = slot_of % per_dev
-    owner_hot = (
-        owner_dev[:, None] == jnp.arange(wide_count, dtype=jnp.int32)[None, :]
-    ) & live_rows[:, None]
-    running = prefix_count(owner_hot)
-    send_rank = jnp.sum(jnp.where(owner_hot, running, 0), axis=1) - 1
-    send_index = jnp.where(live_rows, owner_dev * capacity + send_rank, -1)
+    slot_hot = (slot_of[:, None] == jnp.arange(objects_all, dtype=jnp.int32)[None, :]) & live_rows[:, None]
+    group_size = jnp.sum(slot_hot.astype(jnp.int32), axis=0).reshape(wide_count, per_dev)
+    got_size = lax.all_to_all(group_size, "wide", split_axis=0, concat_axis=0, tiled=True)
+    places = jnp.arange(per_dev, dtype=jnp.int32)
+    earlier_place = (places[:, None] < places[None, :]).astype(jnp.int32)
+    group_start = jnp.sum(group_size[:, :, None] * earlier_place[None, :, :], axis=1)
+    running = prefix_count(slot_hot)
+    rank_in_group = jnp.sum(jnp.where(slot_hot, running, 0), axis=1) - 1
+    start_of_row = jnp.sum(jnp.where(slot_hot, group_start.reshape(1, -1), 0), axis=1)
+    send_index = jnp.where(live_rows, owner_dev * capacity + start_of_row + rank_in_group, -1)
     pick = (
         jnp.arange(rows_total, dtype=jnp.int32)[:, None] == send_index[None, :]
     ).astype(jnp.bfloat16)
-    place_hot = (
-        (local_place[:, None] == jnp.arange(per_dev, dtype=jnp.int32)[None, :]) & live_rows[:, None]
-    ).astype(jnp.bfloat16)
-    sent = jnp.dot(
-        pick, jnp.concatenate([epoch_rows, place_hot], axis=1), preferred_element_type=jnp.float32
-    ).astype(jnp.bfloat16)
-    send_rows = sent[:, :feat_width]
-    send_place = sent[:, feat_width:]
-    got_rows, got_place = (
-        lax.all_to_all(
-            send_rows.reshape(wide_count, capacity, feat_width),
-            "wide",
-            split_axis=0,
-            concat_axis=0,
-            tiled=True,
-        ),
-        lax.all_to_all(
-            send_place.reshape(wide_count, capacity, per_dev),
-            "wide",
-            split_axis=0,
-            concat_axis=0,
-            tiled=True,
-        ),
-    )
-    place_hot = got_place.reshape(-1, per_dev) > 0
-    arrival = prefix_count(place_hot)
-    position = jnp.sum(jnp.where(place_hot, arrival, 0), axis=1) - 1
-    place_code = jnp.sum(
-        jnp.where(place_hot, jnp.arange(per_dev, dtype=jnp.int32)[None, :], 0), axis=1
-    )
-    counts = jnp.sum(place_hot.astype(jnp.int32), axis=0)
-    target = jnp.where(jnp.any(place_hot, axis=1), place_code * SEQ + position, -1)
+    send_rows = jnp.dot(pick, epoch_rows, preferred_element_type=jnp.float32).astype(jnp.bfloat16)
+    got_rows = lax.all_to_all(
+        send_rows.reshape(wide_count, capacity, feat_width),
+        "wide",
+        split_axis=0,
+        concat_axis=0,
+        tiled=True,
+    )
+    sources = jnp.arange(wide_count, dtype=jnp.int32)
+    earlier_source = (sources[:, None] > sources[None, :]).astype(jnp.int32)
+    before_source = jnp.sum(earlier_source[:, :, None] * got_size[None, :, :], axis=1)
+    got_start = jnp.sum(got_size[:, :, None] * earlier_place[None, :, :], axis=1)
+    slots = jnp.arange(capacity, dtype=jnp.int32)[None, :, None]
+    in_group = (slots >= got_start[:, None, :]) & (slots < (got_start + got_size)[:, None, :])
+    position = jnp.sum(
+        jnp.where(in_group, before_source[:, None, :] + slots - got_start[:, None, :], 0), axis=2
+    )
+    place_code = jnp.sum(jnp.where(in_group, places[None, None, :], 0), axis=2)
+    target = jnp.where(jnp.any(in_group, axis=2), place_code * SEQ + position, -1).reshape(-1)
+    counts = jnp.sum(got_size, axis=0)
     put = (
         jnp.arange(per_dev * SEQ, dtype=jnp.int32)[:, None] == target[None, :]
     ).astype(jnp.bfloat16)

time: 147 us -> 147 us (level)
  other arithmetic: 18.1 us -> 21.7 us
  local copies, waits for them, and re-layouts: 13.5 us -> 10.1 us
  waiting for transfers between devices: 70 us -> 67.3 us
  matrix products: 22.1 us -> 24.5 us
    reduce_sum x1 -> x6, other arithmetic: 0.13 us -> 4.05 us  [the longest x1 1.41 us: route_rows(): jnp.sum(slot_hot.astype(jnp.int32), axis=0).reshape(wide_count, per_dev)]
    all_to_all x1, waiting for transfers between devices: 5.38 us -> 1.95 us  [route_rows(): lax.all_to_all(group_size, 'wide', split_axis=0, concat_axis=0, tiled=True)]
    dot_general x2 -> x1, matrix products: 0.31 us -> 2.26 us  [prefix_count(): jnp.einsum('ij,bjk->bik', lower, pieces, preferred_element_type=jnp.float32)]
    reshape x2 -> x0, local copies, waits for them, and re-layouts: 1.87 us -> none  [the longest x1 1.24 us: route_rows(): send_rows.reshape(wide_count, capacity, feat_width)]
    unnamed x39 -> x41, local copies, waits for them, and re-layouts: 6.55 us -> 6.71 us
  transfers between devices with their start and end apart: 11 -> 11, of which waited for: 11 -> 11; matrix products, arithmetic and copies ran while one was open for 4% -> 5% of each run, Pallas kernels for 0% -> 0%
where the time goes in v9:
time: 147 us; the launch traced here: 146 us
  waiting for transfers between devices  67.3 us (46%)
  matrix products  24.5 us (17%)
  other arithmetic  21.7 us (15%)
  starting transfers between devices  20.5 us (14%)
  local copies, waits for them, and re-layouts  10.1 us (7%)
  between operations  1.9 us (1%)
    ppermute x4, waiting for transfers between devices, all_reduce_wide(): buf = keep + lax.ppermute(send, 'wide', pairs)  22.6 us
    all_to_all x1, waiting for transfers between devices, route_rows(): lax.all_to_all(send_rows.reshape(wide_count, capacity, feat_width), 'wide...  18.8 us
    ppermute x4, waiting for transfers between devices, all_reduce_wide(): got = lax.ppermute(buf, 'wide', pairs)  17.4 us
    dot_general x4, matrix products, run_network(): jnp.dot(stacked.reshape(-1, stacked.shape[2]), weights[layer_at], preferr...  8.34 us
    all_to_all x1, starting transfers between devices, route_rows(): lax.all_to_all(group_size, 'wide', split_axis=0, concat_axis=0, tiled=True)  7.36 us
    all_to_all x1, starting transfers between devices, local(): lax.all_to_all(jnp.broadcast_to(stats[None, :], (wide_count, stats.shape[...  6.82 us
    unnamed x41, local copies, waits for them, and re-layouts  6.71 us
    all_to_all x1, waiting for transfers between devices, local(): lax.all_to_all(jnp.broadcast_to(stats[None, :], (wide_count, stats.shape[...  6.52 us
  transfers between devices with their start and end apart: 11, of which 11 were waited for; matrix products, arithmetic and copies ran while one was open for 5% of the time, Pallas kernels for 0%

profile of v9, /device:TPU:0, one launch (start us, length us, event | category | flops | bytes accessed | tf_op | source)
XLA Modules:
  0.0 146.1 jit_solution(13525529354989080837)
XLA Ops:
  2.2 1.3 select_reduce_fusion.1
  3.4 1.4 convert_reduce_fusion
  5.5 7.4 %all-to-all-start = ((s32[16,1,8]{2,1,0:T(1,128)}), s32[16,1,8]{2,1,0:T(1,128)S(1)}, u32[]{:S(2)}, u32[]{:S(2)}) async-start(s32[16,1,8]{2,1,0:T(1,128)} %bitcast), calls=%async_computation | async-start | bytes 16384 | tf_op jit(solution)/shard_map/all_to_all | solution.py:91
  13.6 2.3 %fusion.49 = f32[16,128,128]{1,2,0:T(8,128)S(1)} fusion(s32[16,128]{1,0:T(8,128)S(1)} %bitcast.128, pred[16,128]{1,0:T(8,128)(4,1)S(1)} %fusion.97), kind=kOutput, calls=%fused_computation.85 | convolution fusion | flops 67649536 | bytes 1058816 | tf_op jit(solution)/shard_map/ij,bjk->bik/dot_general | solution.py:69
  17.3 1.9 %all-to-all-done = s32[16,1,8]{2,1,0:T(1,128)S(1)} async-done(((s32[16,1,8]{2,1,0:T(1,128)}), s32[16,1,8]{2,1,0:T(1,128)S(1)}, u32[]{:S(2)}, u32[]{:S(2)}) %all-to-all-start) | async-done | bytes 544 | tf_op jit(solution)/shard_map/all_to_all | solution.py:91
  19.6 1.1 select_reduce_fusion
  20.7 4.2 %fusion.19 = bf16[2048,256]{1,0:T(8,128)(2,1)} fusion(bf16[2048,256]{1,0:T(8,128)(2,1)S(1)} %copy-done, s32[2048]{0:T(1024)S(1)} %fusion.69), kind=kOutput, calls=%fused_computation.29 | convolution fusion | flops 2152202240 | bytes 2105344 | tf_op jit(solution)/shard_map/dot_general | solution.py:102
  24.8 4.7 %all-to-all-start.1 = ((bf16[16,128,256]{2,1,0:T(8,128)(2,1)}), bf16[16,128,256]{2,1,0:T(8,128)(2,1)}, u32[]{:S(2)}, u32[]{:S(2)}) async-start(bf16[16,128,256]{2,1,0:T(8,128)(2,1)} %bitcast.122), calls=%async_computation.1 | async-start | bytes 2097152 | tf_op jit(solution)/shard_map/all_to_all | solution.py:103
  33.4 18.8 %all-to-all-done.1 = bf16[16,128,256]{2,1,0:T(8,128)(2,1)} async-done(((bf16[16,128,256]{2,1,0:T(8,128)(2,1)}), bf16[16,128,256]{2,1,0:T(8,128)(2,1)}, u32[]{:S(2)}, u32[]{:S(2)}) %all-to-all-start.1) | async-done | bytes 1048608 | tf_op jit(solution)/shard_map/all_to_all | solution.py:103
  52.2 4.5 %fusion.20 = bf16[2048,256]{1,0:T(8,128)(2,1)S(1)} fusion(bf16[2048,256]{1,0:T(8,128)(2,1)} %bitcast.12, s32[2048]{0:T(1024)S(1)} %select_bitcast_fusion), kind=kOutput, calls=%fused_computation.30 | convolution fusion | flops 2152202240 | bytes 2105344 | tf_op jit(solution)/shard_map/dot_general | solution.py:125
  56.8 1.5 %fusion.22 = bf16[8,256,256]{2,1,0:T(8,128)(2,1)S(1)} fusion(bf16[8,256,256]{2,1,0:T(8,128)(2,1)S(1)} %bitcast.135, bf16[2,768,256]{2,1,0:T(8,128)(2,1)S(1)} %bitcast.126, bf16[8,254,256]{2,1,0:T(8,128)(2,1)S(1)} %bitcast.136, bf16[8,255,256]{2,1,0:T(8,128)(2,1)S(1)} %bitcast.137), kind=kOutput, calls=%fused_computation.32 | convolution fusion | flops 827850752 | bytes 5636096 | tf_op jit(solution)/shard_map/dot_general | solution.py:49
  58.4 2.5 %fusion.21 = (bf16[8,256,256]{2,1,0:T(8,128)(2,1)S(1)}, f32[8,256,256]{2,1,0:T(8,128)}) fusion(bf16[8,256,256]{2,1,0:T(8,128)(2,1)S(1)} %bitcast.138, bf16[2,768,256]{2,1,0:T(8,128)(2,1)S(1)} %bitcast.118, bf16[8,254,256]{2,1,0:T(8,128)(2,1)S(1)} %bitcast.139, bf16[8,255,256]{2,1,0:T(8,128)(2,1)S(1)} %bitcast.140), kind=kOutput, calls=%fused_computation.31 | convolution fusion | flops 827850752 | bytes 7733248 | tf_op jit(solution)/shard_map/dot_general | solution.py:49
  60.9 2.5 %fusion.92 = (bf16[8,256]{1,0:T(8,128)(2,1)S(1)}, bf16[8,256,256]{2,1,0:T(8,128)(2,1)S(1)}, f32[8,256,256]{2,1,0:T(8,128)}) fusion(bf16[8,256,256]{2,1,0:T(8,128)(2,1)S(1)} %get-tuple-element.28, bf16[2,768,256]{2,1,0:T(8,128)(2,1)S(1)} %bitcast.119, bf16[8,248,256]{2,1,0:T(8,128)(2,1)S(1)} %slice.81, bf16[8,252,256]{2,1,0:T(8,128)(2,1)S(1)} %bitcast.123), kind=kOutput, calls=%fused_computation.162 | convolution fusion | flops 828372992 | bytes 7704576 | tf_op jit(solution)/shard_map/dot_general | solution.py:49
  63.4 1.8 %fusion.29 = (f32[8,256]{1,0:T(8,128)S(1)}, f32[8,256]{1,0:T(8,128)S(1)}, f32[256]{0:T(256)S(1)}, bf16[8,256,256]{2,1,0:T(8,128)(2,1)S(1)}) fusion(bf16[8,256,256]{2,1,0:T(8,128)(2,1)S(1)} %get-tuple-element.17, f32[8,256]{1,0:T(8,128)S(1)} %fusion.73, f32[8,256]{1,0:T(8,128)S(1)} %bitcast.132, bf16[2,768,256]{2,1,0:T(8,128)(2,1)S(1)} %bitcast.127, ...), kind=kOutput, calls=%fused_computation.39 | convolution fusion | flops 832040704 | bytes 6685696 | tf_op jit(solution)/shard_map/dot_general | solution.py:49
  65.9 6.8 %all-to-all-start.2 = ((f32[16,1,384]{2,1,0:T(1,128)}), f32[16,1,384]{2,1,0:T(1,128)S(1)}, u32[]{:S(2)}, u32[]{:S(2)}) async-start(f32[16,1,384]{2,1,0:T(1,128)} %broadcast_in_dim.64), calls=%async_computation.2 | async-start | bytes 49152 | tf_op jit(solution)/shard_map/all_to_all | solution.py:182
  72.8 6.5 %all-to-all-done.2 = f32[16,1,384]{2,1,0:T(1,128)S(1)} async-done(((f32[16,1,384]{2,1,0:T(1,128)}), f32[16,1,384]{2,1,0:T(1,128)S(1)}, u32[]{:S(2)}, u32[]{:S(2)}) %all-to-all-start.2) | async-done | bytes 24608 | tf_op jit(solution)/shard_map/all_to_all | solution.py:182
  81.8 3.7 %multiply_convert_fusion = bf16[8,256,256]{2,1,0:T(8,128)(2,1)S(1)} fusion(f32[8,256,256]{2,1,0:T(8,128)S(1)} %copy-done.6, f32[8,256]{1,0:T(8,128)S(1)} %fusion.36, f32[8,256]{1,0:T(8,128)S(1)} %fusion.33, f32[256]{0:T(256)S(1)} %slice_divide_fusion, bf16[8,256,256]{2,1,0:T(8,128)(2,1)S(1)} %get-tuple-element.31, f32[8,256]{1,0:T(8,128)S(1)} %get-tuple-element.5, ...), kind=kLoop, calls=%fused_computation.55 | loop fusion | flops 10485760 | bytes 5284864 | tf_op jit(solution)/shard_map/convert_element_type | solution.py:197
  85.5 1.0 convolution_bitcast_fusion
  86.6 1.0 fusion.43
  88.4 1.1 copy-done.18
  90.2 3.1 %convolution_bitcast_fusion.1 = f32[1,768,256]{2,1,0:T(8,128)S(1)} fusion(f32[8,256,3,256]{3,1,0,2:T(8,128)S(1)} %fusion.43, f32[8,256,256]{2,1,0:T(8,128)S(1)} %copy-done.18, f32[8,248,256]{2,1,0:T(8,128)S(1)} %slice.91, f32[8,252,256]{2,1,0:T(8,128)S(1)} %slice.89, bf16[8,256,256]{2,1,0:T(8,128)(2,1)S(1)} %copy-done.9, ...), kind=kOutput, calls=%fused_computation.72 | convolution fusion | flops 836239360 | bytes 14394368 | tf_op jit(solution)/shard_map/dot_general | solution.py:199
  94.4 2.4 %collective-permute-done = f32[2,384,256]{2,1,0:T(8,128)} collective-permute-done((f32[2,384,256]{2,1,0:T(8,128)S(1)}, f32[2,384,256]{2,1,0:T(8,128)}, u32[]{:S(2)}, u32[]{:S(2)}) %collective-permute-start) | collective-permute-done | bytes 786464 | tf_op jit(solution)/shard_map/ppermute | solution.py:155
  96.8 1.3 fusion.55
  98.6 7.4 %collective-permute-done.1 = f32[2,192,256]{2,1,0:T(8,128)S(1)} collective-permute-done((f32[2,192,256]{2,1,0:T(8,128)S(1)}, f32[2,192,256]{2,1,0:T(8,128)S(1)}, u32[]{:S(2)}, u32[]{:S(2)}) %collective-permute-start.1) | collective-permute-done | bytes 393248 | tf_op jit(solution)/shard_map/ppermute | solution.py:155
  106.5 7.3 %collective-permute-done.2 = f32[2,96,256]{2,1,0:T(8,128)S(1)} collective-permute-done((f32[2,96,256]{2,1,0:T(8,128)S(1)}, f32[2,96,256]{2,1,0:T(8,128)S(1)}, u32[]{:S(2)}, u32[]{:S(2)}) %collective-permute-start.2) | collective-permute-done | bytes 196640 | tf_op jit(solution)/shard_map/ppermute | solution.py:155
  114.0 5.5 %collective-permute-done.3 = f32[2,48,256]{2,1,0:T(8,128)S(1)} collective-permute-done((f32[2,48,256]{2,1,0:T(8,128)S(1)}, f32[2,48,256]{2,1,0:T(8,128)S(1)}, u32[]{:S(2)}, u32[]{:S(2)}) %collective-permute-start.3) | collective-permute-done | bytes 98336 | tf_op jit(solution)/shard_map/ppermute | solution.py:155
  119.6 5.5 %collective-permute-done.4 = bf16[2,48,256]{2,1,0:T(8,128)(2,1)S(1)} collective-permute-done((bf16[2,48,256]{2,1,0:T(8,128)(2,1)S(1)}, bf16[2,48,256]{2,1,0:T(8,128)(2,1)S(1)}, u32[]{:S(2)}, u32[]{:S(2)}) %collective-permute-start.4) | collective-permute-done | bytes 49184 | tf_op jit(solution)/shard_map/ppermute | solution.py:159
  125.2 5.6 %collective-permute-done.5 = bf16[2,96,256]{2,1,0:T(8,128)(2,1)S(1)} collective-permute-done((bf16[2,96,256]{2,1,0:T(8,128)(2,1)S(1)}, bf16[2,96,256]{2,1,0:T(8,128)(2,1)S(1)}, u32[]{:S(2)}, u32[]{:S(2)}) %collective-permute-start.5) | collective-permute-done | bytes 98336 | tf_op jit(solution)/shard_map/ppermute | solution.py:159
  131.3 5.3 %collective-permute-done.6 = bf16[2,192,256]{2,1,0:T(8,128)(2,1)S(1)} collective-permute-done((bf16[2,192,256]{2,1,0:T(8,128)(2,1)S(1)}, bf16[2,192,256]{2,1,0:T(8,128)(2,1)S(1)}, u32[]{:S(2)}, u32[]{:S(2)}) %collective-permute-start.6) | collective-permute-done | bytes 196640 | tf_op jit(solution)/shard_map/ppermute | solution.py:159
  137.5 1.0 collective-permute-done.7
  138.8 1.2 copy.122
  141.1 5.0 %multiply_add_fusion = (f32[2,196608]{1,0:T(2,128)}, f32[2,196608]{1,0:T(2,128)}, f32[2,196608]{1,0:T(2,128)}) fusion(f32[2,196608]{1,0:T(2,128)S(1)} %copy-done.2, f32[2,196608]{1,0:T(2,128)S(1)} %copy-done.4, f32[2,196608]{1,0:T(2,128)S(1)} %bitcast.117, f32[2,196608]{1,0:T(2,128)S(1)} %copy-done.7), kind=kLoop, calls=%fused_computation.68 | loop fusion | flops 2752512 | bytes 11010048 | tf_op jit(solution)/shard_map/add | solution.py:220
  (104 shorter events, 17.5 us)
Async XLA Ops:
  0.6 20.0 %copy-start = (bf16[2048,256]{1,0:T(8,128)(2,1)S(1)}, bf16[2048,256]{1,0:T(8,128)(2,1)}, u32[]{:S(2)}) copy-start(bf16[2048,256]{1,0:T(8,128)(2,1)} %param.6) | copy-start | bytes 3145732
  0.6 20.0 %copy-start.15 = (s32[2048]{0:T(1024)S(1)}, s32[2048]{0:T(1024)}, u32[]{:S(2)}) copy-start(s32[2048]{0:T(1024)} %param.7) | copy-start | bytes 24580
  5.5 13.7 %all-to-all-start = ((s32[16,1,8]{2,1,0:T(1,128)}), s32[16,1,8]{2,1,0:T(1,128)S(1)}, u32[]{:S(2)}, u32[]{:S(2)}) async-start(s32[16,1,8]{2,1,0:T(1,128)} %bitcast), calls=%async_computation | async-start | bytes 16384 | tf_op jit(solution)/shard_map/all_to_all | solution.py:91
  24.8 4.7 %copy-start.1 = (f32[2,196608]{1,0:T(2,128)S(1)}, f32[2,196608]{1,0:T(2,128)}, u32[]{:S(2)}) copy-start(f32[2,196608]{1,0:T(2,128)} %param.11) | copy-start | bytes 4718596
  24.8 27.4 %all-to-all-start.1 = ((bf16[16,128,256]{2,1,0:T(8,128)(2,1)}), bf16[16,128,256]{2,1,0:T(8,128)(2,1)}, u32[]{:S(2)}, u32[]{:S(2)}) async-start(bf16[16,128,256]{2,1,0:T(8,128)(2,1)} %bitcast.122), calls=%async_computation.1 | async-start | bytes 2097152 | tf_op jit(solution)/shard_map/all_to_all | solution.py:103
  29.5 1.7 %copy-start.3 = (f32[2,196608]{1,0:T(2,128)S(1)}, f32[2,196608]{1,0:T(2,128)}, u32[]{:S(2)}) copy-start(f32[2,196608]{1,0:T(2,128)} %param.9) | copy-start | bytes 4718596
  52.2 4.5 %copy-start.14 = (bf16[1,2,768,256]{3,2,1,0:T(8,128)(2,1)S(1)}, bf16[1,2,768,256]{3,2,1,0:T(8,128)(2,1)}, u32[]{:S(2)}) copy-start(bf16[1,2,768,256]{3,2,1,0:T(8,128)(2,1)} %copy.129) | copy-start | bytes 2359300
  56.7 1.6 %copy-start.16 = (bf16[2048,256]{1,0:T(8,128)(2,1)}, bf16[2048,256]{1,0:T(8,128)(2,1)S(1)}, u32[]{:S(2)}) copy-start(bf16[2048,256]{1,0:T(8,128)(2,1)S(1)} %fusion.20) | copy-start | bytes 3145732
  60.9 2.6 %copy-start.12 = (bf16[8,256,256]{2,1,0:T(8,128)(2,1)}, bf16[8,256,256]{2,1,0:T(8,128)(2,1)S(1)}, u32[]{:S(2)}) copy-start(bf16[8,256,256]{2,1,0:T(8,128)(2,1)S(1)} %get-tuple-element.28) | copy-start | bytes 3145732
  60.9 2.5 %copy-start.10 = (bf16[8,248,256]{2,1,0:T(8,128)(2,1)}, bf16[8,248,256]{2,1,0:T(8,128)(2,1)S(1)}, u32[]{:S(2)}) copy-start(bf16[8,248,256]{2,1,0:T(8,128)(2,1)S(1)} %slice.81) | copy-start | bytes 3047428
  63.4 1.9 %copy-start.8 = (bf16[8,256,256]{2,1,0:T(8,128)(2,1)}, bf16[8,256,256]{2,1,0:T(8,128)(2,1)S(1)}, u32[]{:S(2)}) copy-start(bf16[8,256,256]{2,1,0:T(8,128)(2,1)S(1)} %get-tuple-element.17) | copy-start | bytes 3145732
  65.9 13.4 %all-to-all-start.2 = ((f32[16,1,384]{2,1,0:T(1,128)}), f32[16,1,384]{2,1,0:T(1,128)S(1)}, u32[]{:S(2)}, u32[]{:S(2)}) async-start(f32[16,1,384]{2,1,0:T(1,128)} %broadcast_in_dim.64), calls=%async_computation.2 | async-start | bytes 49152 | tf_op jit(solution)/shard_map/all_to_all | solution.py:182
  79.4 2.4 %copy-start.6 = (f32[8,256,256]{2,1,0:T(8,128)S(1)}, f32[8,256,256]{2,1,0:T(8,128)}, u32[]{:S(2)}) copy-start(f32[8,256,256]{2,1,0:T(8,128)} %get-tuple-element.30) | copy-start | bytes 6291460
  81.8 3.7 %copy-start.11 = (bf16[8,248,256]{2,1,0:T(8,128)(2,1)S(1)}, bf16[8,248,256]{2,1,0:T(8,128)(2,1)}, u32[]{:S(2)}) copy-start(bf16[8,248,256]{2,1,0:T(8,128)(2,1)} %copy-done.10) | copy-start | bytes 3047428
  81.8 3.7 %copy-start.13 = (bf16[8,256,256]{2,1,0:T(8,128)(2,1)S(1)}, bf16[8,256,256]{2,1,0:T(8,128)(2,1)}, u32[]{:S(2)}) copy-start(bf16[8,256,256]{2,1,0:T(8,128)(2,1)} %copy-done.12) | copy-start | bytes 3145732
  88.0 1.6 %copy-start.18 = (f32[8,256,256]{2,1,0:T(8,128)S(1)}, f32[8,256,256]{2,1,0:T(8,128)}, u32[]{:S(2)}) copy-start(f32[8,256,256]{2,1,0:T(8,128)} %get-tuple-element.29) | copy-start | bytes 6291460
  88.2 1.7 %copy-start.9 = (bf16[8,256,256]{2,1,0:T(8,128)(2,1)S(1)}, bf16[8,256,256]{2,1,0:T(8,128)(2,1)}, u32[]{:S(2)}) copy-start(bf16[8,256,256]{2,1,0:T(8,128)(2,1)} %copy-done.8) | copy-start | bytes 3145732
  88.2 2.0 %copy-start.17 = (bf16[2048,256]{1,0:T(8,128)(2,1)S(1)}, bf16[2048,256]{1,0:T(8,128)(2,1)}, u32[]{:S(2)}) copy-start(bf16[2048,256]{1,0:T(8,128)(2,1)} %copy-done.16) | copy-start | bytes 3145732
  93.3 0.9 copy-start.5
  94.3 2.5 %collective-permute-start = (f32[2,384,256]{2,1,0:T(8,128)S(1)}, f32[2,384,256]{2,1,0:T(8,128)}, u32[]{:S(2)}, u32[]{:S(2)}) collective-permute-start(f32[2,384,256]{2,1,0:T(8,128)S(1)} %fusion.53), channel_id=1, source_target_pairs={{0,1},{1,0},{2,3},{3,2},{4,5},{5,4},{6,7},{7,6},{8,9},{9,8},{10,11... | collective-permute-start | bytes 2359304 | tf_op jit(solution)/shard_map/ppermute | solution.py:155
  98.1 7.8 %collective-permute-start.1 = (f32[2,192,256]{2,1,0:T(8,128)S(1)}, f32[2,192,256]{2,1,0:T(8,128)S(1)}, u32[]{:S(2)}, u32[]{:S(2)}) collective-permute-start(f32[2,192,256]{2,1,0:T(8,128)S(1)} %constant_dynamic-slice_fusion.1), channel_id=1, source_target_pairs={{0,2},{1,5},{2,0},{3,7},{4,6},{5,1},{6,4},{7,3},{8,10},{9,13},{10,... | collective-permute-start | bytes 1179656 | tf_op jit(solution)/shard_map/ppermute | solution.py:155
  106.1 7.8 %collective-permute-start.2 = (f32[2,96,256]{2,1,0:T(8,128)S(1)}, f32[2,96,256]{2,1,0:T(8,128)S(1)}, u32[]{:S(2)}, u32[]{:S(2)}) collective-permute-start(f32[2,96,256]{2,1,0:T(8,128)S(1)} %constant_dynamic-slice_fusion), channel_id=1, source_target_pairs={{0,4},{1,9},{2,6},{3,11},{4,0},{5,13},{6,2},{7,15},{8,12},{9,1},{1... | collective-permute-start | bytes 589832 | tf_op jit(solution)/shard_map/ppermute | solution.py:155
  113.9 5.6 %collective-permute-start.3 = (f32[2,48,256]{2,1,0:T(8,128)S(1)}, f32[2,48,256]{2,1,0:T(8,128)S(1)}, u32[]{:S(2)}, u32[]{:S(2)}) collective-permute-start(f32[2,48,256]{2,1,0:T(8,128)S(1)} %constant_dynamic-slice_fusion.2), channel_id=1, source_target_pairs={{0,8},{1,3},{2,10},{3,1},{4,12},{5,7},{6,14},{7,5},{8,0},{9,11},{1... | collective-permute-start | bytes 294920 | tf_op jit(solution)/shard_map/ppermute | solution.py:155
  119.5 5.6 %collective-permute-start.4 = (bf16[2,48,256]{2,1,0:T(8,128)(2,1)S(1)}, bf16[2,48,256]{2,1,0:T(8,128)(2,1)S(1)}, u32[]{:S(2)}, u32[]{:S(2)}) collective-permute-start(bf16[2,48,256]{2,1,0:T(8,128)(2,1)S(1)} %add_convert_fusion.2), channel_id=1, source_target_pairs={{0,8},{1,3},{2,10},{3,1},{4,12},{5,7},{6,14},{7,5},{8,0},{9,11},{1... | collective-permute-start | bytes 147464 | tf_op jit(solution)/shard_map/ppermute | solution.py:159
  125.1 5.7 %collective-permute-start.5 = (bf16[2,96,256]{2,1,0:T(8,128)(2,1)S(1)}, bf16[2,96,256]{2,1,0:T(8,128)(2,1)S(1)}, u32[]{:S(2)}, u32[]{:S(2)}) collective-permute-start(bf16[2,96,256]{2,1,0:T(8,128)(2,1)S(1)} %pad_maximum_fusion.2), channel_id=1, source_target_pairs={{0,4},{1,9},{2,6},{3,11},{4,0},{5,13},{6,2},{7,15},{8,12},{9,1},{1... | collective-permute-start | bytes 294920 | tf_op jit(solution)/shard_map/ppermute | solution.py:159
  130.9 5.7 %collective-permute-start.6 = (bf16[2,192,256]{2,1,0:T(8,128)(2,1)S(1)}, bf16[2,192,256]{2,1,0:T(8,128)(2,1)S(1)}, u32[]{:S(2)}, u32[]{:S(2)}) collective-permute-start(bf16[2,192,256]{2,1,0:T(8,128)(2,1)S(1)} %pad_maximum_fusion.1), channel_id=1, source_target_pairs={{0,2},{1,5},{2,0},{3,7},{4,6},{5,1},{6,4},{7,3},{8,10},{9,13},{10,... | collective-permute-start | bytes 589832 | tf_op jit(solution)/shard_map/ppermute | solution.py:159
  136.7 1.8 %collective-permute-start.7 = (bf16[2,384,256]{2,1,0:T(8,128)(2,1)S(1)}, bf16[2,384,256]{2,1,0:T(8,128)(2,1)S(1)}, u32[]{:S(2)}, u32[]{:S(2)}) collective-permute-start(bf16[2,384,256]{2,1,0:T(8,128)(2,1)S(1)} %pad_maximum_fusion), channel_id=1, source_target_pairs={{0,1},{1,0},{2,3},{3,2},{4,5},{5,4},{6,7},{7,6},{8,9},{9,8},{10,11... | collective-permute-start | bytes 1179656 | tf_op jit(solution)/shard_map/ppermute | solution.py:159
  138.7 1.4 copy-start.7
  138.8 1.8 %copy-start.2 = (f32[2,196608]{1,0:T(2,128)S(1)}, f32[2,196608]{1,0:T(2,128)}, u32[]{:S(2)}) copy-start(f32[2,196608]{1,0:T(2,128)} %param.11) | copy-start | bytes 4718596
  138.8 2.2 %copy-start.4 = (f32[2,196608]{1,0:T(2,128)S(1)}, f32[2,196608]{1,0:T(2,128)}, u32[]{:S(2)}) copy-start(f32[2,196608]{1,0:T(2,128)} %param.9) | copy-start | bytes 4718596

commit v10 on v9

--- a/solution.py
+++ b/solution.py
@@ -88,31 +88,35 @@
     owner_dev = slot_of // per_dev
     slot_hot = (slot_of[:, None] == jnp.arange(objects_all, dtype=jnp.int32)[None, :]) & live_rows[:, None]
     group_size = jnp.sum(slot_hot.astype(jnp.int32), axis=0).reshape(wide_count, per_dev)
-    got_size = lax.all_to_all(group_size, "wide", split_axis=0, concat_axis=0, tiled=True)
     places = jnp.arange(per_dev, dtype=jnp.int32)
     earlier_place = (places[:, None] < places[None, :]).astype(jnp.int32)
     group_start = jnp.sum(group_size[:, :, None] * earlier_place[None, :, :], axis=1)
     running = prefix_count(slot_hot)
     rank_in_group = jnp.sum(jnp.where(slot_hot, running, 0), axis=1) - 1
     start_of_row = jnp.sum(jnp.where(slot_hot, group_start.reshape(1, -1), 0), axis=1)
-    send_index = jnp.where(live_rows, owner_dev * capacity + start_of_row + rank_in_group, -1)
+    chunk = capacity + 16
+    send_index = jnp.where(live_rows, owner_dev * chunk + start_of_row + rank_in_group, -1)
     pick = (
-        jnp.arange(rows_total, dtype=jnp.int32)[:, None] == send_index[None, :]
+        jnp.arange(wide_count * chunk, dtype=jnp.int32)[:, None] == send_index[None, :]
     ).astype(jnp.bfloat16)
-    send_rows = jnp.dot(pick, epoch_rows, preferred_element_type=jnp.float32).astype(jnp.bfloat16)
-    got_rows = lax.all_to_all(
-        send_rows.reshape(wide_count, capacity, feat_width),
-        "wide",
-        split_axis=0,
-        concat_axis=0,
-        tiled=True,
-    )
+    payload = jnp.dot(pick, epoch_rows, preferred_element_type=jnp.float32).astype(jnp.bfloat16)
+    payload = lax.dynamic_update_slice(
+        payload.reshape(wide_count, chunk, feat_width),
+        group_size.astype(jnp.bfloat16).reshape(wide_count, 1, per_dev),
+        (0, capacity, 0),
+    )
+    got = lax.all_to_all(payload, "wide", split_axis=0, concat_axis=0, tiled=True)
+    got_size = got[:, capacity, :per_dev].astype(jnp.int32)
     sources = jnp.arange(wide_count, dtype=jnp.int32)
     earlier_source = (sources[:, None] > sources[None, :]).astype(jnp.int32)
     before_source = jnp.sum(earlier_source[:, :, None] * got_size[None, :, :], axis=1)
     got_start = jnp.sum(got_size[:, :, None] * earlier_place[None, :, :], axis=1)
-    slots = jnp.arange(capacity, dtype=jnp.int32)[None, :, None]
-    in_group = (slots >= got_start[:, None, :]) & (slots < (got_start + got_size)[:, None, :])
+    slots = jnp.arange(chunk, dtype=jnp.int32)[None, :, None]
+    in_group = (
+        (slots >= got_start[:, None, :])
+        & (slots < (got_start + got_size)[:, None, :])
+        & (slots < capacity)
+    )
     position = jnp.sum(
         jnp.where(in_group, before_source[:, None, :] + slots - got_start[:, None, :], 0), axis=2
     )
@@ -123,7 +127,7 @@
         jnp.arange(per_dev * SEQ, dtype=jnp.int32)[:, None] == target[None, :]
     ).astype(jnp.bfloat16)
     sequences = jnp.dot(
-        put, got_rows.reshape(-1, feat_width), preferred_element_type=jnp.float32
+        put, got.reshape(-1, feat_width), preferred_element_type=jnp.float32
     ).astype(jnp.bfloat16)
     return (sequences.reshape(per_dev, SEQ, feat_width), counts)
 

time: 147 us -> 152 us (1.034)
  starting transfers between devices: 20.5 us -> 16.6 us
  matrix products: 24.5 us -> 27.8 us
  local copies, waits for them, and re-layouts: 10.1 us -> 13.1 us
  waiting for transfers between devices: 67.3 us -> 69.8 us
    all_to_all x2 -> x1, starting transfers between devices: 12 us -> 7.42 us  [route_rows(): lax.all_to_all(payload, 'wide', split_axis=0, concat_axis=0, tiled=True)]
    all_to_all x2 -> x1, waiting for transfers between devices: 20.8 us -> 23.4 us  [route_rows(): lax.all_to_all(payload, 'wide', split_axis=0, concat_axis=0, tiled=True)]
    dot_general x4, matrix products: 8.34 us -> 10.9 us  [run_network(): jnp.dot(stacked.reshape(-1, stacked.shape[2]), weights[layer_at], preferr...]
    dynamic_update_slice x0 -> x1, local copies, waits for them, and re-layouts: none -> 1.71 us  [route_rows(): lax.dynamic_update_slice(payload.reshape(wide_count, chunk, feat_width),...]
    unnamed x41 -> x42, local copies, waits for them, and re-layouts: 6.71 us -> 6.8 us
  transfers between devices with their start and end apart: 11 -> 10, of which waited for: 11 -> 10; matrix products, arithmetic and copies ran while one was open for 5% -> 1% of each run, Pallas kernels for 0% -> 0%
where the time goes in v10:
time: 152 us; the launch traced here: 151 us
  waiting for transfers between devices  69.8 us (46%)
  matrix products  27.8 us (18%)
  other arithmetic  21.7 us (14%)
  starting transfers between devices  16.6 us (11%)
  local copies, waits for them, and re-layouts  13.1 us (9%)
  between operations  1.9 us (1%)
    all_to_all x1, waiting for transfers between devices, route_rows(): lax.all_to_all(payload, 'wide', split_axis=0, concat_axis=0, tiled=True)  23.4 us
    ppermute x4, waiting for transfers between devices, all_reduce_wide(): buf = keep + lax.ppermute(send, 'wide', pairs)  22.5 us
    ppermute x4, waiting for transfers between devices, all_reduce_wide(): got = lax.ppermute(buf, 'wide', pairs)  17.4 us
    dot_general x4, matrix products, run_network(): jnp.dot(stacked.reshape(-1, stacked.shape[2]), weights[layer_at], preferr...  10.9 us
    all_to_all x1, starting transfers between devices, local(): lax.all_to_all(jnp.broadcast_to(stats[None, :], (wide_count, stats.shape[...  7.49 us
    all_to_all x1, starting transfers between devices, route_rows(): lax.all_to_all(payload, 'wide', split_axis=0, concat_axis=0, tiled=True)  7.42 us
    unnamed x42, local copies, waits for them, and re-layouts  6.8 us
    all_to_all x1, waiting for transfers between devices, local(): lax.all_to_all(jnp.broadcast_to(stats[None, :], (wide_count, stats.shape[...  6.52 us
  transfers between devices with their start and end apart: 10, of which 10 were waited for; matrix products, arithmetic and copies ran while one was open for 1% of the time, Pallas kernels for 0%

profile of v10, /device:TPU:0, one launch (start us, length us, event | category | flops | bytes accessed | tf_op | source)
XLA Modules:
  0.0 151.0 jit_solution(1484058544544121130)
XLA Ops:
  2.9 1.3 select_reduce_fusion.1
  4.1 1.4 convert_reduce_fusion
  5.6 2.3 %fusion.49 = f32[16,128,128]{1,2,0:T(8,128)S(1)} fusion(s32[16,128]{1,0:T(8,128)S(1)} %bitcast.124, pred[16,128]{1,0:T(8,128)(4,1)S(1)} %fusion.97), kind=kOutput, calls=%fused_computation.85 | convolution fusion | flops 67649536 | bytes 1058816 | tf_op jit(solution)/shard_map/ij,bjk->bik/dot_general | solution.py:69
  9.5 1.1 select_reduce_fusion
  10.7 4.6 %fusion.8 = bf16[2304,256]{1,0:T(8,128)(2,1)} fusion(bf16[2048,256]{1,0:T(8,128)(2,1)S(1)} %copy-done, s32[2048]{0:T(1024)S(1)} %fusion.69), kind=kOutput, calls=%fused_computation.13 | convolution fusion | flops 2421227520 | bytes 2236416 | tf_op jit(solution)/shard_map/dot_general | solution.py:102
  15.3 1.7 %dynamic_update_slice.3 = bf16[16,144,256]{2,1,0:T(8,128)(2,1)} dynamic-update-slice(bf16[16,144,256]{2,1,0:T(8,128)(2,1)} %bitcast.118, bf16[16,1,8]{2,1,0:T(2,128)(2,1)S(1)} %convert_element_type.165, s32[]{:T(128)} %constant.29.clone.1, s32[]{:T(128)} %constant.36.clone.1, s32[]{:T(128)} %constant.29.clone.1) | dynamic-update-slice | bytes 516 | tf_op jit(solution)/shard_map/dynamic_update_slice | solution.py:103
  17.0 7.4 %all-to-all-start = ((bf16[16,144,256]{2,1,0:T(8,128)(2,1)}), bf16[16,144,256]{2,1,0:T(8,128)(2,1)}, u32[]{:S(2)}, u32[]{:S(2)}) async-start(bf16[16,144,256]{2,1,0:T(8,128)(2,1)} %dynamic_update_slice.3), calls=%async_computation | async-start | bytes 2359296 | tf_op jit(solution)/shard_map/all_to_all | solution.py:108
  26.3 23.4 %all-to-all-done = bf16[16,144,256]{2,1,0:T(8,128)(2,1)} async-done(((bf16[16,144,256]{2,1,0:T(8,128)(2,1)}), bf16[16,144,256]{2,1,0:T(8,128)(2,1)}, u32[]{:S(2)}, u32[]{:S(2)}) %all-to-all-start) | async-done | bytes 1179680 | tf_op jit(solution)/shard_map/all_to_all | solution.py:108
  52.2 4.8 %fusion.20 = bf16[2048,256]{1,0:T(8,128)(2,1)S(1)} fusion(bf16[2304,256]{1,0:T(8,128)(2,1)} %bitcast.10, s32[2304]{0:T(1024)S(1)} %select_n.142), kind=kOutput, calls=%fused_computation.30 | convolution fusion | flops 2421161984 | bytes 2237440 | tf_op jit(solution)/shard_map/dot_general | solution.py:129
  57.0 1.5 %fusion.22 = bf16[8,256,256]{2,1,0:T(8,128)(2,1)S(1)} fusion(bf16[8,256,256]{2,1,0:T(8,128)(2,1)S(1)} %bitcast.129, bf16[2,768,256]{2,1,0:T(8,128)(2,1)S(1)} %bitcast.123, bf16[8,254,256]{2,1,0:T(8,128)(2,1)S(1)} %bitcast.130, bf16[8,255,256]{2,1,0:T(8,128)(2,1)S(1)} %bitcast.131), kind=kOutput, calls=%fused_computation.32 | convolution fusion | flops 827850752 | bytes 5636096 | tf_op jit(solution)/shard_map/dot_general | solution.py:49
  58.5 1.1 slice.90
  59.7 2.5 %fusion.21 = (bf16[8,256,256]{2,1,0:T(8,128)(2,1)S(1)}, f32[8,256,256]{2,1,0:T(8,128)}) fusion(bf16[8,256,256]{2,1,0:T(8,128)(2,1)S(1)} %bitcast.132, bf16[2,768,256]{2,1,0:T(8,128)(2,1)S(1)} %bitcast.114, bf16[8,254,256]{2,1,0:T(8,128)(2,1)S(1)} %bitcast.133, bf16[8,255,256]{2,1,0:T(8,128)(2,1)S(1)} %bitcast.134), kind=kOutput, calls=%fused_computation.31 | convolution fusion | flops 827850752 | bytes 7733248 | tf_op jit(solution)/shard_map/dot_general | solution.py:49
  62.2 2.6 %fusion.92 = (bf16[8,256]{1,0:T(8,128)(2,1)S(1)}, bf16[8,256,256]{2,1,0:T(8,128)(2,1)}, f32[8,256,256]{2,1,0:T(8,128)}) fusion(bf16[8,256,256]{2,1,0:T(8,128)(2,1)S(1)} %get-tuple-element.27, bf16[2,768,256]{2,1,0:T(8,128)(2,1)S(1)} %bitcast.115, bf16[8,248,256]{2,1,0:T(8,128)(2,1)S(1)} %slice.86, bf16[8,252,256]{2,1,0:T(8,128)(2,1)S(1)} %bitcast.119), kind=kOutput, calls=%fused_computation.166 | convolution fusion | flops 828372992 | bytes 7704576 | tf_op jit(solution)/shard_map/dot_general | solution.py:49
  65.6 4.3 %fusion.29 = (f32[8,256]{1,0:T(8,128)S(1)}, f32[8,256]{1,0:T(8,128)S(1)}, f32[256]{0:T(256)S(1)}, bf16[8,256,256]{2,1,0:T(8,128)(2,1)S(1)}) fusion(bf16[8,256,256]{2,1,0:T(8,128)(2,1)} %get-tuple-element.15, f32[8,256]{1,0:T(8,128)S(1)} %fusion.73, f32[8,256]{1,0:T(8,128)S(1)} %bitcast.126, bf16[2,768,256]{2,1,0:T(8,128)(2,1)} %bitcast.122, ...), kind=kOutput, calls=%fused_computation.39 | convolution fusion | flops 832040704 | bytes 6685696 | tf_op jit(solution)/shard_map/dot_general | solution.py:49
  70.5 7.5 %all-to-all-start.1 = ((f32[16,1,384]{2,1,0:T(1,128)}), f32[16,1,384]{2,1,0:T(1,128)S(1)}, u32[]{:S(2)}, u32[]{:S(2)}) async-start(f32[16,1,384]{2,1,0:T(1,128)} %broadcast_in_dim.61), calls=%async_computation.1 | async-start | bytes 49152 | tf_op jit(solution)/shard_map/all_to_all | solution.py:186
  78.0 6.5 %all-to-all-done.1 = f32[16,1,384]{2,1,0:T(1,128)S(1)} async-done(((f32[16,1,384]{2,1,0:T(1,128)}), f32[16,1,384]{2,1,0:T(1,128)S(1)}, u32[]{:S(2)}, u32[]{:S(2)}) %all-to-all-start.1) | async-done | bytes 24608 | tf_op jit(solution)/shard_map/all_to_all | solution.py:186
  87.1 3.7 %multiply_convert_fusion = bf16[8,256,256]{2,1,0:T(8,128)(2,1)S(1)} fusion(f32[8,256,256]{2,1,0:T(8,128)S(1)} %copy-done.6, f32[8,256]{1,0:T(8,128)S(1)} %fusion.36, f32[8,256]{1,0:T(8,128)S(1)} %fusion.33, f32[256]{0:T(256)S(1)} %slice_divide_fusion, bf16[8,256,256]{2,1,0:T(8,128)(2,1)S(1)} %get-tuple-element.30, f32[8,256]{1,0:T(8,128)S(1)} %get-tuple-element.5, ...), kind=kLoop, calls=%fused_computation.55 | loop fusion | flops 10485760 | bytes 5284864 | tf_op jit(solution)/shard_map/convert_element_type | solution.py:201
  90.8 1.0 convolution_bitcast_fusion
  91.8 1.0 fusion.43
  93.7 1.1 copy-done.18
  95.5 3.1 %convolution_bitcast_fusion.1 = f32[1,768,256]{2,1,0:T(8,128)S(1)} fusion(f32[8,256,3,256]{3,1,0,2:T(8,128)S(1)} %fusion.43, f32[8,256,256]{2,1,0:T(8,128)S(1)} %copy-done.18, f32[8,248,256]{2,1,0:T(8,128)S(1)} %slice.96, f32[8,252,256]{2,1,0:T(8,128)S(1)} %slice.94, bf16[8,256,256]{2,1,0:T(8,128)(2,1)S(1)} %copy-done.8, ...), kind=kOutput, calls=%fused_computation.72 | convolution fusion | flops 836239360 | bytes 14394368 | tf_op jit(solution)/shard_map/dot_general | solution.py:203
  99.6 2.3 %collective-permute-done = f32[2,384,256]{2,1,0:T(8,128)S(1)} collective-permute-done((f32[2,384,256]{2,1,0:T(8,128)S(1)}, f32[2,384,256]{2,1,0:T(8,128)S(1)}, u32[]{:S(2)}, u32[]{:S(2)}) %collective-permute-start) | collective-permute-done | bytes 786464 | tf_op jit(solution)/shard_map/ppermute | solution.py:159
  101.9 1.1 fusion.55
  103.5 7.4 %collective-permute-done.1 = f32[2,192,256]{2,1,0:T(8,128)S(1)} collective-permute-done((f32[2,192,256]{2,1,0:T(8,128)S(1)}, f32[2,192,256]{2,1,0:T(8,128)S(1)}, u32[]{:S(2)}, u32[]{:S(2)}) %collective-permute-start.1) | collective-permute-done | bytes 393248 | tf_op jit(solution)/shard_map/ppermute | solution.py:159
  111.4 7.3 %collective-permute-done.2 = f32[2,96,256]{2,1,0:T(8,128)S(1)} collective-permute-done((f32[2,96,256]{2,1,0:T(8,128)S(1)}, f32[2,96,256]{2,1,0:T(8,128)S(1)}, u32[]{:S(2)}, u32[]{:S(2)}) %collective-permute-start.2) | collective-permute-done | bytes 196640 | tf_op jit(solution)/shard_map/ppermute | solution.py:159
  118.8 5.5 %collective-permute-done.3 = f32[2,48,256]{2,1,0:T(8,128)S(1)} collective-permute-done((f32[2,48,256]{2,1,0:T(8,128)S(1)}, f32[2,48,256]{2,1,0:T(8,128)S(1)}, u32[]{:S(2)}, u32[]{:S(2)}) %collective-permute-start.3) | collective-permute-done | bytes 98336 | tf_op jit(solution)/shard_map/ppermute | solution.py:159
  124.5 5.5 %collective-permute-done.4 = bf16[2,48,256]{2,1,0:T(8,128)(2,1)S(1)} collective-permute-done((bf16[2,48,256]{2,1,0:T(8,128)(2,1)S(1)}, bf16[2,48,256]{2,1,0:T(8,128)(2,1)S(1)}, u32[]{:S(2)}, u32[]{:S(2)}) %collective-permute-start.4) | collective-permute-done | bytes 49184 | tf_op jit(solution)/shard_map/ppermute | solution.py:163
  130.1 5.6 %collective-permute-done.5 = bf16[2,96,256]{2,1,0:T(8,128)(2,1)S(1)} collective-permute-done((bf16[2,96,256]{2,1,0:T(8,128)(2,1)S(1)}, bf16[2,96,256]{2,1,0:T(8,128)(2,1)S(1)}, u32[]{:S(2)}, u32[]{:S(2)}) %collective-permute-start.5) | collective-permute-done | bytes 98336 | tf_op jit(solution)/shard_map/ppermute | solution.py:163
  136.2 5.3 %collective-permute-done.6 = bf16[2,192,256]{2,1,0:T(8,128)(2,1)S(1)} collective-permute-done((bf16[2,192,256]{2,1,0:T(8,128)(2,1)S(1)}, bf16[2,192,256]{2,1,0:T(8,128)(2,1)S(1)}, u32[]{:S(2)}, u32[]{:S(2)}) %collective-permute-start.6) | collective-permute-done | bytes 196640 | tf_op jit(solution)/shard_map/ppermute | solution.py:163
  142.4 1.0 collective-permute-done.7
  143.7 1.2 copy.119
  146.0 5.0 %multiply_add_fusion = (f32[2,196608]{1,0:T(2,128)}, f32[2,196608]{1,0:T(2,128)}, f32[2,196608]{1,0:T(2,128)}) fusion(f32[2,196608]{1,0:T(2,128)S(1)} %copy-done.2, f32[2,196608]{1,0:T(2,128)S(1)} %copy-done.4, f32[2,196608]{1,0:T(2,128)S(1)} %bitcast.113, f32[2,196608]{1,0:T(2,128)S(1)} %copy-done.7), kind=kLoop, calls=%fused_computation.68 | loop fusion | flops 2752512 | bytes 11010048 | tf_op jit(solution)/shard_map/add | solution.py:224
  (108 shorter events, 17.9 us)
Async XLA Ops:
  0.6 10.1 %copy-start = (bf16[2048,256]{1,0:T(8,128)(2,1)S(1)}, bf16[2048,256]{1,0:T(8,128)(2,1)}, u32[]{:S(2)}) copy-start(bf16[2048,256]{1,0:T(8,128)(2,1)} %param.6) | copy-start | bytes 3145732
  0.6 10.0 %copy-start.15 = (s32[2048]{0:T(1024)S(1)}, s32[2048]{0:T(1024)}, u32[]{:S(2)}) copy-start(s32[2048]{0:T(1024)} %param.7) | copy-start | bytes 24580
  15.3 9.2 %copy-start.1 = (f32[2,196608]{1,0:T(2,128)S(1)}, f32[2,196608]{1,0:T(2,128)}, u32[]{:S(2)}) copy-start(f32[2,196608]{1,0:T(2,128)} %param.11) | copy-start | bytes 4718596
  17.0 32.6 %all-to-all-start = ((bf16[16,144,256]{2,1,0:T(8,128)(2,1)}), bf16[16,144,256]{2,1,0:T(8,128)(2,1)}, u32[]{:S(2)}, u32[]{:S(2)}) async-start(bf16[16,144,256]{2,1,0:T(8,128)(2,1)} %dynamic_update_slice.3), calls=%async_computation | async-start | bytes 2359296 | tf_op jit(solution)/shard_map/all_to_all | solution.py:108
  24.4 1.7 %copy-start.3 = (f32[2,196608]{1,0:T(2,128)S(1)}, f32[2,196608]{1,0:T(2,128)}, u32[]{:S(2)}) copy-start(f32[2,196608]{1,0:T(2,128)} %param.9) | copy-start | bytes 4718596
  52.2 4.8 %copy-start.14 = (bf16[1,2,768,256]{3,2,1,0:T(8,128)(2,1)S(1)}, bf16[1,2,768,256]{3,2,1,0:T(8,128)(2,1)}, u32[]{:S(2)}) copy-start(bf16[1,2,768,256]{3,2,1,0:T(8,128)(2,1)} %copy.126) | copy-start | bytes 2359300
  57.0 2.7 %copy-start.16 = (bf16[2048,256]{1,0:T(8,128)(2,1)}, bf16[2048,256]{1,0:T(8,128)(2,1)S(1)}, u32[]{:S(2)}) copy-start(bf16[2048,256]{1,0:T(8,128)(2,1)S(1)} %fusion.20) | copy-start | bytes 3145732
  58.5 3.6 %copy-start.13 = (bf16[8,256,256]{2,1,0:T(8,128)(2,1)}, bf16[8,256,256]{2,1,0:T(8,128)(2,1)S(1)}, u32[]{:S(2)}) copy-start(bf16[8,256,256]{2,1,0:T(8,128)(2,1)S(1)} %fusion.22) | copy-start | bytes 3145732
  62.1 2.7 %copy-start.11 = (bf16[8,256,256]{2,1,0:T(8,128)(2,1)}, bf16[8,256,256]{2,1,0:T(8,128)(2,1)S(1)}, u32[]{:S(2)}) copy-start(bf16[8,256,256]{2,1,0:T(8,128)(2,1)S(1)} %get-tuple-element.27) | copy-start | bytes 3145732
  62.2 2.7 %copy-start.9 = (bf16[8,248,256]{2,1,0:T(8,128)(2,1)}, bf16[8,248,256]{2,1,0:T(8,128)(2,1)S(1)}, u32[]{:S(2)}) copy-start(bf16[8,248,256]{2,1,0:T(8,128)(2,1)S(1)} %slice.86) | copy-start | bytes 3047428
  70.5 14.1 %all-to-all-start.1 = ((f32[16,1,384]{2,1,0:T(1,128)}), f32[16,1,384]{2,1,0:T(1,128)S(1)}, u32[]{:S(2)}, u32[]{:S(2)}) async-start(f32[16,1,384]{2,1,0:T(1,128)} %broadcast_in_dim.61), calls=%async_computation.1 | async-start | bytes 49152 | tf_op jit(solution)/shard_map/all_to_all | solution.py:186
  84.6 2.4 %copy-start.6 = (f32[8,256,256]{2,1,0:T(8,128)S(1)}, f32[8,256,256]{2,1,0:T(8,128)}, u32[]{:S(2)}) copy-start(f32[8,256,256]{2,1,0:T(8,128)} %get-tuple-element.29) | copy-start | bytes 6291460
  87.0 3.7 %copy-start.10 = (bf16[8,248,256]{2,1,0:T(8,128)(2,1)S(1)}, bf16[8,248,256]{2,1,0:T(8,128)(2,1)}, u32[]{:S(2)}) copy-start(bf16[8,248,256]{2,1,0:T(8,128)(2,1)} %copy-done.9) | copy-start | bytes 3047428
  87.1 3.7 %copy-start.12 = (bf16[8,256,256]{2,1,0:T(8,128)(2,1)S(1)}, bf16[8,256,256]{2,1,0:T(8,128)(2,1)}, u32[]{:S(2)}) copy-start(bf16[8,256,256]{2,1,0:T(8,128)(2,1)} %copy-done.11) | copy-start | bytes 3145732
  93.2 1.6 %copy-start.18 = (f32[8,256,256]{2,1,0:T(8,128)S(1)}, f32[8,256,256]{2,1,0:T(8,128)}, u32[]{:S(2)}) copy-start(f32[8,256,256]{2,1,0:T(8,128)} %get-tuple-element.28) | copy-start | bytes 6291460
  93.5 1.7 %copy-start.8 = (bf16[8,256,256]{2,1,0:T(8,128)(2,1)S(1)}, bf16[8,256,256]{2,1,0:T(8,128)(2,1)}, u32[]{:S(2)}) copy-start(bf16[8,256,256]{2,1,0:T(8,128)(2,1)} %get-tuple-element.15) | copy-start | bytes 3145732
  93.5 2.0 %copy-start.17 = (bf16[2048,256]{1,0:T(8,128)(2,1)S(1)}, bf16[2048,256]{1,0:T(8,128)(2,1)}, u32[]{:S(2)}) copy-start(bf16[2048,256]{1,0:T(8,128)(2,1)} %copy-done.16) | copy-start | bytes 3145732
  98.6 0.9 copy-start.5
  99.5 2.4 %collective-permute-start = (f32[2,384,256]{2,1,0:T(8,128)S(1)}, f32[2,384,256]{2,1,0:T(8,128)S(1)}, u32[]{:S(2)}, u32[]{:S(2)}) collective-permute-start(f32[2,384,256]{2,1,0:T(8,128)S(1)} %fusion.53), channel_id=1, source_target_pairs={{0,1},{1,0},{2,3},{3,2},{4,5},{5,4},{6,7},{7,6},{8,9},{9,8},{10,11... | collective-permute-start | bytes 2359304 | tf_op jit(solution)/shard_map/ppermute | solution.py:159
  103.0 7.8 %collective-permute-start.1 = (f32[2,192,256]{2,1,0:T(8,128)S(1)}, f32[2,192,256]{2,1,0:T(8,128)S(1)}, u32[]{:S(2)}, u32[]{:S(2)}) collective-permute-start(f32[2,192,256]{2,1,0:T(8,128)S(1)} %constant_dynamic-slice_fusion.1), channel_id=1, source_target_pairs={{0,2},{1,5},{2,0},{3,7},{4,6},{5,1},{6,4},{7,3},{8,10},{9,13},{10,... | collective-permute-start | bytes 1179656 | tf_op jit(solution)/shard_map/ppermute | solution.py:159
  110.9 7.8 %collective-permute-start.2 = (f32[2,96,256]{2,1,0:T(8,128)S(1)}, f32[2,96,256]{2,1,0:T(8,128)S(1)}, u32[]{:S(2)}, u32[]{:S(2)}) collective-permute-start(f32[2,96,256]{2,1,0:T(8,128)S(1)} %constant_dynamic-slice_fusion), channel_id=1, source_target_pairs={{0,4},{1,9},{2,6},{3,11},{4,0},{5,13},{6,2},{7,15},{8,12},{9,1},{1... | collective-permute-start | bytes 589832 | tf_op jit(solution)/shard_map/ppermute | solution.py:159
  118.8 5.6 %collective-permute-start.3 = (f32[2,48,256]{2,1,0:T(8,128)S(1)}, f32[2,48,256]{2,1,0:T(8,128)S(1)}, u32[]{:S(2)}, u32[]{:S(2)}) collective-permute-start(f32[2,48,256]{2,1,0:T(8,128)S(1)} %constant_dynamic-slice_fusion.2), channel_id=1, source_target_pairs={{0,8},{1,3},{2,10},{3,1},{4,12},{5,7},{6,14},{7,5},{8,0},{9,11},{1... | collective-permute-start | bytes 294920 | tf_op jit(solution)/shard_map/ppermute | solution.py:159
  124.4 5.6 %collective-permute-start.4 = (bf16[2,48,256]{2,1,0:T(8,128)(2,1)S(1)}, bf16[2,48,256]{2,1,0:T(8,128)(2,1)S(1)}, u32[]{:S(2)}, u32[]{:S(2)}) collective-permute-start(bf16[2,48,256]{2,1,0:T(8,128)(2,1)S(1)} %add_convert_fusion.2), channel_id=1, source_target_pairs={{0,8},{1,3},{2,10},{3,1},{4,12},{5,7},{6,14},{7,5},{8,0},{9,11},{1... | collective-permute-start | bytes 147464 | tf_op jit(solution)/shard_map/ppermute | solution.py:163
  130.0 5.7 %collective-permute-start.5 = (bf16[2,96,256]{2,1,0:T(8,128)(2,1)S(1)}, bf16[2,96,256]{2,1,0:T(8,128)(2,1)S(1)}, u32[]{:S(2)}, u32[]{:S(2)}) collective-permute-start(bf16[2,96,256]{2,1,0:T(8,128)(2,1)S(1)} %pad_maximum_fusion.2), channel_id=1, source_target_pairs={{0,4},{1,9},{2,6},{3,11},{4,0},{5,13},{6,2},{7,15},{8,12},{9,1},{1... | collective-permute-start | bytes 294920 | tf_op jit(solution)/shard_map/ppermute | solution.py:163
  135.8 5.7 %collective-permute-start.6 = (bf16[2,192,256]{2,1,0:T(8,128)(2,1)S(1)}, bf16[2,192,256]{2,1,0:T(8,128)(2,1)S(1)}, u32[]{:S(2)}, u32[]{:S(2)}) collective-permute-start(bf16[2,192,256]{2,1,0:T(8,128)(2,1)S(1)} %pad_maximum_fusion.1), channel_id=1, source_target_pairs={{0,2},{1,5},{2,0},{3,7},{4,6},{5,1},{6,4},{7,3},{8,10},{9,13},{10,... | collective-permute-start | bytes 589832 | tf_op jit(solution)/shard_map/ppermute | solution.py:163
  141.6 1.8 %collective-permute-start.7 = (bf16[2,384,256]{2,1,0:T(8,128)(2,1)S(1)}, bf16[2,384,256]{2,1,0:T(8,128)(2,1)S(1)}, u32[]{:S(2)}, u32[]{:S(2)}) collective-permute-start(bf16[2,384,256]{2,1,0:T(8,128)(2,1)S(1)} %pad_maximum_fusion), channel_id=1, source_target_pairs={{0,1},{1,0},{2,3},{3,2},{4,5},{5,4},{6,7},{7,6},{8,9},{9,8},{10,11... | collective-permute-start | bytes 1179656 | tf_op jit(solution)/shard_map/ppermute | solution.py:163
  143.6 1.4 copy-start.7
  143.7 1.8 %copy-start.2 = (f32[2,196608]{1,0:T(2,128)S(1)}, f32[2,196608]{1,0:T(2,128)}, u32[]{:S(2)}) copy-start(f32[2,196608]{1,0:T(2,128)} %param.11) | copy-start | bytes 4718596
  143.7 2.2 %copy-start.4 = (f32[2,196608]{1,0:T(2,128)S(1)}, f32[2,196608]{1,0:T(2,128)}, u32[]{:S(2)}) copy-start(f32[2,196608]{1,0:T(2,128)} %param.9) | copy-start | bytes 4718596

commit v11 on v8

--- a/solution.py
+++ b/solution.py
@@ -188,11 +188,10 @@
     number = jnp.sum(counts).astype(jnp.float32)
     wide_count = lax.axis_size("wide")
     stats = jnp.concatenate([partial_sum, jnp.full((128,), number, jnp.float32)])
-    gathered = lax.all_to_all(
-        jnp.broadcast_to(stats[None, :], (wide_count, stats.shape[0])),
-        "wide", split_axis=0, concat_axis=0, tiled=True,
-    )
-    stats_all = jnp.sum(gathered, axis=0)
+    stats_all = stats
+    for step in range(wide_count.bit_length() - 1):
+        pairs = [(i, i ^ (1 << step)) for i in range(wide_count)]
+        stats_all = stats_all + lax.ppermute(stats_all, "wide", pairs)
     total_sum = stats_all[:feat_width]
     count_all = stats_all[feat_width]
     center = total_sum / count_all

time: 147 us -> 148 us (level)
  starting transfers between devices: 20.4 us -> 34.9 us
  waiting for transfers between devices: 70 us -> 57.2 us
    ppermute x0 -> x4, starting transfers between devices: none -> 9.4 us  [local(): stats_all = stats_all + lax.ppermute(stats_all, 'wide', pairs)]
    ppermute x4, starting transfers between devices: 0.64 us -> 8.75 us  [all_reduce_wide(): got = lax.ppermute(buf, 'wide', pairs)]
    all_to_all x1 -> x0, starting transfers between devices: 6.81 us -> none  [local(): lax.all_to_all(jnp.broadcast_to(stats[None, :], (wide_count, stats.shape[...]
    ppermute x4, waiting for transfers between devices: 17.4 us -> 10.6 us  [all_reduce_wide(): got = lax.ppermute(buf, 'wide', pairs)]
    all_to_all x1 -> x0, waiting for transfers between devices: 5.79 us -> none  [local(): lax.all_to_all(jnp.broadcast_to(stats[None, :], (wide_count, stats.shape[...]
    ppermute x4, waiting for transfers between devices: 22.6 us -> 17.6 us  [all_reduce_wide(): buf = keep + lax.ppermute(send, 'wide', pairs)]
    ppermute x0 -> x4, waiting for transfers between devices: none -> 4.79 us  [local(): stats_all = stats_all + lax.ppermute(stats_all, 'wide', pairs)]
    ppermute x4, starting transfers between devices: 1.06 us -> 4.85 us  [all_reduce_wide(): buf = keep + lax.ppermute(send, 'wide', pairs)]
  transfers between devices with their start and end apart: 11 -> 14, of which waited for: 11 -> 14; matrix products, arithmetic and copies ran while one was open for 4% -> 4% of each run, Pallas kernels for 0% -> 0%
where the time goes in v11:
time: 148 us; the launch traced here: 147 us
  waiting for transfers between devices  57.2 us (39%)
  starting transfers between devices  34.9 us (24%)
  matrix products  22.1 us (15%)
  other arithmetic  18.2 us (12%)
  local copies, waits for them, and re-layouts  12.9 us (9%)
  between operations  1.82 us (1%)
    all_to_all x1, waiting for transfers between devices, route_rows(): lax.all_to_all(send_rows.reshape(wide_count, capacity, feat_width), 'wide...  18.8 us
    ppermute x4, waiting for transfers between devices, all_reduce_wide(): buf = keep + lax.ppermute(send, 'wide', pairs)  17.6 us
    ppermute x4, waiting for transfers between devices, all_reduce_wide(): got = lax.ppermute(buf, 'wide', pairs)  10.6 us
    ppermute x4, starting transfers between devices, local(): stats_all = stats_all + lax.ppermute(stats_all, 'wide', pairs)  9.4 us
    ppermute x4, starting transfers between devices, all_reduce_wide(): got = lax.ppermute(buf, 'wide', pairs)  8.75 us
    dot_general x4, matrix products, run_network(): jnp.dot(stacked.reshape(-1, stacked.shape[2]), weights[layer_at], preferr...  8.32 us
    all_to_all x1, starting transfers between devices, route_rows(): lax.all_to_all(send_place.reshape(wide_count, capacity, per_dev), 'wide',...  7.36 us
    unnamed x39, local copies, waits for them, and re-layouts  6.55 us
  transfers between devices with their start and end apart: 14, of which 14 were waited for; matrix products, arithmetic and copies ran while one was open for 4% of the time, Pallas kernels for 0%

profile of v11, /device:TPU:0, one launch (start us, length us, event | category | flops | bytes accessed | tf_op | source)
XLA Modules:
  0.0 147.2 jit_solution(7020385488589369360)
XLA Ops:
  5.7 4.8 %fusion.19 = bf16[2048,264]{0,1:T(8,128)(2,1)S(1)} fusion(s32[2048]{0:T(1024)S(1)} %get-tuple-element.29, bf16[2048,8]{1,0:T(8,128)(2,1)S(1)} %copy.85, bf16[2048,256]{1,0:T(8,128)(2,1)} %param.6), kind=kOutput, calls=%fused_computation.29 | convolution fusion | flops 2221490176 | bytes 2170880 | tf_op jit(solution)/shard_map/dot_general | solution.py:102
  11.2 7.4 %all-to-all-start = ((bf16[16,128,8]{1,2,0:T(8,128)(2,1)}), bf16[16,128,8]{1,2,0:T(8,128)(2,1)S(1)}, u32[]{:S(2)}, u32[]{:S(2)}) async-start(bf16[16,128,8]{1,2,0:T(8,128)(2,1)} %slice_bitcast_fusion.10), calls=%async_computation | async-start | bytes 65536 | tf_op jit(solution)/shard_map/all_to_all | solution.py:115
  19.8 5.4 %all-to-all-done = bf16[16,128,8]{1,2,0:T(8,128)(2,1)S(1)} async-done(((bf16[16,128,8]{1,2,0:T(8,128)(2,1)}), bf16[16,128,8]{1,2,0:T(8,128)(2,1)S(1)}, u32[]{:S(2)}, u32[]{:S(2)}) %all-to-all-start) | async-done | bytes 32800 | tf_op jit(solution)/shard_map/all_to_all | solution.py:115
  25.2 4.5 %all-to-all-start.1 = ((bf16[16,128,256]{1,2,0:T(8,128)(2,1)}), bf16[16,128,256]{1,2,0:T(8,128)(2,1)}, u32[]{:S(2)}, u32[]{:S(2)}) async-start(bf16[16,128,256]{1,2,0:T(8,128)(2,1)} %copy_bitcast_fusion.2), calls=%async_computation.1 | async-start | bytes 2097152 | tf_op jit(solution)/shard_map/all_to_all | solution.py:108
  33.7 18.8 %all-to-all-done.1 = bf16[16,128,256]{1,2,0:T(8,128)(2,1)} async-done(((bf16[16,128,256]{1,2,0:T(8,128)(2,1)}), bf16[16,128,256]{1,2,0:T(8,128)(2,1)}, u32[]{:S(2)}, u32[]{:S(2)}) %all-to-all-start.1) | async-done | bytes 1048608 | tf_op jit(solution)/shard_map/all_to_all | solution.py:108
  52.5 1.5 %copy.89 = bf16[16,128,256]{2,1,0:T(8,128)(2,1)S(1)} copy(bf16[16,128,256]{1,2,0:T(8,128)(2,1)} %all-to-all-done.1) | data formatting | bytes 2097152 | tf_op jit(solution)/shard_map/all_to_all | solution.py:108
  54.0 3.2 %fusion.20 = bf16[2048,256]{1,0:T(8,128)(2,1)S(1)} fusion(bf16[2048,256]{1,0:T(8,128)(2,1)S(1)} %bitcast.143, s32[2048]{0:T(1024)S(1)} %select_bitcast_fusion), kind=kOutput, calls=%fused_computation.30 | convolution fusion | flops 2152202240 | bytes 2105344 | tf_op jit(solution)/shard_map/dot_general | solution.py:134
  57.2 1.5 %fusion.22 = bf16[8,256,256]{2,1,0:T(8,128)(2,1)S(1)} fusion(bf16[8,256,256]{2,1,0:T(8,128)(2,1)S(1)} %bitcast.152, bf16[2,768,256]{2,1,0:T(8,128)(2,1)S(1)} %bitcast.147, bf16[8,254,256]{2,1,0:T(8,128)(2,1)S(1)} %bitcast.153, bf16[8,255,256]{2,1,0:T(8,128)(2,1)S(1)} %bitcast.154), kind=kOutput, calls=%fused_computation.32 | convolution fusion | flops 827850752 | bytes 5636096 | tf_op jit(solution)/shard_map/dot_general | solution.py:49
  58.8 2.5 %fusion.21 = (bf16[8,256,256]{2,1,0:T(8,128)(2,1)S(1)}, f32[8,256,256]{2,1,0:T(8,128)}) fusion(bf16[8,256,256]{2,1,0:T(8,128)(2,1)S(1)} %bitcast.155, bf16[2,768,256]{2,1,0:T(8,128)(2,1)S(1)} %bitcast.139, bf16[8,254,256]{2,1,0:T(8,128)(2,1)S(1)} %bitcast.156, bf16[8,255,256]{2,1,0:T(8,128)(2,1)S(1)} %bitcast.157), kind=kOutput, calls=%fused_computation.31 | convolution fusion | flops 827850752 | bytes 7733248 | tf_op jit(solution)/shard_map/dot_general | solution.py:49
  61.4 2.5 %fusion.96 = (bf16[8,256]{1,0:T(8,128)(2,1)S(1)}, bf16[8,256,256]{2,1,0:T(8,128)(2,1)S(1)}, f32[8,256,256]{2,1,0:T(8,128)}) fusion(bf16[8,256,256]{2,1,0:T(8,128)(2,1)S(1)} %get-tuple-element.30, bf16[2,768,256]{2,1,0:T(8,128)(2,1)S(1)} %bitcast.140, bf16[8,248,256]{2,1,0:T(8,128)(2,1)S(1)} %slice.97, bf16[8,252,256]{2,1,0:T(8,128)(2,1)S(1)} %bitcast.144), kind=kOutput, calls=%fused_computation.172 | convolution fusion | flops 828372992 | bytes 7704576 | tf_op jit(solution)/shard_map/dot_general | solution.py:49
  63.9 1.8 %fusion.29 = (f32[8,256]{1,0:T(8,128)S(1)}, f32[8,256]{1,0:T(8,128)S(1)}, f32[256]{0:T(256)S(1)}, bf16[8,256,256]{2,1,0:T(8,128)(2,1)S(1)}) fusion(bf16[8,256,256]{2,1,0:T(8,128)(2,1)S(1)} %get-tuple-element.15, f32[8,256]{1,0:T(8,128)S(1)} %fusion.78, f32[8,256]{1,0:T(8,128)S(1)} %bitcast.149, bf16[2,768,256]{2,1,0:T(8,128)(2,1)S(1)} %bitcast.148, ...), kind=kOutput, calls=%fused_computation.39 | convolution fusion | flops 832040704 | bytes 6685696 | tf_op jit(solution)/shard_map/dot_general | solution.py:49
  67.2 2.0 %collective-permute-start.1 = (f32[384]{0:T(512)S(1)}, f32[384]{0:T(512)S(1)}, u32[]{:S(2)}, u32[]{:S(2)}) collective-permute-start(f32[384]{0:T(512)S(1)} %pad_add_fusion), channel_id=1, source_target_pairs={{0,2},{1,3},{2,0},{3,1},{4,6},{5,7},{6,4},{7,5},{8,10},{9,11},{10,... | collective-permute-start | bytes 4616 | tf_op jit(solution)/shard_map/ppermute | solution.py:194
  69.2 1.6 %collective-permute-done.1 = f32[384]{0:T(512)S(1)} collective-permute-done((f32[384]{0:T(512)S(1)}, f32[384]{0:T(512)S(1)}, u32[]{:S(2)}, u32[]{:S(2)}) %collective-permute-start.1) | collective-permute-done | bytes 1568 | tf_op jit(solution)/shard_map/ppermute | solution.py:194
  70.8 3.4 %collective-permute-start.2 = (f32[384]{0:T(512)S(1)}, f32[384]{0:T(512)S(1)}, u32[]{:S(2)}, u32[]{:S(2)}) collective-permute-start(f32[384]{0:T(512)S(1)} %add.180), channel_id=1, source_target_pairs={{0,4},{1,5},{2,6},{3,7},{4,0},{5,1},{6,2},{7,3},{8,12},{9,13},{10,... | collective-permute-start | bytes 4616 | tf_op jit(solution)/shard_map/ppermute | solution.py:194
  74.2 1.6 %collective-permute-done.2 = f32[384]{0:T(512)S(1)} collective-permute-done((f32[384]{0:T(512)S(1)}, f32[384]{0:T(512)S(1)}, u32[]{:S(2)}, u32[]{:S(2)}) %collective-permute-start.2) | collective-permute-done | bytes 1568 | tf_op jit(solution)/shard_map/ppermute | solution.py:194
  75.7 3.4 %collective-permute-start.3 = (f32[384]{0:T(512)S(1)}, f32[384]{0:T(512)S(1)}, u32[]{:S(2)}, u32[]{:S(2)}) collective-permute-start(f32[384]{0:T(512)S(1)} %add.181), channel_id=1, source_target_pairs={{0,8},{1,9},{2,10},{3,11},{4,12},{5,13},{6,14},{7,15},{8,0},{9,1},... | collective-permute-start | bytes 4616 | tf_op jit(solution)/shard_map/ppermute | solution.py:194
  83.1 3.9 %multiply_convert_fusion = bf16[8,256,256]{2,1,0:T(8,128)(2,1)S(1)} fusion(f32[8,256,256]{2,1,0:T(8,128)S(1)} %copy-done.4, f32[8,256]{1,0:T(8,128)S(1)} %fusion.36, f32[8,256]{1,0:T(8,128)S(1)} %fusion.33, f32[256]{0:T(256)S(1)} %slice_divide_fusion, bf16[8,256,256]{2,1,0:T(8,128)(2,1)S(1)} %get-tuple-element.33, f32[8,256]{1,0:T(8,128)S(1)} %get-tuple-element.5, ...), kind=kLoop, calls=%fused_computation.55 | loop fusion | flops 10485760 | bytes 5284864 | tf_op jit(solution)/shard_map/convert_element_type | solution.py:205
  91.7 3.2 %convolution_bitcast_fusion.1 = f32[1,768,256]{2,1,0:T(8,128)S(1)} fusion(f32[8,256,3,256]{3,1,0,2:T(8,128)S(1)} %fusion.46, f32[8,256,256]{2,1,0:T(8,128)S(1)} %copy-done.17, f32[8,248,256]{2,1,0:T(8,128)S(1)} %slice.107, f32[8,252,256]{2,1,0:T(8,128)S(1)} %slice.105, bf16[8,256,256]{2,1,0:T(8,128)(2,1)S(1)} %copy-done.9, ...), kind=kOutput, calls=%fused_computation.75 | convolution fusion | flops 836239360 | bytes 14394368 | tf_op jit(solution)/shard_map/dot_general | solution.py:207
  96.0 2.4 %collective-permute-done.4 = f32[2,384,256]{2,1,0:T(8,128)} collective-permute-done((f32[2,384,256]{2,1,0:T(8,128)S(1)}, f32[2,384,256]{2,1,0:T(8,128)}, u32[]{:S(2)}, u32[]{:S(2)}) %collective-permute-start.4) | collective-permute-done | bytes 786464 | tf_op jit(solution)/shard_map/ppermute | solution.py:164
  98.3 1.3 fusion.53
  100.8 6.8 %collective-permute-done.5 = f32[2,192,256]{2,1,0:T(8,128)S(1)} collective-permute-done((f32[2,192,256]{2,1,0:T(8,128)S(1)}, f32[2,192,256]{2,1,0:T(8,128)S(1)}, u32[]{:S(2)}, u32[]{:S(2)}) %collective-permute-start.5) | collective-permute-done | bytes 393248 | tf_op jit(solution)/shard_map/ppermute | solution.py:164
  107.6 1.6 %collective-permute-start.6 = (f32[2,96,256]{2,1,0:T(8,128)S(1)}, f32[2,96,256]{2,1,0:T(8,128)S(1)}, u32[]{:S(2)}, u32[]{:S(2)}) collective-permute-start(f32[2,96,256]{2,1,0:T(8,128)S(1)} %constant_dynamic-slice_fusion), channel_id=1, source_target_pairs={{0,4},{1,9},{2,6},{3,11},{4,0},{5,13},{6,2},{7,15},{8,12},{9,1},{1... | collective-permute-start | bytes 589832 | tf_op jit(solution)/shard_map/ppermute | solution.py:164
  109.2 5.0 %collective-permute-done.6 = f32[2,96,256]{2,1,0:T(8,128)S(1)} collective-permute-done((f32[2,96,256]{2,1,0:T(8,128)S(1)}, f32[2,96,256]{2,1,0:T(8,128)S(1)}, u32[]{:S(2)}, u32[]{:S(2)}) %collective-permute-start.6) | collective-permute-done | bytes 196640 | tf_op jit(solution)/shard_map/ppermute | solution.py:164
  114.3 2.1 %collective-permute-start.7 = (f32[2,48,256]{2,1,0:T(8,128)S(1)}, f32[2,48,256]{2,1,0:T(8,128)S(1)}, u32[]{:S(2)}, u32[]{:S(2)}) collective-permute-start(f32[2,48,256]{2,1,0:T(8,128)S(1)} %constant_dynamic-slice_fusion.2), channel_id=1, source_target_pairs={{0,8},{1,3},{2,10},{3,1},{4,12},{5,7},{6,14},{7,5},{8,0},{9,11},{1... | collective-permute-start | bytes 294920 | tf_op jit(solution)/shard_map/ppermute | solution.py:164
  116.4 3.5 %collective-permute-done.7 = f32[2,48,256]{2,1,0:T(8,128)S(1)} collective-permute-done((f32[2,48,256]{2,1,0:T(8,128)S(1)}, f32[2,48,256]{2,1,0:T(8,128)S(1)}, u32[]{:S(2)}, u32[]{:S(2)}) %collective-permute-start.7) | collective-permute-done | bytes 98336 | tf_op jit(solution)/shard_map/ppermute | solution.py:164
  119.9 2.2 %collective-permute-start.8 = (bf16[2,48,256]{2,1,0:T(8,128)(2,1)S(1)}, bf16[2,48,256]{2,1,0:T(8,128)(2,1)S(1)}, u32[]{:S(2)}, u32[]{:S(2)}) collective-permute-start(bf16[2,48,256]{2,1,0:T(8,128)(2,1)S(1)} %add_convert_fusion.2), channel_id=1, source_target_pairs={{0,8},{1,3},{2,10},{3,1},{4,12},{5,7},{6,14},{7,5},{8,0},{9,11},{1... | collective-permute-start | bytes 147464 | tf_op jit(solution)/shard_map/ppermute | solution.py:168
  122.1 2.8 %collective-permute-done.8 = bf16[2,48,256]{2,1,0:T(8,128)(2,1)S(1)} collective-permute-done((bf16[2,48,256]{2,1,0:T(8,128)(2,1)S(1)}, bf16[2,48,256]{2,1,0:T(8,128)(2,1)S(1)}, u32[]{:S(2)}, u32[]{:S(2)}) %collective-permute-start.8) | collective-permute-done | bytes 49184 | tf_op jit(solution)/shard_map/ppermute | solution.py:168
  125.0 2.7 %collective-permute-start.9 = (bf16[2,96,256]{2,1,0:T(8,128)(2,1)S(1)}, bf16[2,96,256]{2,1,0:T(8,128)(2,1)S(1)}, u32[]{:S(2)}, u32[]{:S(2)}) collective-permute-start(bf16[2,96,256]{2,1,0:T(8,128)(2,1)S(1)} %pad_maximum_fusion.2), channel_id=1, source_target_pairs={{0,4},{1,9},{2,6},{3,11},{4,0},{5,13},{6,2},{7,15},{8,12},{9,1},{1... | collective-permute-start | bytes 294920 | tf_op jit(solution)/shard_map/ppermute | solution.py:168
  127.6 3.1 %collective-permute-done.9 = bf16[2,96,256]{2,1,0:T(8,128)(2,1)S(1)} collective-permute-done((bf16[2,96,256]{2,1,0:T(8,128)(2,1)S(1)}, bf16[2,96,256]{2,1,0:T(8,128)(2,1)S(1)}, u32[]{:S(2)}, u32[]{:S(2)}) %collective-permute-start.9) | collective-permute-done | bytes 98336 | tf_op jit(solution)/shard_map/ppermute | solution.py:168
  130.9 3.8 %collective-permute-start.10 = (bf16[2,192,256]{2,1,0:T(8,128)(2,1)S(1)}, bf16[2,192,256]{2,1,0:T(8,128)(2,1)S(1)}, u32[]{:S(2)}, u32[]{:S(2)}) collective-permute-start(bf16[2,192,256]{2,1,0:T(8,128)(2,1)S(1)} %pad_maximum_fusion.1), channel_id=1, source_target_pairs={{0,2},{1,5},{2,0},{3,7},{4,6},{5,1},{6,4},{7,3},{8,10},{9,13},{10,... | collective-permute-start | bytes 589832 | tf_op jit(solution)/shard_map/ppermute | solution.py:168
  134.6 3.6 %collective-permute-done.10 = bf16[2,192,256]{2,1,0:T(8,128)(2,1)S(1)} collective-permute-done((bf16[2,192,256]{2,1,0:T(8,128)(2,1)S(1)}, bf16[2,192,256]{2,1,0:T(8,128)(2,1)S(1)}, u32[]{:S(2)}, u32[]{:S(2)}) %collective-permute-start.10) | collective-permute-done | bytes 196640 | tf_op jit(solution)/shard_map/ppermute | solution.py:168
  142.4 4.8 %multiply_add_fusion = (f32[2,196608]{1,0:T(2,128)}, f32[2,196608]{1,0:T(2,128)}, f32[2,196608]{1,0:T(2,128)}) fusion(f32[2,196608]{1,0:T(2,128)S(1)} %copy-done, f32[2,196608]{1,0:T(2,128)S(1)} %copy-done.2, f32[2,196608]{1,0:T(2,128)S(1)} %bitcast.138, f32[2,196608]{1,0:T(2,128)S(1)} %copy-done.6), kind=kLoop, calls=%fused_computation.71 | loop fusion | flops 2752512 | bytes 11010048 | tf_op jit(solution)/shard_map/add | solution.py:228
  (105 shorter events, 26.6 us)
Async XLA Ops:
  11.2 14.0 %all-to-all-start = ((bf16[16,128,8]{1,2,0:T(8,128)(2,1)}), bf16[16,128,8]{1,2,0:T(8,128)(2,1)S(1)}, u32[]{:S(2)}, u32[]{:S(2)}) async-start(bf16[16,128,8]{1,2,0:T(8,128)(2,1)} %slice_bitcast_fusion.10), calls=%async_computation | async-start | bytes 65536 | tf_op jit(solution)/shard_map/all_to_all | solution.py:115
  18.5 11.2 %copy-start = (f32[2,196608]{1,0:T(2,128)S(1)}, f32[2,196608]{1,0:T(2,128)}, u32[]{:S(2)}) copy-start(f32[2,196608]{1,0:T(2,128)} %param.11) | copy-start | bytes 4718596
  19.8 10.9 %copy-start.1 = (f32[2,196608]{1,0:T(2,128)S(1)}, f32[2,196608]{1,0:T(2,128)}, u32[]{:S(2)}) copy-start(f32[2,196608]{1,0:T(2,128)} %param.9) | copy-start | bytes 4718596
  25.2 27.3 %all-to-all-start.1 = ((bf16[16,128,256]{1,2,0:T(8,128)(2,1)}), bf16[16,128,256]{1,2,0:T(8,128)(2,1)}, u32[]{:S(2)}, u32[]{:S(2)}) async-start(bf16[16,128,256]{1,2,0:T(8,128)(2,1)} %copy_bitcast_fusion.2), calls=%async_computation.1 | async-start | bytes 2097152 | tf_op jit(solution)/shard_map/all_to_all | solution.py:108
  53.9 3.2 %copy-start.14 = (bf16[1,2,768,256]{3,2,1,0:T(8,128)(2,1)S(1)}, bf16[1,2,768,256]{3,2,1,0:T(8,128)(2,1)}, u32[]{:S(2)}) copy-start(bf16[1,2,768,256]{3,2,1,0:T(8,128)(2,1)} %copy.120) | copy-start | bytes 2359300
  57.1 1.6 %copy-start.15 = (bf16[2048,256]{1,0:T(8,128)(2,1)}, bf16[2048,256]{1,0:T(8,128)(2,1)S(1)}, u32[]{:S(2)}) copy-start(bf16[2048,256]{1,0:T(8,128)(2,1)S(1)} %fusion.20) | copy-start | bytes 3145732
  57.2 1.6 %copy-start.5 = (bf16[1,2,768,256]{3,2,1,0:T(8,128)(2,1)S(1)}, bf16[1,2,768,256]{3,2,1,0:T(8,128)(2,1)}, u32[]{:S(2)}) copy-start(bf16[1,2,768,256]{3,2,1,0:T(8,128)(2,1)} %copy.121) | copy-start | bytes 2359300
  61.3 2.6 %copy-start.12 = (bf16[8,256,256]{2,1,0:T(8,128)(2,1)}, bf16[8,256,256]{2,1,0:T(8,128)(2,1)S(1)}, u32[]{:S(2)}) copy-start(bf16[8,256,256]{2,1,0:T(8,128)(2,1)S(1)} %get-tuple-element.30) | copy-start | bytes 3145732
  61.3 2.5 %copy-start.10 = (bf16[8,248,256]{2,1,0:T(8,128)(2,1)}, bf16[8,248,256]{2,1,0:T(8,128)(2,1)S(1)}, u32[]{:S(2)}) copy-start(bf16[8,248,256]{2,1,0:T(8,128)(2,1)S(1)} %slice.97) | copy-start | bytes 3047428
  63.8 1.9 %copy-start.8 = (bf16[8,256,256]{2,1,0:T(8,128)(2,1)}, bf16[8,256,256]{2,1,0:T(8,128)(2,1)S(1)}, u32[]{:S(2)}) copy-start(bf16[8,256,256]{2,1,0:T(8,128)(2,1)S(1)} %get-tuple-element.15) | copy-start | bytes 3145732
  65.7 1.5 collective-permute-start
  67.2 3.6 %collective-permute-start.1 = (f32[384]{0:T(512)S(1)}, f32[384]{0:T(512)S(1)}, u32[]{:S(2)}, u32[]{:S(2)}) collective-permute-start(f32[384]{0:T(512)S(1)} %pad_add_fusion), channel_id=1, source_target_pairs={{0,2},{1,3},{2,0},{3,1},{4,6},{5,7},{6,4},{7,5},{8,10},{9,11},{10,... | collective-permute-start | bytes 4616 | tf_op jit(solution)/shard_map/ppermute | solution.py:194
  70.8 4.9 %collective-permute-start.2 = (f32[384]{0:T(512)S(1)}, f32[384]{0:T(512)S(1)}, u32[]{:S(2)}, u32[]{:S(2)}) collective-permute-start(f32[384]{0:T(512)S(1)} %add.180), channel_id=1, source_target_pairs={{0,4},{1,5},{2,6},{3,7},{4,0},{5,1},{6,2},{7,3},{8,12},{9,13},{10,... | collective-permute-start | bytes 4616 | tf_op jit(solution)/shard_map/ppermute | solution.py:194
  75.7 5.0 %collective-permute-start.3 = (f32[384]{0:T(512)S(1)}, f32[384]{0:T(512)S(1)}, u32[]{:S(2)}, u32[]{:S(2)}) collective-permute-start(f32[384]{0:T(512)S(1)} %add.181), channel_id=1, source_target_pairs={{0,8},{1,9},{2,10},{3,11},{4,12},{5,13},{6,14},{7,15},{8,0},{9,1},... | collective-permute-start | bytes 4616 | tf_op jit(solution)/shard_map/ppermute | solution.py:194
  80.0 3.1 %copy-start.4 = (f32[8,256,256]{2,1,0:T(8,128)S(1)}, f32[8,256,256]{2,1,0:T(8,128)}, u32[]{:S(2)}) copy-start(f32[8,256,256]{2,1,0:T(8,128)} %get-tuple-element.32) | copy-start | bytes 6291460
  83.1 3.9 %copy-start.11 = (bf16[8,248,256]{2,1,0:T(8,128)(2,1)S(1)}, bf16[8,248,256]{2,1,0:T(8,128)(2,1)}, u32[]{:S(2)}) copy-start(bf16[8,248,256]{2,1,0:T(8,128)(2,1)} %copy-done.10) | copy-start | bytes 3047428
  83.1 3.9 %copy-start.13 = (bf16[8,256,256]{2,1,0:T(8,128)(2,1)S(1)}, bf16[8,256,256]{2,1,0:T(8,128)(2,1)}, u32[]{:S(2)}) copy-start(bf16[8,256,256]{2,1,0:T(8,128)(2,1)} %copy-done.12) | copy-start | bytes 3145732
  87.0 1.0 copy-start.7
  89.5 1.6 %copy-start.17 = (f32[8,256,256]{2,1,0:T(8,128)S(1)}, f32[8,256,256]{2,1,0:T(8,128)}, u32[]{:S(2)}) copy-start(f32[8,256,256]{2,1,0:T(8,128)} %get-tuple-element.31) | copy-start | bytes 6291460
  89.7 1.7 %copy-start.9 = (bf16[8,256,256]{2,1,0:T(8,128)(2,1)S(1)}, bf16[8,256,256]{2,1,0:T(8,128)(2,1)}, u32[]{:S(2)}) copy-start(bf16[8,256,256]{2,1,0:T(8,128)(2,1)} %copy-done.8) | copy-start | bytes 3145732
  89.7 2.0 %copy-start.16 = (bf16[2048,256]{1,0:T(8,128)(2,1)S(1)}, bf16[2048,256]{1,0:T(8,128)(2,1)}, u32[]{:S(2)}) copy-start(bf16[2048,256]{1,0:T(8,128)(2,1)} %copy-done.15) | copy-start | bytes 3145732
  94.9 0.9 copy-start.3
  95.9 2.5 %collective-permute-start.4 = (f32[2,384,256]{2,1,0:T(8,128)S(1)}, f32[2,384,256]{2,1,0:T(8,128)}, u32[]{:S(2)}, u32[]{:S(2)}) collective-permute-start(f32[2,384,256]{2,1,0:T(8,128)S(1)} %fusion.51), channel_id=1, source_target_pairs={{0,1},{1,0},{2,3},{3,2},{4,5},{5,4},{6,7},{7,6},{8,9},{9,8},{10,11... | collective-permute-start | bytes 2359304 | tf_op jit(solution)/shard_map/ppermute | solution.py:164
  99.7 7.8 %collective-permute-start.5 = (f32[2,192,256]{2,1,0:T(8,128)S(1)}, f32[2,192,256]{2,1,0:T(8,128)S(1)}, u32[]{:S(2)}, u32[]{:S(2)}) collective-permute-start(f32[2,192,256]{2,1,0:T(8,128)S(1)} %constant_dynamic-slice_fusion.1), channel_id=1, source_target_pairs={{0,2},{1,5},{2,0},{3,7},{4,6},{5,1},{6,4},{7,3},{8,10},{9,13},{10,... | collective-permute-start | bytes 1179656 | tf_op jit(solution)/shard_map/ppermute | solution.py:164
  107.6 6.6 %collective-permute-start.6 = (f32[2,96,256]{2,1,0:T(8,128)S(1)}, f32[2,96,256]{2,1,0:T(8,128)S(1)}, u32[]{:S(2)}, u32[]{:S(2)}) collective-permute-start(f32[2,96,256]{2,1,0:T(8,128)S(1)} %constant_dynamic-slice_fusion), channel_id=1, source_target_pairs={{0,4},{1,9},{2,6},{3,11},{4,0},{5,13},{6,2},{7,15},{8,12},{9,1},{1... | collective-permute-start | bytes 589832 | tf_op jit(solution)/shard_map/ppermute | solution.py:164
  114.3 5.6 %collective-permute-start.7 = (f32[2,48,256]{2,1,0:T(8,128)S(1)}, f32[2,48,256]{2,1,0:T(8,128)S(1)}, u32[]{:S(2)}, u32[]{:S(2)}) collective-permute-start(f32[2,48,256]{2,1,0:T(8,128)S(1)} %constant_dynamic-slice_fusion.2), channel_id=1, source_target_pairs={{0,8},{1,3},{2,10},{3,1},{4,12},{5,7},{6,14},{7,5},{8,0},{9,11},{1... | collective-permute-start | bytes 294920 | tf_op jit(solution)/shard_map/ppermute | solution.py:164
  119.9 5.1 %collective-permute-start.8 = (bf16[2,48,256]{2,1,0:T(8,128)(2,1)S(1)}, bf16[2,48,256]{2,1,0:T(8,128)(2,1)S(1)}, u32[]{:S(2)}, u32[]{:S(2)}) collective-permute-start(bf16[2,48,256]{2,1,0:T(8,128)(2,1)S(1)} %add_convert_fusion.2), channel_id=1, source_target_pairs={{0,8},{1,3},{2,10},{3,1},{4,12},{5,7},{6,14},{7,5},{8,0},{9,11},{1... | collective-permute-start | bytes 147464 | tf_op jit(solution)/shard_map/ppermute | solution.py:168
  125.0 5.8 %collective-permute-start.9 = (bf16[2,96,256]{2,1,0:T(8,128)(2,1)S(1)}, bf16[2,96,256]{2,1,0:T(8,128)(2,1)S(1)}, u32[]{:S(2)}, u32[]{:S(2)}) collective-permute-start(bf16[2,96,256]{2,1,0:T(8,128)(2,1)S(1)} %pad_maximum_fusion.2), channel_id=1, source_target_pairs={{0,4},{1,9},{2,6},{3,11},{4,0},{5,13},{6,2},{7,15},{8,12},{9,1},{1... | collective-permute-start | bytes 294920 | tf_op jit(solution)/shard_map/ppermute | solution.py:168
  130.9 7.4 %collective-permute-start.10 = (bf16[2,192,256]{2,1,0:T(8,128)(2,1)S(1)}, bf16[2,192,256]{2,1,0:T(8,128)(2,1)S(1)}, u32[]{:S(2)}, u32[]{:S(2)}) collective-permute-start(bf16[2,192,256]{2,1,0:T(8,128)(2,1)S(1)} %pad_maximum_fusion.1), channel_id=1, source_target_pairs={{0,2},{1,5},{2,0},{3,7},{4,6},{5,1},{6,4},{7,3},{8,10},{9,13},{10,... | collective-permute-start | bytes 589832 | tf_op jit(solution)/shard_map/ppermute | solution.py:168
  138.4 1.8 %collective-permute-start.11 = (bf16[2,384,256]{2,1,0:T(8,128)(2,1)S(1)}, bf16[2,384,256]{2,1,0:T(8,128)(2,1)S(1)}, u32[]{:S(2)}, u32[]{:S(2)}) collective-permute-start(bf16[2,384,256]{2,1,0:T(8,128)(2,1)S(1)} %pad_maximum_fusion), channel_id=1, source_target_pairs={{0,1},{1,0},{2,3},{3,2},{4,5},{5,4},{6,7},{7,6},{8,9},{9,8},{10,11... | collective-permute-start | bytes 1179656 | tf_op jit(solution)/shard_map/ppermute | solution.py:168
  140.5 1.4 copy-start.2
  140.5 1.9 %copy-start.6 = (f32[2,196608]{1,0:T(2,128)S(1)}, f32[2,196608]{1,0:T(2,128)}, u32[]{:S(2)}) copy-start(f32[2,196608]{1,0:T(2,128)} %param.10) | copy-start | bytes 4718596

commit v12 on v8

--- a/solution.py
+++ b/solution.py
@@ -162,14 +162,14 @@
         keep = lax.dynamic_slice_in_dim(buf, bit * half, half, axis=1)
         send = lax.dynamic_slice_in_dim(buf, (1 - bit) * half, half, axis=1)
         buf = keep + lax.ppermute(send, "wide", pairs)
-    buf = buf.astype(jnp.bfloat16)
+    buf = buf.astype(jnp.bfloat16).reshape(buf.shape[0], -1)
     for step in reversed(range(steps)):
         pairs, bit = exchange_at(step)
         got = lax.ppermute(buf, "wide", pairs)
         low = jnp.where(bit == 0, buf, got)
         high = jnp.where(bit == 0, got, buf)
         buf = jnp.concatenate([low, high], axis=1)
-    return buf.reshape(buf.shape[0], -1).astype(jnp.float32)
+    return buf.astype(jnp.float32)
 
 
 def local(epoch_rows, row_object, object_slot, master, momentum, teacher):

time: 147 us -> 155 us (1.054)
  other arithmetic: 18.1 us -> 27.7 us
    add x1, other arithmetic: 4.81 us -> 10.1 us  [local(): new_teacher = ema_rate * teacher + (1.0 - ema_rate) * new_master]
    select_n x4, other arithmetic: 0.27 us -> 3.37 us  [all_reduce_wide(): low = jnp.where(bit == 0, buf, got)]
    unnamed x39 -> x43, local copies, waits for them, and re-layouts: 6.55 us -> 5.36 us
where the time goes in v12:
time: 155 us
  waiting for transfers between devices  70.3 us (45%)
  other arithmetic  27.7 us (18%)
  matrix products  22.1 us (14%)
  starting transfers between devices  20.5 us (13%)
  local copies, waits for them, and re-layouts  12.3 us (8%)
  between operations  1.85 us (1%)
    ppermute x4, waiting for transfers between devices, all_reduce_wide(): buf = keep + lax.ppermute(send, 'wide', pairs)  22.6 us
    all_to_all x1, waiting for transfers between devices, route_rows(): lax.all_to_all(send_rows.reshape(wide_count, capacity, feat_width), 'wide...  18.8 us
    ppermute x4, waiting for transfers between devices, all_reduce_wide(): got = lax.ppermute(buf, 'wide', pairs)  17.7 us
    add x1, other arithmetic, local(): new_teacher = ema_rate * teacher + (1.0 - ema_rate) * new_master  10.1 us
    dot_general x4, matrix products, run_network(): jnp.dot(stacked.reshape(-1, stacked.shape[2]), weights[layer_at], preferr...  8.32 us
    all_to_all x1, starting transfers between devices, route_rows(): lax.all_to_all(send_place.reshape(wide_count, capacity, per_dev), 'wide',...  7.36 us
    all_to_all x1, starting transfers between devices, local(): lax.all_to_all(jnp.broadcast_to(stats[None, :], (wide_count, stats.shape[...  6.82 us
    all_to_all x1, waiting for transfers between devices, local(): lax.all_to_all(jnp.broadcast_to(stats[None, :], (wide_count, stats.shape[...  5.79 us
  transfers between devices with their start and end apart: 11, of which 11 were waited for; matrix products, arithmetic and copies ran while one was open for 4% of the time, Pallas kernels for 0%

profile of v12, /device:TPU:0, one launch (start us, length us, event | category | flops | bytes accessed | tf_op | source)
XLA Modules:
  0.0 154.6 jit_solution(11596192016225456914)
XLA Ops:
  2.7 1.3 select_reduce_fusion
  5.7 4.8 %fusion.19 = bf16[2048,264]{0,1:T(8,128)(2,1)S(1)} fusion(s32[2048]{0:T(1024)S(1)} %get-tuple-element.29, bf16[2048,8]{1,0:T(8,128)(2,1)S(1)} %copy.102, bf16[2048,256]{1,0:T(8,128)(2,1)} %param.6), kind=kOutput, calls=%fused_computation.29 | convolution fusion | flops 2221490176 | bytes 2170880 | tf_op jit(solution)/shard_map/dot_general | solution.py:102
  11.2 7.4 %all-to-all-start = ((bf16[16,128,8]{1,2,0:T(8,128)(2,1)}), bf16[16,128,8]{1,2,0:T(8,128)(2,1)S(1)}, u32[]{:S(2)}, u32[]{:S(2)}) async-start(bf16[16,128,8]{1,2,0:T(8,128)(2,1)} %slice_bitcast_fusion.10), calls=%async_computation | async-start | bytes 65536 | tf_op jit(solution)/shard_map/all_to_all | solution.py:115
  18.5 1.2 copy_bitcast_fusion.2
  19.8 5.4 %all-to-all-done = bf16[16,128,8]{1,2,0:T(8,128)(2,1)S(1)} async-done(((bf16[16,128,8]{1,2,0:T(8,128)(2,1)}), bf16[16,128,8]{1,2,0:T(8,128)(2,1)S(1)}, u32[]{:S(2)}, u32[]{:S(2)}) %all-to-all-start) | async-done | bytes 32800 | tf_op jit(solution)/shard_map/all_to_all | solution.py:115
  25.2 4.5 %all-to-all-start.1 = ((bf16[16,128,256]{1,2,0:T(8,128)(2,1)}), bf16[16,128,256]{1,2,0:T(8,128)(2,1)}, u32[]{:S(2)}, u32[]{:S(2)}) async-start(bf16[16,128,256]{1,2,0:T(8,128)(2,1)} %copy_bitcast_fusion.2), calls=%async_computation.1 | async-start | bytes 2097152 | tf_op jit(solution)/shard_map/all_to_all | solution.py:108
  33.6 18.8 %all-to-all-done.1 = bf16[16,128,256]{1,2,0:T(8,128)(2,1)} async-done(((bf16[16,128,256]{1,2,0:T(8,128)(2,1)}), bf16[16,128,256]{1,2,0:T(8,128)(2,1)}, u32[]{:S(2)}, u32[]{:S(2)}) %all-to-all-start.1) | async-done | bytes 1048608 | tf_op jit(solution)/shard_map/all_to_all | solution.py:108
  52.4 1.5 copy.106
  53.9 3.2 %fusion.20 = bf16[2048,256]{1,0:T(8,128)(2,1)S(1)} fusion(bf16[2048,256]{1,0:T(8,128)(2,1)S(1)} %bitcast.142, s32[2048]{0:T(1024)S(1)} %select_bitcast_fusion), kind=kOutput, calls=%fused_computation.30 | convolution fusion | flops 2152202240 | bytes 2105344 | tf_op jit(solution)/shard_map/dot_general | solution.py:134
  57.2 1.5 fusion.22
  58.8 2.5 %fusion.21 = (bf16[8,256,256]{2,1,0:T(8,128)(2,1)S(1)}, f32[8,256,256]{2,1,0:T(8,128)}) fusion(bf16[8,256,256]{2,1,0:T(8,128)(2,1)S(1)} %bitcast.156, bf16[2,768,256]{2,1,0:T(8,128)(2,1)S(1)} %bitcast.138, bf16[8,254,256]{2,1,0:T(8,128)(2,1)S(1)} %bitcast.157, bf16[8,255,256]{2,1,0:T(8,128)(2,1)S(1)} %bitcast.158), kind=kOutput, calls=%fused_computation.31 | convolution fusion | flops 827850752 | bytes 7733248 | tf_op jit(solution)/shard_map/dot_general | solution.py:49
  61.4 2.5 %fusion.97 = (bf16[8,256]{1,0:T(8,128)(2,1)S(1)}, bf16[8,256,256]{2,1,0:T(8,128)(2,1)S(1)}, f32[8,256,256]{2,1,0:T(8,128)}) fusion(bf16[8,256,256]{2,1,0:T(8,128)(2,1)S(1)} %get-tuple-element.30, bf16[2,768,256]{2,1,0:T(8,128)(2,1)S(1)} %bitcast.139, bf16[8,248,256]{2,1,0:T(8,128)(2,1)S(1)} %slice.97, bf16[8,252,256]{2,1,0:T(8,128)(2,1)S(1)} %bitcast.143), kind=kOutput, calls=%fused_computation.171 | convolution fusion | flops 828372992 | bytes 7704576 | tf_op jit(solution)/shard_map/dot_general | solution.py:49
  63.9 1.8 %fusion.29 = (f32[8,256]{1,0:T(8,128)S(1)}, f32[8,256]{1,0:T(8,128)S(1)}, f32[256]{0:T(256)S(1)}, bf16[8,256,256]{2,1,0:T(8,128)(2,1)S(1)}) fusion(bf16[8,256,256]{2,1,0:T(8,128)(2,1)S(1)} %get-tuple-element.15, f32[8,256]{1,0:T(8,128)S(1)} %fusion.79, f32[8,256]{1,0:T(8,128)S(1)} %bitcast.150, bf16[2,768,256]{2,1,0:T(8,128)(2,1)S(1)} %bitcast.147, ...), kind=kOutput, calls=%fused_computation.39 | convolution fusion | flops 832040704 | bytes 6685696 | tf_op jit(solution)/shard_map/dot_general | solution.py:49
  66.4 6.8 %all-to-all-start.2 = ((f32[16,1,384]{2,1,0:T(1,128)}), f32[16,1,384]{2,1,0:T(1,128)S(1)}, u32[]{:S(2)}, u32[]{:S(2)}) async-start(f32[16,1,384]{2,1,0:T(1,128)} %broadcast_in_dim.40), calls=%async_computation.2 | async-start | bytes 49152 | tf_op jit(solution)/shard_map/all_to_all | solution.py:191
  74.0 5.8 %all-to-all-done.2 = f32[16,1,384]{2,1,0:T(1,128)S(1)} async-done(((f32[16,1,384]{2,1,0:T(1,128)}), f32[16,1,384]{2,1,0:T(1,128)S(1)}, u32[]{:S(2)}, u32[]{:S(2)}) %all-to-all-start.2) | async-done | bytes 24608 | tf_op jit(solution)/shard_map/all_to_all | solution.py:191
  82.3 3.7 %multiply_convert_fusion = bf16[8,256,256]{2,1,0:T(8,128)(2,1)S(1)} fusion(f32[8,256,256]{2,1,0:T(8,128)S(1)} %copy-done.4, f32[8,256]{1,0:T(8,128)S(1)} %fusion.36, f32[8,256]{1,0:T(8,128)S(1)} %fusion.33, f32[256]{0:T(256)S(1)} %slice_divide_fusion, bf16[8,256,256]{2,1,0:T(8,128)(2,1)S(1)} %get-tuple-element.33, f32[8,256]{1,0:T(8,128)S(1)} %get-tuple-element.5, ...), kind=kLoop, calls=%fused_computation.55 | loop fusion | flops 10485760 | bytes 5284864 | tf_op jit(solution)/shard_map/convert_element_type | solution.py:206
  86.0 1.0 convolution_bitcast_fusion
  88.9 1.1 copy-done.19
  90.7 3.1 %convolution_bitcast_fusion.1 = f32[1,768,256]{2,1,0:T(8,128)S(1)} fusion(f32[8,256,3,256]{3,1,0,2:T(8,128)S(1)} %fusion.46, f32[8,256,256]{2,1,0:T(8,128)S(1)} %copy-done.19, f32[8,248,256]{2,1,0:T(8,128)S(1)} %slice.107, f32[8,252,256]{2,1,0:T(8,128)S(1)} %slice.105, bf16[8,256,256]{2,1,0:T(8,128)(2,1)S(1)} %copy-done.9, ...), kind=kOutput, calls=%fused_computation.74 | convolution fusion | flops 836239360 | bytes 14394368 | tf_op jit(solution)/shard_map/dot_general | solution.py:208
  94.8 2.4 %collective-permute-done = f32[2,384,256]{2,1,0:T(8,128)} collective-permute-done((f32[2,384,256]{2,1,0:T(8,128)S(1)}, f32[2,384,256]{2,1,0:T(8,128)}, u32[]{:S(2)}, u32[]{:S(2)}) %collective-permute-start) | collective-permute-done | bytes 786464 | tf_op jit(solution)/shard_map/ppermute | solution.py:164
  97.2 1.3 fusion.53
  99.1 7.4 %collective-permute-done.1 = f32[2,192,256]{2,1,0:T(8,128)S(1)} collective-permute-done((f32[2,192,256]{2,1,0:T(8,128)S(1)}, f32[2,192,256]{2,1,0:T(8,128)S(1)}, u32[]{:S(2)}, u32[]{:S(2)}) %collective-permute-start.1) | collective-permute-done | bytes 393248 | tf_op jit(solution)/shard_map/ppermute | solution.py:164
  107.0 7.3 %collective-permute-done.2 = f32[2,96,256]{2,1,0:T(8,128)S(1)} collective-permute-done((f32[2,96,256]{2,1,0:T(8,128)S(1)}, f32[2,96,256]{2,1,0:T(8,128)S(1)}, u32[]{:S(2)}, u32[]{:S(2)}) %collective-permute-start.2) | collective-permute-done | bytes 196640 | tf_op jit(solution)/shard_map/ppermute | solution.py:164
  114.4 5.5 %collective-permute-done.3 = f32[2,48,256]{2,1,0:T(8,128)S(1)} collective-permute-done((f32[2,48,256]{2,1,0:T(8,128)S(1)}, f32[2,48,256]{2,1,0:T(8,128)S(1)}, u32[]{:S(2)}, u32[]{:S(2)}) %collective-permute-start.3) | collective-permute-done | bytes 98336 | tf_op jit(solution)/shard_map/ppermute | solution.py:164
  120.1 5.5 %collective-permute-done.4 = bf16[2,12288]{1,0:T(2,128)(2,1)S(1)} collective-permute-done((bf16[2,12288]{1,0:T(2,128)(2,1)S(1)}, bf16[2,12288]{1,0:T(2,128)(2,1)S(1)}, u32[]{:S(2)}, u32[]{:S(2)}) %collective-permute-start.4) | collective-permute-done | bytes 49184 | tf_op jit(solution)/shard_map/ppermute | solution.py:168
  125.9 5.6 %collective-permute-done.5 = bf16[2,24576]{1,0:T(2,128)(2,1)S(1)} collective-permute-done((bf16[2,24576]{1,0:T(2,128)(2,1)S(1)}, bf16[2,24576]{1,0:T(2,128)(2,1)S(1)}, u32[]{:S(2)}, u32[]{:S(2)}) %collective-permute-start.5) | collective-permute-done | bytes 98336 | tf_op jit(solution)/shard_map/ppermute | solution.py:168
  133.0 5.3 %collective-permute-done.6 = bf16[2,49152]{1,0:T(2,128)(2,1)} collective-permute-done((bf16[2,49152]{1,0:T(2,128)(2,1)S(1)}, bf16[2,49152]{1,0:T(2,128)(2,1)}, u32[]{:S(2)}, u32[]{:S(2)}) %collective-permute-start.6) | collective-permute-done | bytes 196640 | tf_op jit(solution)/shard_map/ppermute | solution.py:168
  138.3 1.4 broadcast_select_fusion.3
  139.7 1.1 pad_maximum_fusion
  141.5 1.4 collective-permute-done.7
  142.8 1.7 %broadcast_select_fusion.1 = (bf16[2,98304]{1,0:T(2,128)(2,1)S(1)}, bf16[2,98304]{1,0:T(2,128)(2,1)S(1)}) fusion(bf16[2,98304]{1,0:T(2,128)(2,1)} %collective-permute-done.7, pred[]{:T(512)S(6)} %eq.46, bf16[2,49152]{1,0:T(2,128)(2,1)S(1)} %get-tuple-element.23, bf16[2,49152]{1,0:T(2,128)(2,1)S(1)} %get-tuple-element.22), kind=kLoop, calls=%fused_computation.85 | loop fusion | flops 1179648 | bytes 1572865 | tf_op jit(solution)/shard_map/jit(_where)/select_n | solution.py:169
  144.6 10.1 %multiply_add_fusion = (f32[2,196608]{1,0:T(2,128)}, f32[2,196608]{1,0:T(2,128)}, f32[2,196608]{1,0:T(2,128)}) fusion(f32[2,196608]{1,0:T(2,128)S(1)} %copy-done, f32[2,196608]{1,0:T(2,128)S(1)} %copy-done.2, bf16[2,98304]{1,0:T(2,128)(2,1)S(1)} %get-tuple-element.21, bf16[2,98304]{1,0:T(2,128)(2,1)S(1)} %get-tuple-element.20, f32[2,196608]{1,0:T(2,128)S(1)} %copy-done.6), kind=kLoop, calls=%fused_computation.70 | loop fusion | flops 4325376 | bytes 10223616 | tf_op jit(solution)/shard_map/add | solution.py:229
  (100 shorter events, 18.9 us)
Async XLA Ops:
  11.2 14.0 %all-to-all-start = ((bf16[16,128,8]{1,2,0:T(8,128)(2,1)}), bf16[16,128,8]{1,2,0:T(8,128)(2,1)S(1)}, u32[]{:S(2)}, u32[]{:S(2)}) async-start(bf16[16,128,8]{1,2,0:T(8,128)(2,1)} %slice_bitcast_fusion.10), calls=%async_computation | async-start | bytes 65536 | tf_op jit(solution)/shard_map/all_to_all | solution.py:115
  18.5 11.2 %copy-start = (f32[2,196608]{1,0:T(2,128)S(1)}, f32[2,196608]{1,0:T(2,128)}, u32[]{:S(2)}) copy-start(f32[2,196608]{1,0:T(2,128)} %param.11) | copy-start | bytes 4718596
  19.8 10.9 %copy-start.1 = (f32[2,196608]{1,0:T(2,128)S(1)}, f32[2,196608]{1,0:T(2,128)}, u32[]{:S(2)}) copy-start(f32[2,196608]{1,0:T(2,128)} %param.9) | copy-start | bytes 4718596
  25.2 27.3 %all-to-all-start.1 = ((bf16[16,128,256]{1,2,0:T(8,128)(2,1)}), bf16[16,128,256]{1,2,0:T(8,128)(2,1)}, u32[]{:S(2)}, u32[]{:S(2)}) async-start(bf16[16,128,256]{1,2,0:T(8,128)(2,1)} %copy_bitcast_fusion.2), calls=%async_computation.1 | async-start | bytes 2097152 | tf_op jit(solution)/shard_map/all_to_all | solution.py:108
  53.9 3.2 %copy-start.16 = (bf16[1,2,768,256]{3,2,1,0:T(8,128)(2,1)S(1)}, bf16[1,2,768,256]{3,2,1,0:T(8,128)(2,1)}, u32[]{:S(2)}) copy-start(bf16[1,2,768,256]{3,2,1,0:T(8,128)(2,1)} %copy.141) | copy-start | bytes 2359300
  57.1 1.6 %copy-start.17 = (bf16[2048,256]{1,0:T(8,128)(2,1)}, bf16[2048,256]{1,0:T(8,128)(2,1)S(1)}, u32[]{:S(2)}) copy-start(bf16[2048,256]{1,0:T(8,128)(2,1)S(1)} %fusion.20) | copy-start | bytes 3145732
  57.2 1.6 %copy-start.5 = (bf16[1,2,768,256]{3,2,1,0:T(8,128)(2,1)S(1)}, bf16[1,2,768,256]{3,2,1,0:T(8,128)(2,1)}, u32[]{:S(2)}) copy-start(bf16[1,2,768,256]{3,2,1,0:T(8,128)(2,1)} %copy.142) | copy-start | bytes 2359300
  61.3 2.6 %copy-start.12 = (bf16[8,256,256]{2,1,0:T(8,128)(2,1)}, bf16[8,256,256]{2,1,0:T(8,128)(2,1)S(1)}, u32[]{:S(2)}) copy-start(bf16[8,256,256]{2,1,0:T(8,128)(2,1)S(1)} %get-tuple-element.30) | copy-start | bytes 3145732
  61.3 2.5 %copy-start.10 = (bf16[8,248,256]{2,1,0:T(8,128)(2,1)}, bf16[8,248,256]{2,1,0:T(8,128)(2,1)S(1)}, u32[]{:S(2)}) copy-start(bf16[8,248,256]{2,1,0:T(8,128)(2,1)S(1)} %slice.97) | copy-start | bytes 3047428
  63.8 1.9 %copy-start.8 = (bf16[8,256,256]{2,1,0:T(8,128)(2,1)}, bf16[8,256,256]{2,1,0:T(8,128)(2,1)S(1)}, u32[]{:S(2)}) copy-start(bf16[8,256,256]{2,1,0:T(8,128)(2,1)S(1)} %get-tuple-element.15) | copy-start | bytes 3145732
  66.4 13.4 %all-to-all-start.2 = ((f32[16,1,384]{2,1,0:T(1,128)}), f32[16,1,384]{2,1,0:T(1,128)S(1)}, u32[]{:S(2)}, u32[]{:S(2)}) async-start(f32[16,1,384]{2,1,0:T(1,128)} %broadcast_in_dim.40), calls=%async_computation.2 | async-start | bytes 49152 | tf_op jit(solution)/shard_map/all_to_all | solution.py:191
  79.8 2.4 %copy-start.4 = (f32[8,256,256]{2,1,0:T(8,128)S(1)}, f32[8,256,256]{2,1,0:T(8,128)}, u32[]{:S(2)}) copy-start(f32[8,256,256]{2,1,0:T(8,128)} %get-tuple-element.32) | copy-start | bytes 6291460
  82.2 3.7 %copy-start.11 = (bf16[8,248,256]{2,1,0:T(8,128)(2,1)S(1)}, bf16[8,248,256]{2,1,0:T(8,128)(2,1)}, u32[]{:S(2)}) copy-start(bf16[8,248,256]{2,1,0:T(8,128)(2,1)} %copy-done.10) | copy-start | bytes 3047428
  82.2 3.7 %copy-start.13 = (bf16[8,256,256]{2,1,0:T(8,128)(2,1)S(1)}, bf16[8,256,256]{2,1,0:T(8,128)(2,1)}, u32[]{:S(2)}) copy-start(bf16[8,256,256]{2,1,0:T(8,128)(2,1)} %copy-done.12) | copy-start | bytes 3145732
  86.0 1.0 copy-start.7
  88.4 1.6 %copy-start.19 = (f32[8,256,256]{2,1,0:T(8,128)S(1)}, f32[8,256,256]{2,1,0:T(8,128)}, u32[]{:S(2)}) copy-start(f32[8,256,256]{2,1,0:T(8,128)} %get-tuple-element.31) | copy-start | bytes 6291460
  88.7 1.7 %copy-start.9 = (bf16[8,256,256]{2,1,0:T(8,128)(2,1)S(1)}, bf16[8,256,256]{2,1,0:T(8,128)(2,1)}, u32[]{:S(2)}) copy-start(bf16[8,256,256]{2,1,0:T(8,128)(2,1)} %copy-done.8) | copy-start | bytes 3145732
  88.7 2.0 %copy-start.18 = (bf16[2048,256]{1,0:T(8,128)(2,1)S(1)}, bf16[2048,256]{1,0:T(8,128)(2,1)}, u32[]{:S(2)}) copy-start(bf16[2048,256]{1,0:T(8,128)(2,1)} %copy-done.17) | copy-start | bytes 3145732
  93.8 0.9 copy-start.3
  94.7 2.5 %collective-permute-start = (f32[2,384,256]{2,1,0:T(8,128)S(1)}, f32[2,384,256]{2,1,0:T(8,128)}, u32[]{:S(2)}, u32[]{:S(2)}) collective-permute-start(f32[2,384,256]{2,1,0:T(8,128)S(1)} %fusion.51), channel_id=1, source_target_pairs={{0,1},{1,0},{2,3},{3,2},{4,5},{5,4},{6,7},{7,6},{8,9},{9,8},{10,11... | collective-permute-start | bytes 2359304 | tf_op jit(solution)/shard_map/ppermute | solution.py:164
  98.6 7.8 %collective-permute-start.1 = (f32[2,192,256]{2,1,0:T(8,128)S(1)}, f32[2,192,256]{2,1,0:T(8,128)S(1)}, u32[]{:S(2)}, u32[]{:S(2)}) collective-permute-start(f32[2,192,256]{2,1,0:T(8,128)S(1)} %constant_dynamic-slice_fusion.1), channel_id=1, source_target_pairs={{0,2},{1,5},{2,0},{3,7},{4,6},{5,1},{6,4},{7,3},{8,10},{9,13},{10,... | collective-permute-start | bytes 1179656 | tf_op jit(solution)/shard_map/ppermute | solution.py:164
  106.5 7.8 %collective-permute-start.2 = (f32[2,96,256]{2,1,0:T(8,128)S(1)}, f32[2,96,256]{2,1,0:T(8,128)S(1)}, u32[]{:S(2)}, u32[]{:S(2)}) collective-permute-start(f32[2,96,256]{2,1,0:T(8,128)S(1)} %constant_dynamic-slice_fusion), channel_id=1, source_target_pairs={{0,4},{1,9},{2,6},{3,11},{4,0},{5,13},{6,2},{7,15},{8,12},{9,1},{1... | collective-permute-start | bytes 589832 | tf_op jit(solution)/shard_map/ppermute | solution.py:164
  114.3 5.6 %collective-permute-start.3 = (f32[2,48,256]{2,1,0:T(8,128)S(1)}, f32[2,48,256]{2,1,0:T(8,128)S(1)}, u32[]{:S(2)}, u32[]{:S(2)}) collective-permute-start(f32[2,48,256]{2,1,0:T(8,128)S(1)} %constant_dynamic-slice_fusion.2), channel_id=1, source_target_pairs={{0,8},{1,3},{2,10},{3,1},{4,12},{5,7},{6,14},{7,5},{8,0},{9,11},{1... | collective-permute-start | bytes 294920 | tf_op jit(solution)/shard_map/ppermute | solution.py:164
  120.0 5.6 %collective-permute-start.4 = (bf16[2,12288]{1,0:T(2,128)(2,1)S(1)}, bf16[2,12288]{1,0:T(2,128)(2,1)S(1)}, u32[]{:S(2)}, u32[]{:S(2)}) collective-permute-start(bf16[2,12288]{1,0:T(2,128)(2,1)S(1)} %bitcast.148), channel_id=1, source_target_pairs={{0,8},{1,3},{2,10},{3,1},{4,12},{5,7},{6,14},{7,5},{8,0},{9,11},{1... | collective-permute-start | bytes 147464 | tf_op jit(solution)/shard_map/ppermute | solution.py:168
  125.7 18.9 %copy-start.2 = (f32[2,196608]{1,0:T(2,128)S(1)}, f32[2,196608]{1,0:T(2,128)}, u32[]{:S(2)}) copy-start(f32[2,196608]{1,0:T(2,128)} %param.9) | copy-start | bytes 4718596
  125.8 5.6 %collective-permute-start.5 = (bf16[2,24576]{1,0:T(2,128)(2,1)S(1)}, bf16[2,24576]{1,0:T(2,128)(2,1)S(1)}, u32[]{:S(2)}, u32[]{:S(2)}) collective-permute-start(bf16[2,24576]{1,0:T(2,128)(2,1)S(1)} %pad_maximum_fusion.2), channel_id=1, source_target_pairs={{0,4},{1,9},{2,6},{3,11},{4,0},{5,13},{6,2},{7,15},{8,12},{9,1},{1... | collective-permute-start | bytes 294920 | tf_op jit(solution)/shard_map/ppermute | solution.py:168
  131.6 0.6 copy-start.14
  131.6 0.8 copy-start.15
  132.4 5.8 %collective-permute-start.6 = (bf16[2,49152]{1,0:T(2,128)(2,1)S(1)}, bf16[2,49152]{1,0:T(2,128)(2,1)}, u32[]{:S(2)}, u32[]{:S(2)}) collective-permute-start(bf16[2,49152]{1,0:T(2,128)(2,1)S(1)} %pad_maximum_fusion.1), channel_id=1, source_target_pairs={{0,2},{1,5},{2,0},{3,7},{4,6},{5,1},{6,4},{7,3},{8,10},{9,13},{10,... | collective-permute-start | bytes 589832 | tf_op jit(solution)/shard_map/ppermute | solution.py:168
  140.8 2.1 %collective-permute-start.7 = (bf16[2,98304]{1,0:T(2,128)(2,1)}, bf16[2,98304]{1,0:T(2,128)(2,1)}, u32[]{:S(2)}, u32[]{:S(2)}) collective-permute-start(bf16[2,98304]{1,0:T(2,128)(2,1)} %pad_maximum_fusion), channel_id=1, source_target_pairs={{0,1},{1,0},{2,3},{3,2},{4,5},{5,4},{6,7},{7,6},{8,9},{9,8},{10,11... | collective-permute-start | bytes 1179656 | tf_op jit(solution)/shard_map/ppermute | solution.py:168
  140.8 3.8 %copy-start.6 = (f32[2,196608]{1,0:T(2,128)S(1)}, f32[2,196608]{1,0:T(2,128)}, u32[]{:S(2)}) copy-start(f32[2,196608]{1,0:T(2,128)} %param.10) | copy-start | bytes 4718596

commit v13 on v8

--- a/solution.py
+++ b/solution.py
@@ -104,22 +104,26 @@
     ).astype(jnp.bfloat16)
     send_rows = sent[:, :feat_width]
     send_place = sent[:, feat_width:]
-    got_rows, got_place = (
-        lax.all_to_all(
-            send_rows.reshape(wide_count, capacity, feat_width),
-            "wide",
-            split_axis=0,
-            concat_axis=0,
-            tiled=True,
-        ),
-        lax.all_to_all(
-            send_place.reshape(wide_count, capacity, per_dev),
-            "wide",
-            split_axis=0,
-            concat_axis=0,
-            tiled=True,
-        ),
-    )
+    got_rows = lax.all_to_all(
+        send_rows.reshape(wide_count, capacity, feat_width),
+        "wide",
+        split_axis=0,
+        concat_axis=0,
+        tiled=True,
+    )
+    place_chunks = send_place.reshape(wide_count, capacity, per_dev)
+    if wide_count <= 16 and wide_count & (wide_count - 1) == 0:
+        me = lax.axis_index("wide")
+        arrived = [lax.dynamic_index_in_dim(place_chunks, me, axis=0, keepdims=False)]
+        for shift in range(1, wide_count):
+            outgoing = lax.dynamic_index_in_dim(place_chunks, me ^ shift, axis=0, keepdims=False)
+            pairs = [(i, i ^ shift) for i in range(wide_count)]
+            arrived.append(lax.ppermute(outgoing, "wide", pairs))
+        by_shift = jnp.stack(arrived)
+        sources = jnp.arange(wide_count, dtype=jnp.int32)
+        got_place = jnp.take(by_shift, sources ^ me, axis=0)
+    else:
+        got_place = lax.all_to_all(place_chunks, "wide", split_axis=0, concat_axis=0, tiled=True)
     place_hot = got_place.reshape(-1, per_dev) > 0
     arrival = prefix_count(place_hot)
     position = jnp.sum(jnp.where(place_hot, arrival, 0), axis=1) - 1

time: 147 us -> 153 us (1.041)
  starting transfers between devices: 20.4 us -> 35.9 us
  waiting for transfers between devices: 70 us -> 60.6 us
    ppermute x0 -> x15, starting transfers between devices: none -> 24.4 us  [route_rows(): arrived.append(lax.ppermute(outgoing, 'wide', pairs))]
    all_to_all x1, waiting for transfers between devices: 18.8 us -> 0.01 us  [route_rows(): lax.all_to_all(send_rows.reshape(wide_count, capacity, feat_width), 'wide...]
    ppermute x0 -> x15, waiting for transfers between devices: none -> 15.1 us  [route_rows(): arrived.append(lax.ppermute(outgoing, 'wide', pairs))]
    all_to_all x1 -> x0, starting transfers between devices: 7.36 us -> none  [route_rows(): lax.all_to_all(send_place.reshape(wide_count, capacity, per_dev), 'wide',...]
    all_to_all x1 -> x0, waiting for transfers between devices: 5.38 us -> none  [route_rows(): lax.all_to_all(send_place.reshape(wide_count, capacity, per_dev), 'wide',...]
    all_to_all x1, starting transfers between devices: 6.81 us -> 3.71 us  [local(): lax.all_to_all(jnp.broadcast_to(stats[None, :], (wide_count, stats.shape[...]
    all_to_all x1, starting transfers between devices: 4.52 us -> 6.12 us  [route_rows(): lax.all_to_all(send_rows.reshape(wide_count, capacity, feat_width), 'wide...]
    unnamed x39 -> x51, local copies, waits for them, and re-layouts: 6.55 us -> 6.4 us
  transfers between devices with their start and end apart: 11 -> 25, of which waited for: 11 -> 13; matrix products, arithmetic and copies ran while one was open for 4% -> 4% of each run, Pallas kernels for 0% -> 0%
where the time goes in v13:
time: 153 us; the launch traced here: 152 us
  waiting for transfers between devices  60.6 us (40%)
  starting transfers between devices  35.9 us (23%)
  matrix products  22.1 us (14%)
  other arithmetic  18.2 us (12%)
  local copies, waits for them, and re-layouts  13.4 us (9%)
  between operations  2.08 us (1%)
    ppermute x15, starting transfers between devices, route_rows(): arrived.append(lax.ppermute(outgoing, 'wide', pairs))  24.4 us
    ppermute x4, waiting for transfers between devices, all_reduce_wide(): buf = keep + lax.ppermute(send, 'wide', pairs)  22.6 us
    ppermute x4, waiting for transfers between devices, all_reduce_wide(): got = lax.ppermute(buf, 'wide', pairs)  17.5 us
    ppermute x15, waiting for transfers between devices, route_rows(): arrived.append(lax.ppermute(outgoing, 'wide', pairs))  15.1 us
    dot_general x4, matrix products, run_network(): jnp.dot(stacked.reshape(-1, stacked.shape[2]), weights[layer_at], preferr...  8.33 us
    unnamed x51, local copies, waits for them, and re-layouts  6.4 us
    all_to_all x1, starting transfers between devices, route_rows(): lax.all_to_all(send_rows.reshape(wide_count, capacity, feat_width), 'wide...  6.12 us
    all_to_all x1, waiting for transfers between devices, local(): lax.all_to_all(jnp.broadcast_to(stats[None, :], (wide_count, stats.shape[...  5.5 us
  transfers between devices with their start and end apart: 25, of which 13 were waited for; matrix products, arithmetic and copies ran while one was open for 4% of the time, Pallas kernels for 0%

profile of v13, /device:TPU:0, one launch (start us, length us, event | category | flops | bytes accessed | tf_op | source)
XLA Modules:
  0.0 152.3 jit_solution(5359129497564368360)
XLA Ops:
  5.8 4.8 %fusion.19 = bf16[2048,264]{0,1:T(8,128)(2,1)S(1)} fusion(s32[2048]{0:T(1024)S(1)} %get-tuple-element.45, bf16[2048,8]{1,0:T(8,128)(2,1)S(1)} %copy.102, bf16[2048,256]{1,0:T(8,128)(2,1)} %param.6), kind=kOutput, calls=%fused_computation.30 | convolution fusion | flops 2221490176 | bytes 2170880 | tf_op jit(solution)/shard_map/dot_general | solution.py:102
  11.3 2.6 %collective-permute-start.1 = (bf16[128,8]{0,1:T(8,128)(2,1)S(1)}, bf16[128,8]{0,1:T(8,128)(2,1)S(1)}, u32[]{:S(2)}, u32[]{:S(2)}) collective-permute-start(bf16[128,8]{0,1:T(8,128)(2,1)S(1)} %get-tuple-element.41), channel_id=1, source_target_pairs={{0,2},{1,3},{2,0},{3,1},{4,6},{5,7},{6,4},{7,5},{8,10},{9,11},{10,... | collective-permute-start | bytes 6152 | tf_op jit(solution)/shard_map/ppermute | solution.py:121
  13.9 1.8 %collective-permute-start.3 = (bf16[128,8]{0,1:T(8,128)(2,1)S(1)}, bf16[128,8]{0,1:T(8,128)(2,1)S(1)}, u32[]{:S(2)}, u32[]{:S(2)}) collective-permute-start(bf16[128,8]{0,1:T(8,128)(2,1)S(1)} %get-tuple-element.39), channel_id=1, source_target_pairs={{0,4},{1,5},{2,6},{3,7},{4,0},{5,1},{6,2},{7,3},{8,12},{9,13},{10,... | collective-permute-start | bytes 6152 | tf_op jit(solution)/shard_map/ppermute | solution.py:121
  17.0 6.1 %all-to-all-start = ((bf16[16,128,256]{1,2,0:T(8,128)(2,1)}), bf16[16,128,256]{1,2,0:T(8,128)(2,1)}, u32[]{:S(2)}, u32[]{:S(2)}) async-start(bf16[16,128,256]{1,2,0:T(8,128)(2,1)} %copy_bitcast_fusion.2), calls=%async_computation | async-start | bytes 2097152 | tf_op jit(solution)/shard_map/all_to_all | solution.py:107
  24.9 2.8 %collective-permute-start.5 = (bf16[128,8]{0,1:T(8,128)(2,1)S(1)}, bf16[128,8]{0,1:T(8,128)(2,1)S(1)}, u32[]{:S(2)}, u32[]{:S(2)}) collective-permute-start(bf16[128,8]{0,1:T(8,128)(2,1)S(1)} %get-tuple-element.37), channel_id=1, source_target_pairs={{0,6},{1,7},{2,4},{3,5},{4,2},{5,3},{6,0},{7,1},{8,14},{9,15},{10,... | collective-permute-start | bytes 6152 | tf_op jit(solution)/shard_map/ppermute | solution.py:121
  27.8 2.4 %collective-permute-start.7 = (bf16[128,8]{0,1:T(8,128)(2,1)S(1)}, bf16[128,8]{0,1:T(8,128)(2,1)S(1)}, u32[]{:S(2)}, u32[]{:S(2)}) collective-permute-start(bf16[128,8]{0,1:T(8,128)(2,1)S(1)} %get-tuple-element.35), channel_id=1, source_target_pairs={{0,8},{1,9},{2,10},{3,11},{4,12},{5,13},{6,14},{7,15},{8,0},{9,1},... | collective-permute-start | bytes 6152 | tf_op jit(solution)/shard_map/ppermute | solution.py:121
  30.5 3.5 %collective-permute-start.9 = (bf16[128,8]{0,1:T(8,128)(2,1)S(1)}, bf16[128,8]{0,1:T(8,128)(2,1)S(1)}, u32[]{:S(2)}, u32[]{:S(2)}) collective-permute-start(bf16[128,8]{0,1:T(8,128)(2,1)S(1)} %get-tuple-element.33), channel_id=1, source_target_pairs={{0,10},{1,11},{2,8},{3,9},{4,14},{5,15},{6,12},{7,13},{8,2},{9,3},... | collective-permute-start | bytes 6152 | tf_op jit(solution)/shard_map/ppermute | solution.py:121
  34.0 7.3 %collective-permute-done.5 = bf16[128,8]{0,1:T(8,128)(2,1)S(1)} collective-permute-done((bf16[128,8]{0,1:T(8,128)(2,1)S(1)}, bf16[128,8]{0,1:T(8,128)(2,1)S(1)}, u32[]{:S(2)}, u32[]{:S(2)}) %collective-permute-start.5) | collective-permute-done | bytes 2080 | tf_op jit(solution)/shard_map/ppermute | solution.py:121
  41.3 4.5 %collective-permute-start.10 = (bf16[128,8]{0,1:T(8,128)(2,1)S(1)}, bf16[128,8]{0,1:T(8,128)(2,1)S(1)}, u32[]{:S(2)}, u32[]{:S(2)}) collective-permute-start(bf16[128,8]{0,1:T(8,128)(2,1)S(1)} %get-tuple-element.32), channel_id=1, source_target_pairs={{0,11},{1,10},{2,9},{3,8},{4,15},{5,14},{6,13},{7,12},{8,3},{9,2},... | collective-permute-start | bytes 6152 | tf_op jit(solution)/shard_map/ppermute | solution.py:121
  46.2 3.8 %collective-permute-done.7 = bf16[128,8]{0,1:T(8,128)(2,1)S(1)} collective-permute-done((bf16[128,8]{0,1:T(8,128)(2,1)S(1)}, bf16[128,8]{0,1:T(8,128)(2,1)S(1)}, u32[]{:S(2)}, u32[]{:S(2)}) %collective-permute-start.7) | collective-permute-done | bytes 2080 | tf_op jit(solution)/shard_map/ppermute | solution.py:121
  50.2 3.6 %collective-permute-start.13 = (bf16[128,8]{0,1:T(8,128)(2,1)S(1)}, bf16[128,8]{0,1:T(8,128)(2,1)S(1)}, u32[]{:S(2)}, u32[]{:S(2)}) collective-permute-start(bf16[128,8]{0,1:T(8,128)(2,1)S(1)} %get-tuple-element.29), channel_id=1, source_target_pairs={{0,14},{1,15},{2,12},{3,13},{4,10},{5,11},{6,8},{7,9},{8,6},{9,7},... | collective-permute-start | bytes 6152 | tf_op jit(solution)/shard_map/ppermute | solution.py:121
  53.9 1.7 %collective-permute-start.14 = (bf16[128,8]{0,1:T(8,128)(2,1)S(1)}, bf16[128,8]{0,1:T(8,128)(2,1)S(1)}, u32[]{:S(2)}, u32[]{:S(2)}) collective-permute-start(bf16[128,8]{0,1:T(8,128)(2,1)S(1)} %get-tuple-element.28), channel_id=1, source_target_pairs={{0,15},{1,14},{2,13},{3,12},{4,11},{5,10},{6,9},{7,8},{8,7},{9,6},... | collective-permute-start | bytes 6152 | tf_op jit(solution)/shard_map/ppermute | solution.py:121
  56.5 3.1 %collective-permute-done.14 = bf16[128,8]{0,1:T(8,128)(2,1)S(1)} collective-permute-done((bf16[128,8]{0,1:T(8,128)(2,1)S(1)}, bf16[128,8]{0,1:T(8,128)(2,1)S(1)}, u32[]{:S(2)}, u32[]{:S(2)}) %collective-permute-start.14) | collective-permute-done | bytes 2080 | tf_op jit(solution)/shard_map/ppermute | solution.py:121
  62.2 1.5 copy.106
  63.7 3.2 %fusion.20 = bf16[2048,256]{1,0:T(8,128)(2,1)S(1)} fusion(bf16[2048,256]{1,0:T(8,128)(2,1)S(1)} %bitcast.205, s32[2048]{0:T(1024)S(1)} %select_bitcast_fusion), kind=kOutput, calls=%fused_computation.31 | convolution fusion | flops 2152202240 | bytes 2105344 | tf_op jit(solution)/shard_map/dot_general | solution.py:138
  66.9 1.5 fusion.22
  68.5 2.5 %fusion.21 = (bf16[8,256,256]{2,1,0:T(8,128)(2,1)S(1)}, f32[8,256,256]{2,1,0:T(8,128)}) fusion(bf16[8,256,256]{2,1,0:T(8,128)(2,1)S(1)} %bitcast.217, bf16[2,768,256]{2,1,0:T(8,128)(2,1)S(1)} %bitcast.201, bf16[8,254,256]{2,1,0:T(8,128)(2,1)S(1)} %bitcast.218, bf16[8,255,256]{2,1,0:T(8,128)(2,1)S(1)} %bitcast.219), kind=kOutput, calls=%fused_computation.32 | convolution fusion | flops 827850752 | bytes 7733248 | tf_op jit(solution)/shard_map/dot_general | solution.py:49
  71.1 2.5 %fusion.112 = (bf16[8,256]{1,0:T(8,128)(2,1)S(1)}, bf16[8,256,256]{2,1,0:T(8,128)(2,1)S(1)}, f32[8,256,256]{2,1,0:T(8,128)}) fusion(bf16[8,256,256]{2,1,0:T(8,128)(2,1)S(1)} %get-tuple-element.46, bf16[2,768,256]{2,1,0:T(8,128)(2,1)S(1)} %bitcast.202, bf16[8,248,256]{2,1,0:T(8,128)(2,1)S(1)} %slice.99, bf16[8,252,256]{2,1,0:T(8,128)(2,1)S(1)} %bitcast.206), kind=kOutput, calls=%fused_computation.224 | convolution fusion | flops 828372992 | bytes 7704576 | tf_op jit(solution)/shard_map/dot_general | solution.py:49
  73.6 1.8 %fusion.29 = (f32[8,256]{1,0:T(8,128)S(1)}, f32[8,256]{1,0:T(8,128)S(1)}, f32[256]{0:T(256)S(1)}, bf16[8,256,256]{2,1,0:T(8,128)(2,1)S(1)}) fusion(bf16[8,256,256]{2,1,0:T(8,128)(2,1)S(1)} %get-tuple-element.15, f32[8,256]{1,0:T(8,128)S(1)} %fusion.78, f32[8,256]{1,0:T(8,128)S(1)} %bitcast.211, bf16[2,768,256]{2,1,0:T(8,128)(2,1)S(1)} %bitcast.210, ...), kind=kOutput, calls=%fused_computation.40 | convolution fusion | flops 832040704 | bytes 6685696 | tf_op jit(solution)/shard_map/dot_general | solution.py:49
  76.1 3.7 %all-to-all-start.1 = ((f32[16,1,384]{2,1,0:T(1,128)}), f32[16,1,384]{2,1,0:T(1,128)S(1)}, u32[]{:S(2)}, u32[]{:S(2)}) async-start(f32[16,1,384]{2,1,0:T(1,128)} %broadcast_in_dim.56), calls=%async_computation.1 | async-start | bytes 49152 | tf_op jit(solution)/shard_map/all_to_all | solution.py:195
  80.6 5.5 %all-to-all-done.1 = f32[16,1,384]{2,1,0:T(1,128)S(1)} async-done(((f32[16,1,384]{2,1,0:T(1,128)}), f32[16,1,384]{2,1,0:T(1,128)S(1)}, u32[]{:S(2)}, u32[]{:S(2)}) %all-to-all-start.1) | async-done | bytes 24608 | tf_op jit(solution)/shard_map/all_to_all | solution.py:195
  88.6 3.7 %multiply_convert_fusion = bf16[8,256,256]{2,1,0:T(8,128)(2,1)S(1)} fusion(f32[8,256,256]{2,1,0:T(8,128)S(1)} %copy-done.4, f32[8,256]{1,0:T(8,128)S(1)} %fusion.36, f32[8,256]{1,0:T(8,128)S(1)} %fusion.33, f32[256]{0:T(256)S(1)} %slice_divide_fusion, bf16[8,256,256]{2,1,0:T(8,128)(2,1)S(1)} %get-tuple-element.49, f32[8,256]{1,0:T(8,128)S(1)} %get-tuple-element.5, ...), kind=kLoop, calls=%fused_computation.56 | loop fusion | flops 10485760 | bytes 5284864 | tf_op jit(solution)/shard_map/convert_element_type | solution.py:210
  97.1 3.1 %convolution_bitcast_fusion.1 = f32[1,768,256]{2,1,0:T(8,128)S(1)} fusion(f32[8,256,3,256]{3,1,0,2:T(8,128)S(1)} %fusion.46, f32[8,256,256]{2,1,0:T(8,128)S(1)} %copy-done.16, f32[8,248,256]{2,1,0:T(8,128)S(1)} %slice.109, f32[8,252,256]{2,1,0:T(8,128)S(1)} %slice.107, bf16[8,256,256]{2,1,0:T(8,128)(2,1)S(1)} %copy-done.8, ...), kind=kOutput, calls=%fused_computation.76 | convolution fusion | flops 836239360 | bytes 14394368 | tf_op jit(solution)/shard_map/dot_general | solution.py:212
  101.2 2.4 %collective-permute-done.15 = f32[2,384,256]{2,1,0:T(8,128)} collective-permute-done((f32[2,384,256]{2,1,0:T(8,128)S(1)}, f32[2,384,256]{2,1,0:T(8,128)}, u32[]{:S(2)}, u32[]{:S(2)}) %collective-permute-start.15) | collective-permute-done | bytes 786464 | tf_op jit(solution)/shard_map/ppermute | solution.py:168
  103.6 1.3 fusion.53
  105.4 7.4 %collective-permute-done.16 = f32[2,192,256]{2,1,0:T(8,128)S(1)} collective-permute-done((f32[2,192,256]{2,1,0:T(8,128)S(1)}, f32[2,192,256]{2,1,0:T(8,128)S(1)}, u32[]{:S(2)}, u32[]{:S(2)}) %collective-permute-start.16) | collective-permute-done | bytes 393248 | tf_op jit(solution)/shard_map/ppermute | solution.py:168
  113.4 7.3 %collective-permute-done.17 = f32[2,96,256]{2,1,0:T(8,128)S(1)} collective-permute-done((f32[2,96,256]{2,1,0:T(8,128)S(1)}, f32[2,96,256]{2,1,0:T(8,128)S(1)}, u32[]{:S(2)}, u32[]{:S(2)}) %collective-permute-start.17) | collective-permute-done | bytes 196640 | tf_op jit(solution)/shard_map/ppermute | solution.py:168
  120.8 5.5 %collective-permute-done.18 = f32[2,48,256]{2,1,0:T(8,128)S(1)} collective-permute-done((f32[2,48,256]{2,1,0:T(8,128)S(1)}, f32[2,48,256]{2,1,0:T(8,128)S(1)}, u32[]{:S(2)}, u32[]{:S(2)}) %collective-permute-start.18) | collective-permute-done | bytes 98336 | tf_op jit(solution)/shard_map/ppermute | solution.py:168
  126.4 5.5 %collective-permute-done.19 = bf16[2,48,256]{2,1,0:T(8,128)(2,1)S(1)} collective-permute-done((bf16[2,48,256]{2,1,0:T(8,128)(2,1)S(1)}, bf16[2,48,256]{2,1,0:T(8,128)(2,1)S(1)}, u32[]{:S(2)}, u32[]{:S(2)}) %collective-permute-start.19) | collective-permute-done | bytes 49184 | tf_op jit(solution)/shard_map/ppermute | solution.py:172
  132.1 5.6 %collective-permute-done.20 = bf16[2,96,256]{2,1,0:T(8,128)(2,1)S(1)} collective-permute-done((bf16[2,96,256]{2,1,0:T(8,128)(2,1)S(1)}, bf16[2,96,256]{2,1,0:T(8,128)(2,1)S(1)}, u32[]{:S(2)}, u32[]{:S(2)}) %collective-permute-start.20) | collective-permute-done | bytes 98336 | tf_op jit(solution)/shard_map/ppermute | solution.py:172
  138.2 5.3 %collective-permute-done.21 = bf16[2,192,256]{2,1,0:T(8,128)(2,1)S(1)} collective-permute-done((bf16[2,192,256]{2,1,0:T(8,128)(2,1)S(1)}, bf16[2,192,256]{2,1,0:T(8,128)(2,1)S(1)}, u32[]{:S(2)}, u32[]{:S(2)}) %collective-permute-start.21) | collective-permute-done | bytes 196640 | tf_op jit(solution)/shard_map/ppermute | solution.py:172
  147.5 4.8 %multiply_add_fusion = (f32[2,196608]{1,0:T(2,128)}, f32[2,196608]{1,0:T(2,128)}, f32[2,196608]{1,0:T(2,128)}) fusion(f32[2,196608]{1,0:T(2,128)S(1)} %copy-done, f32[2,196608]{1,0:T(2,128)S(1)} %copy-done.2, f32[2,196608]{1,0:T(2,128)S(1)} %bitcast.200, f32[2,196608]{1,0:T(2,128)S(1)} %copy-done.5), kind=kLoop, calls=%fused_computation.72 | loop fusion | flops 2752512 | bytes 11010048 | tf_op jit(solution)/shard_map/add | solution.py:233
  (143 shorter events, 28.0 us)
Async XLA Ops:
  10.8 14.2 %collective-permute-start = (bf16[128,8]{0,1:T(8,128)(2,1)S(1)}, bf16[128,8]{0,1:T(8,128)(2,1)S(1)}, u32[]{:S(2)}, u32[]{:S(2)}) collective-permute-start(bf16[128,8]{0,1:T(8,128)(2,1)S(1)} %get-tuple-element.42), channel_id=1, source_target_pairs={{0,1},{1,0},{2,3},{3,2},{4,5},{5,4},{6,7},{7,6},{8,9},{9,8},{10,11... | collective-permute-start | bytes 6152 | tf_op jit(solution)/shard_map/ppermute | solution.py:121
  11.3 16.5 %collective-permute-start.1 = (bf16[128,8]{0,1:T(8,128)(2,1)S(1)}, bf16[128,8]{0,1:T(8,128)(2,1)S(1)}, u32[]{:S(2)}, u32[]{:S(2)}) collective-permute-start(bf16[128,8]{0,1:T(8,128)(2,1)S(1)} %get-tuple-element.41), channel_id=1, source_target_pairs={{0,2},{1,3},{2,0},{3,1},{4,6},{5,7},{6,4},{7,5},{8,10},{9,11},{10,... | collective-permute-start | bytes 6152 | tf_op jit(solution)/shard_map/ppermute | solution.py:121
  13.9 13.9 %collective-permute-start.2 = (bf16[128,8]{0,1:T(8,128)(2,1)S(1)}, bf16[128,8]{0,1:T(8,128)(2,1)S(1)}, u32[]{:S(2)}, u32[]{:S(2)}) collective-permute-start(bf16[128,8]{0,1:T(8,128)(2,1)S(1)} %get-tuple-element.40), channel_id=1, source_target_pairs={{0,3},{1,2},{2,1},{3,0},{4,7},{5,6},{6,5},{7,4},{8,11},{9,10},{10,... | collective-permute-start | bytes 6152 | tf_op jit(solution)/shard_map/ppermute | solution.py:121
  13.9 16.3 %collective-permute-start.3 = (bf16[128,8]{0,1:T(8,128)(2,1)S(1)}, bf16[128,8]{0,1:T(8,128)(2,1)S(1)}, u32[]{:S(2)}, u32[]{:S(2)}) collective-permute-start(bf16[128,8]{0,1:T(8,128)(2,1)S(1)} %get-tuple-element.39), channel_id=1, source_target_pairs={{0,4},{1,5},{2,6},{3,7},{4,0},{5,1},{6,2},{7,3},{8,12},{9,13},{10,... | collective-permute-start | bytes 6152 | tf_op jit(solution)/shard_map/ppermute | solution.py:121
  15.8 7.4 %copy-start = (f32[2,196608]{1,0:T(2,128)S(1)}, f32[2,196608]{1,0:T(2,128)}, u32[]{:S(2)}) copy-start(f32[2,196608]{1,0:T(2,128)} %param.11) | copy-start | bytes 4718596
  15.8 14.8 %collective-permute-start.4 = (bf16[128,8]{0,1:T(8,128)(2,1)S(1)}, bf16[128,8]{0,1:T(8,128)(2,1)S(1)}, u32[]{:S(2)}, u32[]{:S(2)}) collective-permute-start(bf16[128,8]{0,1:T(8,128)(2,1)S(1)} %get-tuple-element.38), channel_id=1, source_target_pairs={{0,5},{1,4},{2,7},{3,6},{4,1},{5,0},{6,3},{7,2},{8,13},{9,12},{10,... | collective-permute-start | bytes 6152 | tf_op jit(solution)/shard_map/ppermute | solution.py:121
  17.0 45.2 %all-to-all-start = ((bf16[16,128,256]{1,2,0:T(8,128)(2,1)}), bf16[16,128,256]{1,2,0:T(8,128)(2,1)}, u32[]{:S(2)}, u32[]{:S(2)}) async-start(bf16[16,128,256]{1,2,0:T(8,128)(2,1)} %copy_bitcast_fusion.2), calls=%async_computation | async-start | bytes 2097152 | tf_op jit(solution)/shard_map/all_to_all | solution.py:107
  24.9 16.4 %collective-permute-start.5 = (bf16[128,8]{0,1:T(8,128)(2,1)S(1)}, bf16[128,8]{0,1:T(8,128)(2,1)S(1)}, u32[]{:S(2)}, u32[]{:S(2)}) collective-permute-start(bf16[128,8]{0,1:T(8,128)(2,1)S(1)} %get-tuple-element.37), channel_id=1, source_target_pairs={{0,6},{1,7},{2,4},{3,5},{4,2},{5,3},{6,0},{7,1},{8,14},{9,15},{10,... | collective-permute-start | bytes 6152 | tf_op jit(solution)/shard_map/ppermute | solution.py:121
  27.8 18.0 %collective-permute-start.6 = (bf16[128,8]{0,1:T(8,128)(2,1)S(1)}, bf16[128,8]{0,1:T(8,128)(2,1)S(1)}, u32[]{:S(2)}, u32[]{:S(2)}) collective-permute-start(bf16[128,8]{0,1:T(8,128)(2,1)S(1)} %get-tuple-element.36), channel_id=1, source_target_pairs={{0,7},{1,6},{2,5},{3,4},{4,3},{5,2},{6,1},{7,0},{8,15},{9,14},{10,... | collective-permute-start | bytes 6152 | tf_op jit(solution)/shard_map/ppermute | solution.py:121
  27.8 22.1 %collective-permute-start.7 = (bf16[128,8]{0,1:T(8,128)(2,1)S(1)}, bf16[128,8]{0,1:T(8,128)(2,1)S(1)}, u32[]{:S(2)}, u32[]{:S(2)}) collective-permute-start(bf16[128,8]{0,1:T(8,128)(2,1)S(1)} %get-tuple-element.35), channel_id=1, source_target_pairs={{0,8},{1,9},{2,10},{3,11},{4,12},{5,13},{6,14},{7,15},{8,0},{9,1},... | collective-permute-start | bytes 6152 | tf_op jit(solution)/shard_map/ppermute | solution.py:121
  30.3 20.0 %collective-permute-start.8 = (bf16[128,8]{0,1:T(8,128)(2,1)S(1)}, bf16[128,8]{0,1:T(8,128)(2,1)S(1)}, u32[]{:S(2)}, u32[]{:S(2)}) collective-permute-start(bf16[128,8]{0,1:T(8,128)(2,1)S(1)} %get-tuple-element.34), channel_id=1, source_target_pairs={{0,9},{1,8},{2,11},{3,10},{4,13},{5,12},{6,15},{7,14},{8,1},{9,0},... | collective-permute-start | bytes 6152 | tf_op jit(solution)/shard_map/ppermute | solution.py:121
  30.5 23.3 %collective-permute-start.9 = (bf16[128,8]{0,1:T(8,128)(2,1)S(1)}, bf16[128,8]{0,1:T(8,128)(2,1)S(1)}, u32[]{:S(2)}, u32[]{:S(2)}) collective-permute-start(bf16[128,8]{0,1:T(8,128)(2,1)S(1)} %get-tuple-element.33), channel_id=1, source_target_pairs={{0,10},{1,11},{2,8},{3,9},{4,14},{5,15},{6,12},{7,13},{8,2},{9,3},... | collective-permute-start | bytes 6152 | tf_op jit(solution)/shard_map/ppermute | solution.py:121
  41.3 14.2 %collective-permute-start.10 = (bf16[128,8]{0,1:T(8,128)(2,1)S(1)}, bf16[128,8]{0,1:T(8,128)(2,1)S(1)}, u32[]{:S(2)}, u32[]{:S(2)}) collective-permute-start(bf16[128,8]{0,1:T(8,128)(2,1)S(1)} %get-tuple-element.32), channel_id=1, source_target_pairs={{0,11},{1,10},{2,9},{3,8},{4,15},{5,14},{6,13},{7,12},{8,3},{9,2},... | collective-permute-start | bytes 6152 | tf_op jit(solution)/shard_map/ppermute | solution.py:121
  45.8 9.8 %collective-permute-start.11 = (bf16[128,8]{0,1:T(8,128)(2,1)S(1)}, bf16[128,8]{0,1:T(8,128)(2,1)S(1)}, u32[]{:S(2)}, u32[]{:S(2)}) collective-permute-start(bf16[128,8]{0,1:T(8,128)(2,1)S(1)} %get-tuple-element.31), channel_id=1, source_target_pairs={{0,12},{1,13},{2,14},{3,15},{4,8},{5,9},{6,10},{7,11},{8,4},{9,5},... | collective-permute-start | bytes 6152 | tf_op jit(solution)/shard_map/ppermute | solution.py:121
  49.9 5.7 %collective-permute-start.12 = (bf16[128,8]{0,1:T(8,128)(2,1)S(1)}, bf16[128,8]{0,1:T(8,128)(2,1)S(1)}, u32[]{:S(2)}, u32[]{:S(2)}) collective-permute-start(bf16[128,8]{0,1:T(8,128)(2,1)S(1)} %get-tuple-element.30), channel_id=1, source_target_pairs={{0,13},{1,12},{2,15},{3,14},{4,9},{5,8},{6,11},{7,10},{8,5},{9,4},... | collective-permute-start | bytes 6152 | tf_op jit(solution)/shard_map/ppermute | solution.py:121
  50.2 6.3 %collective-permute-start.13 = (bf16[128,8]{0,1:T(8,128)(2,1)S(1)}, bf16[128,8]{0,1:T(8,128)(2,1)S(1)}, u32[]{:S(2)}, u32[]{:S(2)}) collective-permute-start(bf16[128,8]{0,1:T(8,128)(2,1)S(1)} %get-tuple-element.29), channel_id=1, source_target_pairs={{0,14},{1,15},{2,12},{3,13},{4,10},{5,11},{6,8},{7,9},{8,6},{9,7},... | collective-permute-start | bytes 6152 | tf_op jit(solution)/shard_map/ppermute | solution.py:121
  53.9 5.7 %collective-permute-start.14 = (bf16[128,8]{0,1:T(8,128)(2,1)S(1)}, bf16[128,8]{0,1:T(8,128)(2,1)S(1)}, u32[]{:S(2)}, u32[]{:S(2)}) collective-permute-start(bf16[128,8]{0,1:T(8,128)(2,1)S(1)} %get-tuple-element.28), channel_id=1, source_target_pairs={{0,15},{1,14},{2,13},{3,12},{4,11},{5,10},{6,9},{7,8},{8,7},{9,6},... | collective-permute-start | bytes 6152 | tf_op jit(solution)/shard_map/ppermute | solution.py:121
  63.7 3.2 %copy-start.13 = (bf16[1,2,768,256]{3,2,1,0:T(8,128)(2,1)S(1)}, bf16[1,2,768,256]{3,2,1,0:T(8,128)(2,1)}, u32[]{:S(2)}) copy-start(bf16[1,2,768,256]{3,2,1,0:T(8,128)(2,1)} %copy.141) | copy-start | bytes 2359300
  71.0 2.6 %copy-start.11 = (bf16[8,256,256]{2,1,0:T(8,128)(2,1)}, bf16[8,256,256]{2,1,0:T(8,128)(2,1)S(1)}, u32[]{:S(2)}) copy-start(bf16[8,256,256]{2,1,0:T(8,128)(2,1)S(1)} %get-tuple-element.46) | copy-start | bytes 3145732
  71.1 2.5 %copy-start.9 = (bf16[8,248,256]{2,1,0:T(8,128)(2,1)}, bf16[8,248,256]{2,1,0:T(8,128)(2,1)S(1)}, u32[]{:S(2)}) copy-start(bf16[8,248,256]{2,1,0:T(8,128)(2,1)S(1)} %slice.99) | copy-start | bytes 3047428
  76.1 10.0 %all-to-all-start.1 = ((f32[16,1,384]{2,1,0:T(1,128)}), f32[16,1,384]{2,1,0:T(1,128)S(1)}, u32[]{:S(2)}, u32[]{:S(2)}) async-start(f32[16,1,384]{2,1,0:T(1,128)} %broadcast_in_dim.56), calls=%async_computation.1 | async-start | bytes 49152 | tf_op jit(solution)/shard_map/all_to_all | solution.py:195
  86.2 2.4 %copy-start.4 = (f32[8,256,256]{2,1,0:T(8,128)S(1)}, f32[8,256,256]{2,1,0:T(8,128)}, u32[]{:S(2)}) copy-start(f32[8,256,256]{2,1,0:T(8,128)} %get-tuple-element.48) | copy-start | bytes 6291460
  88.6 3.7 %copy-start.10 = (bf16[8,248,256]{2,1,0:T(8,128)(2,1)S(1)}, bf16[8,248,256]{2,1,0:T(8,128)(2,1)}, u32[]{:S(2)}) copy-start(bf16[8,248,256]{2,1,0:T(8,128)(2,1)} %copy-done.9) | copy-start | bytes 3047428
  88.6 3.7 %copy-start.12 = (bf16[8,256,256]{2,1,0:T(8,128)(2,1)S(1)}, bf16[8,256,256]{2,1,0:T(8,128)(2,1)}, u32[]{:S(2)}) copy-start(bf16[8,256,256]{2,1,0:T(8,128)(2,1)} %copy-done.11) | copy-start | bytes 3145732
  101.1 2.5 %collective-permute-start.15 = (f32[2,384,256]{2,1,0:T(8,128)S(1)}, f32[2,384,256]{2,1,0:T(8,128)}, u32[]{:S(2)}, u32[]{:S(2)}) collective-permute-start(f32[2,384,256]{2,1,0:T(8,128)S(1)} %fusion.51), channel_id=1, source_target_pairs={{0,1},{1,0},{2,3},{3,2},{4,5},{5,4},{6,7},{7,6},{8,9},{9,8},{10,11... | collective-permute-start | bytes 2359304 | tf_op jit(solution)/shard_map/ppermute | solution.py:168
  105.0 7.8 %collective-permute-start.16 = (f32[2,192,256]{2,1,0:T(8,128)S(1)}, f32[2,192,256]{2,1,0:T(8,128)S(1)}, u32[]{:S(2)}, u32[]{:S(2)}) collective-permute-start(f32[2,192,256]{2,1,0:T(8,128)S(1)} %constant_dynamic-slice_fusion.1), channel_id=1, source_target_pairs={{0,2},{1,5},{2,0},{3,7},{4,6},{5,1},{6,4},{7,3},{8,10},{9,13},{10,... | collective-permute-start | bytes 1179656 | tf_op jit(solution)/shard_map/ppermute | solution.py:168
  112.9 7.8 %collective-permute-start.17 = (f32[2,96,256]{2,1,0:T(8,128)S(1)}, f32[2,96,256]{2,1,0:T(8,128)S(1)}, u32[]{:S(2)}, u32[]{:S(2)}) collective-permute-start(f32[2,96,256]{2,1,0:T(8,128)S(1)} %constant_dynamic-slice_fusion), channel_id=1, source_target_pairs={{0,4},{1,9},{2,6},{3,11},{4,0},{5,13},{6,2},{7,15},{8,12},{9,1},{1... | collective-permute-start | bytes 589832 | tf_op jit(solution)/shard_map/ppermute | solution.py:168
  120.7 5.6 %collective-permute-start.18 = (f32[2,48,256]{2,1,0:T(8,128)S(1)}, f32[2,48,256]{2,1,0:T(8,128)S(1)}, u32[]{:S(2)}, u32[]{:S(2)}) collective-permute-start(f32[2,48,256]{2,1,0:T(8,128)S(1)} %constant_dynamic-slice_fusion.18), channel_id=1, source_target_pairs={{0,8},{1,3},{2,10},{3,1},{4,12},{5,7},{6,14},{7,5},{8,0},{9,11},{1... | collective-permute-start | bytes 294920 | tf_op jit(solution)/shard_map/ppermute | solution.py:168
  126.4 5.6 %collective-permute-start.19 = (bf16[2,48,256]{2,1,0:T(8,128)(2,1)S(1)}, bf16[2,48,256]{2,1,0:T(8,128)(2,1)S(1)}, u32[]{:S(2)}, u32[]{:S(2)}) collective-permute-start(bf16[2,48,256]{2,1,0:T(8,128)(2,1)S(1)} %add_convert_fusion.2), channel_id=1, source_target_pairs={{0,8},{1,3},{2,10},{3,1},{4,12},{5,7},{6,14},{7,5},{8,0},{9,11},{1... | collective-permute-start | bytes 147464 | tf_op jit(solution)/shard_map/ppermute | solution.py:172
  132.0 5.7 %collective-permute-start.20 = (bf16[2,96,256]{2,1,0:T(8,128)(2,1)S(1)}, bf16[2,96,256]{2,1,0:T(8,128)(2,1)S(1)}, u32[]{:S(2)}, u32[]{:S(2)}) collective-permute-start(bf16[2,96,256]{2,1,0:T(8,128)(2,1)S(1)} %pad_maximum_fusion.2), channel_id=1, source_target_pairs={{0,4},{1,9},{2,6},{3,11},{4,0},{5,13},{6,2},{7,15},{8,12},{9,1},{1... | collective-permute-start | bytes 294920 | tf_op jit(solution)/shard_map/ppermute | solution.py:172
  137.7 5.7 %collective-permute-start.21 = (bf16[2,192,256]{2,1,0:T(8,128)(2,1)S(1)}, bf16[2,192,256]{2,1,0:T(8,128)(2,1)S(1)}, u32[]{:S(2)}, u32[]{:S(2)}) collective-permute-start(bf16[2,192,256]{2,1,0:T(8,128)(2,1)S(1)} %pad_maximum_fusion.1), channel_id=1, source_target_pairs={{0,2},{1,5},{2,0},{3,7},{4,6},{5,1},{6,4},{7,3},{8,10},{9,13},{10,... | collective-permute-start | bytes 589832 | tf_op jit(solution)/shard_map/ppermute | solution.py:172
  143.6 1.8 %collective-permute-start.22 = (bf16[2,384,256]{2,1,0:T(8,128)(2,1)S(1)}, bf16[2,384,256]{2,1,0:T(8,128)(2,1)S(1)}, u32[]{:S(2)}, u32[]{:S(2)}) collective-permute-start(bf16[2,384,256]{2,1,0:T(8,128)(2,1)S(1)} %pad_maximum_fusion), channel_id=1, source_target_pairs={{0,1},{1,0},{2,3},{3,2},{4,5},{5,4},{6,7},{7,6},{8,9},{9,8},{10,11... | collective-permute-start | bytes 1179656 | tf_op jit(solution)/shard_map/ppermute | solution.py:172
  (10 other events, 15.6 us)

commit v14 on v8

--- a/solution.py
+++ b/solution.py
@@ -72,6 +72,44 @@
     before = (steps[:, None] > steps[None, :]).astype(jnp.bfloat16)
     offsets = jnp.dot(before, totals, preferred_element_type=jnp.float32)
     return (within + offsets[:, None, :]).reshape(rows, width).astype(jnp.int32)
+
+
+def run_pair(states, teacher_w, student_w):
+    width = states.shape[2]
+    stacked = jnp.concatenate([delayed(states, tap_index) for tap_index in range(KER)], axis=2)
+    joint = jnp.dot(
+        stacked.reshape(-1, stacked.shape[2]),
+        jnp.concatenate([teacher_w[0], student_w[0]], axis=1),
+        preferred_element_type=jnp.float32,
+    )
+    teacher_pre = joint[:, :width].reshape(states.shape)
+    student_pre = joint[:, width:].reshape(states.shape)
+    base = states.astype(jnp.float32)
+    teacher_h = (base + jax.nn.silu(teacher_pre)).astype(jnp.bfloat16)
+    student_h = (base + jax.nn.silu(student_pre)).astype(jnp.bfloat16)
+    stacked_list = [stacked]
+    preacts = [student_pre]
+    for layer_at in range(1, student_w.shape[0]):
+        offset = 4**layer_at
+        for is_student in (False, True):
+            current = student_h if is_student else teacher_h
+            weights = student_w if is_student else teacher_w
+            layered = jnp.concatenate(
+                [delayed(current, tap_index * offset) for tap_index in range(KER)], axis=2
+            )
+            preact = jnp.dot(
+                layered.reshape(-1, layered.shape[2]),
+                weights[layer_at],
+                preferred_element_type=jnp.float32,
+            ).reshape(states.shape)
+            updated = (current.astype(jnp.float32) + jax.nn.silu(preact)).astype(jnp.bfloat16)
+            if is_student:
+                student_h = updated
+                stacked_list.append(layered)
+                preacts.append(preact)
+            else:
+                teacher_h = updated
+    return (teacher_h, student_h, stacked_list, preacts)
 
 
 def route_rows(epoch_rows, row_object, object_slot):
@@ -182,8 +220,7 @@
     valid_mask = (jnp.arange(SEQ, dtype=jnp.int32)[None, :] < counts[:, None]).astype(jnp.float32)[
         :, :, None
     ]
-    teacher_out = run_network(sequences, teacher_w)[0]
-    student_out, stacked_list, preacts = run_network(sequences, student_w)
+    teacher_out, student_out, stacked_list, preacts = run_pair(sequences, teacher_w, student_w)
     partial_sum = jnp.sum(valid_mask * teacher_out.astype(jnp.float32), axis=(0, 1))
     number = jnp.sum(counts).astype(jnp.float32)
     wide_count = lax.axis_size("wide")

time: 147 us -> 152 us (1.034)
  local copies, waits for them, and re-layouts: 13.5 us -> 19.3 us
  waiting for transfers between devices: 70 us -> 67.2 us
  other arithmetic: 18.1 us -> 19.8 us
    all_to_all x1, waiting for transfers between devices: 18.8 us -> 16.3 us  [route_rows(): lax.all_to_all(send_rows.reshape(wide_count, capacity, feat_width), 'wide...]
    optimization_barrier x0 -> x2, local copies, waits for them, and re-layouts: none -> 1.67 us  [the longest x1 1.4 us: local(): lax.optimization_barrier(master.reshape(layer_total, KER * feat_width, fe...]
    squeeze x0 -> x2, local copies, waits for them, and re-layouts: none -> 1.65 us  [the longest x1 0.87 us: run_pair(): student_w[0]]
    dot_general x4 -> x3, matrix products: 8.34 us -> 6.79 us  [the longest x2 4.97 us: run_pair(): jnp.dot(layered.reshape(-1, layered.shape[2]), weights[layer_at], preferr...]
    unnamed x39 -> x63, local copies, waits for them, and re-layouts: 6.55 us -> 7.13 us
  transfers between devices with their start and end apart: 11 -> 11, of which waited for: 11 -> 11; matrix products, arithmetic and copies ran while one was open for 4% -> 6% of each run, Pallas kernels for 0% -> 0%
where the time goes in v14:
time: 152 us; the launch traced here: 151 us
  waiting for transfers between devices  67.2 us (44%)
  matrix products  21.8 us (14%)
  starting transfers between devices  20.5 us (13%)
  other arithmetic  19.8 us (13%)
  local copies, waits for them, and re-layouts  19.3 us (13%)
  between operations  2.02 us (1%)
    ppermute x4, waiting for transfers between devices, all_reduce_wide(): buf = keep + lax.ppermute(send, 'wide', pairs)  22.5 us
    ppermute x4, waiting for transfers between devices, all_reduce_wide(): got = lax.ppermute(buf, 'wide', pairs)  17.4 us
    all_to_all x1, waiting for transfers between devices, route_rows(): lax.all_to_all(send_rows.reshape(wide_count, capacity, feat_width), 'wide...  16.3 us
    all_to_all x1, starting transfers between devices, route_rows(): lax.all_to_all(send_place.reshape(wide_count, capacity, per_dev), 'wide',...  7.36 us
    unnamed x63, local copies, waits for them, and re-layouts  7.13 us
    all_to_all x1, starting transfers between devices, local(): lax.all_to_all(jnp.broadcast_to(stats[None, :], (wide_count, stats.shape[...  6.87 us
    all_to_all x1, waiting for transfers between devices, local(): lax.all_to_all(jnp.broadcast_to(stats[None, :], (wide_count, stats.shape[...  5.66 us
    all_to_all x1, waiting for transfers between devices, route_rows(): lax.all_to_all(send_place.reshape(wide_count, capacity, per_dev), 'wide',...  5.38 us
  transfers between devices with their start and end apart: 11, of which 11 were waited for; matrix products, arithmetic and copies ran while one was open for 6% of the time, Pallas kernels for 0%

profile of v14, /device:TPU:0, one launch (start us, length us, event | category | flops | bytes accessed | tf_op | source)
XLA Modules:
  0.0 150.6 jit_solution(12268748900845291505)
XLA Ops:
  2.7 1.3 select_reduce_fusion
  5.7 4.8 %fusion.27 = bf16[2048,264]{0,1:T(8,128)(2,1)S(1)} fusion(s32[2048]{0:T(1024)S(1)} %get-tuple-element.35, bf16[2048,8]{1,0:T(8,128)(2,1)S(1)} %copy.106, bf16[2048,256]{1,0:T(8,128)(2,1)} %param.6), kind=kOutput, calls=%fused_computation.37 | convolution fusion | flops 2221490176 | bytes 2170880 | tf_op jit(solution)/shard_map/dot_general | solution.py:140
  11.2 7.4 %all-to-all-start = ((bf16[16,128,8]{1,2,0:T(8,128)(2,1)}), bf16[16,128,8]{1,2,0:T(8,128)(2,1)S(1)}, u32[]{:S(2)}, u32[]{:S(2)}) async-start(bf16[16,128,8]{1,2,0:T(8,128)(2,1)} %slice_bitcast_fusion.8), calls=%async_computation | async-start | bytes 65536 | tf_op jit(solution)/shard_map/all_to_all | solution.py:153
  18.5 1.2 copy_bitcast_fusion.2
  19.8 5.4 %all-to-all-done = bf16[16,128,8]{1,2,0:T(8,128)(2,1)S(1)} async-done(((bf16[16,128,8]{1,2,0:T(8,128)(2,1)}), bf16[16,128,8]{1,2,0:T(8,128)(2,1)S(1)}, u32[]{:S(2)}, u32[]{:S(2)}) %all-to-all-start) | async-done | bytes 32800 | tf_op jit(solution)/shard_map/all_to_all | solution.py:153
  25.8 4.5 %all-to-all-start.1 = ((bf16[16,128,256]{1,2,0:T(8,128)(2,1)}), bf16[16,128,256]{1,2,0:T(8,128)(2,1)}, u32[]{:S(2)}, u32[]{:S(2)}) async-start(bf16[16,128,256]{1,2,0:T(8,128)(2,1)} %copy_bitcast_fusion.2), calls=%async_computation.1 | async-start | bytes 2097152 | tf_op jit(solution)/shard_map/all_to_all | solution.py:146
  30.3 1.0 copy.142
  31.3 1.4 copy.112
  36.8 16.3 %all-to-all-done.1 = bf16[16,128,256]{1,2,0:T(8,128)(2,1)} async-done(((bf16[16,128,256]{1,2,0:T(8,128)(2,1)}), bf16[16,128,256]{1,2,0:T(8,128)(2,1)}, u32[]{:S(2)}, u32[]{:S(2)}) %all-to-all-start.1) | async-done | bytes 1048608 | tf_op jit(solution)/shard_map/all_to_all | solution.py:146
  53.1 2.3 %copy.110 = bf16[16,128,256]{2,1,0:T(8,128)(2,1)} copy(bf16[16,128,256]{1,2,0:T(8,128)(2,1)} %all-to-all-done.1) | data formatting | bytes 2097152 | tf_op jit(solution)/shard_map/all_to_all | solution.py:146
  55.3 4.4 %fusion.28 = bf16[2048,256]{1,0:T(8,128)(2,1)S(1)} fusion(bf16[2048,256]{1,0:T(8,128)(2,1)} %bitcast.150, s32[2048]{0:T(1024)S(1)} %select_bitcast_fusion), kind=kOutput, calls=%fused_computation.38 | convolution fusion | flops 2152202240 | bytes 2105344 | tf_op jit(solution)/shard_map/dot_general | solution.py:172
  60.9 1.8 %fusion.19 = f32[2048,512]{1,0:T(8,128)S(1)} fusion(bf16[2048,256]{1,0:T(8,128)(2,1)S(1)} %bitcast.149, bf16[2048,256]{1,0:T(8,128)(2,1)S(1)} %bitcast.148, bf16[2048,256]{1,0:T(8,128)(2,1)S(1)} %fusion.28, bf16[768,256]{0,1:T(8,128)(2,1)S(1)} %copy-done.23, bf16[768,256]{0,1:T(8,128)(2,1)S(1)} %copy-done.22), kind=kOutput, calls=%fused_computation.24 | convolution fusion | flops 1621622784 | bytes 8126464 | tf_op jit(solution)/shard_map/dot_general | solution.py:80
  63.1 1.1 fusion.30
  64.8 2.5 %fusion.108 = (bf16[8,256]{1,0:T(8,128)(2,1)S(1)}, bf16[8,256,256]{2,1,0:T(8,128)(2,1)S(1)}, f32[8,256,256]{2,1,0:T(8,128)}) fusion(bf16[8,256,256]{2,1,0:T(8,128)(2,1)S(1)} %get-tuple-element.23, bf16[2,768,256]{1,2,0:T(8,128)(2,1)S(1)} %copy-done.7, bf16[8,248,256]{2,1,0:T(8,128)(2,1)S(1)} %slice.105, bf16[8,252,256]{2,1,0:T(8,128)(2,1)S(1)} %bitcast.142), kind=kOutput, calls=%fused_computation.183 | convolution fusion | flops 828372992 | bytes 7704576 | tf_op jit(solution)/shard_map/dot_general | solution.py:100
  67.4 2.5 %fusion.37 = (f32[8,256]{1,0:T(8,128)}, f32[8,256]{1,0:T(8,128)}, f32[256]{0:T(256)S(1)}, bf16[8,256,256]{2,1,0:T(8,128)(2,1)S(1)}) fusion(bf16[8,256,256]{2,1,0:T(8,128)(2,1)S(1)} %get-tuple-element.15, f32[8,256]{1,0:T(8,128)S(1)} %fusion.91, f32[8,256]{1,0:T(8,128)S(1)} %bitcast.151, bf16[2,768,256]{1,2,0:T(8,128)(2,1)S(1)} %copy-done.11, ...), kind=kOutput, calls=%fused_computation.47 | convolution fusion | flops 832040704 | bytes 6685696 | tf_op jit(solution)/shard_map/dot_general | solution.py:100
  70.5 6.9 %all-to-all-start.2 = ((f32[16,1,384]{2,1,0:T(1,128)}), f32[16,1,384]{2,1,0:T(1,128)}, u32[]{:S(2)}, u32[]{:S(2)}) async-start(f32[16,1,384]{2,1,0:T(1,128)} %broadcast_in_dim.40), calls=%async_computation.2 | async-start | bytes 49152 | tf_op jit(solution)/shard_map/all_to_all | solution.py:228
  78.3 5.7 %all-to-all-done.2 = f32[16,1,384]{2,1,0:T(1,128)} async-done(((f32[16,1,384]{2,1,0:T(1,128)}), f32[16,1,384]{2,1,0:T(1,128)}, u32[]{:S(2)}, u32[]{:S(2)}) %all-to-all-start.2) | async-done | bytes 24608 | tf_op jit(solution)/shard_map/all_to_all | solution.py:228
  87.2 3.6 %multiply_convert_fusion = bf16[8,256,256]{2,1,0:T(8,128)(2,1)S(1)} fusion(f32[8,256,256]{2,1,0:T(8,128)S(1)} %copy-done.9, f32[8,256]{1,0:T(8,128)S(1)} %fusion.44, f32[8,256]{1,0:T(8,128)S(1)} %fusion.41, f32[256]{0:T(256)S(1)} %slice_divide_fusion, bf16[8,256,256]{2,1,0:T(8,128)(2,1)S(1)} %get-tuple-element.37, f32[8,256]{1,0:T(8,128)S(1)} %copy-done.26, ...), kind=kLoop, calls=%fused_computation.63 | loop fusion | flops 10485760 | bytes 5284864 | tf_op jit(solution)/shard_map/convert_element_type | solution.py:243
  90.8 1.0 convolution_bitcast_fusion
  91.9 1.0 fusion.57
  95.9 3.2 %fusion.54 = f32[1,768,256]{2,1,0:T(8,128)S(1)} fusion(bf16[8,256,256]{2,1,0:T(8,128)(2,1)S(1)} %copy-done.17, bf16[8,256,256]{2,1,0:T(8,128)(2,1)S(1)} %copy-done.15, bf16[8,256,256]{2,1,0:T(8,128)(2,1)S(1)} %bitcast.135, f32[8,256,3,256]{3,1,0,2:T(8,128)S(1)} %fusion.57, f32[8,256,256]{2,1,0:T(8,128)S(1)} %bitcast.137, f32[8,248,256]{2,1,0:T(8,128)S(1)} %slice.115, ...), kind=kOutput, calls=%fused_computation.83 | convolution fusion | flops 826802176 | bytes 14394368 | tf_op jit(solution)/shard_map/dot_general | solution.py:245
  99.3 2.3 %collective-permute-done = f32[2,384,256]{2,1,0:T(8,128)S(1)} collective-permute-done((f32[2,384,256]{2,1,0:T(8,128)S(1)}, f32[2,384,256]{2,1,0:T(8,128)S(1)}, u32[]{:S(2)}, u32[]{:S(2)}) %collective-permute-start) | collective-permute-done | bytes 786464 | tf_op jit(solution)/shard_map/ppermute | solution.py:202
  101.5 1.1 fusion.64
  103.1 7.4 %collective-permute-done.1 = f32[2,192,256]{2,1,0:T(8,128)S(1)} collective-permute-done((f32[2,192,256]{2,1,0:T(8,128)S(1)}, f32[2,192,256]{2,1,0:T(8,128)S(1)}, u32[]{:S(2)}, u32[]{:S(2)}) %collective-permute-start.1) | collective-permute-done | bytes 393248 | tf_op jit(solution)/shard_map/ppermute | solution.py:202
  111.1 7.3 %collective-permute-done.2 = f32[2,96,256]{2,1,0:T(8,128)S(1)} collective-permute-done((f32[2,96,256]{2,1,0:T(8,128)S(1)}, f32[2,96,256]{2,1,0:T(8,128)S(1)}, u32[]{:S(2)}, u32[]{:S(2)}) %collective-permute-start.2) | collective-permute-done | bytes 196640 | tf_op jit(solution)/shard_map/ppermute | solution.py:202
  118.5 5.5 %collective-permute-done.3 = f32[2,48,256]{2,1,0:T(8,128)S(1)} collective-permute-done((f32[2,48,256]{2,1,0:T(8,128)S(1)}, f32[2,48,256]{2,1,0:T(8,128)S(1)}, u32[]{:S(2)}, u32[]{:S(2)}) %collective-permute-start.3) | collective-permute-done | bytes 98336 | tf_op jit(solution)/shard_map/ppermute | solution.py:202
  124.2 5.5 %collective-permute-done.4 = bf16[2,48,256]{2,1,0:T(8,128)(2,1)S(1)} collective-permute-done((bf16[2,48,256]{2,1,0:T(8,128)(2,1)S(1)}, bf16[2,48,256]{2,1,0:T(8,128)(2,1)S(1)}, u32[]{:S(2)}, u32[]{:S(2)}) %collective-permute-start.4) | collective-permute-done | bytes 49184 | tf_op jit(solution)/shard_map/ppermute | solution.py:206
  129.8 5.6 %collective-permute-done.5 = bf16[2,96,256]{2,1,0:T(8,128)(2,1)S(1)} collective-permute-done((bf16[2,96,256]{2,1,0:T(8,128)(2,1)S(1)}, bf16[2,96,256]{2,1,0:T(8,128)(2,1)S(1)}, u32[]{:S(2)}, u32[]{:S(2)}) %collective-permute-start.5) | collective-permute-done | bytes 98336 | tf_op jit(solution)/shard_map/ppermute | solution.py:206
  135.9 5.3 %collective-permute-done.6 = bf16[2,192,256]{2,1,0:T(8,128)(2,1)S(1)} collective-permute-done((bf16[2,192,256]{2,1,0:T(8,128)(2,1)S(1)}, bf16[2,192,256]{2,1,0:T(8,128)(2,1)S(1)}, u32[]{:S(2)}, u32[]{:S(2)}) %collective-permute-start.6) | collective-permute-done | bytes 196640 | tf_op jit(solution)/shard_map/ppermute | solution.py:206
  142.1 1.0 collective-permute-done.7
  143.4 1.2 copy.138
  145.6 5.0 %multiply_add_fusion = (f32[2,196608]{1,0:T(2,128)}, f32[2,196608]{1,0:T(2,128)}, f32[2,196608]{1,0:T(2,128)}) fusion(f32[2,196608]{1,0:T(2,128)S(1)} %copy-done.3, f32[2,196608]{1,0:T(2,128)S(1)} %copy-done.5, f32[2,196608]{1,0:T(2,128)S(1)} %bitcast.141, f32[2,196608]{1,0:T(2,128)S(1)} %copy-done.12), kind=kLoop, calls=%fused_computation.79 | loop fusion | flops 2752512 | bytes 11010048 | tf_op jit(solution)/shard_map/add | solution.py:266
  (128 shorter events, 22.2 us)
Async XLA Ops:
  11.2 14.0 %all-to-all-start = ((bf16[16,128,8]{1,2,0:T(8,128)(2,1)}), bf16[16,128,8]{1,2,0:T(8,128)(2,1)S(1)}, u32[]{:S(2)}, u32[]{:S(2)}) async-start(bf16[16,128,8]{1,2,0:T(8,128)(2,1)} %slice_bitcast_fusion.8), calls=%async_computation | async-start | bytes 65536 | tf_op jit(solution)/shard_map/all_to_all | solution.py:153
  18.5 11.8 %copy-start.4 = (f32[2,196608]{1,0:T(2,128)S(1)}, f32[2,196608]{1,0:T(2,128)}, u32[]{:S(2)}) copy-start(f32[2,196608]{1,0:T(2,128)} %param.9) | copy-start | bytes 4718596
  25.8 27.3 %all-to-all-start.1 = ((bf16[16,128,256]{1,2,0:T(8,128)(2,1)}), bf16[16,128,256]{1,2,0:T(8,128)(2,1)}, u32[]{:S(2)}, u32[]{:S(2)}) async-start(bf16[16,128,256]{1,2,0:T(8,128)(2,1)} %copy_bitcast_fusion.2), calls=%async_computation.1 | async-start | bytes 2097152 | tf_op jit(solution)/shard_map/all_to_all | solution.py:146
  30.3 2.4 %copy-start.2 = (f32[2,196608]{1,0:T(2,128)S(1)}, f32[2,196608]{1,0:T(2,128)}, u32[]{:S(2)}) copy-start(f32[2,196608]{1,0:T(2,128)} %param.11) | copy-start | bytes 4718596
  32.8 2.0 %copy-start.25 = (bf16[16,128,8]{1,2,0:T(8,128)(2,1)S(1)}, bf16[16,128,8]{1,2,0:T(8,128)(2,1)}, u32[]{:S(2)}) copy-start(bf16[16,128,8]{1,2,0:T(8,128)(2,1)} %copy-done.24) | copy-start | bytes 98308
  33.1 22.2 %copy-start.10 = (bf16[2,768,256]{1,2,0:T(8,128)(2,1)}, bf16[2,768,256]{1,2,0:T(8,128)(2,1)S(1)}, u32[]{:S(2)}) copy-start(bf16[2,768,256]{1,2,0:T(8,128)(2,1)S(1)} %copy.111) | copy-start | bytes 2359300
  36.0 23.7 %copy-start.28 = (s32[8]{0:T(128)}, s32[8]{0:T(128)S(1)}, u32[]{:S(2)}) copy-start(s32[8]{0:T(128)S(1)} %get-tuple-element.7) | copy-start | bytes 100
  60.0 2.7 %copy-start.14 = (bf16[8,256,256]{2,1,0:T(8,128)(2,1)}, bf16[8,256,256]{2,1,0:T(8,128)(2,1)S(1)}, u32[]{:S(2)}) copy-start(bf16[8,256,256]{2,1,0:T(8,128)(2,1)S(1)} %concatenate.62) | copy-start | bytes 3145732
  60.3 2.4 %copy-start.16 = (bf16[8,256,256]{2,1,0:T(8,128)(2,1)}, bf16[8,256,256]{2,1,0:T(8,128)(2,1)S(1)}, u32[]{:S(2)}) copy-start(bf16[8,256,256]{2,1,0:T(8,128)(2,1)S(1)} %concatenate.63) | copy-start | bytes 3145732
  63.1 1.7 %copy-start.7 = (bf16[2,768,256]{1,2,0:T(8,128)(2,1)S(1)}, bf16[2,768,256]{1,2,0:T(8,128)(2,1)}, u32[]{:S(2)}) copy-start(bf16[2,768,256]{1,2,0:T(8,128)(2,1)} %copy-done.6) | copy-start | bytes 2359300
  64.4 2.8 %copy-start.20 = (bf16[8,248,256]{2,1,0:T(8,128)(2,1)}, bf16[8,248,256]{2,1,0:T(8,128)(2,1)S(1)}, u32[]{:S(2)}) copy-start(bf16[8,248,256]{2,1,0:T(8,128)(2,1)S(1)} %slice.105) | copy-start | bytes 3047428
  64.8 2.6 %copy-start.11 = (bf16[2,768,256]{1,2,0:T(8,128)(2,1)S(1)}, bf16[2,768,256]{1,2,0:T(8,128)(2,1)}, u32[]{:S(2)}) copy-start(bf16[2,768,256]{1,2,0:T(8,128)(2,1)} %copy-done.10) | copy-start | bytes 2359300
  67.3 2.6 %copy-start.18 = (bf16[8,256,256]{2,1,0:T(8,128)(2,1)}, bf16[8,256,256]{2,1,0:T(8,128)(2,1)S(1)}, u32[]{:S(2)}) copy-start(bf16[8,256,256]{2,1,0:T(8,128)(2,1)S(1)} %get-tuple-element.15) | copy-start | bytes 3145732
  70.5 13.5 %all-to-all-start.2 = ((f32[16,1,384]{2,1,0:T(1,128)}), f32[16,1,384]{2,1,0:T(1,128)}, u32[]{:S(2)}, u32[]{:S(2)}) async-start(f32[16,1,384]{2,1,0:T(1,128)} %broadcast_in_dim.40), calls=%async_computation.2 | async-start | bytes 49152 | tf_op jit(solution)/shard_map/all_to_all | solution.py:228
  78.3 8.9 %copy-start.26 = (f32[8,256]{1,0:T(8,128)S(1)}, f32[8,256]{1,0:T(8,128)}, u32[]{:S(2)}) copy-start(f32[8,256]{1,0:T(8,128)} %get-tuple-element.5) | copy-start | bytes 24580
  84.7 2.4 %copy-start.9 = (f32[8,256,256]{2,1,0:T(8,128)S(1)}, f32[8,256,256]{2,1,0:T(8,128)}, u32[]{:S(2)}) copy-start(f32[8,256,256]{2,1,0:T(8,128)} %get-tuple-element.36) | copy-start | bytes 6291460
  87.2 3.6 %copy-start.21 = (bf16[8,248,256]{2,1,0:T(8,128)(2,1)S(1)}, bf16[8,248,256]{2,1,0:T(8,128)(2,1)}, u32[]{:S(2)}) copy-start(bf16[8,248,256]{2,1,0:T(8,128)(2,1)} %copy-done.20) | copy-start | bytes 3047428
  91.9 7.2 %copy-start.8 = (f32[1,768,256]{2,1,0:T(8,128)}, f32[1,768,256]{2,1,0:T(8,128)S(1)}, u32[]{:S(2)}) copy-start(f32[1,768,256]{2,1,0:T(8,128)S(1)} %convolution_bitcast_fusion) | copy-start | bytes 2359300
  93.6 2.1 %copy-start.1 = (f32[2048,256]{1,0:T(8,128)S(1)}, f32[2048,256]{1,0:T(8,128)}, u32[]{:S(2)}) copy-start(f32[2048,256]{1,0:T(8,128)} %copy-done) | copy-start | bytes 6291460
  93.6 2.3 %copy-start.15 = (bf16[8,256,256]{2,1,0:T(8,128)(2,1)S(1)}, bf16[8,256,256]{2,1,0:T(8,128)(2,1)}, u32[]{:S(2)}) copy-start(bf16[8,256,256]{2,1,0:T(8,128)(2,1)} %copy-done.14) | copy-start | bytes 3145732
  99.2 2.4 %collective-permute-start = (f32[2,384,256]{2,1,0:T(8,128)S(1)}, f32[2,384,256]{2,1,0:T(8,128)S(1)}, u32[]{:S(2)}, u32[]{:S(2)}) collective-permute-start(f32[2,384,256]{2,1,0:T(8,128)S(1)} %fusion.62), channel_id=1, source_target_pairs={{0,1},{1,0},{2,3},{3,2},{4,5},{5,4},{6,7},{7,6},{8,9},{9,8},{10,11... | collective-permute-start | bytes 2359304 | tf_op jit(solution)/shard_map/ppermute | solution.py:202
  102.7 7.8 %collective-permute-start.1 = (f32[2,192,256]{2,1,0:T(8,128)S(1)}, f32[2,192,256]{2,1,0:T(8,128)S(1)}, u32[]{:S(2)}, u32[]{:S(2)}) collective-permute-start(f32[2,192,256]{2,1,0:T(8,128)S(1)} %constant_dynamic-slice_fusion.1), channel_id=1, source_target_pairs={{0,2},{1,5},{2,0},{3,7},{4,6},{5,1},{6,4},{7,3},{8,10},{9,13},{10,... | collective-permute-start | bytes 1179656 | tf_op jit(solution)/shard_map/ppermute | solution.py:202
  110.6 30.8 %copy-start.29 = (s32[8]{0:T(128)S(1)}, s32[8]{0:T(128)}, u32[]{:S(2)}) copy-start(s32[8]{0:T(128)} %copy-done.28) | copy-start | bytes 100
  110.6 30.8 %copy-start.27 = (f32[8,256]{1,0:T(8,128)S(1)}, f32[8,256]{1,0:T(8,128)}, u32[]{:S(2)}) copy-start(f32[8,256]{1,0:T(8,128)} %get-tuple-element.4) | copy-start | bytes 24580
  110.6 7.8 %collective-permute-start.2 = (f32[2,96,256]{2,1,0:T(8,128)S(1)}, f32[2,96,256]{2,1,0:T(8,128)S(1)}, u32[]{:S(2)}, u32[]{:S(2)}) collective-permute-start(f32[2,96,256]{2,1,0:T(8,128)S(1)} %constant_dynamic-slice_fusion), channel_id=1, source_target_pairs={{0,4},{1,9},{2,6},{3,11},{4,0},{5,13},{6,2},{7,15},{8,12},{9,1},{1... | collective-permute-start | bytes 589832 | tf_op jit(solution)/shard_map/ppermute | solution.py:202
  118.4 5.6 %collective-permute-start.3 = (f32[2,48,256]{2,1,0:T(8,128)S(1)}, f32[2,48,256]{2,1,0:T(8,128)S(1)}, u32[]{:S(2)}, u32[]{:S(2)}) collective-permute-start(f32[2,48,256]{2,1,0:T(8,128)S(1)} %constant_dynamic-slice_fusion.2), channel_id=1, source_target_pairs={{0,8},{1,3},{2,10},{3,1},{4,12},{5,7},{6,14},{7,5},{8,0},{9,11},{1... | collective-permute-start | bytes 294920 | tf_op jit(solution)/shard_map/ppermute | solution.py:202
  124.1 5.6 %collective-permute-start.4 = (bf16[2,48,256]{2,1,0:T(8,128)(2,1)S(1)}, bf16[2,48,256]{2,1,0:T(8,128)(2,1)S(1)}, u32[]{:S(2)}, u32[]{:S(2)}) collective-permute-start(bf16[2,48,256]{2,1,0:T(8,128)(2,1)S(1)} %add_convert_fusion.2), channel_id=1, source_target_pairs={{0,8},{1,3},{2,10},{3,1},{4,12},{5,7},{6,14},{7,5},{8,0},{9,11},{1... | collective-permute-start | bytes 147464 | tf_op jit(solution)/shard_map/ppermute | solution.py:206
  129.7 5.7 %collective-permute-start.5 = (bf16[2,96,256]{2,1,0:T(8,128)(2,1)S(1)}, bf16[2,96,256]{2,1,0:T(8,128)(2,1)S(1)}, u32[]{:S(2)}, u32[]{:S(2)}) collective-permute-start(bf16[2,96,256]{2,1,0:T(8,128)(2,1)S(1)} %pad_maximum_fusion.2), channel_id=1, source_target_pairs={{0,4},{1,9},{2,6},{3,11},{4,0},{5,13},{6,2},{7,15},{8,12},{9,1},{1... | collective-permute-start | bytes 294920 | tf_op jit(solution)/shard_map/ppermute | solution.py:206
  135.5 5.7 %collective-permute-start.6 = (bf16[2,192,256]{2,1,0:T(8,128)(2,1)S(1)}, bf16[2,192,256]{2,1,0:T(8,128)(2,1)S(1)}, u32[]{:S(2)}, u32[]{:S(2)}) collective-permute-start(bf16[2,192,256]{2,1,0:T(8,128)(2,1)S(1)} %pad_maximum_fusion.1), channel_id=1, source_target_pairs={{0,2},{1,5},{2,0},{3,7},{4,6},{5,1},{6,4},{7,3},{8,10},{9,13},{10,... | collective-permute-start | bytes 589832 | tf_op jit(solution)/shard_map/ppermute | solution.py:206
  141.3 1.8 %collective-permute-start.7 = (bf16[2,384,256]{2,1,0:T(8,128)(2,1)S(1)}, bf16[2,384,256]{2,1,0:T(8,128)(2,1)S(1)}, u32[]{:S(2)}, u32[]{:S(2)}) collective-permute-start(bf16[2,384,256]{2,1,0:T(8,128)(2,1)S(1)} %pad_maximum_fusion), channel_id=1, source_target_pairs={{0,1},{1,0},{2,3},{3,2},{4,5},{5,4},{6,7},{7,6},{8,9},{9,8},{10,11... | collective-permute-start | bytes 1179656 | tf_op jit(solution)/shard_map/ppermute | solution.py:206
  143.4 1.8 %copy-start.3 = (f32[2,196608]{1,0:T(2,128)S(1)}, f32[2,196608]{1,0:T(2,128)}, u32[]{:S(2)}) copy-start(f32[2,196608]{1,0:T(2,128)} %param.11) | copy-start | bytes 4718596
  143.4 2.2 %copy-start.5 = (f32[2,196608]{1,0:T(2,128)S(1)}, f32[2,196608]{1,0:T(2,128)}, u32[]{:S(2)}) copy-start(f32[2,196608]{1,0:T(2,128)} %param.9) | copy-start | bytes 4718596
  (9 other events, 10.6 us)

commit v15 on v8

--- a/solution.py
+++ b/solution.py
@@ -99,11 +99,8 @@
     place_hot = (
         (local_place[:, None] == jnp.arange(per_dev, dtype=jnp.int32)[None, :]) & live_rows[:, None]
     ).astype(jnp.bfloat16)
-    sent = jnp.dot(
-        pick, jnp.concatenate([epoch_rows, place_hot], axis=1), preferred_element_type=jnp.float32
-    ).astype(jnp.bfloat16)
-    send_rows = sent[:, :feat_width]
-    send_place = sent[:, feat_width:]
+    send_place = jnp.dot(pick, place_hot, preferred_element_type=jnp.float32).astype(jnp.bfloat16)
+    send_rows = jnp.dot(pick, epoch_rows, preferred_element_type=jnp.float32).astype(jnp.bfloat16)
     got_rows, got_place = (
         lax.all_to_all(
             send_rows.reshape(wide_count, capacity, feat_width),

time: 147 us -> 145 us (0.986)
  matrix products: 22.1 us -> 26.4 us
  local copies, waits for them, and re-layouts: 13.5 us -> 9.27 us
  waiting for transfers between devices: 70 us -> 68 us
    dot_general x1 -> x2, matrix products: 4.85 us -> 7.9 us  [the longest x1 4.15 us: route_rows(): jnp.dot(pick, epoch_rows, preferred_element_type=jnp.float32)]
    all_to_all x1, waiting for transfers between devices: 5.38 us -> 2.47 us  [route_rows(): lax.all_to_all(send_place.reshape(wide_count, capacity, per_dev), 'wide',...]
    reshape x2 -> x0, local copies, waits for them, and re-layouts: 1.87 us -> none  [the longest x1 1.24 us: route_rows(): send_rows.reshape(wide_count, capacity, feat_width)]
    all_to_all x1 -> x0, local copies, waits for them, and re-layouts: 1.48 us -> none  [route_rows(): lax.all_to_all(send_rows.reshape(wide_count, capacity, feat_width), 'wide...]
  transfers between devices with their start and end apart: 11 -> 11, of which waited for: 11 -> 11; matrix products, arithmetic and copies ran while one was open for 4% -> 5% of each run, Pallas kernels for 0% -> 0%
where the time goes in v15:
time: 145 us; the launch traced here: 144 us
  waiting for transfers between devices  68 us (47%)
  matrix products  26.4 us (18%)
  starting transfers between devices  20.4 us (14%)
  other arithmetic  18.4 us (13%)
  local copies, waits for them, and re-layouts  9.27 us (6%)
  between operations  1.84 us (1%)
    ppermute x4, waiting for transfers between devices, all_reduce_wide(): buf = keep + lax.ppermute(send, 'wide', pairs)  22.6 us
    all_to_all x1, waiting for transfers between devices, route_rows(): lax.all_to_all(send_rows.reshape(wide_count, capacity, feat_width), 'wide...  19 us
    ppermute x4, waiting for transfers between devices, all_reduce_wide(): got = lax.ppermute(buf, 'wide', pairs)  17.4 us
    dot_general x4, matrix products, run_network(): jnp.dot(stacked.reshape(-1, stacked.shape[2]), weights[layer_at], preferr...  8.34 us
    all_to_all x1, starting transfers between devices, route_rows(): lax.all_to_all(send_place.reshape(wide_count, capacity, per_dev), 'wide',...  7.35 us
    all_to_all x1, starting transfers between devices, local(): lax.all_to_all(jnp.broadcast_to(stats[None, :], (wide_count, stats.shape[...  6.82 us
    unnamed x39, local copies, waits for them, and re-layouts  6.71 us
    all_to_all x1, waiting for transfers between devices, local(): lax.all_to_all(jnp.broadcast_to(stats[None, :], (wide_count, stats.shape[...  6.52 us
  transfers between devices with their start and end apart: 11, of which 11 were waited for; matrix products, arithmetic and copies ran while one was open for 5% of the time, Pallas kernels for 0%

profile of v15, /device:TPU:0, one launch (start us, length us, event | category | flops | bytes accessed | tf_op | source)
XLA Modules:
  0.0 144.4 jit_solution(7728897574265011197)
XLA Ops:
  2.8 1.3 select_reduce_fusion
  5.5 3.8 %fusion.46 = bf16[16,128,8]{1,2,0:T(8,128)(2,1)} fusion(s32[2048]{0:T(1024)S(1)} %get-tuple-element.29, s32[2048]{0:T(1024)S(1)} %get-tuple-element.28, pred[2048]{0:T(1024)(128)(4,1)S(1)} %broadcast_compare_fusion.1), kind=kOutput, calls=%fused_computation.76 | convolution fusion | flops 71352320 | bytes 51200 | tf_op jit(solution)/shard_map/dot_general | solution.py:102
  9.3 7.4 %all-to-all-start = ((bf16[16,128,8]{1,2,0:T(8,128)(2,1)}), bf16[16,128,8]{1,2,0:T(8,128)(2,1)S(1)}, u32[]{:S(2)}, u32[]{:S(2)}) async-start(bf16[16,128,8]{1,2,0:T(8,128)(2,1)} %fusion.46), calls=%async_computation | async-start | bytes 65536 | tf_op jit(solution)/shard_map/all_to_all | solution.py:112
  16.6 4.2 %fusion.22 = bf16[2048,256]{1,0:T(8,128)(2,1)} fusion(bf16[2048,256]{1,0:T(8,128)(2,1)S(1)} %copy-done, s32[2048]{0:T(1024)S(1)} %get-tuple-element.29), kind=kOutput, calls=%fused_computation.32 | convolution fusion | flops 2152202240 | bytes 2105344 | tf_op jit(solution)/shard_map/dot_general | solution.py:103
  20.8 2.5 %all-to-all-done = bf16[16,128,8]{1,2,0:T(8,128)(2,1)S(1)} async-done(((bf16[16,128,8]{1,2,0:T(8,128)(2,1)}), bf16[16,128,8]{1,2,0:T(8,128)(2,1)S(1)}, u32[]{:S(2)}, u32[]{:S(2)}) %all-to-all-start) | async-done | bytes 32800 | tf_op jit(solution)/shard_map/all_to_all | solution.py:112
  23.2 4.5 %all-to-all-start.1 = ((bf16[16,128,256]{2,1,0:T(8,128)(2,1)}), bf16[16,128,256]{2,1,0:T(8,128)(2,1)}, u32[]{:S(2)}, u32[]{:S(2)}) async-start(bf16[16,128,256]{2,1,0:T(8,128)(2,1)} %bitcast.140), calls=%async_computation.1 | async-start | bytes 2097152 | tf_op jit(solution)/shard_map/all_to_all | solution.py:105
  27.8 1.0 copy.86
  31.5 19.0 %all-to-all-done.1 = bf16[16,128,256]{2,1,0:T(8,128)(2,1)} async-done(((bf16[16,128,256]{2,1,0:T(8,128)(2,1)}), bf16[16,128,256]{2,1,0:T(8,128)(2,1)}, u32[]{:S(2)}, u32[]{:S(2)}) %all-to-all-start.1) | async-done | bytes 1048608 | tf_op jit(solution)/shard_map/all_to_all | solution.py:105
  50.5 4.5 %fusion.21 = bf16[2048,256]{1,0:T(8,128)(2,1)S(1)} fusion(bf16[2048,256]{1,0:T(8,128)(2,1)} %bitcast.12, s32[2048]{0:T(1024)S(1)} %select_bitcast_fusion), kind=kOutput, calls=%fused_computation.31 | convolution fusion | flops 2152202240 | bytes 2105344 | tf_op jit(solution)/shard_map/dot_general | solution.py:131
  55.0 1.5 %fusion.25 = bf16[8,256,256]{2,1,0:T(8,128)(2,1)S(1)} fusion(bf16[8,256,256]{2,1,0:T(8,128)(2,1)S(1)} %bitcast.149, bf16[2,768,256]{2,1,0:T(8,128)(2,1)S(1)} %bitcast.144, bf16[8,254,256]{2,1,0:T(8,128)(2,1)S(1)} %bitcast.150, bf16[8,255,256]{2,1,0:T(8,128)(2,1)S(1)} %bitcast.151), kind=kOutput, calls=%fused_computation.35 | convolution fusion | flops 827850752 | bytes 5636096 | tf_op jit(solution)/shard_map/dot_general | solution.py:49
  56.7 2.5 %fusion.24 = (bf16[8,256,256]{2,1,0:T(8,128)(2,1)S(1)}, f32[8,256,256]{2,1,0:T(8,128)}) fusion(bf16[8,256,256]{2,1,0:T(8,128)(2,1)S(1)} %bitcast.152, bf16[2,768,256]{2,1,0:T(8,128)(2,1)S(1)} %bitcast.136, bf16[8,254,256]{2,1,0:T(8,128)(2,1)S(1)} %bitcast.153, bf16[8,255,256]{2,1,0:T(8,128)(2,1)S(1)} %bitcast.154), kind=kOutput, calls=%fused_computation.34 | convolution fusion | flops 827850752 | bytes 7733248 | tf_op jit(solution)/shard_map/dot_general | solution.py:49
  59.2 2.5 %fusion.98 = (bf16[8,256]{1,0:T(8,128)(2,1)S(1)}, bf16[8,256,256]{2,1,0:T(8,128)(2,1)S(1)}, f32[8,256,256]{2,1,0:T(8,128)}) fusion(bf16[8,256,256]{2,1,0:T(8,128)(2,1)S(1)} %get-tuple-element.30, bf16[2,768,256]{2,1,0:T(8,128)(2,1)S(1)} %bitcast.137, bf16[8,248,256]{2,1,0:T(8,128)(2,1)S(1)} %slice.87, bf16[8,252,256]{2,1,0:T(8,128)(2,1)S(1)} %bitcast.141), kind=kOutput, calls=%fused_computation.169 | convolution fusion | flops 828372992 | bytes 7704576 | tf_op jit(solution)/shard_map/dot_general | solution.py:49
  61.7 1.8 %fusion.32 = (f32[8,256]{1,0:T(8,128)S(1)}, f32[8,256]{1,0:T(8,128)S(1)}, f32[256]{0:T(256)S(1)}, bf16[8,256,256]{2,1,0:T(8,128)(2,1)S(1)}) fusion(bf16[8,256,256]{2,1,0:T(8,128)(2,1)S(1)} %get-tuple-element.15, f32[8,256]{1,0:T(8,128)S(1)} %fusion.81, f32[8,256]{1,0:T(8,128)S(1)} %bitcast.146, bf16[2,768,256]{2,1,0:T(8,128)(2,1)S(1)} %bitcast.145, ...), kind=kOutput, calls=%fused_computation.42 | convolution fusion | flops 832040704 | bytes 6685696 | tf_op jit(solution)/shard_map/dot_general | solution.py:49
  64.2 6.8 %all-to-all-start.2 = ((f32[16,1,384]{2,1,0:T(1,128)}), f32[16,1,384]{2,1,0:T(1,128)S(1)}, u32[]{:S(2)}, u32[]{:S(2)}) async-start(f32[16,1,384]{2,1,0:T(1,128)} %broadcast_in_dim.40), calls=%async_computation.2 | async-start | bytes 49152 | tf_op jit(solution)/shard_map/all_to_all | solution.py:188
  71.1 6.5 %all-to-all-done.2 = f32[16,1,384]{2,1,0:T(1,128)S(1)} async-done(((f32[16,1,384]{2,1,0:T(1,128)}), f32[16,1,384]{2,1,0:T(1,128)S(1)}, u32[]{:S(2)}, u32[]{:S(2)}) %all-to-all-start.2) | async-done | bytes 24608 | tf_op jit(solution)/shard_map/all_to_all | solution.py:188
  80.1 3.7 %multiply_convert_fusion = bf16[8,256,256]{2,1,0:T(8,128)(2,1)S(1)} fusion(f32[8,256,256]{2,1,0:T(8,128)S(1)} %copy-done.6, f32[8,256]{1,0:T(8,128)S(1)} %fusion.39, f32[8,256]{1,0:T(8,128)S(1)} %fusion.36, f32[256]{0:T(256)S(1)} %slice_divide_fusion, bf16[8,256,256]{2,1,0:T(8,128)(2,1)S(1)} %get-tuple-element.33, f32[8,256]{1,0:T(8,128)S(1)} %get-tuple-element.5, ...), kind=kLoop, calls=%fused_computation.58 | loop fusion | flops 10485760 | bytes 5284864 | tf_op jit(solution)/shard_map/convert_element_type | solution.py:203
  83.8 1.0 convolution_bitcast_fusion
  84.9 1.0 fusion.47
  86.7 1.1 copy-done.17
  88.5 3.1 %convolution_bitcast_fusion.1 = f32[1,768,256]{2,1,0:T(8,128)S(1)} fusion(f32[8,256,3,256]{3,1,0,2:T(8,128)S(1)} %fusion.47, f32[8,256,256]{2,1,0:T(8,128)S(1)} %copy-done.17, f32[8,248,256]{2,1,0:T(8,128)S(1)} %slice.97, f32[8,252,256]{2,1,0:T(8,128)S(1)} %slice.95, bf16[8,256,256]{2,1,0:T(8,128)(2,1)S(1)} %copy-done.9, ...), kind=kOutput, calls=%fused_computation.75 | convolution fusion | flops 836239360 | bytes 14394368 | tf_op jit(solution)/shard_map/dot_general | solution.py:205
  91.7 0.9 copy-done.5
  92.7 2.4 %collective-permute-done = f32[2,384,256]{2,1,0:T(8,128)} collective-permute-done((f32[2,384,256]{2,1,0:T(8,128)S(1)}, f32[2,384,256]{2,1,0:T(8,128)}, u32[]{:S(2)}, u32[]{:S(2)}) %collective-permute-start) | collective-permute-done | bytes 786464 | tf_op jit(solution)/shard_map/ppermute | solution.py:161
  95.1 1.3 fusion.56
  96.9 7.4 %collective-permute-done.1 = f32[2,192,256]{2,1,0:T(8,128)S(1)} collective-permute-done((f32[2,192,256]{2,1,0:T(8,128)S(1)}, f32[2,192,256]{2,1,0:T(8,128)S(1)}, u32[]{:S(2)}, u32[]{:S(2)}) %collective-permute-start.1) | collective-permute-done | bytes 393248 | tf_op jit(solution)/shard_map/ppermute | solution.py:161
  104.8 7.3 %collective-permute-done.2 = f32[2,96,256]{2,1,0:T(8,128)S(1)} collective-permute-done((f32[2,96,256]{2,1,0:T(8,128)S(1)}, f32[2,96,256]{2,1,0:T(8,128)S(1)}, u32[]{:S(2)}, u32[]{:S(2)}) %collective-permute-start.2) | collective-permute-done | bytes 196640 | tf_op jit(solution)/shard_map/ppermute | solution.py:161
  112.3 5.5 %collective-permute-done.3 = f32[2,48,256]{2,1,0:T(8,128)S(1)} collective-permute-done((f32[2,48,256]{2,1,0:T(8,128)S(1)}, f32[2,48,256]{2,1,0:T(8,128)S(1)}, u32[]{:S(2)}, u32[]{:S(2)}) %collective-permute-start.3) | collective-permute-done | bytes 98336 | tf_op jit(solution)/shard_map/ppermute | solution.py:161
  117.9 5.5 %collective-permute-done.4 = bf16[2,48,256]{2,1,0:T(8,128)(2,1)S(1)} collective-permute-done((bf16[2,48,256]{2,1,0:T(8,128)(2,1)S(1)}, bf16[2,48,256]{2,1,0:T(8,128)(2,1)S(1)}, u32[]{:S(2)}, u32[]{:S(2)}) %collective-permute-start.4) | collective-permute-done | bytes 49184 | tf_op jit(solution)/shard_map/ppermute | solution.py:165
  123.5 5.6 %collective-permute-done.5 = bf16[2,96,256]{2,1,0:T(8,128)(2,1)S(1)} collective-permute-done((bf16[2,96,256]{2,1,0:T(8,128)(2,1)S(1)}, bf16[2,96,256]{2,1,0:T(8,128)(2,1)S(1)}, u32[]{:S(2)}, u32[]{:S(2)}) %collective-permute-start.5) | collective-permute-done | bytes 98336 | tf_op jit(solution)/shard_map/ppermute | solution.py:165
  129.6 5.3 %collective-permute-done.6 = bf16[2,192,256]{2,1,0:T(8,128)(2,1)S(1)} collective-permute-done((bf16[2,192,256]{2,1,0:T(8,128)(2,1)S(1)}, bf16[2,192,256]{2,1,0:T(8,128)(2,1)S(1)}, u32[]{:S(2)}, u32[]{:S(2)}) %collective-permute-start.6) | collective-permute-done | bytes 196640 | tf_op jit(solution)/shard_map/ppermute | solution.py:165
  135.8 1.0 collective-permute-done.7
  137.1 1.2 copy.83
  139.4 5.0 %multiply_add_fusion = (f32[2,196608]{1,0:T(2,128)}, f32[2,196608]{1,0:T(2,128)}, f32[2,196608]{1,0:T(2,128)}) fusion(f32[2,196608]{1,0:T(2,128)S(1)} %copy-done.2, f32[2,196608]{1,0:T(2,128)S(1)} %copy-done.4, f32[2,196608]{1,0:T(2,128)S(1)} %bitcast.135, f32[2,196608]{1,0:T(2,128)S(1)} %copy-done.7), kind=kLoop, calls=%fused_computation.71 | loop fusion | flops 2752512 | bytes 11010048 | tf_op jit(solution)/shard_map/add | solution.py:226
  (93 shorter events, 14.4 us)
Async XLA Ops:
  0.6 16.0 %copy-start = (bf16[2048,256]{1,0:T(8,128)(2,1)S(1)}, bf16[2048,256]{1,0:T(8,128)(2,1)}, u32[]{:S(2)}) copy-start(bf16[2048,256]{1,0:T(8,128)(2,1)} %param.6) | copy-start | bytes 3145732
  9.3 14.0 %all-to-all-start = ((bf16[16,128,8]{1,2,0:T(8,128)(2,1)}), bf16[16,128,8]{1,2,0:T(8,128)(2,1)S(1)}, u32[]{:S(2)}, u32[]{:S(2)}) async-start(bf16[16,128,8]{1,2,0:T(8,128)(2,1)} %fusion.46), calls=%async_computation | async-start | bytes 65536 | tf_op jit(solution)/shard_map/all_to_all | solution.py:112
  20.8 7.0 %copy-start.1 = (f32[2,196608]{1,0:T(2,128)S(1)}, f32[2,196608]{1,0:T(2,128)}, u32[]{:S(2)}) copy-start(f32[2,196608]{1,0:T(2,128)} %param.11) | copy-start | bytes 4718596
  23.2 27.3 %all-to-all-start.1 = ((bf16[16,128,256]{2,1,0:T(8,128)(2,1)}), bf16[16,128,256]{2,1,0:T(8,128)(2,1)}, u32[]{:S(2)}, u32[]{:S(2)}) async-start(bf16[16,128,256]{2,1,0:T(8,128)(2,1)} %bitcast.140), calls=%async_computation.1 | async-start | bytes 2097152 | tf_op jit(solution)/shard_map/all_to_all | solution.py:105
  27.8 1.7 %copy-start.3 = (f32[2,196608]{1,0:T(2,128)S(1)}, f32[2,196608]{1,0:T(2,128)}, u32[]{:S(2)}) copy-start(f32[2,196608]{1,0:T(2,128)} %param.9) | copy-start | bytes 4718596
  50.5 4.5 %copy-start.14 = (bf16[1,2,768,256]{3,2,1,0:T(8,128)(2,1)S(1)}, bf16[1,2,768,256]{3,2,1,0:T(8,128)(2,1)}, u32[]{:S(2)}) copy-start(bf16[1,2,768,256]{3,2,1,0:T(8,128)(2,1)} %copy.86) | copy-start | bytes 2359300
  55.0 1.6 %copy-start.15 = (bf16[2048,256]{1,0:T(8,128)(2,1)}, bf16[2048,256]{1,0:T(8,128)(2,1)S(1)}, u32[]{:S(2)}) copy-start(bf16[2048,256]{1,0:T(8,128)(2,1)S(1)} %fusion.21) | copy-start | bytes 3145732
  59.1 2.6 %copy-start.12 = (bf16[8,256,256]{2,1,0:T(8,128)(2,1)}, bf16[8,256,256]{2,1,0:T(8,128)(2,1)S(1)}, u32[]{:S(2)}) copy-start(bf16[8,256,256]{2,1,0:T(8,128)(2,1)S(1)} %get-tuple-element.30) | copy-start | bytes 3145732
  59.2 2.5 %copy-start.10 = (bf16[8,248,256]{2,1,0:T(8,128)(2,1)}, bf16[8,248,256]{2,1,0:T(8,128)(2,1)S(1)}, u32[]{:S(2)}) copy-start(bf16[8,248,256]{2,1,0:T(8,128)(2,1)S(1)} %slice.87) | copy-start | bytes 3047428
  61.7 1.9 %copy-start.8 = (bf16[8,256,256]{2,1,0:T(8,128)(2,1)}, bf16[8,256,256]{2,1,0:T(8,128)(2,1)S(1)}, u32[]{:S(2)}) copy-start(bf16[8,256,256]{2,1,0:T(8,128)(2,1)S(1)} %get-tuple-element.15) | copy-start | bytes 3145732
  64.2 13.4 %all-to-all-start.2 = ((f32[16,1,384]{2,1,0:T(1,128)}), f32[16,1,384]{2,1,0:T(1,128)S(1)}, u32[]{:S(2)}, u32[]{:S(2)}) async-start(f32[16,1,384]{2,1,0:T(1,128)} %broadcast_in_dim.40), calls=%async_computation.2 | async-start | bytes 49152 | tf_op jit(solution)/shard_map/all_to_all | solution.py:188
  77.7 2.4 %copy-start.6 = (f32[8,256,256]{2,1,0:T(8,128)S(1)}, f32[8,256,256]{2,1,0:T(8,128)}, u32[]{:S(2)}) copy-start(f32[8,256,256]{2,1,0:T(8,128)} %get-tuple-element.32) | copy-start | bytes 6291460
  80.1 3.7 %copy-start.11 = (bf16[8,248,256]{2,1,0:T(8,128)(2,1)S(1)}, bf16[8,248,256]{2,1,0:T(8,128)(2,1)}, u32[]{:S(2)}) copy-start(bf16[8,248,256]{2,1,0:T(8,128)(2,1)} %copy-done.10) | copy-start | bytes 3047428
  80.1 3.7 %copy-start.13 = (bf16[8,256,256]{2,1,0:T(8,128)(2,1)S(1)}, bf16[8,256,256]{2,1,0:T(8,128)(2,1)}, u32[]{:S(2)}) copy-start(bf16[8,256,256]{2,1,0:T(8,128)(2,1)} %copy-done.12) | copy-start | bytes 3145732
  86.3 1.6 %copy-start.17 = (f32[8,256,256]{2,1,0:T(8,128)S(1)}, f32[8,256,256]{2,1,0:T(8,128)}, u32[]{:S(2)}) copy-start(f32[8,256,256]{2,1,0:T(8,128)} %get-tuple-element.31) | copy-start | bytes 6291460
  86.5 1.7 %copy-start.9 = (bf16[8,256,256]{2,1,0:T(8,128)(2,1)S(1)}, bf16[8,256,256]{2,1,0:T(8,128)(2,1)}, u32[]{:S(2)}) copy-start(bf16[8,256,256]{2,1,0:T(8,128)(2,1)} %copy-done.8) | copy-start | bytes 3145732
  86.5 2.0 %copy-start.16 = (bf16[2048,256]{1,0:T(8,128)(2,1)S(1)}, bf16[2048,256]{1,0:T(8,128)(2,1)}, u32[]{:S(2)}) copy-start(bf16[2048,256]{1,0:T(8,128)(2,1)} %copy-done.15) | copy-start | bytes 3145732
  91.6 0.9 copy-start.5
  92.6 2.5 %collective-permute-start = (f32[2,384,256]{2,1,0:T(8,128)S(1)}, f32[2,384,256]{2,1,0:T(8,128)}, u32[]{:S(2)}, u32[]{:S(2)}) collective-permute-start(f32[2,384,256]{2,1,0:T(8,128)S(1)} %fusion.54), channel_id=1, source_target_pairs={{0,1},{1,0},{2,3},{3,2},{4,5},{5,4},{6,7},{7,6},{8,9},{9,8},{10,11... | collective-permute-start | bytes 2359304 | tf_op jit(solution)/shard_map/ppermute | solution.py:161
  96.4 7.8 %collective-permute-start.1 = (f32[2,192,256]{2,1,0:T(8,128)S(1)}, f32[2,192,256]{2,1,0:T(8,128)S(1)}, u32[]{:S(2)}, u32[]{:S(2)}) collective-permute-start(f32[2,192,256]{2,1,0:T(8,128)S(1)} %constant_dynamic-slice_fusion.1), channel_id=1, source_target_pairs={{0,2},{1,5},{2,0},{3,7},{4,6},{5,1},{6,4},{7,3},{8,10},{9,13},{10,... | collective-permute-start | bytes 1179656 | tf_op jit(solution)/shard_map/ppermute | solution.py:161
  104.4 7.8 %collective-permute-start.2 = (f32[2,96,256]{2,1,0:T(8,128)S(1)}, f32[2,96,256]{2,1,0:T(8,128)S(1)}, u32[]{:S(2)}, u32[]{:S(2)}) collective-permute-start(f32[2,96,256]{2,1,0:T(8,128)S(1)} %constant_dynamic-slice_fusion), channel_id=1, source_target_pairs={{0,4},{1,9},{2,6},{3,11},{4,0},{5,13},{6,2},{7,15},{8,12},{9,1},{1... | collective-permute-start | bytes 589832 | tf_op jit(solution)/shard_map/ppermute | solution.py:161
  112.2 5.6 %collective-permute-start.3 = (f32[2,48,256]{2,1,0:T(8,128)S(1)}, f32[2,48,256]{2,1,0:T(8,128)S(1)}, u32[]{:S(2)}, u32[]{:S(2)}) collective-permute-start(f32[2,48,256]{2,1,0:T(8,128)S(1)} %constant_dynamic-slice_fusion.2), channel_id=1, source_target_pairs={{0,8},{1,3},{2,10},{3,1},{4,12},{5,7},{6,14},{7,5},{8,0},{9,11},{1... | collective-permute-start | bytes 294920 | tf_op jit(solution)/shard_map/ppermute | solution.py:161
  117.8 5.6 %collective-permute-start.4 = (bf16[2,48,256]{2,1,0:T(8,128)(2,1)S(1)}, bf16[2,48,256]{2,1,0:T(8,128)(2,1)S(1)}, u32[]{:S(2)}, u32[]{:S(2)}) collective-permute-start(bf16[2,48,256]{2,1,0:T(8,128)(2,1)S(1)} %add_convert_fusion.2), channel_id=1, source_target_pairs={{0,8},{1,3},{2,10},{3,1},{4,12},{5,7},{6,14},{7,5},{8,0},{9,11},{1... | collective-permute-start | bytes 147464 | tf_op jit(solution)/shard_map/ppermute | solution.py:165
  123.4 5.7 %collective-permute-start.5 = (bf16[2,96,256]{2,1,0:T(8,128)(2,1)S(1)}, bf16[2,96,256]{2,1,0:T(8,128)(2,1)S(1)}, u32[]{:S(2)}, u32[]{:S(2)}) collective-permute-start(bf16[2,96,256]{2,1,0:T(8,128)(2,1)S(1)} %pad_maximum_fusion.2), channel_id=1, source_target_pairs={{0,4},{1,9},{2,6},{3,11},{4,0},{5,13},{6,2},{7,15},{8,12},{9,1},{1... | collective-permute-start | bytes 294920 | tf_op jit(solution)/shard_map/ppermute | solution.py:165
  129.2 5.7 %collective-permute-start.6 = (bf16[2,192,256]{2,1,0:T(8,128)(2,1)S(1)}, bf16[2,192,256]{2,1,0:T(8,128)(2,1)S(1)}, u32[]{:S(2)}, u32[]{:S(2)}) collective-permute-start(bf16[2,192,256]{2,1,0:T(8,128)(2,1)S(1)} %pad_maximum_fusion.1), channel_id=1, source_target_pairs={{0,2},{1,5},{2,0},{3,7},{4,6},{5,1},{6,4},{7,3},{8,10},{9,13},{10,... | collective-permute-start | bytes 589832 | tf_op jit(solution)/shard_map/ppermute | solution.py:165
  135.0 1.8 %collective-permute-start.7 = (bf16[2,384,256]{2,1,0:T(8,128)(2,1)S(1)}, bf16[2,384,256]{2,1,0:T(8,128)(2,1)S(1)}, u32[]{:S(2)}, u32[]{:S(2)}) collective-permute-start(bf16[2,384,256]{2,1,0:T(8,128)(2,1)S(1)} %pad_maximum_fusion), channel_id=1, source_target_pairs={{0,1},{1,0},{2,3},{3,2},{4,5},{5,4},{6,7},{7,6},{8,9},{9,8},{10,11... | collective-permute-start | bytes 1179656 | tf_op jit(solution)/shard_map/ppermute | solution.py:165
  137.0 1.4 copy-start.7
  137.1 1.8 %copy-start.2 = (f32[2,196608]{1,0:T(2,128)S(1)}, f32[2,196608]{1,0:T(2,128)}, u32[]{:S(2)}) copy-start(f32[2,196608]{1,0:T(2,128)} %param.11) | copy-start | bytes 4718596
  137.1 2.2 %copy-start.4 = (f32[2,196608]{1,0:T(2,128)S(1)}, f32[2,196608]{1,0:T(2,128)}, u32[]{:S(2)}) copy-start(f32[2,196608]{1,0:T(2,128)} %param.9) | copy-start | bytes 4718596

commit v16 on v15

--- a/solution.py
+++ b/solution.py
@@ -125,9 +125,9 @@
     )
     counts = jnp.sum(place_hot.astype(jnp.int32), axis=0)
     target = jnp.where(jnp.any(place_hot, axis=1), place_code * SEQ + position, -1)
-    put = (
-        jnp.arange(per_dev * SEQ, dtype=jnp.int32)[:, None] == target[None, :]
-    ).astype(jnp.bfloat16)
+    put = lax.optimization_barrier(
+        (jnp.arange(per_dev * SEQ, dtype=jnp.int32)[:, None] == target[None, :]).astype(jnp.bfloat16)
+    )
     sequences = jnp.dot(
         put, got_rows.reshape(-1, feat_width), preferred_element_type=jnp.float32
     ).astype(jnp.bfloat16)

time: 145 us -> 147 us (1.014)
  waiting for transfers between devices: 68 us -> 60.6 us
  other arithmetic: 18.4 us -> 25.6 us
    convert_element_type x0 -> x1, other arithmetic: none -> 7.4 us  [route_rows(): (jnp.arange(per_dev * SEQ, dtype=jnp.int32)[:, None] == target[None, :])....]
    all_to_all x1, waiting for transfers between devices: 19 us -> 13.6 us  [route_rows(): lax.all_to_all(send_rows.reshape(wide_count, capacity, feat_width), 'wide...]
    all_to_all x1, waiting for transfers between devices: 2.47 us -> 0.68 us  [route_rows(): lax.all_to_all(send_place.reshape(wide_count, capacity, per_dev), 'wide',...]
  transfers between devices with their start and end apart: 11 -> 11, of which waited for: 11 -> 11; matrix products, arithmetic and copies ran while one was open for 5% -> 10% of each run, Pallas kernels for 0% -> 0%
where the time goes in v16:
time: 147 us; the launch traced here: 146 us
  waiting for transfers between devices  60.6 us (41%)
  matrix products  27.8 us (19%)
  other arithmetic  25.6 us (17%)
  starting transfers between devices  21.3 us (14%)
  local copies, waits for them, and re-layouts  9.29 us (6%)
  between operations  1.84 us (1%)
    ppermute x4, waiting for transfers between devices, all_reduce_wide(): buf = keep + lax.ppermute(send, 'wide', pairs)  22.5 us
    ppermute x4, waiting for transfers between devices, all_reduce_wide(): got = lax.ppermute(buf, 'wide', pairs)  17.4 us
    all_to_all x1, waiting for transfers between devices, route_rows(): lax.all_to_all(send_rows.reshape(wide_count, capacity, feat_width), 'wide...  13.6 us
    dot_general x4, matrix products, run_network(): jnp.dot(stacked.reshape(-1, stacked.shape[2]), weights[layer_at], preferr...  8.35 us
    convert_element_type x1, other arithmetic, route_rows(): (jnp.arange(per_dev * SEQ, dtype=jnp.int32)[:, None] == target[None, :])....  7.4 us
    all_to_all x1, starting transfers between devices, route_rows(): lax.all_to_all(send_place.reshape(wide_count, capacity, per_dev), 'wide',...  7.35 us
    all_to_all x1, starting transfers between devices, local(): lax.all_to_all(jnp.broadcast_to(stats[None, :], (wide_count, stats.shape[...  6.86 us
    unnamed x39, local copies, waits for them, and re-layouts  6.72 us
  transfers between devices with their start and end apart: 11, of which 11 were waited for; matrix products, arithmetic and copies ran while one was open for 10% of the time, Pallas kernels for 0%

profile of v16, /device:TPU:0, one launch (start us, length us, event | category | flops | bytes accessed | tf_op | source)
XLA Modules:
  0.0 146.4 jit_solution(8576245090983778074)
XLA Ops:
  2.8 1.3 select_reduce_fusion
  5.5 3.8 %fusion.44 = bf16[16,128,8]{1,2,0:T(8,128)(2,1)} fusion(s32[2048]{0:T(1024)S(1)} %get-tuple-element.29, s32[2048]{0:T(1024)S(1)} %get-tuple-element.28, pred[2048]{0:T(1024)(128)(4,1)S(1)} %broadcast_compare_fusion.1), kind=kOutput, calls=%fused_computation.75 | convolution fusion | flops 71352320 | bytes 51200 | tf_op jit(solution)/shard_map/dot_general | solution.py:102
  9.3 7.4 %all-to-all-start = ((bf16[16,128,8]{1,2,0:T(8,128)(2,1)}), bf16[16,128,8]{1,2,0:T(8,128)(2,1)S(1)}, u32[]{:S(2)}, u32[]{:S(2)}) async-start(bf16[16,128,8]{1,2,0:T(8,128)(2,1)} %fusion.44), calls=%async_computation | async-start | bytes 65536 | tf_op jit(solution)/shard_map/all_to_all | solution.py:112
  16.6 4.1 %fusion.20 = bf16[2048,256]{1,0:T(8,128)(2,1)} fusion(bf16[2048,256]{1,0:T(8,128)(2,1)S(1)} %copy-done, s32[2048]{0:T(1024)S(1)} %get-tuple-element.29), kind=kOutput, calls=%fused_computation.30 | convolution fusion | flops 2152202240 | bytes 2105344 | tf_op jit(solution)/shard_map/dot_general | solution.py:103
  20.8 1.0 copy.86
  23.2 5.4 %all-to-all-start.1 = ((bf16[16,128,256]{2,1,0:T(8,128)(2,1)}), bf16[16,128,256]{2,1,0:T(8,128)(2,1)S(1)}, u32[]{:S(2)}, u32[]{:S(2)}) async-start(bf16[16,128,256]{2,1,0:T(8,128)(2,1)} %bitcast.11), calls=%async_computation.1 | async-start | bytes 2097152 | tf_op jit(solution)/shard_map/all_to_all | solution.py:105
  29.9 7.4 %fusion.2 = bf16[2048,2048]{1,0:T(8,128)(2,1)} fusion(s32[2048]{0:T(1024)S(1)} %select_bitcast_fusion), kind=kLoop, calls=%fused_computation.4 | loop fusion | flops 8388608 | bytes 8396800 | tf_op jit(solution)/shard_map/convert_element_type | solution.py:129
  38.0 13.6 %all-to-all-done.1 = bf16[16,128,256]{2,1,0:T(8,128)(2,1)S(1)} async-done(((bf16[16,128,256]{2,1,0:T(8,128)(2,1)}), bf16[16,128,256]{2,1,0:T(8,128)(2,1)S(1)}, u32[]{:S(2)}, u32[]{:S(2)}) %all-to-all-start.1) | async-done | bytes 1048608 | tf_op jit(solution)/shard_map/all_to_all | solution.py:105
  51.5 5.8 %convolution_convert_fusion = bf16[2048,256]{1,0:T(8,128)(2,1)S(1)} fusion(bf16[2048,2048]{1,0:T(8,128)(2,1)} %fusion.2, bf16[2048,256]{1,0:T(8,128)(2,1)S(1)} %bitcast.141), kind=kOutput, calls=%fused_computation.31 | convolution fusion | flops 2148007936 | bytes 10485760 | tf_op jit(solution)/shard_map/dot_general | solution.py:131
  57.4 1.5 %fusion.23 = bf16[8,256,256]{2,1,0:T(8,128)(2,1)S(1)} fusion(bf16[8,256,256]{2,1,0:T(8,128)(2,1)S(1)} %bitcast.150, bf16[2,768,256]{2,1,0:T(8,128)(2,1)S(1)} %bitcast.145, bf16[8,254,256]{2,1,0:T(8,128)(2,1)S(1)} %bitcast.151, bf16[8,255,256]{2,1,0:T(8,128)(2,1)S(1)} %bitcast.152), kind=kOutput, calls=%fused_computation.34 | convolution fusion | flops 827850752 | bytes 5636096 | tf_op jit(solution)/shard_map/dot_general | solution.py:49
  59.0 2.5 %fusion.22 = (bf16[8,256,256]{2,1,0:T(8,128)(2,1)S(1)}, f32[8,256,256]{2,1,0:T(8,128)}) fusion(bf16[8,256,256]{2,1,0:T(8,128)(2,1)S(1)} %bitcast.153, bf16[2,768,256]{2,1,0:T(8,128)(2,1)S(1)} %bitcast.137, bf16[8,254,256]{2,1,0:T(8,128)(2,1)S(1)} %bitcast.154, bf16[8,255,256]{2,1,0:T(8,128)(2,1)S(1)} %bitcast.155), kind=kOutput, calls=%fused_computation.33 | convolution fusion | flops 827850752 | bytes 7733248 | tf_op jit(solution)/shard_map/dot_general | solution.py:49
  61.6 2.5 %fusion.96 = (bf16[8,256]{1,0:T(8,128)(2,1)S(1)}, bf16[8,256,256]{2,1,0:T(8,128)(2,1)S(1)}, f32[8,256,256]{2,1,0:T(8,128)}) fusion(bf16[8,256,256]{2,1,0:T(8,128)(2,1)S(1)} %get-tuple-element.30, bf16[2,768,256]{2,1,0:T(8,128)(2,1)S(1)} %bitcast.138, bf16[8,248,256]{2,1,0:T(8,128)(2,1)S(1)} %slice.87, bf16[8,252,256]{2,1,0:T(8,128)(2,1)S(1)} %bitcast.142), kind=kOutput, calls=%fused_computation.168 | convolution fusion | flops 828372992 | bytes 7704576 | tf_op jit(solution)/shard_map/dot_general | solution.py:49
  64.1 1.8 %fusion.30 = (f32[8,256]{1,0:T(8,128)S(1)}, f32[8,256]{1,0:T(8,128)S(1)}, f32[256]{0:T(256)S(1)}, bf16[8,256,256]{2,1,0:T(8,128)(2,1)S(1)}) fusion(bf16[8,256,256]{2,1,0:T(8,128)(2,1)S(1)} %get-tuple-element.15, f32[8,256]{1,0:T(8,128)S(1)} %fusion.79, f32[8,256]{1,0:T(8,128)S(1)} %bitcast.147, bf16[2,768,256]{2,1,0:T(8,128)(2,1)S(1)} %bitcast.146, ...), kind=kOutput, calls=%fused_computation.41 | convolution fusion | flops 832040704 | bytes 6685696 | tf_op jit(solution)/shard_map/dot_general | solution.py:49
  66.6 6.9 %all-to-all-start.2 = ((f32[16,1,384]{2,1,0:T(1,128)}), f32[16,1,384]{2,1,0:T(1,128)S(1)}, u32[]{:S(2)}, u32[]{:S(2)}) async-start(f32[16,1,384]{2,1,0:T(1,128)} %broadcast_in_dim.40), calls=%async_computation.2 | async-start | bytes 49152 | tf_op jit(solution)/shard_map/all_to_all | solution.py:188
  73.5 6.5 %all-to-all-done.2 = f32[16,1,384]{2,1,0:T(1,128)S(1)} async-done(((f32[16,1,384]{2,1,0:T(1,128)}), f32[16,1,384]{2,1,0:T(1,128)S(1)}, u32[]{:S(2)}, u32[]{:S(2)}) %all-to-all-start.2) | async-done | bytes 24608 | tf_op jit(solution)/shard_map/all_to_all | solution.py:188
  82.5 3.7 %multiply_convert_fusion = bf16[8,256,256]{2,1,0:T(8,128)(2,1)S(1)} fusion(f32[8,256,256]{2,1,0:T(8,128)S(1)} %copy-done.6, f32[8,256]{1,0:T(8,128)S(1)} %fusion.37, f32[8,256]{1,0:T(8,128)S(1)} %fusion.34, f32[256]{0:T(256)S(1)} %slice_divide_fusion, bf16[8,256,256]{2,1,0:T(8,128)(2,1)S(1)} %get-tuple-element.33, f32[8,256]{1,0:T(8,128)S(1)} %get-tuple-element.5, ...), kind=kLoop, calls=%fused_computation.57 | loop fusion | flops 10485760 | bytes 5284864 | tf_op jit(solution)/shard_map/convert_element_type | solution.py:203
  86.2 1.0 convolution_bitcast_fusion
  87.3 1.0 fusion.45
  89.1 1.1 copy-done.17
  90.9 3.1 %convolution_bitcast_fusion.1 = f32[1,768,256]{2,1,0:T(8,128)S(1)} fusion(f32[8,256,3,256]{3,1,0,2:T(8,128)S(1)} %fusion.45, f32[8,256,256]{2,1,0:T(8,128)S(1)} %copy-done.17, f32[8,248,256]{2,1,0:T(8,128)S(1)} %slice.97, f32[8,252,256]{2,1,0:T(8,128)S(1)} %slice.95, bf16[8,256,256]{2,1,0:T(8,128)(2,1)S(1)} %copy-done.9, ...), kind=kOutput, calls=%fused_computation.74 | convolution fusion | flops 836239360 | bytes 14394368 | tf_op jit(solution)/shard_map/dot_general | solution.py:205
  94.0 0.9 copy-done.5
  95.1 2.3 %collective-permute-done = f32[2,384,256]{2,1,0:T(8,128)S(1)} collective-permute-done((f32[2,384,256]{2,1,0:T(8,128)S(1)}, f32[2,384,256]{2,1,0:T(8,128)S(1)}, u32[]{:S(2)}, u32[]{:S(2)}) %collective-permute-start) | collective-permute-done | bytes 786464 | tf_op jit(solution)/shard_map/ppermute | solution.py:161
  97.3 1.1 fusion.54
  98.9 7.4 %collective-permute-done.1 = f32[2,192,256]{2,1,0:T(8,128)S(1)} collective-permute-done((f32[2,192,256]{2,1,0:T(8,128)S(1)}, f32[2,192,256]{2,1,0:T(8,128)S(1)}, u32[]{:S(2)}, u32[]{:S(2)}) %collective-permute-start.1) | collective-permute-done | bytes 393248 | tf_op jit(solution)/shard_map/ppermute | solution.py:161
  106.8 7.3 %collective-permute-done.2 = f32[2,96,256]{2,1,0:T(8,128)S(1)} collective-permute-done((f32[2,96,256]{2,1,0:T(8,128)S(1)}, f32[2,96,256]{2,1,0:T(8,128)S(1)}, u32[]{:S(2)}, u32[]{:S(2)}) %collective-permute-start.2) | collective-permute-done | bytes 196640 | tf_op jit(solution)/shard_map/ppermute | solution.py:161
  114.3 5.5 %collective-permute-done.3 = f32[2,48,256]{2,1,0:T(8,128)S(1)} collective-permute-done((f32[2,48,256]{2,1,0:T(8,128)S(1)}, f32[2,48,256]{2,1,0:T(8,128)S(1)}, u32[]{:S(2)}, u32[]{:S(2)}) %collective-permute-start.3) | collective-permute-done | bytes 98336 | tf_op jit(solution)/shard_map/ppermute | solution.py:161
  119.9 5.5 %collective-permute-done.4 = bf16[2,48,256]{2,1,0:T(8,128)(2,1)S(1)} collective-permute-done((bf16[2,48,256]{2,1,0:T(8,128)(2,1)S(1)}, bf16[2,48,256]{2,1,0:T(8,128)(2,1)S(1)}, u32[]{:S(2)}, u32[]{:S(2)}) %collective-permute-start.4) | collective-permute-done | bytes 49184 | tf_op jit(solution)/shard_map/ppermute | solution.py:165
  125.5 5.6 %collective-permute-done.5 = bf16[2,96,256]{2,1,0:T(8,128)(2,1)S(1)} collective-permute-done((bf16[2,96,256]{2,1,0:T(8,128)(2,1)S(1)}, bf16[2,96,256]{2,1,0:T(8,128)(2,1)S(1)}, u32[]{:S(2)}, u32[]{:S(2)}) %collective-permute-start.5) | collective-permute-done | bytes 98336 | tf_op jit(solution)/shard_map/ppermute | solution.py:165
  131.6 5.3 %collective-permute-done.6 = bf16[2,192,256]{2,1,0:T(8,128)(2,1)S(1)} collective-permute-done((bf16[2,192,256]{2,1,0:T(8,128)(2,1)S(1)}, bf16[2,192,256]{2,1,0:T(8,128)(2,1)S(1)}, u32[]{:S(2)}, u32[]{:S(2)}) %collective-permute-start.6) | collective-permute-done | bytes 196640 | tf_op jit(solution)/shard_map/ppermute | solution.py:165
  137.8 1.0 collective-permute-done.7
  139.2 1.2 copy.83
  141.4 5.0 %multiply_add_fusion = (f32[2,196608]{1,0:T(2,128)}, f32[2,196608]{1,0:T(2,128)}, f32[2,196608]{1,0:T(2,128)}) fusion(f32[2,196608]{1,0:T(2,128)S(1)} %copy-done.2, f32[2,196608]{1,0:T(2,128)S(1)} %copy-done.4, f32[2,196608]{1,0:T(2,128)S(1)} %bitcast.136, f32[2,196608]{1,0:T(2,128)S(1)} %copy-done.7), kind=kLoop, calls=%fused_computation.70 | loop fusion | flops 2752512 | bytes 11010048 | tf_op jit(solution)/shard_map/add | solution.py:226
  (94 shorter events, 15.1 us)
Async XLA Ops:
  0.6 16.0 %copy-start = (bf16[2048,256]{1,0:T(8,128)(2,1)S(1)}, bf16[2048,256]{1,0:T(8,128)(2,1)}, u32[]{:S(2)}) copy-start(bf16[2048,256]{1,0:T(8,128)(2,1)} %param.6) | copy-start | bytes 3145732
  9.3 14.0 %all-to-all-start = ((bf16[16,128,8]{1,2,0:T(8,128)(2,1)}), bf16[16,128,8]{1,2,0:T(8,128)(2,1)S(1)}, u32[]{:S(2)}, u32[]{:S(2)}) async-start(bf16[16,128,8]{1,2,0:T(8,128)(2,1)} %fusion.44), calls=%async_computation | async-start | bytes 65536 | tf_op jit(solution)/shard_map/all_to_all | solution.py:112
  16.6 4.2 %copy-start.1 = (f32[2,196608]{1,0:T(2,128)S(1)}, f32[2,196608]{1,0:T(2,128)}, u32[]{:S(2)}) copy-start(f32[2,196608]{1,0:T(2,128)} %param.11) | copy-start | bytes 4718596
  20.8 1.7 %copy-start.3 = (f32[2,196608]{1,0:T(2,128)S(1)}, f32[2,196608]{1,0:T(2,128)}, u32[]{:S(2)}) copy-start(f32[2,196608]{1,0:T(2,128)} %param.9) | copy-start | bytes 4718596
  23.2 28.3 %all-to-all-start.1 = ((bf16[16,128,256]{2,1,0:T(8,128)(2,1)}), bf16[16,128,256]{2,1,0:T(8,128)(2,1)S(1)}, u32[]{:S(2)}, u32[]{:S(2)}) async-start(bf16[16,128,256]{2,1,0:T(8,128)(2,1)} %bitcast.11), calls=%async_computation.1 | async-start | bytes 2097152 | tf_op jit(solution)/shard_map/all_to_all | solution.py:105
  51.5 5.8 %copy-start.14 = (bf16[1,2,768,256]{3,2,1,0:T(8,128)(2,1)S(1)}, bf16[1,2,768,256]{3,2,1,0:T(8,128)(2,1)}, u32[]{:S(2)}) copy-start(bf16[1,2,768,256]{3,2,1,0:T(8,128)(2,1)} %copy.86) | copy-start | bytes 2359300
  57.4 1.6 %copy-start.15 = (bf16[2048,256]{1,0:T(8,128)(2,1)}, bf16[2048,256]{1,0:T(8,128)(2,1)S(1)}, u32[]{:S(2)}) copy-start(bf16[2048,256]{1,0:T(8,128)(2,1)S(1)} %convolution_convert_fusion) | copy-start | bytes 3145732
  61.5 2.6 %copy-start.12 = (bf16[8,256,256]{2,1,0:T(8,128)(2,1)}, bf16[8,256,256]{2,1,0:T(8,128)(2,1)S(1)}, u32[]{:S(2)}) copy-start(bf16[8,256,256]{2,1,0:T(8,128)(2,1)S(1)} %get-tuple-element.30) | copy-start | bytes 3145732
  61.6 2.5 %copy-start.10 = (bf16[8,248,256]{2,1,0:T(8,128)(2,1)}, bf16[8,248,256]{2,1,0:T(8,128)(2,1)S(1)}, u32[]{:S(2)}) copy-start(bf16[8,248,256]{2,1,0:T(8,128)(2,1)S(1)} %slice.87) | copy-start | bytes 3047428
  64.1 1.9 %copy-start.8 = (bf16[8,256,256]{2,1,0:T(8,128)(2,1)}, bf16[8,256,256]{2,1,0:T(8,128)(2,1)S(1)}, u32[]{:S(2)}) copy-start(bf16[8,256,256]{2,1,0:T(8,128)(2,1)S(1)} %get-tuple-element.15) | copy-start | bytes 3145732
  66.6 13.4 %all-to-all-start.2 = ((f32[16,1,384]{2,1,0:T(1,128)}), f32[16,1,384]{2,1,0:T(1,128)S(1)}, u32[]{:S(2)}, u32[]{:S(2)}) async-start(f32[16,1,384]{2,1,0:T(1,128)} %broadcast_in_dim.40), calls=%async_computation.2 | async-start | bytes 49152 | tf_op jit(solution)/shard_map/all_to_all | solution.py:188
  80.0 2.4 %copy-start.6 = (f32[8,256,256]{2,1,0:T(8,128)S(1)}, f32[8,256,256]{2,1,0:T(8,128)}, u32[]{:S(2)}) copy-start(f32[8,256,256]{2,1,0:T(8,128)} %get-tuple-element.32) | copy-start | bytes 6291460
  82.5 3.7 %copy-start.11 = (bf16[8,248,256]{2,1,0:T(8,128)(2,1)S(1)}, bf16[8,248,256]{2,1,0:T(8,128)(2,1)}, u32[]{:S(2)}) copy-start(bf16[8,248,256]{2,1,0:T(8,128)(2,1)} %copy-done.10) | copy-start | bytes 3047428
  82.5 3.7 %copy-start.13 = (bf16[8,256,256]{2,1,0:T(8,128)(2,1)S(1)}, bf16[8,256,256]{2,1,0:T(8,128)(2,1)}, u32[]{:S(2)}) copy-start(bf16[8,256,256]{2,1,0:T(8,128)(2,1)} %copy-done.12) | copy-start | bytes 3145732
  88.7 1.6 %copy-start.17 = (f32[8,256,256]{2,1,0:T(8,128)S(1)}, f32[8,256,256]{2,1,0:T(8,128)}, u32[]{:S(2)}) copy-start(f32[8,256,256]{2,1,0:T(8,128)} %get-tuple-element.31) | copy-start | bytes 6291460
  88.9 1.7 %copy-start.9 = (bf16[8,256,256]{2,1,0:T(8,128)(2,1)S(1)}, bf16[8,256,256]{2,1,0:T(8,128)(2,1)}, u32[]{:S(2)}) copy-start(bf16[8,256,256]{2,1,0:T(8,128)(2,1)} %copy-done.8) | copy-start | bytes 3145732
  88.9 2.0 %copy-start.16 = (bf16[2048,256]{1,0:T(8,128)(2,1)S(1)}, bf16[2048,256]{1,0:T(8,128)(2,1)}, u32[]{:S(2)}) copy-start(bf16[2048,256]{1,0:T(8,128)(2,1)} %copy-done.15) | copy-start | bytes 3145732
  94.0 0.9 copy-start.5
  95.0 2.4 %collective-permute-start = (f32[2,384,256]{2,1,0:T(8,128)S(1)}, f32[2,384,256]{2,1,0:T(8,128)S(1)}, u32[]{:S(2)}, u32[]{:S(2)}) collective-permute-start(f32[2,384,256]{2,1,0:T(8,128)S(1)} %fusion.52), channel_id=1, source_target_pairs={{0,1},{1,0},{2,3},{3,2},{4,5},{5,4},{6,7},{7,6},{8,9},{9,8},{10,11... | collective-permute-start | bytes 2359304 | tf_op jit(solution)/shard_map/ppermute | solution.py:161
  98.5 7.8 %collective-permute-start.1 = (f32[2,192,256]{2,1,0:T(8,128)S(1)}, f32[2,192,256]{2,1,0:T(8,128)S(1)}, u32[]{:S(2)}, u32[]{:S(2)}) collective-permute-start(f32[2,192,256]{2,1,0:T(8,128)S(1)} %constant_dynamic-slice_fusion.1), channel_id=1, source_target_pairs={{0,2},{1,5},{2,0},{3,7},{4,6},{5,1},{6,4},{7,3},{8,10},{9,13},{10,... | collective-permute-start | bytes 1179656 | tf_op jit(solution)/shard_map/ppermute | solution.py:161
  106.4 7.8 %collective-permute-start.2 = (f32[2,96,256]{2,1,0:T(8,128)S(1)}, f32[2,96,256]{2,1,0:T(8,128)S(1)}, u32[]{:S(2)}, u32[]{:S(2)}) collective-permute-start(f32[2,96,256]{2,1,0:T(8,128)S(1)} %constant_dynamic-slice_fusion), channel_id=1, source_target_pairs={{0,4},{1,9},{2,6},{3,11},{4,0},{5,13},{6,2},{7,15},{8,12},{9,1},{1... | collective-permute-start | bytes 589832 | tf_op jit(solution)/shard_map/ppermute | solution.py:161
  114.2 5.6 %collective-permute-start.3 = (f32[2,48,256]{2,1,0:T(8,128)S(1)}, f32[2,48,256]{2,1,0:T(8,128)S(1)}, u32[]{:S(2)}, u32[]{:S(2)}) collective-permute-start(f32[2,48,256]{2,1,0:T(8,128)S(1)} %constant_dynamic-slice_fusion.2), channel_id=1, source_target_pairs={{0,8},{1,3},{2,10},{3,1},{4,12},{5,7},{6,14},{7,5},{8,0},{9,11},{1... | collective-permute-start | bytes 294920 | tf_op jit(solution)/shard_map/ppermute | solution.py:161
  119.8 5.6 %collective-permute-start.4 = (bf16[2,48,256]{2,1,0:T(8,128)(2,1)S(1)}, bf16[2,48,256]{2,1,0:T(8,128)(2,1)S(1)}, u32[]{:S(2)}, u32[]{:S(2)}) collective-permute-start(bf16[2,48,256]{2,1,0:T(8,128)(2,1)S(1)} %add_convert_fusion.2), channel_id=1, source_target_pairs={{0,8},{1,3},{2,10},{3,1},{4,12},{5,7},{6,14},{7,5},{8,0},{9,11},{1... | collective-permute-start | bytes 147464 | tf_op jit(solution)/shard_map/ppermute | solution.py:165
  125.4 5.7 %collective-permute-start.5 = (bf16[2,96,256]{2,1,0:T(8,128)(2,1)S(1)}, bf16[2,96,256]{2,1,0:T(8,128)(2,1)S(1)}, u32[]{:S(2)}, u32[]{:S(2)}) collective-permute-start(bf16[2,96,256]{2,1,0:T(8,128)(2,1)S(1)} %pad_maximum_fusion.2), channel_id=1, source_target_pairs={{0,4},{1,9},{2,6},{3,11},{4,0},{5,13},{6,2},{7,15},{8,12},{9,1},{1... | collective-permute-start | bytes 294920 | tf_op jit(solution)/shard_map/ppermute | solution.py:165
  131.2 5.7 %collective-permute-start.6 = (bf16[2,192,256]{2,1,0:T(8,128)(2,1)S(1)}, bf16[2,192,256]{2,1,0:T(8,128)(2,1)S(1)}, u32[]{:S(2)}, u32[]{:S(2)}) collective-permute-start(bf16[2,192,256]{2,1,0:T(8,128)(2,1)S(1)} %pad_maximum_fusion.1), channel_id=1, source_target_pairs={{0,2},{1,5},{2,0},{3,7},{4,6},{5,1},{6,4},{7,3},{8,10},{9,13},{10,... | collective-permute-start | bytes 589832 | tf_op jit(solution)/shard_map/ppermute | solution.py:165
  137.1 1.8 %collective-permute-start.7 = (bf16[2,384,256]{2,1,0:T(8,128)(2,1)S(1)}, bf16[2,384,256]{2,1,0:T(8,128)(2,1)S(1)}, u32[]{:S(2)}, u32[]{:S(2)}) collective-permute-start(bf16[2,384,256]{2,1,0:T(8,128)(2,1)S(1)} %pad_maximum_fusion), channel_id=1, source_target_pairs={{0,1},{1,0},{2,3},{3,2},{4,5},{5,4},{6,7},{7,6},{8,9},{9,8},{10,11... | collective-permute-start | bytes 1179656 | tf_op jit(solution)/shard_map/ppermute | solution.py:165
  139.0 1.4 copy-start.7
  139.1 1.8 %copy-start.2 = (f32[2,196608]{1,0:T(2,128)S(1)}, f32[2,196608]{1,0:T(2,128)}, u32[]{:S(2)}) copy-start(f32[2,196608]{1,0:T(2,128)} %param.11) | copy-start | bytes 4718596
  139.1 2.2 %copy-start.4 = (f32[2,196608]{1,0:T(2,128)S(1)}, f32[2,196608]{1,0:T(2,128)}, u32[]{:S(2)}) copy-start(f32[2,196608]{1,0:T(2,128)} %param.9) | copy-start | bytes 4718596

commit v17 on v15

--- a/solution.py
+++ b/solution.py
@@ -152,8 +152,15 @@
         bit_odd = (me >> order_odd[step]) & 1
         return pairs, jnp.where(odd == 1, bit_odd, bit_even)
 
-    buf = grads
-    for step in range(steps):
+    pairs, bit = exchange_at(0)
+    half = grads[0].shape[0] // 2
+    per_layer = []
+    for layer_grad in grads:
+        keep = lax.dynamic_slice_in_dim(layer_grad, bit * half, half, axis=0)
+        send = lax.dynamic_slice_in_dim(layer_grad, (1 - bit) * half, half, axis=0)
+        per_layer.append(keep + lax.ppermute(send, "wide", pairs))
+    buf = jnp.stack(per_layer)
+    for step in range(1, steps):
         pairs, bit = exchange_at(step)
         half = buf.shape[1] // 2
         keep = lax.dynamic_slice_in_dim(buf, bit * half, half, axis=1)
@@ -219,8 +226,7 @@
             offset = 4**layer_at
             for tap_index in range(KER):
                 upstream = upstream + advanced(back_rows[:, :, tap_index], tap_index * offset)
-    stacked_grads = jnp.stack(gradients)
-    full_grad = all_reduce_wide(stacked_grads)
+    full_grad = all_reduce_wide(gradients)
     new_momentum = momentum_rate * momentum + full_grad
     new_master = master - learn_rate * new_momentum
     new_teacher = ema_rate * teacher + (1.0 - ema_rate) * new_master

time: 145 us -> 145 us (level)
  waiting for transfers between devices: 68 us -> 66 us
    ppermute x4 -> x3, waiting for transfers between devices: 22.6 us -> 20.2 us  [all_reduce_wide(): buf = keep + lax.ppermute(send, 'wide', pairs)]
    another operation x3 -> x5, other arithmetic: 0.08 us -> 2.16 us  [the longest x3 2.13 us: all_reduce_wide(): buf = jnp.stack(per_layer)]
  transfers between devices with their start and end apart: 11 -> 12, of which waited for: 11 -> 11; matrix products, arithmetic and copies ran while one was open for 5% -> 9% of each run, Pallas kernels for 0% -> 0%
where the time goes in v17:
time: 145 us
  waiting for transfers between devices  66 us (46%)
  matrix products  26.4 us (18%)
  starting transfers between devices  21.1 us (15%)
  other arithmetic  19.1 us (13%)
  local copies, waits for them, and re-layouts  10.1 us (7%)
  between operations  1.83 us (1%)
    ppermute x3, waiting for transfers between devices, all_reduce_wide(): buf = keep + lax.ppermute(send, 'wide', pairs)  20.2 us
    all_to_all x1, waiting for transfers between devices, route_rows(): lax.all_to_all(send_rows.reshape(wide_count, capacity, feat_width), 'wide...  19 us
    ppermute x4, waiting for transfers between devices, all_reduce_wide(): got = lax.ppermute(buf, 'wide', pairs)  17.5 us
    dot_general x4, matrix products, run_network(): jnp.dot(stacked.reshape(-1, stacked.shape[2]), weights[layer_at], preferr...  8.33 us
    all_to_all x1, starting transfers between devices, route_rows(): lax.all_to_all(send_place.reshape(wide_count, capacity, per_dev), 'wide',...  7.35 us
    all_to_all x1, starting transfers between devices, local(): lax.all_to_all(jnp.broadcast_to(stats[None, :], (wide_count, stats.shape[...  6.83 us
    unnamed x39, local copies, waits for them, and re-layouts  6.71 us
    all_to_all x1, waiting for transfers between devices, local(): lax.all_to_all(jnp.broadcast_to(stats[None, :], (wide_count, stats.shape[...  6.51 us
  transfers between devices with their start and end apart: 12, of which 11 were waited for; matrix products, arithmetic and copies ran while one was open for 9% of the time, Pallas kernels for 0%

profile of v17, /device:TPU:0, one launch (start us, length us, event | category | flops | bytes accessed | tf_op | source)
XLA Modules:
  0.0 144.6 jit_solution(9584399725594202046)
XLA Ops:
  2.8 1.3 select_reduce_fusion
  5.5 3.8 %fusion.46 = bf16[16,128,8]{1,2,0:T(8,128)(2,1)} fusion(s32[2048]{0:T(1024)S(1)} %get-tuple-element.29, s32[2048]{0:T(1024)S(1)} %get-tuple-element.28, pred[2048]{0:T(1024)(128)(4,1)S(1)} %broadcast_compare_fusion.1), kind=kOutput, calls=%fused_computation.72 | convolution fusion | flops 71352320 | bytes 51200 | tf_op jit(solution)/shard_map/dot_general | solution.py:102
  9.3 7.4 %all-to-all-start = ((bf16[16,128,8]{1,2,0:T(8,128)(2,1)}), bf16[16,128,8]{1,2,0:T(8,128)(2,1)S(1)}, u32[]{:S(2)}, u32[]{:S(2)}) async-start(bf16[16,128,8]{1,2,0:T(8,128)(2,1)} %fusion.46), calls=%async_computation | async-start | bytes 65536 | tf_op jit(solution)/shard_map/all_to_all | solution.py:112
  16.6 4.2 %fusion.22 = bf16[2048,256]{1,0:T(8,128)(2,1)} fusion(bf16[2048,256]{1,0:T(8,128)(2,1)S(1)} %copy-done, s32[2048]{0:T(1024)S(1)} %get-tuple-element.29), kind=kOutput, calls=%fused_computation.32 | convolution fusion | flops 2152202240 | bytes 2105344 | tf_op jit(solution)/shard_map/dot_general | solution.py:103
  20.8 2.5 %all-to-all-done = bf16[16,128,8]{1,2,0:T(8,128)(2,1)S(1)} async-done(((bf16[16,128,8]{1,2,0:T(8,128)(2,1)}), bf16[16,128,8]{1,2,0:T(8,128)(2,1)S(1)}, u32[]{:S(2)}, u32[]{:S(2)}) %all-to-all-start) | async-done | bytes 32800 | tf_op jit(solution)/shard_map/all_to_all | solution.py:112
  23.2 4.5 %all-to-all-start.1 = ((bf16[16,128,256]{2,1,0:T(8,128)(2,1)}), bf16[16,128,256]{2,1,0:T(8,128)(2,1)}, u32[]{:S(2)}, u32[]{:S(2)}) async-start(bf16[16,128,256]{2,1,0:T(8,128)(2,1)} %bitcast.142), calls=%async_computation.1 | async-start | bytes 2097152 | tf_op jit(solution)/shard_map/all_to_all | solution.py:105
  27.8 1.0 copy.86
  31.5 19.0 %all-to-all-done.1 = bf16[16,128,256]{2,1,0:T(8,128)(2,1)} async-done(((bf16[16,128,256]{2,1,0:T(8,128)(2,1)}), bf16[16,128,256]{2,1,0:T(8,128)(2,1)}, u32[]{:S(2)}, u32[]{:S(2)}) %all-to-all-start.1) | async-done | bytes 1048608 | tf_op jit(solution)/shard_map/all_to_all | solution.py:105
  50.5 4.5 %fusion.21 = bf16[2048,256]{1,0:T(8,128)(2,1)S(1)} fusion(bf16[2048,256]{1,0:T(8,128)(2,1)} %bitcast.12, s32[2048]{0:T(1024)S(1)} %select_bitcast_fusion), kind=kOutput, calls=%fused_computation.31 | convolution fusion | flops 2152202240 | bytes 2105344 | tf_op jit(solution)/shard_map/dot_general | solution.py:131
  55.0 1.5 %fusion.25 = bf16[8,256,256]{2,1,0:T(8,128)(2,1)S(1)} fusion(bf16[8,256,256]{2,1,0:T(8,128)(2,1)S(1)} %bitcast.151, bf16[2,768,256]{2,1,0:T(8,128)(2,1)S(1)} %bitcast.146, bf16[8,254,256]{2,1,0:T(8,128)(2,1)S(1)} %bitcast.152, bf16[8,255,256]{2,1,0:T(8,128)(2,1)S(1)} %bitcast.153), kind=kOutput, calls=%fused_computation.35 | convolution fusion | flops 827850752 | bytes 5636096 | tf_op jit(solution)/shard_map/dot_general | solution.py:49
  56.6 2.5 %fusion.24 = (bf16[8,256,256]{2,1,0:T(8,128)(2,1)S(1)}, f32[8,256,256]{2,1,0:T(8,128)}) fusion(bf16[8,256,256]{2,1,0:T(8,128)(2,1)S(1)} %bitcast.154, bf16[2,768,256]{2,1,0:T(8,128)(2,1)S(1)} %bitcast.138, bf16[8,254,256]{2,1,0:T(8,128)(2,1)S(1)} %bitcast.155, bf16[8,255,256]{2,1,0:T(8,128)(2,1)S(1)} %bitcast.156), kind=kOutput, calls=%fused_computation.34 | convolution fusion | flops 827850752 | bytes 7733248 | tf_op jit(solution)/shard_map/dot_general | solution.py:49
  59.2 2.5 %fusion.98 = (bf16[8,256]{1,0:T(8,128)(2,1)S(1)}, bf16[8,256,256]{2,1,0:T(8,128)(2,1)S(1)}, f32[8,256,256]{2,1,0:T(8,128)}) fusion(bf16[8,256,256]{2,1,0:T(8,128)(2,1)S(1)} %get-tuple-element.30, bf16[2,768,256]{2,1,0:T(8,128)(2,1)S(1)} %bitcast.139, bf16[8,248,256]{2,1,0:T(8,128)(2,1)S(1)} %slice.87, bf16[8,252,256]{2,1,0:T(8,128)(2,1)S(1)} %bitcast.143), kind=kOutput, calls=%fused_computation.171 | convolution fusion | flops 828372992 | bytes 7704576 | tf_op jit(solution)/shard_map/dot_general | solution.py:49
  61.7 1.8 %fusion.32 = (f32[8,256]{1,0:T(8,128)S(1)}, f32[8,256]{1,0:T(8,128)S(1)}, f32[256]{0:T(256)S(1)}, bf16[8,256,256]{2,1,0:T(8,128)(2,1)S(1)}) fusion(bf16[8,256,256]{2,1,0:T(8,128)(2,1)S(1)} %get-tuple-element.15, f32[8,256]{1,0:T(8,128)S(1)} %fusion.81, f32[8,256]{1,0:T(8,128)S(1)} %bitcast.148, bf16[2,768,256]{2,1,0:T(8,128)(2,1)S(1)} %bitcast.147, ...), kind=kOutput, calls=%fused_computation.42 | convolution fusion | flops 832040704 | bytes 6685696 | tf_op jit(solution)/shard_map/dot_general | solution.py:49
  64.2 6.8 %all-to-all-start.2 = ((f32[16,1,384]{2,1,0:T(1,128)}), f32[16,1,384]{2,1,0:T(1,128)S(1)}, u32[]{:S(2)}, u32[]{:S(2)}) async-start(f32[16,1,384]{2,1,0:T(1,128)} %broadcast_in_dim.40), calls=%async_computation.2 | async-start | bytes 49152 | tf_op jit(solution)/shard_map/all_to_all | solution.py:195
  71.1 6.5 %all-to-all-done.2 = f32[16,1,384]{2,1,0:T(1,128)S(1)} async-done(((f32[16,1,384]{2,1,0:T(1,128)}), f32[16,1,384]{2,1,0:T(1,128)S(1)}, u32[]{:S(2)}, u32[]{:S(2)}) %all-to-all-start.2) | async-done | bytes 24608 | tf_op jit(solution)/shard_map/all_to_all | solution.py:195
  80.1 3.7 %multiply_convert_fusion = bf16[8,256,256]{2,1,0:T(8,128)(2,1)S(1)} fusion(f32[8,256,256]{2,1,0:T(8,128)S(1)} %copy-done.5, f32[8,256]{1,0:T(8,128)S(1)} %fusion.39, f32[8,256]{1,0:T(8,128)S(1)} %fusion.36, f32[256]{0:T(256)S(1)} %slice_divide_fusion, bf16[8,256,256]{2,1,0:T(8,128)(2,1)S(1)} %get-tuple-element.33, f32[8,256]{1,0:T(8,128)S(1)} %get-tuple-element.5, ...), kind=kLoop, calls=%fused_computation.58 | loop fusion | flops 10485760 | bytes 5284864 | tf_op jit(solution)/shard_map/convert_element_type | solution.py:210
  83.8 1.0 convolution_bitcast_fusion
  85.7 1.0 fusion.47
  87.5 1.1 copy-done.17
  89.3 3.1 %convolution_bitcast_fusion.1 = f32[768,256]{1,0:T(8,128)S(1)} fusion(f32[8,256,3,256]{3,1,0,2:T(8,128)S(1)} %fusion.47, f32[8,256,256]{2,1,0:T(8,128)S(1)} %copy-done.17, f32[8,248,256]{2,1,0:T(8,128)S(1)} %slice.97, f32[8,252,256]{2,1,0:T(8,128)S(1)} %slice.95, bf16[8,256,256]{2,1,0:T(8,128)(2,1)S(1)} %copy-done.8, ...), kind=kOutput, calls=%fused_computation.71 | convolution fusion | flops 836239360 | bytes 14394368 | tf_op jit(solution)/shard_map/dot_general | solution.py:212
  92.4 0.9 copy-done.13
  93.9 1.0 add_bitcast_fusion
  95.3 1.0 add_bitcast_fusion.1
  96.8 7.4 %collective-permute-done.2 = f32[2,192,256]{2,1,0:T(8,128)S(1)} collective-permute-done((f32[2,192,256]{2,1,0:T(8,128)S(1)}, f32[2,192,256]{2,1,0:T(8,128)S(1)}, u32[]{:S(2)}, u32[]{:S(2)}) %collective-permute-start.2) | collective-permute-done | bytes 393248 | tf_op jit(solution)/shard_map/ppermute | solution.py:168
  104.8 7.3 %collective-permute-done.3 = f32[2,96,256]{2,1,0:T(8,128)S(1)} collective-permute-done((f32[2,96,256]{2,1,0:T(8,128)S(1)}, f32[2,96,256]{2,1,0:T(8,128)S(1)}, u32[]{:S(2)}, u32[]{:S(2)}) %collective-permute-start.3) | collective-permute-done | bytes 196640 | tf_op jit(solution)/shard_map/ppermute | solution.py:168
  112.2 5.6 %collective-permute-done.4 = f32[2,48,256]{2,1,0:T(8,128)S(1)} collective-permute-done((f32[2,48,256]{2,1,0:T(8,128)S(1)}, f32[2,48,256]{2,1,0:T(8,128)S(1)}, u32[]{:S(2)}, u32[]{:S(2)}) %collective-permute-start.4) | collective-permute-done | bytes 98336 | tf_op jit(solution)/shard_map/ppermute | solution.py:168
  117.8 5.8 %collective-permute-done.5 = bf16[2,48,256]{2,1,0:T(8,128)(2,1)S(1)} collective-permute-done((bf16[2,48,256]{2,1,0:T(8,128)(2,1)S(1)}, bf16[2,48,256]{2,1,0:T(8,128)(2,1)S(1)}, u32[]{:S(2)}, u32[]{:S(2)}) %collective-permute-start.5) | collective-permute-done | bytes 49184 | tf_op jit(solution)/shard_map/ppermute | solution.py:172
  123.7 5.6 %collective-permute-done.6 = bf16[2,96,256]{2,1,0:T(8,128)(2,1)S(1)} collective-permute-done((bf16[2,96,256]{2,1,0:T(8,128)(2,1)S(1)}, bf16[2,96,256]{2,1,0:T(8,128)(2,1)S(1)}, u32[]{:S(2)}, u32[]{:S(2)}) %collective-permute-start.6) | collective-permute-done | bytes 98336 | tf_op jit(solution)/shard_map/ppermute | solution.py:172
  130.0 5.1 %collective-permute-done.7 = bf16[2,192,256]{2,1,0:T(8,128)(2,1)S(1)} collective-permute-done((bf16[2,192,256]{2,1,0:T(8,128)(2,1)S(1)}, bf16[2,192,256]{2,1,0:T(8,128)(2,1)S(1)}, u32[]{:S(2)}, u32[]{:S(2)}) %collective-permute-start.7) | collective-permute-done | bytes 196640 | tf_op jit(solution)/shard_map/ppermute | solution.py:172
  136.0 1.0 collective-permute-done.8
  137.3 1.2 copy.83
  139.6 5.0 %multiply_add_fusion = (f32[2,196608]{1,0:T(2,128)}, f32[2,196608]{1,0:T(2,128)}, f32[2,196608]{1,0:T(2,128)}) fusion(f32[2,196608]{1,0:T(2,128)S(1)} %copy-done.2, f32[2,196608]{1,0:T(2,128)S(1)} %copy-done.4, f32[2,196608]{1,0:T(2,128)S(1)} %bitcast.137, f32[2,196608]{1,0:T(2,128)S(1)} %copy-done.6), kind=kLoop, calls=%fused_computation.67 | loop fusion | flops 2752512 | bytes 11010048 | tf_op jit(solution)/shard_map/add | solution.py:232
  (97 shorter events, 16.2 us)
Async XLA Ops:
  0.6 16.0 %copy-start = (bf16[2048,256]{1,0:T(8,128)(2,1)S(1)}, bf16[2048,256]{1,0:T(8,128)(2,1)}, u32[]{:S(2)}) copy-start(bf16[2048,256]{1,0:T(8,128)(2,1)} %param.6) | copy-start | bytes 3145732
  9.3 14.0 %all-to-all-start = ((bf16[16,128,8]{1,2,0:T(8,128)(2,1)}), bf16[16,128,8]{1,2,0:T(8,128)(2,1)S(1)}, u32[]{:S(2)}, u32[]{:S(2)}) async-start(bf16[16,128,8]{1,2,0:T(8,128)(2,1)} %fusion.46), calls=%async_computation | async-start | bytes 65536 | tf_op jit(solution)/shard_map/all_to_all | solution.py:112
  20.8 7.0 %copy-start.1 = (f32[2,196608]{1,0:T(2,128)S(1)}, f32[2,196608]{1,0:T(2,128)}, u32[]{:S(2)}) copy-start(f32[2,196608]{1,0:T(2,128)} %param.11) | copy-start | bytes 4718596
  23.2 27.3 %all-to-all-start.1 = ((bf16[16,128,256]{2,1,0:T(8,128)(2,1)}), bf16[16,128,256]{2,1,0:T(8,128)(2,1)}, u32[]{:S(2)}, u32[]{:S(2)}) async-start(bf16[16,128,256]{2,1,0:T(8,128)(2,1)} %bitcast.142), calls=%async_computation.1 | async-start | bytes 2097152 | tf_op jit(solution)/shard_map/all_to_all | solution.py:105
  27.8 1.7 %copy-start.3 = (f32[2,196608]{1,0:T(2,128)S(1)}, f32[2,196608]{1,0:T(2,128)}, u32[]{:S(2)}) copy-start(f32[2,196608]{1,0:T(2,128)} %param.9) | copy-start | bytes 4718596
  50.5 4.5 %copy-start.14 = (bf16[1,2,768,256]{3,2,1,0:T(8,128)(2,1)S(1)}, bf16[1,2,768,256]{3,2,1,0:T(8,128)(2,1)}, u32[]{:S(2)}) copy-start(bf16[1,2,768,256]{3,2,1,0:T(8,128)(2,1)} %copy.86) | copy-start | bytes 2359300
  55.0 1.6 %copy-start.15 = (bf16[2048,256]{1,0:T(8,128)(2,1)}, bf16[2048,256]{1,0:T(8,128)(2,1)S(1)}, u32[]{:S(2)}) copy-start(bf16[2048,256]{1,0:T(8,128)(2,1)S(1)} %fusion.21) | copy-start | bytes 3145732
  59.1 2.6 %copy-start.11 = (bf16[8,256,256]{2,1,0:T(8,128)(2,1)}, bf16[8,256,256]{2,1,0:T(8,128)(2,1)S(1)}, u32[]{:S(2)}) copy-start(bf16[8,256,256]{2,1,0:T(8,128)(2,1)S(1)} %get-tuple-element.30) | copy-start | bytes 3145732
  59.2 2.5 %copy-start.9 = (bf16[8,248,256]{2,1,0:T(8,128)(2,1)}, bf16[8,248,256]{2,1,0:T(8,128)(2,1)S(1)}, u32[]{:S(2)}) copy-start(bf16[8,248,256]{2,1,0:T(8,128)(2,1)S(1)} %slice.87) | copy-start | bytes 3047428
  61.7 1.9 %copy-start.7 = (bf16[8,256,256]{2,1,0:T(8,128)(2,1)}, bf16[8,256,256]{2,1,0:T(8,128)(2,1)S(1)}, u32[]{:S(2)}) copy-start(bf16[8,256,256]{2,1,0:T(8,128)(2,1)S(1)} %get-tuple-element.15) | copy-start | bytes 3145732
  64.2 13.4 %all-to-all-start.2 = ((f32[16,1,384]{2,1,0:T(1,128)}), f32[16,1,384]{2,1,0:T(1,128)S(1)}, u32[]{:S(2)}, u32[]{:S(2)}) async-start(f32[16,1,384]{2,1,0:T(1,128)} %broadcast_in_dim.40), calls=%async_computation.2 | async-start | bytes 49152 | tf_op jit(solution)/shard_map/all_to_all | solution.py:195
  77.7 2.4 %copy-start.5 = (f32[8,256,256]{2,1,0:T(8,128)S(1)}, f32[8,256,256]{2,1,0:T(8,128)}, u32[]{:S(2)}) copy-start(f32[8,256,256]{2,1,0:T(8,128)} %get-tuple-element.32) | copy-start | bytes 6291460
  80.1 3.7 %copy-start.10 = (bf16[8,248,256]{2,1,0:T(8,128)(2,1)S(1)}, bf16[8,248,256]{2,1,0:T(8,128)(2,1)}, u32[]{:S(2)}) copy-start(bf16[8,248,256]{2,1,0:T(8,128)(2,1)} %copy-done.9) | copy-start | bytes 3047428
  80.1 3.7 %copy-start.12 = (bf16[8,256,256]{2,1,0:T(8,128)(2,1)S(1)}, bf16[8,256,256]{2,1,0:T(8,128)(2,1)}, u32[]{:S(2)}) copy-start(bf16[8,256,256]{2,1,0:T(8,128)(2,1)} %copy-done.11) | copy-start | bytes 3145732
  85.7 8.3 %collective-permute-start.1 = (f32[384,256]{1,0:T(8,128)}, f32[384,256]{1,0:T(8,128)}, u32[]{:S(2)}, u32[]{:S(2)}) collective-permute-start(f32[384,256]{1,0:T(8,128)} %constant_dynamic-slice_fusion.2), channel_id=1, source_target_pairs={{0,1},{1,0},{2,3},{3,2},{4,5},{5,4},{6,7},{7,6},{8,9},{9,8},{10,11... | collective-permute-start | bytes 1179656 | tf_op jit(solution)/shard_map/ppermute | solution.py:161
  87.1 1.6 %copy-start.17 = (f32[8,256,256]{2,1,0:T(8,128)S(1)}, f32[8,256,256]{2,1,0:T(8,128)}, u32[]{:S(2)}) copy-start(f32[8,256,256]{2,1,0:T(8,128)} %get-tuple-element.31) | copy-start | bytes 6291460
  87.3 1.7 %copy-start.8 = (bf16[8,256,256]{2,1,0:T(8,128)(2,1)S(1)}, bf16[8,256,256]{2,1,0:T(8,128)(2,1)}, u32[]{:S(2)}) copy-start(bf16[8,256,256]{2,1,0:T(8,128)(2,1)} %copy-done.7) | copy-start | bytes 3145732
  87.3 2.0 %copy-start.16 = (bf16[2048,256]{1,0:T(8,128)(2,1)S(1)}, bf16[2048,256]{1,0:T(8,128)(2,1)}, u32[]{:S(2)}) copy-start(bf16[2048,256]{1,0:T(8,128)(2,1)} %copy-done.15) | copy-start | bytes 3145732
  92.4 0.9 copy-start.13
  93.3 1.9 %collective-permute-start = (f32[384,256]{1,0:T(8,128)S(1)}, f32[384,256]{1,0:T(8,128)S(1)}, u32[]{:S(2)}, u32[]{:S(2)}) collective-permute-start(f32[384,256]{1,0:T(8,128)S(1)} %constant_dynamic-slice_fusion.3), channel_id=1, source_target_pairs={{0,1},{1,0},{2,3},{3,2},{4,5},{5,4},{6,7},{7,6},{8,9},{9,8},{10,11... | collective-permute-start | bytes 1179656 | tf_op jit(solution)/shard_map/ppermute | solution.py:161
  96.4 7.8 %collective-permute-start.2 = (f32[2,192,256]{2,1,0:T(8,128)S(1)}, f32[2,192,256]{2,1,0:T(8,128)S(1)}, u32[]{:S(2)}, u32[]{:S(2)}) collective-permute-start(f32[2,192,256]{2,1,0:T(8,128)S(1)} %fusion.56), channel_id=1, source_target_pairs={{0,2},{1,5},{2,0},{3,7},{4,6},{5,1},{6,4},{7,3},{8,10},{9,13},{10,... | collective-permute-start | bytes 1179656 | tf_op jit(solution)/shard_map/ppermute | solution.py:168
  104.3 7.7 %collective-permute-start.3 = (f32[2,96,256]{2,1,0:T(8,128)S(1)}, f32[2,96,256]{2,1,0:T(8,128)S(1)}, u32[]{:S(2)}, u32[]{:S(2)}) collective-permute-start(f32[2,96,256]{2,1,0:T(8,128)S(1)} %constant_dynamic-slice_fusion), channel_id=1, source_target_pairs={{0,4},{1,9},{2,6},{3,11},{4,0},{5,13},{6,2},{7,15},{8,12},{9,1},{1... | collective-permute-start | bytes 589832 | tf_op jit(solution)/shard_map/ppermute | solution.py:168
  112.1 5.6 %collective-permute-start.4 = (f32[2,48,256]{2,1,0:T(8,128)S(1)}, f32[2,48,256]{2,1,0:T(8,128)S(1)}, u32[]{:S(2)}, u32[]{:S(2)}) collective-permute-start(f32[2,48,256]{2,1,0:T(8,128)S(1)} %constant_dynamic-slice_fusion.1), channel_id=1, source_target_pairs={{0,8},{1,3},{2,10},{3,1},{4,12},{5,7},{6,14},{7,5},{8,0},{9,11},{1... | collective-permute-start | bytes 294920 | tf_op jit(solution)/shard_map/ppermute | solution.py:168
  117.7 5.9 %collective-permute-start.5 = (bf16[2,48,256]{2,1,0:T(8,128)(2,1)S(1)}, bf16[2,48,256]{2,1,0:T(8,128)(2,1)S(1)}, u32[]{:S(2)}, u32[]{:S(2)}) collective-permute-start(bf16[2,48,256]{2,1,0:T(8,128)(2,1)S(1)} %add_convert_fusion.2), channel_id=1, source_target_pairs={{0,8},{1,3},{2,10},{3,1},{4,12},{5,7},{6,14},{7,5},{8,0},{9,11},{1... | collective-permute-start | bytes 147464 | tf_op jit(solution)/shard_map/ppermute | solution.py:172
  123.6 5.7 %collective-permute-start.6 = (bf16[2,96,256]{2,1,0:T(8,128)(2,1)S(1)}, bf16[2,96,256]{2,1,0:T(8,128)(2,1)S(1)}, u32[]{:S(2)}, u32[]{:S(2)}) collective-permute-start(bf16[2,96,256]{2,1,0:T(8,128)(2,1)S(1)} %pad_maximum_fusion.2), channel_id=1, source_target_pairs={{0,4},{1,9},{2,6},{3,11},{4,0},{5,13},{6,2},{7,15},{8,12},{9,1},{1... | collective-permute-start | bytes 294920 | tf_op jit(solution)/shard_map/ppermute | solution.py:172
  129.4 5.7 %collective-permute-start.7 = (bf16[2,192,256]{2,1,0:T(8,128)(2,1)S(1)}, bf16[2,192,256]{2,1,0:T(8,128)(2,1)S(1)}, u32[]{:S(2)}, u32[]{:S(2)}) collective-permute-start(bf16[2,192,256]{2,1,0:T(8,128)(2,1)S(1)} %pad_maximum_fusion.1), channel_id=1, source_target_pairs={{0,2},{1,5},{2,0},{3,7},{4,6},{5,1},{6,4},{7,3},{8,10},{9,13},{10,... | collective-permute-start | bytes 589832 | tf_op jit(solution)/shard_map/ppermute | solution.py:172
  135.2 1.8 %collective-permute-start.8 = (bf16[2,384,256]{2,1,0:T(8,128)(2,1)S(1)}, bf16[2,384,256]{2,1,0:T(8,128)(2,1)S(1)}, u32[]{:S(2)}, u32[]{:S(2)}) collective-permute-start(bf16[2,384,256]{2,1,0:T(8,128)(2,1)S(1)} %pad_maximum_fusion), channel_id=1, source_target_pairs={{0,1},{1,0},{2,3},{3,2},{4,5},{5,4},{6,7},{7,6},{8,9},{9,8},{10,11... | collective-permute-start | bytes 1179656 | tf_op jit(solution)/shard_map/ppermute | solution.py:172
  137.2 1.4 copy-start.6
  137.3 1.8 %copy-start.2 = (f32[2,196608]{1,0:T(2,128)S(1)}, f32[2,196608]{1,0:T(2,128)}, u32[]{:S(2)}) copy-start(f32[2,196608]{1,0:T(2,128)} %param.11) | copy-start | bytes 4718596
  137.3 2.2 %copy-start.4 = (f32[2,196608]{1,0:T(2,128)S(1)}, f32[2,196608]{1,0:T(2,128)}, u32[]{:S(2)}) copy-start(f32[2,196608]{1,0:T(2,128)} %param.9) | copy-start | bytes 4718596

commit v18 on v9

--- a/solution.py
+++ b/solution.py
@@ -86,12 +86,16 @@
     match_table = safe_object[:, None] == jnp.arange(objects_all, dtype=jnp.int32)[None, :]
     slot_of = jnp.sum(jnp.where(match_table, object_slot[None, :], 0), axis=1)
     owner_dev = slot_of // per_dev
+    local_place = slot_of % per_dev
     slot_hot = (slot_of[:, None] == jnp.arange(objects_all, dtype=jnp.int32)[None, :]) & live_rows[:, None]
     group_size = jnp.sum(slot_hot.astype(jnp.int32), axis=0).reshape(wide_count, per_dev)
-    got_size = lax.all_to_all(group_size, "wide", split_axis=0, concat_axis=0, tiled=True)
     places = jnp.arange(per_dev, dtype=jnp.int32)
     earlier_place = (places[:, None] < places[None, :]).astype(jnp.int32)
     group_start = jnp.sum(group_size[:, :, None] * earlier_place[None, :, :], axis=1)
+    slots = jnp.arange(capacity, dtype=jnp.int32)[None, :, None]
+    place_chunks = (
+        (slots >= group_start[:, None, :]) & (slots < (group_start + group_size)[:, None, :])
+    ).astype(jnp.bfloat16)
     running = prefix_count(slot_hot)
     rank_in_group = jnp.sum(jnp.where(slot_hot, running, 0), axis=1) - 1
     start_of_row = jnp.sum(jnp.where(slot_hot, group_start.reshape(1, -1), 0), axis=1)
@@ -100,6 +104,7 @@
         jnp.arange(rows_total, dtype=jnp.int32)[:, None] == send_index[None, :]
     ).astype(jnp.bfloat16)
     send_rows = jnp.dot(pick, epoch_rows, preferred_element_type=jnp.float32).astype(jnp.bfloat16)
+    got_place = lax.all_to_all(place_chunks, "wide", split_axis=0, concat_axis=0, tiled=True)
     got_rows = lax.all_to_all(
         send_rows.reshape(wide_count, capacity, feat_width),
         "wide",
@@ -107,18 +112,14 @@
         concat_axis=0,
         tiled=True,
     )
-    sources = jnp.arange(wide_count, dtype=jnp.int32)
-    earlier_source = (sources[:, None] > sources[None, :]).astype(jnp.int32)
-    before_source = jnp.sum(earlier_source[:, :, None] * got_size[None, :, :], axis=1)
-    got_start = jnp.sum(got_size[:, :, None] * earlier_place[None, :, :], axis=1)
-    slots = jnp.arange(capacity, dtype=jnp.int32)[None, :, None]
-    in_group = (slots >= got_start[:, None, :]) & (slots < (got_start + got_size)[:, None, :])
-    position = jnp.sum(
-        jnp.where(in_group, before_source[:, None, :] + slots - got_start[:, None, :], 0), axis=2
-    )
-    place_code = jnp.sum(jnp.where(in_group, places[None, None, :], 0), axis=2)
-    target = jnp.where(jnp.any(in_group, axis=2), place_code * SEQ + position, -1).reshape(-1)
-    counts = jnp.sum(got_size, axis=0)
+    place_hot = got_place.reshape(-1, per_dev) > 0
+    arrival = prefix_count(place_hot)
+    position = jnp.sum(jnp.where(place_hot, arrival, 0), axis=1) - 1
+    place_code = jnp.sum(
+        jnp.where(place_hot, jnp.arange(per_dev, dtype=jnp.int32)[None, :], 0), axis=1
+    )
+    counts = jnp.sum(place_hot.astype(jnp.int32), axis=0)
+    target = jnp.where(jnp.any(place_hot, axis=1), place_code * SEQ + position, -1)
     put = (
         jnp.arange(per_dev * SEQ, dtype=jnp.int32)[:, None] == target[None, :]
     ).astype(jnp.bfloat16)

time: 147 us -> 147 us (level)
  starting transfers between devices: 20.5 us -> 22.1 us
  waiting for transfers between devices: 67.3 us -> 65.8 us
    all_to_all x1, waiting for transfers between devices: 1.95 us -> 0.01 us  [route_rows(): lax.all_to_all(place_chunks, 'wide', split_axis=0, concat_axis=0, tiled=T...]
    all_to_all x1, starting transfers between devices: 4.65 us -> 6.2 us  [route_rows(): lax.all_to_all(send_rows.reshape(wide_count, capacity, feat_width), 'wide...]
  transfers between devices with their start and end apart: 11 -> 11, of which waited for: 11 -> 10; matrix products, arithmetic and copies ran while one was open for 5% -> 9% of each run, Pallas kernels for 0% -> 0%
where the time goes in v18:
time: 147 us; the launch traced here: 146 us
  waiting for transfers between devices  65.8 us (45%)
  matrix products  24.8 us (17%)
  starting transfers between devices  22.1 us (15%)
  other arithmetic  22 us (15%)
  local copies, waits for them, and re-layouts  9.48 us (6%)
  between operations  1.9 us (1%)
    ppermute x4, waiting for transfers between devices, all_reduce_wide(): buf = keep + lax.ppermute(send, 'wide', pairs)  22.6 us
    all_to_all x1, waiting for transfers between devices, route_rows(): lax.all_to_all(send_rows.reshape(wide_count, capacity, feat_width), 'wide...  19.2 us
    ppermute x4, waiting for transfers between devices, all_reduce_wide(): got = lax.ppermute(buf, 'wide', pairs)  17.4 us
    dot_general x4, matrix products, run_network(): jnp.dot(stacked.reshape(-1, stacked.shape[2]), weights[layer_at], preferr...  8.34 us
    all_to_all x1, starting transfers between devices, route_rows(): lax.all_to_all(place_chunks, 'wide', split_axis=0, concat_axis=0, tiled=T...  7.36 us
    all_to_all x1, starting transfers between devices, local(): lax.all_to_all(jnp.broadcast_to(stats[None, :], (wide_count, stats.shape[...  6.86 us
    unnamed x41, local copies, waits for them, and re-layouts  6.71 us
    all_to_all x1, waiting for transfers between devices, local(): lax.all_to_all(jnp.broadcast_to(stats[None, :], (wide_count, stats.shape[...  6.52 us
  transfers between devices with their start and end apart: 11, of which 10 were waited for; matrix products, arithmetic and copies ran while one was open for 9% of the time, Pallas kernels for 0%

profile of v18, /device:TPU:0, one launch (start us, length us, event | category | flops | bytes accessed | tf_op | source)
XLA Modules:
  0.0 146.0 jit_solution(13825661308498429895)
XLA Ops:
  2.2 1.3 select_reduce_fusion.1
  3.4 1.4 convert_reduce_fusion
  6.0 7.4 %all-to-all-start = ((bf16[16,128,8]{1,2,0:T(8,128)(2,1)}), bf16[16,128,8]{1,2,0:T(8,128)(2,1)S(1)}, u32[]{:S(2)}, u32[]{:S(2)}) async-start(bf16[16,128,8]{1,2,0:T(8,128)(2,1)} %fusion.63), calls=%async_computation | async-start | bytes 65536 | tf_op jit(solution)/shard_map/all_to_all | solution.py:107
  14.1 2.3 %fusion.49 = f32[16,128,128]{1,2,0:T(8,128)S(1)} fusion(s32[16,128]{1,0:T(8,128)S(1)} %bitcast.131, pred[16,128]{1,0:T(8,128)(4,1)S(1)} %fusion.101), kind=kOutput, calls=%fused_computation.85 | convolution fusion | flops 67649536 | bytes 1058816 | tf_op jit(solution)/shard_map/ij,bjk->bik/dot_general | solution.py:69
  16.6 1.0 fusion.45
  17.7 1.1 select_reduce_fusion
  18.8 4.2 %fusion.19 = bf16[2048,256]{1,0:T(8,128)(2,1)} fusion(bf16[2048,256]{1,0:T(8,128)(2,1)S(1)} %copy-done, s32[2048]{0:T(1024)S(1)} %fusion.72), kind=kOutput, calls=%fused_computation.29 | convolution fusion | flops 2152202240 | bytes 2105344 | tf_op jit(solution)/shard_map/dot_general | solution.py:106
  22.9 6.2 %all-to-all-start.1 = ((bf16[16,128,256]{2,1,0:T(8,128)(2,1)}), bf16[16,128,256]{2,1,0:T(8,128)(2,1)}, u32[]{:S(2)}, u32[]{:S(2)}) async-start(bf16[16,128,256]{2,1,0:T(8,128)(2,1)} %bitcast.125), calls=%async_computation.1 | async-start | bytes 2097152 | tf_op jit(solution)/shard_map/all_to_all | solution.py:108
  32.9 19.2 %all-to-all-done.1 = bf16[16,128,256]{2,1,0:T(8,128)(2,1)} async-done(((bf16[16,128,256]{2,1,0:T(8,128)(2,1)}), bf16[16,128,256]{2,1,0:T(8,128)(2,1)}, u32[]{:S(2)}, u32[]{:S(2)}) %all-to-all-start.1) | async-done | bytes 1048608 | tf_op jit(solution)/shard_map/all_to_all | solution.py:108
  52.1 4.5 %fusion.20 = bf16[2048,256]{1,0:T(8,128)(2,1)S(1)} fusion(bf16[2048,256]{1,0:T(8,128)(2,1)} %bitcast.11, s32[2048]{0:T(1024)S(1)} %select_bitcast_fusion), kind=kOutput, calls=%fused_computation.30 | convolution fusion | flops 2152202240 | bytes 2105344 | tf_op jit(solution)/shard_map/dot_general | solution.py:126
  56.6 1.5 %fusion.22 = bf16[8,256,256]{2,1,0:T(8,128)(2,1)S(1)} fusion(bf16[8,256,256]{2,1,0:T(8,128)(2,1)S(1)} %bitcast.136, bf16[2,768,256]{2,1,0:T(8,128)(2,1)S(1)} %bitcast.129, bf16[8,254,256]{2,1,0:T(8,128)(2,1)S(1)} %bitcast.137, bf16[8,255,256]{2,1,0:T(8,128)(2,1)S(1)} %bitcast.138), kind=kOutput, calls=%fused_computation.32 | convolution fusion | flops 827850752 | bytes 5636096 | tf_op jit(solution)/shard_map/dot_general | solution.py:49
  58.3 2.5 %fusion.21 = (bf16[8,256,256]{2,1,0:T(8,128)(2,1)S(1)}, f32[8,256,256]{2,1,0:T(8,128)}) fusion(bf16[8,256,256]{2,1,0:T(8,128)(2,1)S(1)} %bitcast.139, bf16[2,768,256]{2,1,0:T(8,128)(2,1)S(1)} %bitcast.121, bf16[8,254,256]{2,1,0:T(8,128)(2,1)S(1)} %bitcast.140, bf16[8,255,256]{2,1,0:T(8,128)(2,1)S(1)} %bitcast.141), kind=kOutput, calls=%fused_computation.31 | convolution fusion | flops 827850752 | bytes 7733248 | tf_op jit(solution)/shard_map/dot_general | solution.py:49
  60.8 2.5 %fusion.94 = (bf16[8,256]{1,0:T(8,128)(2,1)S(1)}, bf16[8,256,256]{2,1,0:T(8,128)(2,1)S(1)}, f32[8,256,256]{2,1,0:T(8,128)}) fusion(bf16[8,256,256]{2,1,0:T(8,128)(2,1)S(1)} %get-tuple-element.28, bf16[2,768,256]{2,1,0:T(8,128)(2,1)S(1)} %bitcast.122, bf16[8,248,256]{2,1,0:T(8,128)(2,1)S(1)} %slice.87, bf16[8,252,256]{2,1,0:T(8,128)(2,1)S(1)} %bitcast.126), kind=kOutput, calls=%fused_computation.164 | convolution fusion | flops 828372992 | bytes 7704576 | tf_op jit(solution)/shard_map/dot_general | solution.py:49
  63.3 1.8 %fusion.29 = (f32[8,256]{1,0:T(8,128)S(1)}, f32[8,256]{1,0:T(8,128)S(1)}, f32[256]{0:T(256)S(1)}, bf16[8,256,256]{2,1,0:T(8,128)(2,1)S(1)}) fusion(bf16[8,256,256]{2,1,0:T(8,128)(2,1)S(1)} %get-tuple-element.15, f32[8,256]{1,0:T(8,128)S(1)} %fusion.76, f32[8,256]{1,0:T(8,128)S(1)} %bitcast.133, bf16[2,768,256]{2,1,0:T(8,128)(2,1)S(1)} %bitcast.130, ...), kind=kOutput, calls=%fused_computation.39 | convolution fusion | flops 832040704 | bytes 6685696 | tf_op jit(solution)/shard_map/dot_general | solution.py:49
  65.8 6.9 %all-to-all-start.2 = ((f32[16,1,384]{2,1,0:T(1,128)}), f32[16,1,384]{2,1,0:T(1,128)S(1)}, u32[]{:S(2)}, u32[]{:S(2)}) async-start(f32[16,1,384]{2,1,0:T(1,128)} %broadcast_in_dim.57), calls=%async_computation.2 | async-start | bytes 49152 | tf_op jit(solution)/shard_map/all_to_all | solution.py:183
  72.7 6.5 %all-to-all-done.2 = f32[16,1,384]{2,1,0:T(1,128)S(1)} async-done(((f32[16,1,384]{2,1,0:T(1,128)}), f32[16,1,384]{2,1,0:T(1,128)S(1)}, u32[]{:S(2)}, u32[]{:S(2)}) %all-to-all-start.2) | async-done | bytes 24608 | tf_op jit(solution)/shard_map/all_to_all | solution.py:183
  81.8 3.7 %multiply_convert_fusion = bf16[8,256,256]{2,1,0:T(8,128)(2,1)S(1)} fusion(f32[8,256,256]{2,1,0:T(8,128)S(1)} %copy-done.6, f32[8,256]{1,0:T(8,128)S(1)} %fusion.36, f32[8,256]{1,0:T(8,128)S(1)} %fusion.33, f32[256]{0:T(256)S(1)} %slice_divide_fusion, bf16[8,256,256]{2,1,0:T(8,128)(2,1)S(1)} %get-tuple-element.31, f32[8,256]{1,0:T(8,128)S(1)} %get-tuple-element.5, ...), kind=kLoop, calls=%fused_computation.55 | loop fusion | flops 10485760 | bytes 5284864 | tf_op jit(solution)/shard_map/convert_element_type | solution.py:198
  85.5 1.0 convolution_bitcast_fusion
  86.5 1.0 fusion.43
  88.4 1.1 copy-done.18
  90.2 3.1 %convolution_bitcast_fusion.1 = f32[1,768,256]{2,1,0:T(8,128)S(1)} fusion(f32[8,256,3,256]{3,1,0,2:T(8,128)S(1)} %fusion.43, f32[8,256,256]{2,1,0:T(8,128)S(1)} %copy-done.18, f32[8,248,256]{2,1,0:T(8,128)S(1)} %slice.97, f32[8,252,256]{2,1,0:T(8,128)S(1)} %slice.95, bf16[8,256,256]{2,1,0:T(8,128)(2,1)S(1)} %copy-done.9, ...), kind=kOutput, calls=%fused_computation.72 | convolution fusion | flops 836239360 | bytes 14394368 | tf_op jit(solution)/shard_map/dot_general | solution.py:200
  94.3 2.4 %collective-permute-done = f32[2,384,256]{2,1,0:T(8,128)} collective-permute-done((f32[2,384,256]{2,1,0:T(8,128)S(1)}, f32[2,384,256]{2,1,0:T(8,128)}, u32[]{:S(2)}, u32[]{:S(2)}) %collective-permute-start) | collective-permute-done | bytes 786464 | tf_op jit(solution)/shard_map/ppermute | solution.py:156
  96.7 1.3 fusion.55
  98.6 7.4 %collective-permute-done.1 = f32[2,192,256]{2,1,0:T(8,128)S(1)} collective-permute-done((f32[2,192,256]{2,1,0:T(8,128)S(1)}, f32[2,192,256]{2,1,0:T(8,128)S(1)}, u32[]{:S(2)}, u32[]{:S(2)}) %collective-permute-start.1) | collective-permute-done | bytes 393248 | tf_op jit(solution)/shard_map/ppermute | solution.py:156
  106.5 7.3 %collective-permute-done.2 = f32[2,96,256]{2,1,0:T(8,128)S(1)} collective-permute-done((f32[2,96,256]{2,1,0:T(8,128)S(1)}, f32[2,96,256]{2,1,0:T(8,128)S(1)}, u32[]{:S(2)}, u32[]{:S(2)}) %collective-permute-start.2) | collective-permute-done | bytes 196640 | tf_op jit(solution)/shard_map/ppermute | solution.py:156
  113.9 5.5 %collective-permute-done.3 = f32[2,48,256]{2,1,0:T(8,128)S(1)} collective-permute-done((f32[2,48,256]{2,1,0:T(8,128)S(1)}, f32[2,48,256]{2,1,0:T(8,128)S(1)}, u32[]{:S(2)}, u32[]{:S(2)}) %collective-permute-start.3) | collective-permute-done | bytes 98336 | tf_op jit(solution)/shard_map/ppermute | solution.py:156
  119.5 5.5 %collective-permute-done.4 = bf16[2,48,256]{2,1,0:T(8,128)(2,1)S(1)} collective-permute-done((bf16[2,48,256]{2,1,0:T(8,128)(2,1)S(1)}, bf16[2,48,256]{2,1,0:T(8,128)(2,1)S(1)}, u32[]{:S(2)}, u32[]{:S(2)}) %collective-permute-start.4) | collective-permute-done | bytes 49184 | tf_op jit(solution)/shard_map/ppermute | solution.py:160
  125.2 5.6 %collective-permute-done.5 = bf16[2,96,256]{2,1,0:T(8,128)(2,1)S(1)} collective-permute-done((bf16[2,96,256]{2,1,0:T(8,128)(2,1)S(1)}, bf16[2,96,256]{2,1,0:T(8,128)(2,1)S(1)}, u32[]{:S(2)}, u32[]{:S(2)}) %collective-permute-start.5) | collective-permute-done | bytes 98336 | tf_op jit(solution)/shard_map/ppermute | solution.py:160
  131.3 5.3 %collective-permute-done.6 = bf16[2,192,256]{2,1,0:T(8,128)(2,1)S(1)} collective-permute-done((bf16[2,192,256]{2,1,0:T(8,128)(2,1)S(1)}, bf16[2,192,256]{2,1,0:T(8,128)(2,1)S(1)}, u32[]{:S(2)}, u32[]{:S(2)}) %collective-permute-start.6) | collective-permute-done | bytes 196640 | tf_op jit(solution)/shard_map/ppermute | solution.py:160
  137.5 1.0 collective-permute-done.7
  138.8 1.2 copy.94
  141.0 5.0 %multiply_add_fusion = (f32[2,196608]{1,0:T(2,128)}, f32[2,196608]{1,0:T(2,128)}, f32[2,196608]{1,0:T(2,128)}) fusion(f32[2,196608]{1,0:T(2,128)S(1)} %copy-done.2, f32[2,196608]{1,0:T(2,128)S(1)} %copy-done.4, f32[2,196608]{1,0:T(2,128)S(1)} %bitcast.120, f32[2,196608]{1,0:T(2,128)S(1)} %copy-done.7), kind=kLoop, calls=%fused_computation.68 | loop fusion | flops 2752512 | bytes 11010048 | tf_op jit(solution)/shard_map/add | solution.py:221
  (104 shorter events, 16.4 us)
Async XLA Ops:
  0.6 18.2 %copy-start = (bf16[2048,256]{1,0:T(8,128)(2,1)S(1)}, bf16[2048,256]{1,0:T(8,128)(2,1)}, u32[]{:S(2)}) copy-start(bf16[2048,256]{1,0:T(8,128)(2,1)} %param.6) | copy-start | bytes 3145732
  0.6 18.1 %copy-start.15 = (s32[2048]{0:T(1024)S(1)}, s32[2048]{0:T(1024)}, u32[]{:S(2)}) copy-start(s32[2048]{0:T(1024)} %param.7) | copy-start | bytes 24580
  6.0 17.0 %all-to-all-start = ((bf16[16,128,8]{1,2,0:T(8,128)(2,1)}), bf16[16,128,8]{1,2,0:T(8,128)(2,1)S(1)}, u32[]{:S(2)}, u32[]{:S(2)}) async-start(bf16[16,128,8]{1,2,0:T(8,128)(2,1)} %fusion.63), calls=%async_computation | async-start | bytes 65536 | tf_op jit(solution)/shard_map/all_to_all | solution.py:107
  22.9 6.2 %copy-start.1 = (f32[2,196608]{1,0:T(2,128)S(1)}, f32[2,196608]{1,0:T(2,128)}, u32[]{:S(2)}) copy-start(f32[2,196608]{1,0:T(2,128)} %param.11) | copy-start | bytes 4718596
  22.9 29.2 %all-to-all-start.1 = ((bf16[16,128,256]{2,1,0:T(8,128)(2,1)}), bf16[16,128,256]{2,1,0:T(8,128)(2,1)}, u32[]{:S(2)}, u32[]{:S(2)}) async-start(bf16[16,128,256]{2,1,0:T(8,128)(2,1)} %bitcast.125), calls=%async_computation.1 | async-start | bytes 2097152 | tf_op jit(solution)/shard_map/all_to_all | solution.py:108
  29.2 1.7 %copy-start.3 = (f32[2,196608]{1,0:T(2,128)S(1)}, f32[2,196608]{1,0:T(2,128)}, u32[]{:S(2)}) copy-start(f32[2,196608]{1,0:T(2,128)} %param.9) | copy-start | bytes 4718596
  52.1 4.5 %copy-start.14 = (bf16[1,2,768,256]{3,2,1,0:T(8,128)(2,1)S(1)}, bf16[1,2,768,256]{3,2,1,0:T(8,128)(2,1)}, u32[]{:S(2)}) copy-start(bf16[1,2,768,256]{3,2,1,0:T(8,128)(2,1)} %copy.101) | copy-start | bytes 2359300
  56.6 1.6 %copy-start.16 = (bf16[2048,256]{1,0:T(8,128)(2,1)}, bf16[2048,256]{1,0:T(8,128)(2,1)S(1)}, u32[]{:S(2)}) copy-start(bf16[2048,256]{1,0:T(8,128)(2,1)S(1)} %fusion.20) | copy-start | bytes 3145732
  60.8 2.6 %copy-start.12 = (bf16[8,256,256]{2,1,0:T(8,128)(2,1)}, bf16[8,256,256]{2,1,0:T(8,128)(2,1)S(1)}, u32[]{:S(2)}) copy-start(bf16[8,256,256]{2,1,0:T(8,128)(2,1)S(1)} %get-tuple-element.28) | copy-start | bytes 3145732
  60.8 2.5 %copy-start.10 = (bf16[8,248,256]{2,1,0:T(8,128)(2,1)}, bf16[8,248,256]{2,1,0:T(8,128)(2,1)S(1)}, u32[]{:S(2)}) copy-start(bf16[8,248,256]{2,1,0:T(8,128)(2,1)S(1)} %slice.87) | copy-start | bytes 3047428
  63.3 1.9 %copy-start.8 = (bf16[8,256,256]{2,1,0:T(8,128)(2,1)}, bf16[8,256,256]{2,1,0:T(8,128)(2,1)S(1)}, u32[]{:S(2)}) copy-start(bf16[8,256,256]{2,1,0:T(8,128)(2,1)S(1)} %get-tuple-element.15) | copy-start | bytes 3145732
  65.8 13.4 %all-to-all-start.2 = ((f32[16,1,384]{2,1,0:T(1,128)}), f32[16,1,384]{2,1,0:T(1,128)S(1)}, u32[]{:S(2)}, u32[]{:S(2)}) async-start(f32[16,1,384]{2,1,0:T(1,128)} %broadcast_in_dim.57), calls=%async_computation.2 | async-start | bytes 49152 | tf_op jit(solution)/shard_map/all_to_all | solution.py:183
  79.3 2.4 %copy-start.6 = (f32[8,256,256]{2,1,0:T(8,128)S(1)}, f32[8,256,256]{2,1,0:T(8,128)}, u32[]{:S(2)}) copy-start(f32[8,256,256]{2,1,0:T(8,128)} %get-tuple-element.30) | copy-start | bytes 6291460
  81.7 3.7 %copy-start.11 = (bf16[8,248,256]{2,1,0:T(8,128)(2,1)S(1)}, bf16[8,248,256]{2,1,0:T(8,128)(2,1)}, u32[]{:S(2)}) copy-start(bf16[8,248,256]{2,1,0:T(8,128)(2,1)} %copy-done.10) | copy-start | bytes 3047428
  81.7 3.7 %copy-start.13 = (bf16[8,256,256]{2,1,0:T(8,128)(2,1)S(1)}, bf16[8,256,256]{2,1,0:T(8,128)(2,1)}, u32[]{:S(2)}) copy-start(bf16[8,256,256]{2,1,0:T(8,128)(2,1)} %copy-done.12) | copy-start | bytes 3145732
  87.9 1.6 %copy-start.18 = (f32[8,256,256]{2,1,0:T(8,128)S(1)}, f32[8,256,256]{2,1,0:T(8,128)}, u32[]{:S(2)}) copy-start(f32[8,256,256]{2,1,0:T(8,128)} %get-tuple-element.29) | copy-start | bytes 6291460
  88.2 1.7 %copy-start.9 = (bf16[8,256,256]{2,1,0:T(8,128)(2,1)S(1)}, bf16[8,256,256]{2,1,0:T(8,128)(2,1)}, u32[]{:S(2)}) copy-start(bf16[8,256,256]{2,1,0:T(8,128)(2,1)} %copy-done.8) | copy-start | bytes 3145732
  88.2 2.0 %copy-start.17 = (bf16[2048,256]{1,0:T(8,128)(2,1)S(1)}, bf16[2048,256]{1,0:T(8,128)(2,1)}, u32[]{:S(2)}) copy-start(bf16[2048,256]{1,0:T(8,128)(2,1)} %copy-done.16) | copy-start | bytes 3145732
  93.3 0.9 copy-start.5
  94.2 2.5 %collective-permute-start = (f32[2,384,256]{2,1,0:T(8,128)S(1)}, f32[2,384,256]{2,1,0:T(8,128)}, u32[]{:S(2)}, u32[]{:S(2)}) collective-permute-start(f32[2,384,256]{2,1,0:T(8,128)S(1)} %fusion.53), channel_id=1, source_target_pairs={{0,1},{1,0},{2,3},{3,2},{4,5},{5,4},{6,7},{7,6},{8,9},{9,8},{10,11... | collective-permute-start | bytes 2359304 | tf_op jit(solution)/shard_map/ppermute | solution.py:156
  98.1 7.8 %collective-permute-start.1 = (f32[2,192,256]{2,1,0:T(8,128)S(1)}, f32[2,192,256]{2,1,0:T(8,128)S(1)}, u32[]{:S(2)}, u32[]{:S(2)}) collective-permute-start(f32[2,192,256]{2,1,0:T(8,128)S(1)} %constant_dynamic-slice_fusion.1), channel_id=1, source_target_pairs={{0,2},{1,5},{2,0},{3,7},{4,6},{5,1},{6,4},{7,3},{8,10},{9,13},{10,... | collective-permute-start | bytes 1179656 | tf_op jit(solution)/shard_map/ppermute | solution.py:156
  106.0 7.8 %collective-permute-start.2 = (f32[2,96,256]{2,1,0:T(8,128)S(1)}, f32[2,96,256]{2,1,0:T(8,128)S(1)}, u32[]{:S(2)}, u32[]{:S(2)}) collective-permute-start(f32[2,96,256]{2,1,0:T(8,128)S(1)} %constant_dynamic-slice_fusion), channel_id=1, source_target_pairs={{0,4},{1,9},{2,6},{3,11},{4,0},{5,13},{6,2},{7,15},{8,12},{9,1},{1... | collective-permute-start | bytes 589832 | tf_op jit(solution)/shard_map/ppermute | solution.py:156
  113.8 5.6 %collective-permute-start.3 = (f32[2,48,256]{2,1,0:T(8,128)S(1)}, f32[2,48,256]{2,1,0:T(8,128)S(1)}, u32[]{:S(2)}, u32[]{:S(2)}) collective-permute-start(f32[2,48,256]{2,1,0:T(8,128)S(1)} %constant_dynamic-slice_fusion.2), channel_id=1, source_target_pairs={{0,8},{1,3},{2,10},{3,1},{4,12},{5,7},{6,14},{7,5},{8,0},{9,11},{1... | collective-permute-start | bytes 294920 | tf_op jit(solution)/shard_map/ppermute | solution.py:156
  119.5 5.6 %collective-permute-start.4 = (bf16[2,48,256]{2,1,0:T(8,128)(2,1)S(1)}, bf16[2,48,256]{2,1,0:T(8,128)(2,1)S(1)}, u32[]{:S(2)}, u32[]{:S(2)}) collective-permute-start(bf16[2,48,256]{2,1,0:T(8,128)(2,1)S(1)} %add_convert_fusion.2), channel_id=1, source_target_pairs={{0,8},{1,3},{2,10},{3,1},{4,12},{5,7},{6,14},{7,5},{8,0},{9,11},{1... | collective-permute-start | bytes 147464 | tf_op jit(solution)/shard_map/ppermute | solution.py:160
  125.1 5.7 %collective-permute-start.5 = (bf16[2,96,256]{2,1,0:T(8,128)(2,1)S(1)}, bf16[2,96,256]{2,1,0:T(8,128)(2,1)S(1)}, u32[]{:S(2)}, u32[]{:S(2)}) collective-permute-start(bf16[2,96,256]{2,1,0:T(8,128)(2,1)S(1)} %pad_maximum_fusion.2), channel_id=1, source_target_pairs={{0,4},{1,9},{2,6},{3,11},{4,0},{5,13},{6,2},{7,15},{8,12},{9,1},{1... | collective-permute-start | bytes 294920 | tf_op jit(solution)/shard_map/ppermute | solution.py:160
  130.8 5.7 %collective-permute-start.6 = (bf16[2,192,256]{2,1,0:T(8,128)(2,1)S(1)}, bf16[2,192,256]{2,1,0:T(8,128)(2,1)S(1)}, u32[]{:S(2)}, u32[]{:S(2)}) collective-permute-start(bf16[2,192,256]{2,1,0:T(8,128)(2,1)S(1)} %pad_maximum_fusion.1), channel_id=1, source_target_pairs={{0,2},{1,5},{2,0},{3,7},{4,6},{5,1},{6,4},{7,3},{8,10},{9,13},{10,... | collective-permute-start | bytes 589832 | tf_op jit(solution)/shard_map/ppermute | solution.py:160
  136.7 1.8 %collective-permute-start.7 = (bf16[2,384,256]{2,1,0:T(8,128)(2,1)S(1)}, bf16[2,384,256]{2,1,0:T(8,128)(2,1)S(1)}, u32[]{:S(2)}, u32[]{:S(2)}) collective-permute-start(bf16[2,384,256]{2,1,0:T(8,128)(2,1)S(1)} %pad_maximum_fusion), channel_id=1, source_target_pairs={{0,1},{1,0},{2,3},{3,2},{4,5},{5,4},{6,7},{7,6},{8,9},{9,8},{10,11... | collective-permute-start | bytes 1179656 | tf_op jit(solution)/shard_map/ppermute | solution.py:160
  138.6 1.4 copy-start.7
  138.8 1.8 %copy-start.2 = (f32[2,196608]{1,0:T(2,128)S(1)}, f32[2,196608]{1,0:T(2,128)}, u32[]{:S(2)}) copy-start(f32[2,196608]{1,0:T(2,128)} %param.11) | copy-start | bytes 4718596
  138.8 2.2 %copy-start.4 = (f32[2,196608]{1,0:T(2,128)S(1)}, f32[2,196608]{1,0:T(2,128)}, u32[]{:S(2)}) copy-start(f32[2,196608]{1,0:T(2,128)} %param.9) | copy-start | bytes 4718596
